TPU v7x, 128 devices: a whole 4x4x4 slice. The times are simulated.
128 devices in a mesh: tok: 8 (over z, y_hi), head: 16 (over x, y_lo, core).
Axes of the slice: x: 4, y: 4 (y_hi: 2, y_lo: 2; y = y_hi * 2 + y_lo), z: 4, core: 2. Of those that a mesh axis runs over, the one named last changes fastest.
Arguments:
- states: bfloat16 [4096, 4096], P('tok', 'head'), may hold values from -400 to 400
- pre_gain: float32 [4096], replicated, may hold values from 0.5 to 1.5
- pre_shift: float32 [4096], replicated, may hold values from -1.75 to 1.75
- mlp_gain: float32 [4096], replicated, may hold values from 0.5 to 1.5
- mlp_shift: float32 [4096], replicated, may hold values from -1.75 to 1.75
- qkv_weight: bfloat16 [4096, 12288], P('tok', 'head'), may hold values from -0.09375 to 0.09375
- qkv_bias: float32 [12288], P('head'), may hold values from -1.75 to 1.75
- out_weight: bfloat16 [4096, 4096], P('head', 'tok'), may hold values from -0.125 to 0.125
- out_bias: float32 [4096], P('head'), may hold values from -1.75 to 1.75
- up_weight: bfloat16 [4096, 16384], P(None, 'head'), may hold values from -0.09375 to 0.09375
- up_bias: float32 [16384], P('head'), may hold values from -1.75 to 1.75
- down_weight: bfloat16 [16384, 4096], P('head'), may hold values from -0.0625 to 0.0625
- down_bias: float32 [4096], P('head'), may hold values from -1.75 to 1.75
- kv_cache: bfloat16 [1152, 2, 16, 4096], P(('tok', 'head')), may hold values from -320 to 320, as said below
- token_request: int32 [4096], P('tok'), may hold values from 0 to 15, as said below
- cached_len: int32 [16], P('tok'), may hold values from 128 to 1024, as said below
- page_table: int32 [16, 64], P('tok'), may hold values from 0 to 143, as said below
- migrations: int32 [64, 2], P('tok'), may hold values from 0 to 143, as said below
Outputs:
- update: bfloat16 [4096, 4096], P('tok', 'head')
Inputs may be any that keep to these rules, and one draw needn't show every extreme that they name: `token_request`: ids never fall; the tokens of request r lie among tokens (r // 2) * 512 to that plus 512 - 1, and every request has one token or more. `cached_len`: some request holds exactly 1024. `page_table`: the entries of one block are distinct. `migrations`: targets of one block are distinct and none is also a source of that block. `kv_cache`: keys are stored already rotated.
All inputs are finite; a program needn't handle non-finite values.
Results may differ from a plain program's by a relative error of at most 0.018.
The roundings to bfloat16 on the way count: a program that leaves them out, or rounds other values in their place, can miss the bound.
Values may be sent and summed in bfloat16 or wider, within the bound.
No kernel may reach another device: no remote copies, remote signals or barrier semaphores. Data moves between devices by JAX's collectives and lax.ppermute only.
A program may use at most 128 MiB of HBM per device.

v0:
```python
import jax
import jax.numpy as jnp
from jax import lax
from jax.sharding import PartitionSpec as P

HD = 128
ROT = 32


epsilon = 1e-05


def layer_norm(wide, gain, shift):
    row_mean = jnp.mean(wide, axis=1, keepdims=True)
    centred = wide - row_mean
    row_var = jnp.mean(centred * centred, axis=1, keepdims=True)
    return (centred * lax.rsqrt(row_var + epsilon) * gain + shift).astype(jnp.bfloat16)


def rotate(vectors, positions):
    half_rot = ROT // 2
    inv_freq = 10000.0 ** (-2.0 * jnp.arange(half_rot, dtype=jnp.float32) / ROT)
    angles = positions.astype(jnp.float32)[:, None] * inv_freq[None, :]
    cosine = jnp.cos(angles)[:, None, :]
    sine_part = jnp.sin(angles)[:, None, :]
    lower_half = vectors[..., :half_rot]
    upper_half = vectors[..., half_rot:ROT]
    return jnp.concatenate(
        [
            lower_half * cosine - upper_half * sine_part,
            upper_half * cosine + lower_half * sine_part,
            vectors[..., ROT:],
        ],
        axis=-1,
    )


def token_positions(local_req, cached):
    onehot = local_req[:, None] == jnp.arange(cached.shape[0], dtype=jnp.int32)[None, :]
    stretch_sizes = jnp.sum(onehot.astype(jnp.int32), axis=0)
    starts = jnp.cumsum(stretch_sizes) - stretch_sizes
    own_start = jnp.sum(jnp.where(onehot, starts[None, :], 0), axis=1)
    own_cached = jnp.sum(jnp.where(onehot, cached[None, :], 0), axis=1)
    return own_cached + jnp.arange(local_req.shape[0], dtype=jnp.int32) - own_start


def attend(queries, new_keys, new_values, cache_keys, cache_values, local_req, cached, positions):
    span = cache_keys.shape[0] // cached.shape[0]
    key_slot = jnp.arange(cache_keys.shape[0], dtype=jnp.int32)
    key_owner = key_slot // span
    key_place = key_slot % span
    cache_ok = (local_req[:, None] == key_owner[None, :]) & (
        key_place[None, :] < jnp.repeat(cached, span)[None, :]
    )
    new_ok = (local_req[:, None] == local_req[None, :]) & (positions[None, :] <= positions[:, None])
    allowed = jnp.concatenate([cache_ok, new_ok], axis=1)
    all_keys = jnp.concatenate([cache_keys, new_keys], axis=0)
    all_values = jnp.concatenate([cache_values, new_values], axis=0)
    scores = jnp.einsum(
        "thd,khd->htk", queries, all_keys, preferred_element_type=jnp.float32
    ) * HD ** (-0.5)
    scores = jnp.where(allowed[None], scores, -1e30)
    peak = jnp.max(scores, axis=2, keepdims=True)
    exp_scores = jnp.exp(scores - peak)
    attn_probs = (exp_scores / jnp.sum(exp_scores, axis=2, keepdims=True)).astype(jnp.bfloat16)
    return jnp.einsum(
        "htk,khd->thd", attn_probs, all_values, preferred_element_type=jnp.float32
    ).astype(jnp.bfloat16)


def share_pages(local_pool, groups):
    grouped = local_pool.reshape(
        local_pool.shape[0], 2, local_pool.shape[2], groups, local_pool.shape[3] // groups
    )
    shared = lax.all_to_all(grouped, "head", split_axis=3, concat_axis=0, tiled=True)
    return shared.reshape(shared.shape[0], 2, shared.shape[2], shared.shape[4])


def shards(
    states,
    pre_gain,
    pre_shift,
    mlp_gain,
    mlp_shift,
    qkv_weight,
    qkv_bias,
    out_weight,
    out_bias,
    up_weight,
    up_bias,
    down_weight,
    down_bias,
    kv_cache,
    token_request,
    cached_len,
    page_table,
    migrations,
):
    gathered = lax.all_gather(states, "head", axis=1, tiled=True)
    wide = gathered.astype(jnp.float32)
    pre_normed = layer_norm(wide, pre_gain, pre_shift)
    mlp_normed = layer_norm(wide, mlp_gain, mlp_shift)
    tok_rows = gathered.shape[0]
    joined = jnp.dot(
        pre_normed,
        lax.all_gather(qkv_weight, "tok", axis=0, tiled=True),
        preferred_element_type=jnp.float32,
    )
    joined = (joined + qkv_bias).reshape(tok_rows, -1, 3, HD)
    local_req = token_request - lax.axis_index("tok") * cached_len.shape[0]
    positions = token_positions(local_req, cached_len)
    queries = rotate(joined[:, :, 0], positions).astype(jnp.bfloat16)
    new_keys = rotate(joined[:, :, 1], positions).astype(jnp.bfloat16)
    new_values = joined[:, :, 2].astype(jnp.bfloat16)
    head_groups = lax.axis_size("head")
    pool_size = kv_cache.shape[0]
    sources = migrations[:, 0]
    targets = migrations[:, 1]
    own_index = lax.axis_index("head")
    owner_mask = sources // pool_size == own_index
    picked = jnp.where(
        owner_mask[:, None, None, None], kv_cache[sources % pool_size], jnp.zeros((), jnp.bfloat16)
    )
    moved_pages = lax.psum(picked, "head").astype(jnp.float32).astype(jnp.bfloat16)
    landing = jnp.where(targets // pool_size == own_index, targets % pool_size, pool_size)
    local_pool = kv_cache.at[landing].set(moved_pages, mode="drop")
    page_pool = share_pages(local_pool, head_groups)
    pages = page_pool[page_table.reshape(-1)]
    cache_keys = pages[:, 0].reshape(-1, queries.shape[1], HD)
    cache_values = pages[:, 1].reshape(-1, queries.shape[1], HD)
    heads_out = attend(
        queries, new_keys, new_values, cache_keys, cache_values, local_req, cached_len, positions
    ).reshape(tok_rows, -1)
    attention_part = jnp.dot(
        heads_out,
        lax.all_gather(out_weight, "tok", axis=1, tiled=True),
        preferred_element_type=jnp.float32,
    )
    hidden = jax.nn.gelu(
        jnp.dot(mlp_normed, up_weight, preferred_element_type=jnp.float32) + up_bias,
        approximate=False,
    ).astype(jnp.bfloat16)
    feed_part = jnp.dot(hidden, down_weight, preferred_element_type=jnp.float32)
    summed = lax.psum_scatter(
        (attention_part + feed_part).astype(jnp.bfloat16), "head", scatter_dimension=1, tiled=True
    ).astype(jnp.float32)
    return (summed + out_bias + down_bias).astype(jnp.bfloat16)


def solution(mesh):
    in_specs = (
        P("tok", "head"),
        P(),
        P(),
        P(),
        P(),
        P("tok", "head"),
        P("head"),
        P("head", "tok"),
        P("head"),
        P(None, "head"),
        P("head"),
        P("head", None),
        P("head"),
        P(("tok", "head"), None, None, None),
        P("tok"),
        P("tok"),
        P("tok", None),
        P("tok", None),
    )
    out_specs = P("tok", "head")
    return jax.shard_map(shards, mesh=mesh, in_specs=in_specs, out_specs=out_specs, check_vma=False)
```

profile of v0, /device:TPU:0, one launch (start us, length us, event | category | flops | bytes accessed | tf_op | source)
XLA Modules:
  0.0 436.5 jit_solution(8468783990483172287)
XLA Ops:
  6.5 0.0 all-reduce.2.cloned.1.call-start
  6.5 1.7 copy.59
  8.2 0.0 copy-done.8
  8.3 2.0 gather_fusion
  10.3 3.1 broadcast_select_fusion
  13.4 0.0 all-reduce.2.cloned.1.call-update
  13.4 0.0 all-gather.4.cloned.1.call-start
  13.5 0.7 all-gather.4.cloned.1.call-update
  14.2 0.0 all-gather.6.cloned.1.call-start
  14.2 0.7 all-gather.6.cloned.1.call-update
  14.9 0.0 all-gather.8.cloned.1.call-start
  15.0 0.5 all-gather.8.cloned.1.call-update
  15.5 0.0 copy-done.5
  15.5 0.1 convert_reduce_fusion.1
  15.7 0.2 reduce-window.8
  15.8 0.0 copy-done.4
  15.8 0.1 select_reduce_fusion.1
  15.9 123.9 %all-reduce.2.cloned.1.call-done = bf16[8,2,16,4096]{3,2,1,0:T(8,128)(2,1)} async-done(((bf16[8,2,16,4096]{3,2,1,0:T(8,128)(2,1)}), bf16[8,2,16,4096]{3,2,1,0:T(8,128)(2,1)}) %all-reduce.2.cloned.1.call-update) | async-done | bytes 2097168 | tf_op jit(solution)/shard_map/psum | solution.py:124
  139.8 3.2 scatter_fusion
  143.0 1.8 copy.55
  144.8 4.8 %all-to-all-start = ((bf16[9,2,16,16,256]{4,2,1,0,3:T(8,128)(2,1)}), bf16[9,2,16,16,256]{4,2,1,0,3:T(8,128)(2,1)S(1)}, u32[]{:S(2)}, u32[]{:S(2)}) async-start(bf16[9,2,16,16,256]{4,2,1,0,3:T(8,128)(2,1)} %bitcast.48), calls=%async_computation | async-start | bytes 4718592 | tf_op jit(solution)/shard_map/all_to_all | solution.py:75
  149.6 0.0 reduce-scatter.2.cloned.1.call-start
  149.7 0.2 multiply_cosine_fusion
  149.9 0.1 copy.41
  150.0 0.8 copy.42
  150.9 0.1 reshape.237
  151.0 0.1 broadcast_bitcast_fusion
  151.1 0.3 compare_and_fusion.1
  151.3 0.7 compare_and_fusion
  152.1 1.2 pad_add_fusion
  153.3 33.0 %all-to-all-done = bf16[9,2,16,16,256]{4,2,1,0,3:T(8,128)(2,1)S(1)} async-done(((bf16[9,2,16,16,256]{4,2,1,0,3:T(8,128)(2,1)}), bf16[9,2,16,16,256]{4,2,1,0,3:T(8,128)(2,1)S(1)}, u32[]{:S(2)}, u32[]{:S(2)}) %all-to-all-start) | async-done | bytes 2359328 | tf_op jit(solution)/shard_map/all_to_all | solution.py:75
  186.3 2.0 gather_fusion.1
  188.3 1.7 fusion.146
  190.0 0.3 reshape_squeeze.7
  190.3 1.2 copy.44
  191.5 0.3 reshape_squeeze.6
  191.8 2.1 copy.39
  193.8 16.8 %all-gather.4.cloned.1.call-done = bf16[512,4096]{1,0:T(8,128)(2,1)} async-done(((bf16[512,256]{1,0:T(8,128)(2,1)}), bf16[512,4096]{1,0:T(8,128)(2,1)}) %all-gather.4.cloned.1.call-update) | async-done | bytes 4194320 | tf_op jit(solution)/shard_map/all_gather | solution.py:99
  210.6 3.0 convert_reduce_fusion
  213.6 0.5 copy-done
  214.1 1.2 fusion.9
  215.3 0.0 copy-start.11
  215.3 0.0 copy-start.12
  215.4 0.0 copy-start.14
  215.4 24.2 %fusion.40 = f32[512,4096]{1,0:T(8,128)} fusion(bf16[1024,4096]{1,0:T(8,128)(2,1)} %param.29, bf16[4096,1024]{1,0:T(8,128)(2,1)} %param.27, bf16[512,4096]{1,0:T(8,128)(2,1)} %all-gather.4.cloned.1.call-done, f32[4096]{0:T(1024)S(1)} %copy-done.9, f32[4096]{0:T(1024)S(1)} %copy-done.10, f32[512]{0:T(512)S(1)} %add_rsqrt_fusion, ...), kind=kOutput, calls=%fused_computation.57 | convolution fusion | flops 8637120512 | bytes 29401088 | tf_op jit(solution)/shard_map/dot_general | solution.py:143
  239.5 61.7 %all-gather.6.cloned.1.call-done = bf16[4096,768]{1,0:T(8,128)(2,1)} async-done(((bf16[512,768]{1,0:T(8,128)(2,1)}), bf16[4096,768]{1,0:T(8,128)(2,1)}) %all-gather.6.cloned.1.call-update) | async-done | bytes 6291472 | tf_op jit(solution)/shard_map/all_gather | solution.py:106
  301.2 0.0 copy-done.11
  301.2 0.0 copy-done.14
  301.2 9.1 %fusion.42 = f32[512,768]{1,0:T(8,128)} fusion(bf16[4096,768]{1,0:T(8,128)(2,1)} %all-gather.6.cloned.1.call-done, bf16[512,4096]{1,0:T(8,128)(2,1)} %all-gather.4.cloned.1.call-done, f32[4096]{0:T(1024)S(1)} %copy-done.11, f32[4096]{0:T(1024)S(1)} %copy-done.12, f32[512]{0:T(512)S(1)} %add_rsqrt_fusion, f32[512]{0:T(512)S(1)} %broadcast_multiply_fusion, ...), kind=kOutput, calls=%fused_computation.58 | convolution fusion | flops 3234201600 | bytes 12098560 | tf_op jit(solution)/shard_map/dot_general | solution.py:104
  310.4 1.9 copy.37
  312.3 0.1 fusion.147
  312.4 0.2 copy.45
  312.6 0.2 copy.46
  312.8 0.8 slice.83
  313.6 0.9 slice.84
  314.5 0.7 fusion.94
  315.2 2.2 subtract_convert_fusion.1
  317.4 10.0 %fusion.148 = (f32[2,512]{1,0:T(2,128)S(1)}, f32[2,512,2560]{2,1,0:T(8,128)}) fusion(pred[512,2560]{1,0:T(8,128)(4,1)S(1)} %copy-done.1, bf16[512,2,96]{2,0,1:T(8,128)(2,1)} %slice.83, bf16[512,2,16]{2,0,1:T(8,128)(2,1)S(1)} %get-tuple-element.17, bf16[512,2,16]{2,0,1:T(8,128)(2,1)} %get-tuple-element.18, bf16[2048,2,128]{2,0,1:T(8,128)(2,1)} %copy.44, ...), kind=kOutput, calls=%fused_computation.190 | convolution fusion | flops 687606272 | bytes 13373440 | tf_op jit(solution)/shard_map/sub | solution.py:64
  327.4 5.9 %fusion.56 = bf16[2,128,512]{2,1,0:T(8,128)(2,1)S(1)} fusion(f32[2,512,2560]{2,1,0:T(8,128)} %get-tuple-element.24, f32[2,512]{1,0:T(2,128)S(1)} %get-tuple-element.23, bf16[512,2,128]{0,2,1:T(8,128)(2,1)S(1)} %copy-done.3, bf16[2048,2,128]{0,2,1:T(8,128)(2,1)S(1)} %copy-done.2), kind=kOutput, calls=%fused_computation.70 | convolution fusion | flops 679084032 | bytes 12062720 | tf_op jit(solution)/shard_map/htk,khd->thd/dot_general | solution.py:66
  333.3 22.3 %all-gather.8.cloned.1.call-done = bf16[256,4096]{1,0:T(8,128)(2,1)} async-done(((bf16[256,512]{1,0:T(8,128)(2,1)}), bf16[256,4096]{1,0:T(8,128)(2,1)}) %all-gather.8.cloned.1.call-update) | async-done | bytes 2097168 | tf_op jit(solution)/shard_map/all_gather | solution.py:136
  355.6 7.2 %add_convert_fusion = bf16[512,4096]{1,0:T(8,128)(2,1)} fusion(f32[512,4096]{1,0:T(8,128)} %fusion.40, bf16[512,256]{0,1:T(8,128)(2,1)S(1)} %bitcast.56, bf16[256,4096]{1,0:T(8,128)(2,1)} %all-gather.8.cloned.1.call-done), kind=kOutput, calls=%fused_computation.18 | convolution fusion | flops 1077936128 | bytes 14942208 | tf_op jit(solution)/shard_map/dot_general | solution.py:134
  362.9 0.0 reduce-scatter.2.cloned.1.call-update
  362.9 65.4 %reduce-scatter.2.cloned.1.call-done = bf16[512,256]{1,0:T(8,128)(2,1)} async-done(((bf16[512,4096]{1,0:T(8,128)(2,1)}), bf16[512,256]{1,0:T(8,128)(2,1)}) %reduce-scatter.2.cloned.1.call-update) | async-done | bytes 262160 | tf_op jit(solution)/shard_map/reduce_scatter | solution.py:144
  428.3 1.7 add_convert_fusion.1
  (36 shorter events, 0.2 us)
Async XLA Ops:
  6.5 1.7 copy-start.8
  6.5 133.3 %all-reduce.2.cloned.1.call-start = ((), (), s32[]{:S(2)}) async-start(), calls=%async_computation.2 | async-start | bytes 4194304 | tf_op jit(solution)/shard_map/psum | solution.py:124
  13.4 2.1 copy-start.5
  13.4 2.4 copy-start.4
  13.4 197.2 %all-gather.4.cloned.1.call-start = ((), (), s32[]{:S(2)}) async-start(), calls=%async_computation.3 | async-start | bytes 4456448 | tf_op jit(solution)/shard_map/all_gather | solution.py:99
  14.2 287.0 %all-gather.6.cloned.1.call-start = ((), (), s32[]{:S(2)}) async-start(), calls=%async_computation.4 | async-start | bytes 7077888 | tf_op jit(solution)/shard_map/all_gather | solution.py:106
  14.9 340.7 %all-gather.8.cloned.1.call-start = ((), (), s32[]{:S(2)}) async-start(), calls=%async_computation.5 | async-start | bytes 2359296 | tf_op jit(solution)/shard_map/all_gather | solution.py:136
  144.8 6.1 %copy-start.15 = (s32[2,64]{1,0:T(2,128)S(1)}, s32[2,64]{1,0:T(2,128)}, u32[]{:S(2)}) copy-start(s32[2,64]{1,0:T(2,128)} %param.34) | copy-start | bytes 1540
  144.8 41.5 %all-to-all-start = ((bf16[9,2,16,16,256]{4,2,1,0,3:T(8,128)(2,1)}), bf16[9,2,16,16,256]{4,2,1,0,3:T(8,128)(2,1)S(1)}, u32[]{:S(2)}, u32[]{:S(2)}) async-start(bf16[9,2,16,16,256]{4,2,1,0,3:T(8,128)(2,1)} %bitcast.48), calls=%async_computation | async-start | bytes 4718592 | tf_op jit(solution)/shard_map/all_to_all | solution.py:75
  149.6 278.6 %reduce-scatter.2.cloned.1.call-start = ((), (), s32[]{:S(2)}) async-start(), calls=%async_computation.6 | async-start | bytes 4456448 | tf_op jit(solution)/shard_map/reduce_scatter | solution.py:144
  210.6 3.4 copy-start
  214.1 1.2 copy-start.9
  214.1 1.2 copy-start.10
  214.1 1.3 copy-start.13
  215.3 85.9 %copy-start.11 = (f32[4096]{0:T(1024)S(1)}, f32[4096]{0:T(1024)}, u32[]{:S(2)}) copy-start(f32[4096]{0:T(1024)} %param.20) | copy-start | bytes 49156
  215.3 85.9 %copy-start.12 = (f32[4096]{0:T(1024)S(1)}, f32[4096]{0:T(1024)}, u32[]{:S(2)}) copy-start(f32[4096]{0:T(1024)} %param.19) | copy-start | bytes 49156
  215.4 85.9 %copy-start.14 = (f32[768]{0:T(1024)S(1)}, f32[768]{0:T(1024)}, u32[]{:S(2)}) copy-start(f32[768]{0:T(1024)} %param.24) | copy-start | bytes 9220
  315.2 2.2 copy-start.1
  317.4 10.0 %copy-start.2 = (bf16[2048,2,128]{0,2,1:T(8,128)(2,1)S(1)}, bf16[2048,2,128]{0,2,1:T(8,128)(2,1)}, u32[]{:S(2)}) copy-start(bf16[2048,2,128]{0,2,1:T(8,128)(2,1)} %copy.39) | copy-start | bytes 3145732
  317.4 10.0 %copy-start.3 = (bf16[512,2,128]{0,2,1:T(8,128)(2,1)S(1)}, bf16[512,2,128]{0,2,1:T(8,128)(2,1)}, u32[]{:S(2)}) copy-start(bf16[512,2,128]{0,2,1:T(8,128)(2,1)} %fusion.94) | copy-start | bytes 786436
  362.9 65.4 %copy-start.6 = (f32[256]{0:T(256)S(1)}, f32[256]{0:T(256)}, u32[]{:S(2)}) copy-start(f32[256]{0:T(256)} %param.30) | copy-start | bytes 3076
  362.9 65.4 %copy-start.7 = (f32[256]{0:T(256)S(1)}, f32[256]{0:T(256)}, u32[]{:S(2)}) copy-start(f32[256]{0:T(256)} %param.26) | copy-start | bytes 3076
Sparse Core Ops, SparseCore 0:
  13.6 126.1 all-reduce.1
  141.4 69.1 all-gather.3
  212.9 88.2 all-gather.5
  303.3 52.3 all-gather.7
  363.0 65.1 reduce-scatter.1
where the time goes:
time: 437 us
  waiting for transfers between devices  325 us (74%)
  matrix products  56.5 us (13%)
  local copies, waits for them, and re-layouts  22.7 us (5%)
  other arithmetic  14.1 us (3%)
  between operations  13.4 us (3%)
  starting transfers between devices  4.98 us (1%)
    psum x1, waiting for transfers between devices, shards(): lax.psum(picked, 'head').astype(jnp.float32).astype(jnp.bfloat16)  124 us
    reduce_scatter x1, waiting for transfers between devices, shards(): lax.psum_scatter((attention_part + feed_part).astype(jnp.bfloat16), 'head...  65.4 us
    all_gather x1, waiting for transfers between devices, shards(): lax.all_gather(qkv_weight, 'tok', axis=0, tiled=True)  61.7 us
    all_to_all x1, waiting for transfers between devices, share_pages(): lax.all_to_all(grouped, 'head', split_axis=3, concat_axis=0, tiled=True)  33 us
    dot_general x1, matrix products, shards(): feed_part = jnp.dot(hidden, down_weight, preferred_element_type=jnp.float32)  24.2 us
    all_gather x1, waiting for transfers between devices, shards(): lax.all_gather(out_weight, 'tok', axis=1, tiled=True)  22.3 us
    all_gather x1, waiting for transfers between devices, shards(): gathered = lax.all_gather(states, 'head', axis=1, tiled=True)  16.8 us
    sub x1, matrix products, attend(): exp_scores = jnp.exp(scores - peak)  9.98 us
  transfers between devices with their start and end apart: 6, of which 6 were waited for; matrix products, arithmetic and copies ran while one was open for 18% of the time, Pallas kernels for 0%

commit v1 on v0

--- a/solution.py
+++ b/solution.py
@@ -113,19 +113,14 @@
     new_keys = rotate(joined[:, :, 1], positions).astype(jnp.bfloat16)
     new_values = joined[:, :, 2].astype(jnp.bfloat16)
     head_groups = lax.axis_size("head")
-    pool_size = kv_cache.shape[0]
     sources = migrations[:, 0]
     targets = migrations[:, 1]
-    own_index = lax.axis_index("head")
-    owner_mask = sources // pool_size == own_index
-    picked = jnp.where(
-        owner_mask[:, None, None, None], kv_cache[sources % pool_size], jnp.zeros((), jnp.bfloat16)
-    )
-    moved_pages = lax.psum(picked, "head").astype(jnp.float32).astype(jnp.bfloat16)
-    landing = jnp.where(targets // pool_size == own_index, targets % pool_size, pool_size)
-    local_pool = kv_cache.at[landing].set(moved_pages, mode="drop")
-    page_pool = share_pages(local_pool, head_groups)
-    pages = page_pool[page_table.reshape(-1)]
+    page_pool = share_pages(kv_cache, head_groups)
+    table = page_table.reshape(-1)
+    match = table[:, None] == targets[None, :]
+    moved_from = jnp.sum(jnp.where(match, sources[None, :], 0), axis=1)
+    table = jnp.where(jnp.any(match, axis=1), moved_from, table)
+    pages = page_pool[table]
     cache_keys = pages[:, 0].reshape(-1, queries.shape[1], HD)
     cache_values = pages[:, 1].reshape(-1, queries.shape[1], HD)
     heads_out = attend(

time: 437 us -> 306 us (0.70)
  waiting for transfers between devices: 325 us -> 204 us
  local copies, waits for them, and re-layouts: 22.7 us -> 16.1 us
    psum x1 -> x0, waiting for transfers between devices: 124 us -> none  [shards(): lax.psum(picked, 'head').astype(jnp.float32).astype(jnp.bfloat16)]
  transfers between devices with their start and end apart: 6 -> 5, of which waited for: 6 -> 5; matrix products, arithmetic and copies ran while one was open for 18% -> 24% of each run, Pallas kernels for 0% -> 0%
where the time goes in v1:
time: 306 us; the launch traced here: 305 us
  waiting for transfers between devices  204 us (67%)
  matrix products  54.7 us (18%)
  local copies, waits for them, and re-layouts  16.1 us (5%)
  between operations  13.3 us (4%)
  other arithmetic  11.2 us (4%)
  starting transfers between devices  5.76 us (2%)
    reduce_scatter x1, waiting for transfers between devices, shards(): lax.psum_scatter((attention_part + feed_part).astype(jnp.bfloat16), 'head...  65.4 us
    all_gather x1, waiting for transfers between devices, shards(): lax.all_gather(qkv_weight, 'tok', axis=0, tiled=True)  62.9 us
    all_to_all x1, waiting for transfers between devices, share_pages(): lax.all_to_all(grouped, 'head', split_axis=3, concat_axis=0, tiled=True)  30.2 us
    all_gather x1, waiting for transfers between devices, shards(): lax.all_gather(out_weight, 'tok', axis=1, tiled=True)  25.2 us
    dot_general x1, matrix products, shards(): feed_part = jnp.dot(hidden, down_weight, preferred_element_type=jnp.float32)  23.9 us
    all_gather x1, waiting for transfers between devices, shards(): gathered = lax.all_gather(states, 'head', axis=1, tiled=True)  18.5 us
    sub x1, matrix products, attend(): exp_scores = jnp.exp(scores - peak)  10.1 us
    dot_general x1, matrix products, shards(): jnp.dot(pre_normed, lax.all_gather(qkv_weight, 'tok', axis=0, tiled=True)...  7.6 us
  transfers between devices with their start and end apart: 5, of which 5 were waited for; matrix products, arithmetic and copies ran while one was open for 24% of the time, Pallas kernels for 0%

profile of v1, /device:TPU:0, one launch (start us, length us, event | category | flops | bytes accessed | tf_op | source)
XLA Modules:
  0.0 305.4 jit_solution(14172348098167316449)
XLA Ops:
  6.5 0.0 all-gather.4.cloned.1.call-start
  6.5 0.7 all-gather.4.cloned.1.call-update
  7.3 0.0 all-gather.6.cloned.1.call-start
  7.3 0.7 all-gather.6.cloned.1.call-update
  8.0 3.4 %copy.68 = bf16[9,2,2,16,8,256]{5,4,2,1,0,3:T(8,128)(2,1)} copy(bf16[9,2,2,16,8,256]{5,4,3,2,1,0:T(8,128)(2,1)} %bitcast.56) | data formatting | bytes 4718592 | tf_op jit(solution)/shard_map/reshape | solution.py:72
  11.4 5.6 %all-to-all-start = ((bf16[9,2,16,16,256]{4,2,1,0,3:T(8,128)(2,1)}), bf16[9,2,16,16,256]{4,2,1,0,3:T(8,128)(2,1)S(1)}, u32[]{:S(2)}, u32[]{:S(2)}) async-start(bf16[9,2,16,16,256]{4,2,1,0,3:T(8,128)(2,1)} %bitcast.48), calls=%async_computation | async-start | bytes 4718592 | tf_op jit(solution)/shard_map/all_to_all | solution.py:75
  17.1 0.0 all-gather.8.cloned.1.call-start
  17.1 0.7 all-gather.8.cloned.1.call-update
  17.8 0.0 reduce-scatter.2.cloned.1.call-start
  17.9 0.0 copy-done.5
  17.9 0.1 convert_reduce_fusion.1
  18.0 0.2 reduce-window.8
  18.2 0.0 copy-done.4
  18.2 0.1 select_reduce_fusion.1
  18.3 0.2 multiply_cosine_fusion
  18.5 0.0 copy-done.8
  18.5 0.0 copy-done.15
  18.5 0.1 eq.58
  18.6 0.1 reshape.210
  18.7 0.1 copy.54
  18.8 0.8 copy.55
  19.7 0.1 compare_reduce_fusion
  19.8 0.1 fusion.103
  19.9 0.1 broadcast_bitcast_fusion
  19.9 0.3 compare_and_fusion.1
  20.2 0.7 compare_and_fusion
  21.0 1.1 pad_add_fusion
  22.1 30.2 %all-to-all-done = bf16[9,2,16,16,256]{4,2,1,0,3:T(8,128)(2,1)S(1)} async-done(((bf16[9,2,16,16,256]{4,2,1,0,3:T(8,128)(2,1)}), bf16[9,2,16,16,256]{4,2,1,0,3:T(8,128)(2,1)S(1)}, u32[]{:S(2)}, u32[]{:S(2)}) %all-to-all-start) | async-done | bytes 2359328 | tf_op jit(solution)/shard_map/all_to_all | solution.py:75
  52.4 2.0 gather_fusion
  54.4 1.8 fusion.144
  56.2 0.3 reshape_squeeze.7
  56.5 1.1 copy.57
  57.6 0.3 reshape_squeeze.6
  57.9 2.1 copy.52
  60.0 18.5 %all-gather.4.cloned.1.call-done = bf16[512,4096]{1,0:T(8,128)(2,1)} async-done(((bf16[512,256]{1,0:T(8,128)(2,1)}), bf16[512,4096]{1,0:T(8,128)(2,1)}) %all-gather.4.cloned.1.call-update) | async-done | bytes 4194320 | tf_op jit(solution)/shard_map/all_gather | solution.py:99
  78.5 3.0 convert_reduce_fusion
  81.4 0.5 copy-done
  81.9 1.2 fusion.9
  83.2 0.0 copy-done.9
  83.2 0.0 copy-done.10
  83.2 0.0 copy-start.11
  83.2 0.0 copy-start.12
  83.2 0.0 copy-start.14
  83.2 23.9 %fusion.40 = f32[512,4096]{1,0:T(8,128)} fusion(bf16[1024,4096]{1,0:T(8,128)(2,1)} %param.29, bf16[4096,1024]{1,0:T(8,128)(2,1)} %param.27, bf16[512,4096]{1,0:T(8,128)(2,1)} %all-gather.4.cloned.1.call-done, f32[4096]{0:T(1024)S(1)} %copy-done.9, f32[4096]{0:T(1024)S(1)} %copy-done.10, f32[512]{0:T(512)S(1)} %add_rsqrt_fusion, ...), kind=kOutput, calls=%fused_computation.54 | convolution fusion | flops 8637120512 | bytes 29401088 | tf_op jit(solution)/shard_map/dot_general | solution.py:138
  107.1 62.9 %all-gather.6.cloned.1.call-done = bf16[4096,768]{1,0:T(8,128)(2,1)} async-done(((bf16[512,768]{1,0:T(8,128)(2,1)}), bf16[4096,768]{1,0:T(8,128)(2,1)}) %all-gather.6.cloned.1.call-update) | async-done | bytes 6291472 | tf_op jit(solution)/shard_map/all_gather | solution.py:106
  170.0 0.0 copy-done.11
  170.0 7.6 %fusion.42 = f32[512,768]{1,0:T(8,128)S(1)} fusion(bf16[4096,768]{1,0:T(8,128)(2,1)} %all-gather.6.cloned.1.call-done, bf16[512,4096]{1,0:T(8,128)(2,1)} %all-gather.4.cloned.1.call-done, f32[4096]{0:T(1024)S(1)} %copy-done.11, f32[4096]{0:T(1024)S(1)} %copy-done.12, f32[512]{0:T(512)S(1)} %add_rsqrt_fusion, f32[512]{0:T(512)S(1)} %broadcast_multiply_fusion, ...), kind=kOutput, calls=%fused_computation.55 | convolution fusion | flops 3234201600 | bytes 12098560 | tf_op jit(solution)/shard_map/dot_general | solution.py:104
  177.6 0.5 copy.50
  178.1 0.1 fusion.145
  178.1 0.2 copy.58
  178.3 0.2 copy.59
  178.5 0.8 slice.80
  179.4 0.9 slice.81
  180.3 0.7 fusion.94
  181.0 2.3 subtract_convert_fusion.1
  183.3 10.1 %fusion.146 = (f32[2,512]{1,0:T(2,128)S(1)}, f32[2,512,2560]{2,1,0:T(8,128)}) fusion(pred[512,2560]{1,0:T(8,128)(4,1)S(1)} %copy-done.1, bf16[512,2,96]{2,0,1:T(8,128)(2,1)} %slice.80, bf16[512,2,16]{2,0,1:T(8,128)(2,1)} %get-tuple-element.17, bf16[512,2,16]{2,0,1:T(8,128)(2,1)} %get-tuple-element.18, bf16[2048,2,128]{2,0,1:T(8,128)(2,1)} %copy.57, ...), kind=kOutput, calls=%fused_computation.182 | convolution fusion | flops 687606272 | bytes 13373440 | tf_op jit(solution)/shard_map/sub | solution.py:64
  193.4 0.0 copy-done.2
  193.4 5.9 %fusion.56 = bf16[2,128,512]{2,1,0:T(8,128)(2,1)S(1)} fusion(f32[2,512,2560]{2,1,0:T(8,128)} %get-tuple-element.24, f32[2,512]{1,0:T(2,128)S(1)} %get-tuple-element.23, bf16[512,2,128]{0,2,1:T(8,128)(2,1)S(1)} %copy-done.3, bf16[2048,2,128]{0,2,1:T(8,128)(2,1)S(1)} %copy-done.2), kind=kOutput, calls=%fused_computation.67 | convolution fusion | flops 679084032 | bytes 12062720 | tf_op jit(solution)/shard_map/htk,khd->thd/dot_general | solution.py:66
  199.3 25.2 %all-gather.8.cloned.1.call-done = bf16[256,4096]{1,0:T(8,128)(2,1)} async-done(((bf16[256,512]{1,0:T(8,128)(2,1)}), bf16[256,4096]{1,0:T(8,128)(2,1)}) %all-gather.8.cloned.1.call-update) | async-done | bytes 2097168 | tf_op jit(solution)/shard_map/all_gather | solution.py:131
  224.5 7.2 %add_convert_fusion = bf16[512,4096]{1,0:T(8,128)(2,1)} fusion(f32[512,4096]{1,0:T(8,128)} %fusion.40, bf16[512,256]{0,1:T(8,128)(2,1)S(1)} %bitcast.57, bf16[256,4096]{1,0:T(8,128)(2,1)} %all-gather.8.cloned.1.call-done), kind=kOutput, calls=%fused_computation.16 | convolution fusion | flops 1077936128 | bytes 14942208 | tf_op jit(solution)/shard_map/dot_general | solution.py:129
  231.8 0.0 reduce-scatter.2.cloned.1.call-update
  231.8 65.4 %reduce-scatter.2.cloned.1.call-done = bf16[512,256]{1,0:T(8,128)(2,1)} async-done(((bf16[512,4096]{1,0:T(8,128)(2,1)}), bf16[512,256]{1,0:T(8,128)(2,1)}) %reduce-scatter.2.cloned.1.call-update) | async-done | bytes 262160 | tf_op jit(solution)/shard_map/reduce_scatter | solution.py:139
  297.2 0.0 copy-done.6
  297.2 1.7 add_convert_fusion.1
  (30 shorter events, 0.1 us)
Async XLA Ops:
  6.5 71.9 %all-gather.4.cloned.1.call-start = ((), (), s32[]{:S(2)}) async-start(), calls=%async_computation.2 | async-start | bytes 4456448 | tf_op jit(solution)/shard_map/all_gather | solution.py:99
  7.3 162.7 %all-gather.6.cloned.1.call-start = ((), (), s32[]{:S(2)}) async-start(), calls=%async_computation.3 | async-start | bytes 7077888 | tf_op jit(solution)/shard_map/all_gather | solution.py:106
  11.4 6.5 %copy-start.5 = (s32[512]{0:T(512)S(1)}, s32[512]{0:T(512)}, u32[]{:S(2)}) copy-start(s32[512]{0:T(512)} %param.32) | copy-start | bytes 6148
  11.4 6.8 %copy-start.4 = (s32[2]{0:T(128)S(1)}, s32[2]{0:T(128)}, u32[]{:S(2)}) copy-start(s32[2]{0:T(128)} %param.33) | copy-start | bytes 28
  11.4 7.1 %copy-start.8 = (s32[8,2]{0,1:T(2,128)S(1)}, s32[8,2]{0,1:T(2,128)}, u32[]{:S(2)}) copy-start(s32[8,2]{0,1:T(2,128)} %param.35) | copy-start | bytes 196
  11.4 7.1 %copy-start.15 = (s32[2,64]{1,0:T(2,128)S(1)}, s32[2,64]{1,0:T(2,128)}, u32[]{:S(2)}) copy-start(s32[2,64]{1,0:T(2,128)} %param.34) | copy-start | bytes 1540
  11.4 40.9 %all-to-all-start = ((bf16[9,2,16,16,256]{4,2,1,0,3:T(8,128)(2,1)}), bf16[9,2,16,16,256]{4,2,1,0,3:T(8,128)(2,1)S(1)}, u32[]{:S(2)}, u32[]{:S(2)}) async-start(bf16[9,2,16,16,256]{4,2,1,0,3:T(8,128)(2,1)} %bitcast.48), calls=%async_computation | async-start | bytes 4718592 | tf_op jit(solution)/shard_map/all_to_all | solution.py:75
  17.1 207.5 %all-gather.8.cloned.1.call-start = ((), (), s32[]{:S(2)}) async-start(), calls=%async_computation.4 | async-start | bytes 2359296 | tf_op jit(solution)/shard_map/all_gather | solution.py:131
  17.8 279.3 %reduce-scatter.2.cloned.1.call-start = ((), (), s32[]{:S(2)}) async-start(), calls=%async_computation.5 | async-start | bytes 4456448 | tf_op jit(solution)/shard_map/reduce_scatter | solution.py:139
  78.5 3.4 %copy-start = (bf16[512,4096]{1,0:T(8,128)(2,1)S(1)}, bf16[512,4096]{1,0:T(8,128)(2,1)}, u32[]{:S(2)}) copy-start(bf16[512,4096]{1,0:T(8,128)(2,1)} %all-gather.4.cloned.1.call-done) | copy-start | bytes 12582916
  81.9 1.2 copy-start.9
  81.9 1.2 copy-start.10
  81.9 1.3 copy-start.13
  83.2 86.8 %copy-start.11 = (f32[4096]{0:T(1024)S(1)}, f32[4096]{0:T(1024)}, u32[]{:S(2)}) copy-start(f32[4096]{0:T(1024)} %param.20) | copy-start | bytes 49156
  83.2 86.8 %copy-start.12 = (f32[4096]{0:T(1024)S(1)}, f32[4096]{0:T(1024)}, u32[]{:S(2)}) copy-start(f32[4096]{0:T(1024)} %param.19) | copy-start | bytes 49156
  83.2 86.8 %copy-start.14 = (f32[768]{0:T(1024)S(1)}, f32[768]{0:T(1024)}, u32[]{:S(2)}) copy-start(f32[768]{0:T(1024)} %param.24) | copy-start | bytes 9220
  181.0 2.3 copy-start.1
  183.3 10.1 %copy-start.2 = (bf16[2048,2,128]{0,2,1:T(8,128)(2,1)S(1)}, bf16[2048,2,128]{0,2,1:T(8,128)(2,1)}, u32[]{:S(2)}) copy-start(bf16[2048,2,128]{0,2,1:T(8,128)(2,1)} %copy.52) | copy-start | bytes 3145732
  183.3 10.1 %copy-start.3 = (bf16[512,2,128]{0,2,1:T(8,128)(2,1)S(1)}, bf16[512,2,128]{0,2,1:T(8,128)(2,1)}, u32[]{:S(2)}) copy-start(bf16[512,2,128]{0,2,1:T(8,128)(2,1)} %fusion.94) | copy-start | bytes 786436
  231.8 65.4 %copy-start.6 = (f32[256]{0:T(256)S(1)}, f32[256]{0:T(256)}, u32[]{:S(2)}) copy-start(f32[256]{0:T(256)} %param.30) | copy-start | bytes 3076
  231.8 65.4 %copy-start.7 = (f32[256]{0:T(256)S(1)}, f32[256]{0:T(256)}, u32[]{:S(2)}) copy-start(f32[256]{0:T(256)} %param.26) | copy-start | bytes 3076
Sparse Core Ops, SparseCore 0:
  9.0 69.4 all-gather.3
  80.8 89.1 all-gather.5
  172.2 52.3 all-gather.7
  231.9 65.1 reduce-scatter.1

commit v2 on v1

--- a/solution.py
+++ b/solution.py
@@ -76,6 +76,34 @@
     return shared.reshape(shared.shape[0], 2, shared.shape[2], shared.shape[4])
 
 
+def tok_blocks(block):
+    count = lax.axis_size("tok")
+    me = lax.axis_index("tok")
+    received = [(me, block)]
+    for shift in range(1, count):
+        perm = [(i, (i + shift) % count) for i in range(count)]
+        received.append(((me - shift) % count, lax.ppermute(block, "tok", perm)))
+    return received
+
+
+def qkv_by_blocks(pre_normed, qkv_weight):
+    rows = qkv_weight.shape[0]
+    total = None
+    for owner, block in tok_blocks(qkv_weight):
+        part = lax.dynamic_slice_in_dim(pre_normed, owner * rows, rows, axis=1)
+        product = jnp.dot(part, block, preferred_element_type=jnp.float32)
+        total = product if total is None else total + product
+    return total
+
+
+def gather_tok_columns(out_weight):
+    cols = out_weight.shape[1]
+    full = jnp.zeros((out_weight.shape[0], cols * lax.axis_size("tok")), out_weight.dtype)
+    for owner, block in tok_blocks(out_weight):
+        full = lax.dynamic_update_slice_in_dim(full, block, owner * cols, axis=1)
+    return full
+
+
 def shards(
     states,
     pre_gain,
@@ -101,11 +129,7 @@
     pre_normed = layer_norm(wide, pre_gain, pre_shift)
     mlp_normed = layer_norm(wide, mlp_gain, mlp_shift)
     tok_rows = gathered.shape[0]
-    joined = jnp.dot(
-        pre_normed,
-        lax.all_gather(qkv_weight, "tok", axis=0, tiled=True),
-        preferred_element_type=jnp.float32,
-    )
+    joined = qkv_by_blocks(pre_normed, qkv_weight)
     joined = (joined + qkv_bias).reshape(tok_rows, -1, 3, HD)
     local_req = token_request - lax.axis_index("tok") * cached_len.shape[0]
     positions = token_positions(local_req, cached_len)
@@ -127,9 +151,7 @@
         queries, new_keys, new_values, cache_keys, cache_values, local_req, cached_len, positions
     ).reshape(tok_rows, -1)
     attention_part = jnp.dot(
-        heads_out,
-        lax.all_gather(out_weight, "tok", axis=1, tiled=True),
-        preferred_element_type=jnp.float32,
+        heads_out, gather_tok_columns(out_weight), preferred_element_type=jnp.float32
     )
     hidden = jax.nn.gelu(
         jnp.dot(mlp_normed, up_weight, preferred_element_type=jnp.float32) + up_bias,

time: 306 us -> 299 us (0.977)
  waiting for transfers between devices: 204 us -> 128 us
  starting transfers between devices: 5.76 us -> 58.5 us
  local copies, waits for them, and re-layouts: 16.1 us -> 26 us
  matrix products: 54.7 us -> 59.9 us
    all_gather x2 -> x0, waiting for transfers between devices: 88 us -> none  [the longest x1 62.9 us: shards(): lax.all_gather(qkv_weight, 'tok', axis=0, tiled=True)]
    ppermute x0 -> x14, waiting for transfers between devices: none -> 60.3 us  [tok_blocks(): received.append(((me - shift) % count, lax.ppermute(block, 'tok', perm)))]
    ppermute x0 -> x14, starting transfers between devices: none -> 53.9 us  [tok_blocks(): received.append(((me - shift) % count, lax.ppermute(block, 'tok', perm)))]
    all_to_all x1, waiting for transfers between devices: 30.2 us -> 0.01 us  [share_pages(): lax.all_to_all(grouped, 'head', split_axis=3, concat_axis=0, tiled=True)]
    all_gather x1, waiting for transfers between devices: 18.5 us -> 0.01 us  [shards(): gathered = lax.all_gather(states, 'head', axis=1, tiled=True)]
    dynamic_update_slice x0 -> x8, local copies, waits for them, and re-layouts: none -> 6.03 us  [gather_tok_columns(): full = lax.dynamic_update_slice_in_dim(full, block, owner * cols, axis=1)]
    dot_general x2 -> x9, matrix products: 14.8 us -> 20.2 us  [the longest x8 12.9 us: qkv_by_blocks(): product = jnp.dot(part, block, preferred_element_type=jnp.float32)]
  transfers between devices with their start and end apart: 5 -> 17, of which waited for: 5 -> 6; matrix products, arithmetic and copies ran while one was open for 24% -> 14% of each run, Pallas kernels for 0% -> 0%
where the time goes in v2:
time: 299 us
  waiting for transfers between devices  128 us (43%)
  matrix products  59.9 us (20%)
  starting transfers between devices  58.5 us (20%)
  local copies, waits for them, and re-layouts  26 us (9%)
  between operations  13.7 us (5%)
  other arithmetic  12.4 us (4%)
    reduce_scatter x1, waiting for transfers between devices, shards(): lax.psum_scatter((attention_part + feed_part).astype(jnp.bfloat16), 'head...  66.9 us
    ppermute x14, waiting for transfers between devices, tok_blocks(): received.append(((me - shift) % count, lax.ppermute(block, 'tok', perm)))  60.3 us
    ppermute x14, starting transfers between devices, tok_blocks(): received.append(((me - shift) % count, lax.ppermute(block, 'tok', perm)))  53.9 us
    dot_general x1, matrix products, shards(): feed_part = jnp.dot(hidden, down_weight, preferred_element_type=jnp.float32)  23.8 us
    dot_general x8, matrix products, qkv_by_blocks(): product = jnp.dot(part, block, preferred_element_type=jnp.float32)  12.9 us
    sub x1, matrix products, attend(): exp_scores = jnp.exp(scores - peak)  10.1 us
    dot_general x1, matrix products, shards(): jnp.dot(heads_out, gather_tok_columns(out_weight), preferred_element_type...  7.27 us
    dynamic_update_slice x8, local copies, waits for them, and re-layouts, gather_tok_columns(): full = lax.dynamic_update_slice_in_dim(full, block, owner * cols, axis=1)  6.03 us
  transfers between devices with their start and end apart: 17, of which 6 were waited for; matrix products, arithmetic and copies ran while one was open for 14% of the time, Pallas kernels for 0%

profile of v2, /device:TPU:0, one launch (start us, length us, event | category | flops | bytes accessed | tf_op | source)
XLA Modules:
  0.0 298.6 jit_solution(12856324371819304637)
XLA Ops:
  6.5 0.7 all-gather.2.cloned.1.call-update
  7.3 4.2 %collective-permute-start.5 = (bf16[512,768]{1,0:T(8,128)(2,1)}, bf16[512,768]{1,0:T(8,128)(2,1)}, u32[]{:S(2)}, u32[]{:S(2)}) collective-permute-start(bf16[512,768]{1,0:T(8,128)(2,1)} %param.23), channel_id=1, source_target_pairs={{0,96},{16,112},{32,0},{48,16},{64,32},{80,48},{96,64},{112,80},{1... | collective-permute-start | bytes 2359304 | tf_op jit(solution)/shard_map/ppermute | solution.py:85
  11.4 2.6 collective-permute-start.4
  14.0 0.8 collective-permute-start.7
  14.8 1.6 collective-permute-start.8
  16.4 3.5 %collective-permute-start.9 = (bf16[256,512]{1,0:T(8,128)(2,1)}, bf16[256,512]{1,0:T(8,128)(2,1)S(1)}, u32[]{:S(2)}, u32[]{:S(2)}) collective-permute-start(bf16[256,512]{1,0:T(8,128)(2,1)} %param.25), channel_id=1, source_target_pairs={{0,48},{16,64},{32,80},{48,96},{64,112},{80,0},{96,16},{112,32},{1... | collective-permute-start | bytes 786440 | tf_op jit(solution)/shard_map/ppermute | solution.py:85
  20.0 3.5 %copy.68 = bf16[9,2,2,16,8,256]{5,4,2,1,0,3:T(8,128)(2,1)} copy(bf16[9,2,2,16,8,256]{5,4,3,2,1,0:T(8,128)(2,1)} %bitcast.63) | data formatting | bytes 4718592 | tf_op jit(solution)/shard_map/reshape | solution.py:72
  23.5 4.6 %all-to-all-start = ((bf16[9,2,16,16,256]{4,2,1,0,3:T(8,128)(2,1)}), bf16[9,2,16,16,256]{4,2,1,0,3:T(8,128)(2,1)S(1)}, u32[]{:S(2)}, u32[]{:S(2)}) async-start(bf16[9,2,16,16,256]{4,2,1,0,3:T(8,128)(2,1)} %bitcast.55), calls=%async_computation | async-start | bytes 4718592 | tf_op jit(solution)/shard_map/all_to_all | solution.py:75
  29.2 0.3 compare_and_fusion.1
  29.5 0.7 compare_and_fusion
  30.3 1.2 pad_add_fusion
  31.5 1.5 broadcast_in_dim.57
  33.0 0.7 constant_dynamic-update-slice_fusion.7
  33.8 0.9 copy.54
  34.6 0.8 copy.55
  35.4 33.4 %collective-permute-done.7 = bf16[256,512]{1,0:T(8,128)(2,1)S(1)} collective-permute-done((bf16[256,512]{1,0:T(8,128)(2,1)}, bf16[256,512]{1,0:T(8,128)(2,1)S(1)}, u32[]{:S(2)}, u32[]{:S(2)}) %collective-permute-start.7) | collective-permute-done | bytes 262176 | tf_op jit(solution)/shard_map/ppermute | solution.py:85
  68.9 4.1 %collective-permute-start.10 = (bf16[256,512]{1,0:T(8,128)(2,1)S(1)}, bf16[256,512]{1,0:T(8,128)(2,1)S(1)}, u32[]{:S(2)}, u32[]{:S(2)}) collective-permute-start(bf16[256,512]{1,0:T(8,128)(2,1)S(1)} %copy-done.5), channel_id=1, source_target_pairs={{0,64},{16,80},{32,96},{48,112},{64,0},{80,16},{96,32},{112,48},{1... | collective-permute-start | bytes 786440 | tf_op jit(solution)/shard_map/ppermute | solution.py:85
  73.0 0.7 constant_dynamic-update-slice_fusion.6
  73.7 3.3 %collective-permute-start.11 = (bf16[256,512]{1,0:T(8,128)(2,1)S(1)}, bf16[256,512]{1,0:T(8,128)(2,1)S(1)}, u32[]{:S(2)}, u32[]{:S(2)}) collective-permute-start(bf16[256,512]{1,0:T(8,128)(2,1)S(1)} %copy-done.5), channel_id=1, source_target_pairs={{0,80},{16,96},{32,112},{48,0},{64,16},{80,32},{96,48},{112,64},{1... | collective-permute-start | bytes 786440 | tf_op jit(solution)/shard_map/ppermute | solution.py:85
  77.0 0.7 constant_dynamic-update-slice_fusion.5
  77.8 2.3 collective-permute-done.9
  80.1 4.5 %collective-permute-start.12 = (bf16[256,512]{1,0:T(8,128)(2,1)S(1)}, bf16[256,512]{1,0:T(8,128)(2,1)S(1)}, u32[]{:S(2)}, u32[]{:S(2)}) collective-permute-start(bf16[256,512]{1,0:T(8,128)(2,1)S(1)} %copy-done.5), channel_id=1, source_target_pairs={{0,96},{16,112},{32,0},{48,16},{64,32},{80,48},{96,64},{112,80},{1... | collective-permute-start | bytes 786440 | tf_op jit(solution)/shard_map/ppermute | solution.py:85
  84.6 0.8 constant_dynamic-update-slice_fusion.4
  85.4 2.9 collective-permute-start.13
  88.3 0.7 constant_dynamic-update-slice_fusion.3
  89.0 7.3 %collective-permute-done.11 = bf16[256,512]{1,0:T(8,128)(2,1)S(1)} collective-permute-done((bf16[256,512]{1,0:T(8,128)(2,1)S(1)}, bf16[256,512]{1,0:T(8,128)(2,1)S(1)}, u32[]{:S(2)}, u32[]{:S(2)}) %collective-permute-start.11) | collective-permute-done | bytes 262176 | tf_op jit(solution)/shard_map/ppermute | solution.py:85
  96.3 1.3 collective-permute-start.3
  97.6 0.8 constant_dynamic-update-slice_fusion.2
  98.4 4.7 %collective-permute-start.2 = (bf16[512,768]{1,0:T(8,128)(2,1)}, bf16[512,768]{1,0:T(8,128)(2,1)}, u32[]{:S(2)}, u32[]{:S(2)}) collective-permute-start(bf16[512,768]{1,0:T(8,128)(2,1)} %param.23), channel_id=1, source_target_pairs={{0,48},{16,64},{32,80},{48,96},{64,112},{80,0},{96,16},{112,32},{1... | collective-permute-start | bytes 2359304 | tf_op jit(solution)/shard_map/ppermute | solution.py:85
  103.1 0.7 constant_dynamic-update-slice_fusion.1
  103.8 2.1 collective-permute-start.1
  106.0 0.7 constant_dynamic-update-slice_fusion
  106.7 2.0 gather_fusion
  108.7 1.7 fusion.161
  110.4 0.3 reshape_squeeze.7
  110.7 1.1 copy.57
  112.1 2.1 copy.52
  114.3 3.0 convert_reduce_fusion
  117.2 0.5 copy-done
  117.7 1.2 fusion.9
  119.0 2.3 fusion.6
  121.3 1.7 fusion.101
  123.0 15.0 %collective-permute-start = (bf16[512,768]{1,0:T(8,128)(2,1)}, bf16[512,768]{1,0:T(8,128)(2,1)S(1)}, u32[]{:S(2)}, u32[]{:S(2)}) collective-permute-start(bf16[512,768]{1,0:T(8,128)(2,1)} %param.23), channel_id=1, source_target_pairs={{0,16},{16,32},{32,48},{48,64},{64,80},{80,96},{96,112},{112,0},{1... | collective-permute-start | bytes 2359304 | tf_op jit(solution)/shard_map/ppermute | solution.py:85
  137.9 1.7 fusion.89
  139.7 3.4 %collective-permute-start.6 = (bf16[512,768]{1,0:T(8,128)(2,1)}, bf16[512,768]{1,0:T(8,128)(2,1)S(1)}, u32[]{:S(2)}, u32[]{:S(2)}) collective-permute-start(bf16[512,768]{1,0:T(8,128)(2,1)} %param.23), channel_id=1, source_target_pairs={{0,112},{16,0},{32,16},{48,32},{64,48},{80,64},{96,80},{112,96},{1... | collective-permute-start | bytes 2359304 | tf_op jit(solution)/shard_map/ppermute | solution.py:85
  143.0 1.7 fusion.91
  144.7 1.1 collective-permute-done.3
  145.8 1.7 fusion.93
  147.5 1.7 fusion.95
  149.2 16.1 %collective-permute-done.1 = bf16[512,768]{1,0:T(8,128)(2,1)} collective-permute-done((bf16[512,768]{1,0:T(8,128)(2,1)}, bf16[512,768]{1,0:T(8,128)(2,1)}, u32[]{:S(2)}, u32[]{:S(2)}) %collective-permute-start.1) | collective-permute-done | bytes 786464 | tf_op jit(solution)/shard_map/ppermute | solution.py:85
  165.3 1.7 fusion.97
  167.1 0.6 fusion.99
  167.7 2.1 add_add_fusion
  169.8 1.9 copy.50
  171.8 0.8 fusion.103
  173.0 0.8 slice.80
  173.9 0.9 slice.81
  174.7 1.2 subtract_convert_fusion.1
  176.0 10.1 %fusion.163 = (f32[2,512]{1,0:T(2,128)S(1)}, f32[2,512,2560]{2,1,0:T(8,128)}) fusion(pred[512,2560]{1,0:T(8,128)(4,1)S(1)} %copy-done.1, bf16[512,2,96]{2,0,1:T(8,128)(2,1)} %slice.80, bf16[512,2,16]{2,0,1:T(8,128)(2,1)} %get-tuple-element.17, bf16[512,2,16]{2,0,1:T(8,128)(2,1)} %get-tuple-element.18, bf16[2048,2,128]{2,0,1:T(8,128)(2,1)} %copy.57, ...), kind=kOutput, calls=%fused_computation.209 | convolution fusion | flops 687606272 | bytes 13373440 | tf_op jit(solution)/shard_map/sub | solution.py:64
  186.1 5.9 %fusion.47 = bf16[2,128,512]{2,1,0:T(8,128)(2,1)S(1)} fusion(f32[2,512,2560]{2,1,0:T(8,128)} %get-tuple-element.24, f32[2,512]{1,0:T(2,128)S(1)} %get-tuple-element.23, bf16[512,2,128]{0,2,1:T(8,128)(2,1)S(1)} %copy-done.6, bf16[2048,2,128]{0,2,1:T(8,128)(2,1)S(1)} %copy-done.4), kind=kOutput, calls=%fused_computation.62 | convolution fusion | flops 679084032 | bytes 12062720 | tf_op jit(solution)/shard_map/htk,khd->thd/dot_general | solution.py:66
  192.0 23.8 %fusion.34 = f32[512,4096]{1,0:T(8,128)} fusion(bf16[1024,4096]{1,0:T(8,128)(2,1)} %param.29, bf16[4096,1024]{1,0:T(8,128)(2,1)} %param.27, bf16[512,4096]{1,0:T(8,128)(2,1)} %all-gather.2.cloned.1.call-done, f32[4096]{0:T(1024)S(1)} %copy-done.15, f32[4096]{0:T(1024)S(1)} %copy-done.16, f32[512]{0:T(512)S(1)} %add_rsqrt_fusion, ...), kind=kOutput, calls=%fused_computation.50 | convolution fusion | flops 8637120512 | bytes 29401088 | tf_op jit(solution)/shard_map/dot_general | solution.py:160
  215.8 7.3 %add_convert_fusion = bf16[512,4096]{1,0:T(8,128)(2,1)} fusion(f32[512,4096]{1,0:T(8,128)} %fusion.34, bf16[512,256]{0,1:T(8,128)(2,1)S(1)} %bitcast.64, bf16[256,4096]{1,0:T(8,128)(2,1)} %constant_dynamic-update-slice_fusion), kind=kOutput, calls=%fused_computation.16 | convolution fusion | flops 1077936128 | bytes 14942208 | tf_op jit(solution)/shard_map/dot_general | solution.py:153
  223.1 66.9 %reduce-scatter.2.cloned.1.call-done = bf16[512,256]{1,0:T(8,128)(2,1)} async-done(((bf16[512,4096]{1,0:T(8,128)(2,1)}), bf16[512,256]{1,0:T(8,128)(2,1)}) %reduce-scatter.2.cloned.1.call-update) | async-done | bytes 262160 | tf_op jit(solution)/shard_map/reduce_scatter | solution.py:161
  290.0 1.7 add_convert_fusion.1
  (75 shorter events, 2.1 us)
Async XLA Ops:
  6.5 107.7 %all-gather.2.cloned.1.call-start = ((), (), s32[]{:S(2)}) async-start(), calls=%async_computation.2 | async-start | bytes 4456448 | tf_op jit(solution)/shard_map/all_gather | solution.py:127
  7.3 115.7 %collective-permute-start.5 = (bf16[512,768]{1,0:T(8,128)(2,1)}, bf16[512,768]{1,0:T(8,128)(2,1)}, u32[]{:S(2)}, u32[]{:S(2)}) collective-permute-start(bf16[512,768]{1,0:T(8,128)(2,1)} %param.23), channel_id=1, source_target_pairs={{0,96},{16,112},{32,0},{48,16},{64,32},{80,48},{96,64},{112,80},{1... | collective-permute-start | bytes 2359304 | tf_op jit(solution)/shard_map/ppermute | solution.py:85
  11.4 128.2 %collective-permute-start.4 = (bf16[512,768]{1,0:T(8,128)(2,1)}, bf16[512,768]{1,0:T(8,128)(2,1)}, u32[]{:S(2)}, u32[]{:S(2)}) collective-permute-start(bf16[512,768]{1,0:T(8,128)(2,1)} %param.23), channel_id=1, source_target_pairs={{0,80},{16,96},{32,112},{48,0},{64,16},{80,32},{96,48},{112,64},{1... | collective-permute-start | bytes 2359304 | tf_op jit(solution)/shard_map/ppermute | solution.py:85
  14.0 54.9 %collective-permute-start.7 = (bf16[256,512]{1,0:T(8,128)(2,1)}, bf16[256,512]{1,0:T(8,128)(2,1)S(1)}, u32[]{:S(2)}, u32[]{:S(2)}) collective-permute-start(bf16[256,512]{1,0:T(8,128)(2,1)} %param.25), channel_id=1, source_target_pairs={{0,16},{16,32},{32,48},{48,64},{64,80},{80,96},{96,112},{112,0},{1... | collective-permute-start | bytes 786440 | tf_op jit(solution)/shard_map/ppermute | solution.py:85
  14.8 58.9 %collective-permute-start.8 = (bf16[256,512]{1,0:T(8,128)(2,1)}, bf16[256,512]{1,0:T(8,128)(2,1)S(1)}, u32[]{:S(2)}, u32[]{:S(2)}) collective-permute-start(bf16[256,512]{1,0:T(8,128)(2,1)} %param.25), channel_id=1, source_target_pairs={{0,32},{16,48},{32,64},{48,80},{64,96},{80,112},{96,0},{112,16},{1... | collective-permute-start | bytes 786440 | tf_op jit(solution)/shard_map/ppermute | solution.py:85
  16.4 63.7 %collective-permute-start.9 = (bf16[256,512]{1,0:T(8,128)(2,1)}, bf16[256,512]{1,0:T(8,128)(2,1)S(1)}, u32[]{:S(2)}, u32[]{:S(2)}) collective-permute-start(bf16[256,512]{1,0:T(8,128)(2,1)} %param.25), channel_id=1, source_target_pairs={{0,48},{16,64},{32,80},{48,96},{64,112},{80,0},{96,16},{112,32},{1... | collective-permute-start | bytes 786440 | tf_op jit(solution)/shard_map/ppermute | solution.py:85
  23.5 4.6 %copy-start.18 = (s32[2,64]{1,0:T(2,128)S(1)}, s32[2,64]{1,0:T(2,128)}, u32[]{:S(2)}) copy-start(s32[2,64]{1,0:T(2,128)} %param.34) | copy-start | bytes 1540
  23.5 4.8 %copy-start.11 = (s32[512]{0:T(512)S(1)}, s32[512]{0:T(512)}, u32[]{:S(2)}) copy-start(s32[512]{0:T(512)} %param.32) | copy-start | bytes 6148
  23.5 5.1 %copy-start.14 = (s32[8,2]{0,1:T(2,128)S(1)}, s32[8,2]{0,1:T(2,128)}, u32[]{:S(2)}) copy-start(s32[8,2]{0,1:T(2,128)} %param.35) | copy-start | bytes 196
  23.5 5.3 %copy-start.10 = (s32[2]{0:T(128)S(1)}, s32[2]{0:T(128)}, u32[]{:S(2)}) copy-start(s32[2]{0:T(128)} %param.33) | copy-start | bytes 28
  23.5 83.2 %all-to-all-start = ((bf16[9,2,16,16,256]{4,2,1,0,3:T(8,128)(2,1)}), bf16[9,2,16,16,256]{4,2,1,0,3:T(8,128)(2,1)S(1)}, u32[]{:S(2)}, u32[]{:S(2)}) async-start(bf16[9,2,16,16,256]{4,2,1,0,3:T(8,128)(2,1)} %bitcast.55), calls=%async_computation | async-start | bytes 4718592 | tf_op jit(solution)/shard_map/all_to_all | solution.py:75
  28.1 261.9 %reduce-scatter.2.cloned.1.call-start = ((), (), s32[]{:S(2)}) async-start(), calls=%async_computation.3 | async-start | bytes 4456448 | tf_op jit(solution)/shard_map/reduce_scatter | solution.py:161
  30.3 2.7 copy-start.5
  68.9 16.5 %collective-permute-start.10 = (bf16[256,512]{1,0:T(8,128)(2,1)S(1)}, bf16[256,512]{1,0:T(8,128)(2,1)S(1)}, u32[]{:S(2)}, u32[]{:S(2)}) collective-permute-start(bf16[256,512]{1,0:T(8,128)(2,1)S(1)} %copy-done.5), channel_id=1, source_target_pairs={{0,64},{16,80},{32,96},{48,112},{64,0},{80,16},{96,32},{112,48},{1... | collective-permute-start | bytes 786440 | tf_op jit(solution)/shard_map/ppermute | solution.py:85
  73.7 22.6 %collective-permute-start.11 = (bf16[256,512]{1,0:T(8,128)(2,1)S(1)}, bf16[256,512]{1,0:T(8,128)(2,1)S(1)}, u32[]{:S(2)}, u32[]{:S(2)}) collective-permute-start(bf16[256,512]{1,0:T(8,128)(2,1)S(1)} %copy-done.5), channel_id=1, source_target_pairs={{0,80},{16,96},{32,112},{48,0},{64,16},{80,32},{96,48},{112,64},{1... | collective-permute-start | bytes 786440 | tf_op jit(solution)/shard_map/ppermute | solution.py:85
  80.1 18.2 %collective-permute-start.12 = (bf16[256,512]{1,0:T(8,128)(2,1)S(1)}, bf16[256,512]{1,0:T(8,128)(2,1)S(1)}, u32[]{:S(2)}, u32[]{:S(2)}) collective-permute-start(bf16[256,512]{1,0:T(8,128)(2,1)S(1)} %copy-done.5), channel_id=1, source_target_pairs={{0,96},{16,112},{32,0},{48,16},{64,32},{80,48},{96,64},{112,80},{1... | collective-permute-start | bytes 786440 | tf_op jit(solution)/shard_map/ppermute | solution.py:85
  85.4 18.4 %collective-permute-start.13 = (bf16[256,512]{1,0:T(8,128)(2,1)S(1)}, bf16[256,512]{1,0:T(8,128)(2,1)S(1)}, u32[]{:S(2)}, u32[]{:S(2)}) collective-permute-start(bf16[256,512]{1,0:T(8,128)(2,1)S(1)} %copy-done.5), channel_id=1, source_target_pairs={{0,112},{16,0},{32,16},{48,32},{64,48},{80,64},{96,80},{112,96},{1... | collective-permute-start | bytes 786440 | tf_op jit(solution)/shard_map/ppermute | solution.py:85
  96.3 49.5 %collective-permute-start.3 = (bf16[512,768]{1,0:T(8,128)(2,1)}, bf16[512,768]{1,0:T(8,128)(2,1)}, u32[]{:S(2)}, u32[]{:S(2)}) collective-permute-start(bf16[512,768]{1,0:T(8,128)(2,1)} %param.23), channel_id=1, source_target_pairs={{0,64},{16,80},{32,96},{48,112},{64,0},{80,16},{96,32},{112,48},{1... | collective-permute-start | bytes 2359304 | tf_op jit(solution)/shard_map/ppermute | solution.py:85
  98.4 49.2 %collective-permute-start.2 = (bf16[512,768]{1,0:T(8,128)(2,1)}, bf16[512,768]{1,0:T(8,128)(2,1)}, u32[]{:S(2)}, u32[]{:S(2)}) collective-permute-start(bf16[512,768]{1,0:T(8,128)(2,1)} %param.23), channel_id=1, source_target_pairs={{0,48},{16,64},{32,80},{48,96},{64,112},{80,0},{96,16},{112,32},{1... | collective-permute-start | bytes 2359304 | tf_op jit(solution)/shard_map/ppermute | solution.py:85
  103.8 61.5 %collective-permute-start.1 = (bf16[512,768]{1,0:T(8,128)(2,1)}, bf16[512,768]{1,0:T(8,128)(2,1)}, u32[]{:S(2)}, u32[]{:S(2)}) collective-permute-start(bf16[512,768]{1,0:T(8,128)(2,1)} %param.23), channel_id=1, source_target_pairs={{0,32},{16,48},{32,64},{48,80},{64,96},{80,112},{96,0},{112,16},{1... | collective-permute-start | bytes 2359304 | tf_op jit(solution)/shard_map/ppermute | solution.py:85
  114.2 3.4 %copy-start = (bf16[512,4096]{1,0:T(8,128)(2,1)S(1)}, bf16[512,4096]{1,0:T(8,128)(2,1)}, u32[]{:S(2)}) copy-start(bf16[512,4096]{1,0:T(8,128)(2,1)} %all-gather.2.cloned.1.call-done) | copy-start | bytes 12582916
  117.7 1.2 copy-start.7
  117.7 1.2 copy-start.8
  123.0 44.1 %collective-permute-start = (bf16[512,768]{1,0:T(8,128)(2,1)}, bf16[512,768]{1,0:T(8,128)(2,1)S(1)}, u32[]{:S(2)}, u32[]{:S(2)}) collective-permute-start(bf16[512,768]{1,0:T(8,128)(2,1)} %param.23), channel_id=1, source_target_pairs={{0,16},{16,32},{32,48},{48,64},{64,80},{80,96},{96,112},{112,0},{1... | collective-permute-start | bytes 2359304 | tf_op jit(solution)/shard_map/ppermute | solution.py:85
  139.7 28.0 %collective-permute-start.6 = (bf16[512,768]{1,0:T(8,128)(2,1)}, bf16[512,768]{1,0:T(8,128)(2,1)S(1)}, u32[]{:S(2)}, u32[]{:S(2)}) collective-permute-start(bf16[512,768]{1,0:T(8,128)(2,1)} %param.23), channel_id=1, source_target_pairs={{0,112},{16,0},{32,16},{48,32},{64,48},{80,64},{96,80},{112,96},{1... | collective-permute-start | bytes 2359304 | tf_op jit(solution)/shard_map/ppermute | solution.py:85
  167.0 0.7 copy-start.9
  171.8 2.9 copy-start.2
  171.8 2.9 copy-start.3
  173.8 2.1 copy-start.1
  175.9 10.1 %copy-start.4 = (bf16[2048,2,128]{0,2,1:T(8,128)(2,1)S(1)}, bf16[2048,2,128]{0,2,1:T(8,128)(2,1)}, u32[]{:S(2)}) copy-start(bf16[2048,2,128]{0,2,1:T(8,128)(2,1)} %copy.52) | copy-start | bytes 3145732
  175.9 10.1 %copy-start.6 = (bf16[512,2,128]{0,2,1:T(8,128)(2,1)S(1)}, bf16[512,2,128]{0,2,1:T(8,128)(2,1)}, u32[]{:S(2)}) copy-start(bf16[512,2,128]{0,2,1:T(8,128)(2,1)} %fusion.103) | copy-start | bytes 786436
  186.0 6.0 %copy-start.15 = (f32[4096]{0:T(1024)S(1)}, f32[4096]{0:T(1024)}, u32[]{:S(2)}) copy-start(f32[4096]{0:T(1024)} %param.22) | copy-start | bytes 49156
  186.0 6.0 %copy-start.16 = (f32[4096]{0:T(1024)S(1)}, f32[4096]{0:T(1024)}, u32[]{:S(2)}) copy-start(f32[4096]{0:T(1024)} %param.21) | copy-start | bytes 49156
  186.0 6.0 %copy-start.17 = (f32[1024]{0:T(1024)S(1)}, f32[1024]{0:T(1024)}, u32[]{:S(2)}) copy-start(f32[1024]{0:T(1024)} %param.28) | copy-start | bytes 12292
  223.1 67.0 %copy-start.12 = (f32[256]{0:T(256)S(1)}, f32[256]{0:T(256)}, u32[]{:S(2)}) copy-start(f32[256]{0:T(256)} %param.30) | copy-start | bytes 3076
  223.1 67.0 %copy-start.13 = (f32[256]{0:T(256)S(1)}, f32[256]{0:T(256)}, u32[]{:S(2)}) copy-start(f32[256]{0:T(256)} %param.26) | copy-start | bytes 3076
Sparse Core Ops, SparseCore 0:
  9.0 75.3 all-gather.1
  223.2 66.7 reduce-scatter.1

commit v3 on v1

--- a/solution.py
+++ b/solution.py
@@ -76,6 +76,11 @@
     return shared.reshape(shared.shape[0], 2, shared.shape[2], shared.shape[4])
 
 
+def gather_by_all_to_all(block, axis):
+    copies = jnp.concatenate([block] * lax.axis_size(axis), axis=0)
+    return lax.all_to_all(copies, axis, split_axis=0, concat_axis=0, tiled=True)
+
+
 def shards(
     states,
     pre_gain,
@@ -97,25 +102,33 @@
     migrations,
 ):
     gathered = lax.all_gather(states, "head", axis=1, tiled=True)
+    qkv_full = gather_by_all_to_all(qkv_weight, "tok")
+    out_full = lax.all_gather(out_weight, "tok", axis=1, tiled=True)
     wide = gathered.astype(jnp.float32)
     pre_normed = layer_norm(wide, pre_gain, pre_shift)
     mlp_normed = layer_norm(wide, mlp_gain, mlp_shift)
     tok_rows = gathered.shape[0]
-    joined = jnp.dot(
-        pre_normed,
-        lax.all_gather(qkv_weight, "tok", axis=0, tiled=True),
-        preferred_element_type=jnp.float32,
-    )
+    half = tok_rows // 2
+
+    def feed(normed):
+        hidden = jax.nn.gelu(
+            jnp.dot(normed, up_weight, preferred_element_type=jnp.float32) + up_bias,
+            approximate=False,
+        ).astype(jnp.bfloat16)
+        return jnp.dot(hidden, down_weight, preferred_element_type=jnp.float32)
+
+    feed_first = feed(mlp_normed[:half])
+    kv_cache, feed_first = lax.optimization_barrier((kv_cache, feed_first))
+    page_pool = share_pages(kv_cache, lax.axis_size("head"))
+    joined = jnp.dot(pre_normed, qkv_full, preferred_element_type=jnp.float32)
     joined = (joined + qkv_bias).reshape(tok_rows, -1, 3, HD)
     local_req = token_request - lax.axis_index("tok") * cached_len.shape[0]
     positions = token_positions(local_req, cached_len)
     queries = rotate(joined[:, :, 0], positions).astype(jnp.bfloat16)
     new_keys = rotate(joined[:, :, 1], positions).astype(jnp.bfloat16)
     new_values = joined[:, :, 2].astype(jnp.bfloat16)
-    head_groups = lax.axis_size("head")
     sources = migrations[:, 0]
     targets = migrations[:, 1]
-    page_pool = share_pages(kv_cache, head_groups)
     table = page_table.reshape(-1)
     match = table[:, None] == targets[None, :]
     moved_from = jnp.sum(jnp.where(match, sources[None, :], 0), axis=1)
@@ -126,19 +139,13 @@
     heads_out = attend(
         queries, new_keys, new_values, cache_keys, cache_values, local_req, cached_len, positions
     ).reshape(tok_rows, -1)
-    attention_part = jnp.dot(
-        heads_out,
-        lax.all_gather(out_weight, "tok", axis=1, tiled=True),
-        preferred_element_type=jnp.float32,
-    )
-    hidden = jax.nn.gelu(
-        jnp.dot(mlp_normed, up_weight, preferred_element_type=jnp.float32) + up_bias,
-        approximate=False,
-    ).astype(jnp.bfloat16)
-    feed_part = jnp.dot(hidden, down_weight, preferred_element_type=jnp.float32)
-    summed = lax.psum_scatter(
-        (attention_part + feed_part).astype(jnp.bfloat16), "head", scatter_dimension=1, tiled=True
-    ).astype(jnp.float32)
+    attention_part = jnp.dot(heads_out, out_full, preferred_element_type=jnp.float32)
+    both_first = (attention_part[:half] + feed_first).astype(jnp.bfloat16)
+    both_first, normed_second = lax.optimization_barrier((both_first, mlp_normed[half:]))
+    summed_first = lax.psum_scatter(both_first, "head", scatter_dimension=1, tiled=True)
+    both_second = (attention_part[half:] + feed(normed_second)).astype(jnp.bfloat16)
+    summed_second = lax.psum_scatter(both_second, "head", scatter_dimension=1, tiled=True)
+    summed = jnp.concatenate([summed_first, summed_second], axis=0).astype(jnp.float32)
     return (summed + out_bias + down_bias).astype(jnp.bfloat16)
 
 

time: 306 us -> 334 us (1.092)
  local copies, waits for them, and re-layouts: 16.1 us -> 31.3 us
  starting transfers between devices: 5.76 us -> 12.6 us
  other arithmetic: 11.2 us -> 16.8 us
  matrix products: 54.7 us -> 58.7 us
  waiting for transfers between devices: 204 us -> 200 us
    all_gather x2 -> x1, waiting for transfers between devices: 88 us -> 0.02 us  [shards(): out_full = lax.all_gather(out_weight, 'tok', axis=1, tiled=True)]
    reduce_scatter x1 -> x2, waiting for transfers between devices: 65.4 us -> 127 us  [the longest x1 64.9 us: shards(): lax.psum_scatter(both_first, 'head', scatter_dimension=1, tiled=True)]
    all_to_all x0 -> x1, waiting for transfers between devices: none -> 27.1 us  [gather_by_all_to_all(): return lax.all_to_all(copies, axis, split_axis=0, concat_axis=0, tiled=True)]
    all_to_all x1, waiting for transfers between devices: 30.2 us -> 8.67 us  [share_pages(): lax.all_to_all(grouped, 'head', split_axis=3, concat_axis=0, tiled=True)]
    all_gather x1, waiting for transfers between devices: 18.5 us -> 35.1 us  [shards(): gathered = lax.all_gather(states, 'head', axis=1, tiled=True)]
    unnamed x35 -> x50, local copies, waits for them, and re-layouts: 1 us -> 12.8 us
    all_to_all x0 -> x1, starting transfers between devices: none -> 8.17 us  [gather_by_all_to_all(): return lax.all_to_all(copies, axis, split_axis=0, concat_axis=0, tiled=True)]
    convert_element_type x0 -> x2, other arithmetic: none -> 5.42 us  [the longest x1 3.55 us: layer_norm(): (centred * lax.rsqrt(row_var + epsilon) * gain + shift).astype(jnp.bfloat16)]
  transfers between devices with their start and end apart: 5 -> 6, of which waited for: 5 -> 5; matrix products, arithmetic and copies ran while one was open for 24% -> 24% of each run, Pallas kernels for 0% -> 0%
where the time goes in v3:
time: 334 us; the launch traced here: 333 us
  waiting for transfers between devices  200 us (60%)
  matrix products  58.7 us (18%)
  local copies, waits for them, and re-layouts  31.3 us (9%)
  other arithmetic  16.8 us (5%)
  between operations  13.4 us (4%)
  starting transfers between devices  12.6 us (4%)
    reduce_scatter x1, waiting for transfers between devices, shards(): lax.psum_scatter(both_first, 'head', scatter_dimension=1, tiled=True)  64.9 us
    reduce_scatter x1, waiting for transfers between devices, shards(): lax.psum_scatter(both_second, 'head', scatter_dimension=1, tiled=True)  62.5 us
    all_gather x1, waiting for transfers between devices, shards(): gathered = lax.all_gather(states, 'head', axis=1, tiled=True)  35.1 us
    dot_general x2, matrix products, feed(): return jnp.dot(hidden, down_weight, preferred_element_type=jnp.float32)  30.5 us
    all_to_all x1, waiting for transfers between devices, gather_by_all_to_all(): return lax.all_to_all(copies, axis, split_axis=0, concat_axis=0, tiled=True)  27.1 us
    unnamed x50, local copies, waits for them, and re-layouts  12.8 us
    sub x1, matrix products, attend(): exp_scores = jnp.exp(scores - peak)  10.2 us
    dot_general x1, matrix products, shards(): joined = jnp.dot(pre_normed, qkv_full, preferred_element_type=jnp.float32)  9.12 us
  transfers between devices with their start and end apart: 6, of which 5 were waited for; matrix products, arithmetic and copies ran while one was open for 24% of the time, Pallas kernels for 0%

profile of v3, /device:TPU:0, one launch (start us, length us, event | category | flops | bytes accessed | tf_op | source)
XLA Modules:
  0.0 333.2 jit_solution(9796448847202854535)
XLA Ops:
  6.5 0.7 all-gather.3.cloned.1.call-update
  7.3 1.2 constant_dynamic-update-slice_fusion.7
  8.4 1.2 constant_dynamic-update-slice_fusion.6
  9.6 1.2 constant_dynamic-update-slice_fusion.5
  10.8 1.2 constant_dynamic-update-slice_fusion.4
  12.0 0.1 constant_dynamic-update-slice_fusion.3
  12.1 0.1 constant_dynamic-update-slice_fusion.2
  12.2 0.1 constant_dynamic-update-slice_fusion.1
  12.2 0.1 constant_dynamic-update-slice_fusion
  12.3 2.6 copy-done.3
  14.9 8.2 %all-to-all-start.1 = ((bf16[8,512,768]{2,1,0:T(8,128)(2,1)}), bf16[8,512,768]{2,1,0:T(8,128)(2,1)}, u32[]{:S(2)}, u32[]{:S(2)}) async-start(bf16[8,512,768]{2,1,0:T(8,128)(2,1)} %bitcast.55), calls=%async_computation.1 | async-start | bytes 12582912 | tf_op jit(solution)/shard_map/all_to_all | solution.py:81
  23.1 0.0 all-gather.5.cloned.1.call-start
  23.2 0.7 all-gather.5.cloned.1.call-update
  23.9 0.1 eq.58
  24.0 0.1 reshape.212
  24.1 0.1 convert_reduce_fusion.1
  24.2 0.2 reduce-window.8
  24.4 0.1 broadcast_bitcast_fusion
  24.4 0.1 select_reduce_fusion.1
  24.5 0.2 multiply_cosine_fusion
  24.7 0.8 copy.54
  25.6 0.8 copy.55
  26.4 0.1 compare_reduce_fusion
  26.5 0.1 fusion.145
  26.6 0.3 compare_and_fusion.1
  26.9 0.7 compare_and_fusion
  27.7 1.2 pad_add_fusion
  28.8 35.1 %all-gather.3.cloned.1.call-done = bf16[512,4096]{1,0:T(8,128)(2,1)} async-done(((bf16[512,256]{1,0:T(8,128)(2,1)}), bf16[512,4096]{1,0:T(8,128)(2,1)}) %all-gather.3.cloned.1.call-update) | async-done | bytes 4194320 | tf_op jit(solution)/shard_map/all_gather | solution.py:104
  63.9 3.0 convert_reduce_fusion
  66.9 0.5 copy-done.1
  67.4 1.2 fusion.9
  68.6 3.6 %fusion.6 = bf16[512,4096]{1,0:T(8,128)(2,1)} fusion(bf16[512,4096]{1,0:T(8,128)(2,1)S(1)} %copy-done.1, f32[4096]{0:T(1024)S(1)} %copy-done.8, f32[4096]{0:T(1024)S(1)} %copy-done.9, f32[512]{0:T(512)S(1)} %add_rsqrt_fusion, f32[512]{0:T(512)S(1)} %broadcast_multiply_fusion), kind=kLoop, calls=%fused_computation.12 | loop fusion | flops 12582912 | bytes 8425472 | tf_op jit(solution)/shard_map/convert_element_type | solution.py:17
  72.2 15.4 %fusion.68 = f32[256,4096]{1,0:T(8,128)} fusion(bf16[1024,4096]{1,0:T(8,128)(2,1)} %param.29, bf16[4096,1024]{1,0:T(8,128)(2,1)} %param.27, bf16[512,4096]{1,0:T(8,128)(2,1)} %fusion.6, f32[1024]{0:T(1024)S(1)} %copy-done.18), kind=kOutput, calls=%fused_computation.89 | convolution fusion | flops 4312268800 | bytes 23072768 | tf_op jit(solution)/shard_map/dot_general | solution.py:118
  87.6 1.8 copy.68
  89.4 27.1 %all-to-all-done.1 = bf16[8,512,768]{2,1,0:T(8,128)(2,1)} async-done(((bf16[8,512,768]{2,1,0:T(8,128)(2,1)}), bf16[8,512,768]{2,1,0:T(8,128)(2,1)}, u32[]{:S(2)}, u32[]{:S(2)}) %all-to-all-start.1) | async-done | bytes 6291488 | tf_op jit(solution)/shard_map/all_to_all | solution.py:81
  116.5 4.1 %all-to-all-start = ((bf16[9,2,16,16,256]{4,2,1,0,3:T(8,128)(2,1)}), bf16[9,2,16,16,256]{4,2,1,0,3:T(8,128)(2,1)S(1)}, u32[]{:S(2)}, u32[]{:S(2)}) async-start(bf16[9,2,16,16,256]{4,2,1,0,3:T(8,128)(2,1)} %bitcast.53), calls=%async_computation | async-start | bytes 4718592 | tf_op jit(solution)/shard_map/all_to_all | solution.py:75
  120.6 0.2 reduce-scatter.5.cloned.1.call-start
  120.9 9.1 %fusion.25 = f32[512,768]{1,0:T(8,128)} fusion(bf16[4096,768]{1,0:T(8,128)(2,1)} %bitcast.9, bf16[512,4096]{1,0:T(8,128)(2,1)} %all-gather.3.cloned.1.call-done, f32[4096]{0:T(1024)S(1)} %copy-done.15, f32[4096]{0:T(1024)S(1)} %copy-done.16, f32[512]{0:T(512)S(1)} %add_rsqrt_fusion, f32[512]{0:T(512)S(1)} %broadcast_multiply_fusion, f32[768]{0:T(1024)S(1)} %copy-done.17), kind=kOutput, calls=%fused_computation.37 | convolution fusion | flops 3234201600 | bytes 12098560 | tf_op jit(solution)/shard_map/dot_general | solution.py:123
  130.0 3.1 copy.50
  133.1 2.1 fusion.217
  135.2 0.2 copy.58
  135.4 1.2 copy.59
  136.6 0.8 slice.112
  137.5 0.8 slice.113
  138.3 1.8 fusion.136
  140.1 2.5 subtract_convert_fusion.1
  142.5 8.7 %all-to-all-done = bf16[9,2,16,16,256]{4,2,1,0,3:T(8,128)(2,1)S(1)} async-done(((bf16[9,2,16,16,256]{4,2,1,0,3:T(8,128)(2,1)}), bf16[9,2,16,16,256]{4,2,1,0,3:T(8,128)(2,1)S(1)}, u32[]{:S(2)}, u32[]{:S(2)}) %all-to-all-start) | async-done | bytes 2359328 | tf_op jit(solution)/shard_map/all_to_all | solution.py:75
  151.2 2.0 gather_fusion
  153.2 1.7 fusion.216
  154.9 0.3 reshape_squeeze.7
  155.2 1.1 copy.57
  156.4 0.3 reshape_squeeze.6
  156.6 0.8 copy.52
  157.5 10.2 %fusion.218 = (f32[2,512]{1,0:T(2,128)S(1)}, f32[2,512,2560]{2,1,0:T(8,128)}) fusion(pred[512,2560]{1,0:T(8,128)(4,1)S(1)} %copy-done.6, bf16[512,2,96]{2,0,1:T(8,128)(2,1)} %slice.112, bf16[512,2,16]{2,0,1:T(8,128)(2,1)} %get-tuple-element.25, bf16[512,2,16]{2,0,1:T(8,128)(2,1)} %get-tuple-element.26, bf16[2048,2,128]{2,0,1:T(8,128)(2,1)} %copy.57, ...), kind=kOutput, calls=%fused_computation.272 | convolution fusion | flops 687606272 | bytes 13373440 | tf_op jit(solution)/shard_map/sub | solution.py:64
  167.7 5.9 %fusion.42 = bf16[2,128,512]{2,1,0:T(8,128)(2,1)S(1)} fusion(f32[2,512,2560]{2,1,0:T(8,128)} %get-tuple-element.32, f32[2,512]{1,0:T(2,128)S(1)} %get-tuple-element.31, bf16[512,2,128]{0,2,1:T(8,128)(2,1)S(1)} %copy-done.7, bf16[2048,2,128]{0,2,1:T(8,128)(2,1)S(1)} %copy.52), kind=kOutput, calls=%fused_computation.51 | convolution fusion | flops 679084032 | bytes 12062720 | tf_op jit(solution)/shard_map/htk,khd->thd/dot_general | solution.py:66
  173.6 3.0 fusion.221
  176.6 3.2 copy-done.2
  179.9 1.9 fusion.18
  181.7 15.1 %fusion.15 = bf16[256,4096]{1,0:T(8,128)(2,1)} fusion(bf16[1024,4096]{1,0:T(8,128)(2,1)} %param.29, f32[512,4096]{1,0:T(8,128)} %copy-done.2, bf16[256,4096]{1,0:T(8,128)(2,1)S(1)} %slice-done, bf16[4096,1024]{1,0:T(8,128)(2,1)} %param.27, f32[1024]{0:T(1024)S(1)} %copy-done.18), kind=kOutput, calls=%fused_computation.23 | convolution fusion | flops 4314365952 | bytes 25169920 | tf_op jit(solution)/shard_map/dot_general | solution.py:118
  196.9 0.0 reduce-scatter.3.cloned.1.call-start
  196.9 0.5 reduce-scatter.3.cloned.1.call-update
  197.4 62.5 %reduce-scatter.5.cloned.1.call-done = bf16[256,256]{1,0:T(8,128)(2,1)} async-done(((bf16[256,4096]{1,0:T(8,128)(2,1)}), bf16[256,256]{1,0:T(8,128)(2,1)}) %reduce-scatter.5.cloned.1.call-update) | async-done | bytes 131088 | tf_op jit(solution)/shard_map/reduce_scatter | solution.py:147
  260.0 64.9 %reduce-scatter.3.cloned.1.call-done = bf16[256,256]{1,0:T(8,128)(2,1)} async-done(((bf16[256,4096]{1,0:T(8,128)(2,1)}), bf16[256,256]{1,0:T(8,128)(2,1)}) %reduce-scatter.3.cloned.1.call-update) | async-done | bytes 131088 | tf_op jit(solution)/shard_map/reduce_scatter | solution.py:145
  324.9 1.7 add_convert_fusion
  (53 shorter events, 0.2 us)
Async XLA Ops:
  6.5 5.5 %copy-start = (bf16[512,768]{1,0:T(8,128)(2,1)S(1)}, bf16[512,768]{1,0:T(8,128)(2,1)}, u32[]{:S(2)}) copy-start(bf16[512,768]{1,0:T(8,128)(2,1)} %param.23) | copy-start | bytes 2359300
  6.5 57.4 %all-gather.3.cloned.1.call-start = ((), (), s32[]{:S(2)}) async-start(), calls=%async_computation.4 | async-start | bytes 4456448 | tf_op jit(solution)/shard_map/all_gather | solution.py:104
  12.3 2.7 copy-start.3
  14.9 9.0 %copy-start.19 = (s32[2,64]{1,0:T(2,128)S(1)}, s32[2,64]{1,0:T(2,128)}, u32[]{:S(2)}) copy-start(s32[2,64]{1,0:T(2,128)} %param.34) | copy-start | bytes 1540
  14.9 9.1 %copy-start.11 = (s32[512]{0:T(512)S(1)}, s32[512]{0:T(512)}, u32[]{:S(2)}) copy-start(s32[512]{0:T(512)} %param.32) | copy-start | bytes 6148
  14.9 9.4 %copy-start.10 = (s32[2]{0:T(128)S(1)}, s32[2]{0:T(128)}, u32[]{:S(2)}) copy-start(s32[2]{0:T(128)} %param.33) | copy-start | bytes 28
  14.9 11.5 %copy-start.14 = (s32[8,2]{0,1:T(2,128)S(1)}, s32[8,2]{0,1:T(2,128)}, u32[]{:S(2)}) copy-start(s32[8,2]{0,1:T(2,128)} %param.35) | copy-start | bytes 196
  14.9 101.6 %all-to-all-start.1 = ((bf16[8,512,768]{2,1,0:T(8,128)(2,1)}), bf16[8,512,768]{2,1,0:T(8,128)(2,1)}, u32[]{:S(2)}, u32[]{:S(2)}) async-start(bf16[8,512,768]{2,1,0:T(8,128)(2,1)} %bitcast.55), calls=%async_computation.1 | async-start | bytes 12582912 | tf_op jit(solution)/shard_map/all_to_all | solution.py:81
  23.1 150.5 %all-gather.5.cloned.1.call-start = ((), (), s32[]{:S(2)}) async-start(), calls=%async_computation.5 | async-start | bytes 2359296 | tf_op jit(solution)/shard_map/all_gather | solution.py:106
  25.6 43.0 %copy-start.8 = (f32[4096]{0:T(1024)S(1)}, f32[4096]{0:T(1024)}, u32[]{:S(2)}) copy-start(f32[4096]{0:T(1024)} %param.22) | copy-start | bytes 49156
  25.6 43.0 %copy-start.9 = (f32[4096]{0:T(1024)S(1)}, f32[4096]{0:T(1024)}, u32[]{:S(2)}) copy-start(f32[4096]{0:T(1024)} %param.21) | copy-start | bytes 49156
  63.9 3.4 %copy-start.1 = (bf16[512,4096]{1,0:T(8,128)(2,1)S(1)}, bf16[512,4096]{1,0:T(8,128)(2,1)}, u32[]{:S(2)}) copy-start(bf16[512,4096]{1,0:T(8,128)(2,1)} %all-gather.3.cloned.1.call-done) | copy-start | bytes 12582916
  67.4 4.8 %copy-start.18 = (f32[1024]{0:T(1024)S(1)}, f32[1024]{0:T(1024)}, u32[]{:S(2)}) copy-start(f32[1024]{0:T(1024)} %param.28) | copy-start | bytes 12292
  72.2 15.4 %copy-start.5 = (bf16[9,2,16,4096]{3,2,1,0:T(8,128)(2,1)S(1)}, bf16[9,2,16,4096]{3,2,1,0:T(8,128)(2,1)}, u32[]{:S(2)}) copy-start(bf16[9,2,16,4096]{3,2,1,0:T(8,128)(2,1)} %param.31) | copy-start | bytes 7077892
  87.6 33.3 %copy-start.15 = (f32[4096]{0:T(1024)S(1)}, f32[4096]{0:T(1024)}, u32[]{:S(2)}) copy-start(f32[4096]{0:T(1024)} %param.20) | copy-start | bytes 49156
  87.6 33.3 %copy-start.16 = (f32[4096]{0:T(1024)S(1)}, f32[4096]{0:T(1024)}, u32[]{:S(2)}) copy-start(f32[4096]{0:T(1024)} %param.19) | copy-start | bytes 49156
  87.6 33.3 %copy-start.17 = (f32[768]{0:T(1024)S(1)}, f32[768]{0:T(1024)}, u32[]{:S(2)}) copy-start(f32[768]{0:T(1024)} %param.24) | copy-start | bytes 9220
  116.5 34.7 %all-to-all-start = ((bf16[9,2,16,16,256]{4,2,1,0,3:T(8,128)(2,1)}), bf16[9,2,16,16,256]{4,2,1,0,3:T(8,128)(2,1)S(1)}, u32[]{:S(2)}, u32[]{:S(2)}) async-start(bf16[9,2,16,16,256]{4,2,1,0,3:T(8,128)(2,1)} %bitcast.53), calls=%async_computation | async-start | bytes 4718592 | tf_op jit(solution)/shard_map/all_to_all | solution.py:75
  120.6 139.4 %reduce-scatter.5.cloned.1.call-start = ((), (), s32[]{:S(2)}) async-start(), calls=%async_computation.7 | async-start | bytes 2228224 | tf_op jit(solution)/shard_map/reduce_scatter | solution.py:147
  155.2 2.2 copy-start.6
  157.5 10.2 %copy-start.7 = (bf16[512,2,128]{0,2,1:T(8,128)(2,1)S(1)}, bf16[512,2,128]{0,2,1:T(8,128)(2,1)}, u32[]{:S(2)}) copy-start(bf16[512,2,128]{0,2,1:T(8,128)(2,1)} %fusion.136) | copy-start | bytes 786436
  173.6 6.3 %copy-start.4 = (f32[256,4096]{1,0:T(8,128)S(1)}, f32[256,4096]{1,0:T(8,128)}, u32[]{:S(2)}) copy-start(f32[256,4096]{1,0:T(8,128)} %fusion.68) | copy-start | bytes 12582916
  176.6 3.2 copy-start.2
  179.9 1.9 slice-start
  181.7 143.1 %copy-start.12 = (f32[256]{0:T(256)S(1)}, f32[256]{0:T(256)}, u32[]{:S(2)}) copy-start(f32[256]{0:T(256)} %param.30) | copy-start | bytes 3076
  181.7 143.1 %copy-start.13 = (f32[256]{0:T(256)S(1)}, f32[256]{0:T(256)}, u32[]{:S(2)}) copy-start(f32[256]{0:T(256)} %param.26) | copy-start | bytes 3076
  196.9 128.0 %reduce-scatter.3.cloned.1.call-start = ((), (), s32[]{:S(2)}) async-start(), calls=%async_computation.6 | async-start | bytes 2228224 | tf_op jit(solution)/shard_map/reduce_scatter | solution.py:145
Sparse Core Ops, SparseCore 0:
  9.0 54.9 all-gather.2
  66.1 83.3 all-gather.4
  197.0 62.9 reduce-scatter.4
  262.2 62.6 reduce-scatter.2

commit v4 on v3

--- a/solution.py
+++ b/solution.py
@@ -77,7 +77,10 @@
 
 
 def gather_by_all_to_all(block, axis):
-    copies = jnp.concatenate([block] * lax.axis_size(axis), axis=0)
+    count = lax.axis_size(axis)
+    copies = jnp.broadcast_to(block[None], (count,) + block.shape).reshape(
+        (count * block.shape[0],) + block.shape[1:]
+    )
     return lax.all_to_all(copies, axis, split_axis=0, concat_axis=0, tiled=True)
 
 
@@ -108,7 +111,6 @@
     pre_normed = layer_norm(wide, pre_gain, pre_shift)
     mlp_normed = layer_norm(wide, mlp_gain, mlp_shift)
     tok_rows = gathered.shape[0]
-    half = tok_rows // 2
 
     def feed(normed):
         hidden = jax.nn.gelu(
@@ -117,8 +119,8 @@
         ).astype(jnp.bfloat16)
         return jnp.dot(hidden, down_weight, preferred_element_type=jnp.float32)
 
-    feed_first = feed(mlp_normed[:half])
-    kv_cache, feed_first = lax.optimization_barrier((kv_cache, feed_first))
+    feed_part = feed(mlp_normed)
+    kv_cache, feed_part = lax.optimization_barrier((kv_cache, feed_part))
     page_pool = share_pages(kv_cache, lax.axis_size("head"))
     joined = jnp.dot(pre_normed, qkv_full, preferred_element_type=jnp.float32)
     joined = (joined + qkv_bias).reshape(tok_rows, -1, 3, HD)
@@ -140,12 +142,9 @@
         queries, new_keys, new_values, cache_keys, cache_values, local_req, cached_len, positions
     ).reshape(tok_rows, -1)
     attention_part = jnp.dot(heads_out, out_full, preferred_element_type=jnp.float32)
-    both_first = (attention_part[:half] + feed_first).astype(jnp.bfloat16)
-    both_first, normed_second = lax.optimization_barrier((both_first, mlp_normed[half:]))
-    summed_first = lax.psum_scatter(both_first, "head", scatter_dimension=1, tiled=True)
-    both_second = (attention_part[half:] + feed(normed_second)).astype(jnp.bfloat16)
-    summed_second = lax.psum_scatter(both_second, "head", scatter_dimension=1, tiled=True)
-    summed = jnp.concatenate([summed_first, summed_second], axis=0).astype(jnp.float32)
+    summed = lax.psum_scatter(
+        (attention_part + feed_part).astype(jnp.bfloat16), "head", scatter_dimension=1, tiled=True
+    ).astype(jnp.float32)
     return (summed + out_bias + down_bias).astype(jnp.bfloat16)
 
 

time: 334 us -> 259 us (0.78)
  waiting for transfers between devices: 200 us -> 139 us
  other arithmetic: 16.8 us -> 11.4 us
  local copies, waits for them, and re-layouts: 31.3 us -> 26 us
    reduce_scatter x2 -> x1, waiting for transfers between devices: 127 us -> 65.1 us  [shards(): lax.psum_scatter((attention_part + feed_part).astype(jnp.bfloat16), 'head...]
    unnamed x50 -> x37, local copies, waits for them, and re-layouts: 12.8 us -> 2.04 us
    dot_general x2 -> x1, matrix products: 30.5 us -> 23.9 us  [feed(): return jnp.dot(hidden, down_weight, preferred_element_type=jnp.float32)]
    all_to_all x1, waiting for transfers between devices: 27.1 us -> 20.8 us  [gather_by_all_to_all(): return lax.all_to_all(copies, axis, split_axis=0, concat_axis=0, tiled=True)]
    convert_element_type x2 -> x0, other arithmetic: 5.42 us -> none  [the longest x1 3.55 us: layer_norm(): (centred * lax.rsqrt(row_var + epsilon) * gain + shift).astype(jnp.bfloat16)]
    dot_general x1, matrix products: 3.02 us -> 7.27 us  [shards(): jnp.dot(heads_out, out_full, preferred_element_type=jnp.float32)]
    broadcast_in_dim x0 -> x1, local copies, waits for them, and re-layouts: none -> 4.14 us  [gather_by_all_to_all(): jnp.broadcast_to(block[None], (count,) + block.shape)]
    all_gather x1, waiting for transfers between devices: 35.1 us -> 39 us  [shards(): gathered = lax.all_gather(states, 'head', axis=1, tiled=True)]
  transfers between devices with their start and end apart: 6 -> 5, of which waited for: 5 -> 4; matrix products, arithmetic and copies ran while one was open for 24% -> 33% of each run, Pallas kernels for 0% -> 0%
where the time goes in v4:
time: 259 us
  waiting for transfers between devices  139 us (54%)
  matrix products  56.3 us (22%)
  local copies, waits for them, and re-layouts  26 us (10%)
  between operations  13.4 us (5%)
  starting transfers between devices  12.6 us (5%)
  other arithmetic  11.4 us (4%)
    reduce_scatter x1, waiting for transfers between devices, shards(): lax.psum_scatter((attention_part + feed_part).astype(jnp.bfloat16), 'head...  65.1 us
    all_gather x1, waiting for transfers between devices, shards(): gathered = lax.all_gather(states, 'head', axis=1, tiled=True)  39 us
    dot_general x1, matrix products, feed(): return jnp.dot(hidden, down_weight, preferred_element_type=jnp.float32)  23.9 us
    all_to_all x1, waiting for transfers between devices, gather_by_all_to_all(): return lax.all_to_all(copies, axis, split_axis=0, concat_axis=0, tiled=True)  20.8 us
    all_to_all x1, waiting for transfers between devices, share_pages(): lax.all_to_all(grouped, 'head', split_axis=3, concat_axis=0, tiled=True)  12.5 us
    sub x1, matrix products, attend(): exp_scores = jnp.exp(scores - peak)  9.86 us
    dot_general x1, matrix products, shards(): joined = jnp.dot(pre_normed, qkv_full, preferred_element_type=jnp.float32)  9.21 us
    all_to_all x1, starting transfers between devices, gather_by_all_to_all(): return lax.all_to_all(copies, axis, split_axis=0, concat_axis=0, tiled=True)  8.17 us
  transfers between devices with their start and end apart: 5, of which 4 were waited for; matrix products, arithmetic and copies ran while one was open for 33% of the time, Pallas kernels for 0%

profile of v4, /device:TPU:0, one launch (start us, length us, event | category | flops | bytes accessed | tf_op | source)
XLA Modules:
  0.0 258.6 jit_solution(3675836591766926590)
XLA Ops:
  6.5 0.0 all-gather.3.cloned.1.call-start
  6.5 0.7 all-gather.3.cloned.1.call-update
  7.3 4.1 %broadcast_in_dim.47 = bf16[8,512,768]{2,1,0:T(8,128)(2,1)} broadcast(bf16[512,768]{1,0:T(8,128)(2,1)} %param.23), dimensions={1,2} | broadcast | bytes 7077888 | tf_op jit(solution)/shard_map/broadcast_in_dim | solution.py:81
  11.4 8.2 %all-to-all-start.1 = ((bf16[8,512,768]{2,1,0:T(8,128)(2,1)}), bf16[8,512,768]{2,1,0:T(8,128)(2,1)}, u32[]{:S(2)}, u32[]{:S(2)}) async-start(bf16[8,512,768]{2,1,0:T(8,128)(2,1)} %broadcast_in_dim.47), calls=%async_computation.1 | async-start | bytes 12582912 | tf_op jit(solution)/shard_map/all_to_all | solution.py:84
  19.6 0.0 all-gather.5.cloned.1.call-start
  19.6 0.7 all-gather.5.cloned.1.call-update
  20.4 0.0 copy-done.6
  20.4 0.1 convert_reduce_fusion.1
  20.5 0.2 reduce-window.8
  20.7 0.0 copy-done.5
  20.7 0.1 broadcast_bitcast_fusion
  20.8 0.1 select_reduce_fusion.1
  20.9 0.0 copy-done.9
  20.9 0.0 copy-done.16
  20.9 0.1 eq.58
  21.0 0.1 compare_reduce_fusion
  21.1 0.1 fusion.103
  21.2 0.2 multiply_cosine_fusion
  21.4 0.1 reshape.215
  21.4 0.8 copy.54
  22.3 0.8 copy.55
  23.1 0.3 compare_and_fusion.1
  23.4 0.7 compare_and_fusion
  24.1 1.2 pad_add_fusion
  25.3 39.0 %all-gather.3.cloned.1.call-done = bf16[512,4096]{1,0:T(8,128)(2,1)} async-done(((bf16[512,256]{1,0:T(8,128)(2,1)}), bf16[512,4096]{1,0:T(8,128)(2,1)}) %all-gather.3.cloned.1.call-update) | async-done | bytes 4194320 | tf_op jit(solution)/shard_map/all_gather | solution.py:107
  64.3 3.0 %convert_reduce_fusion = f32[512]{0:T(512)S(1)} fusion(bf16[512,4096]{1,0:T(8,128)(2,1)} %all-gather.3.cloned.1.call-done), kind=kLoop, calls=%fused_computation.3 | loop fusion | flops 4193792 | bytes 4196352 | tf_op jit(solution)/shard_map/reduce_sum | solution.py:14
  67.2 0.5 copy-done
  67.7 1.2 fusion.9
  69.0 0.0 copy-done.10
  69.0 0.0 copy-done.11
  69.0 0.0 copy-start.1
  69.0 23.9 %fusion.40 = f32[512,4096]{1,0:T(8,128)} fusion(bf16[1024,4096]{1,0:T(8,128)(2,1)} %param.29, bf16[4096,1024]{1,0:T(8,128)(2,1)} %param.27, bf16[512,4096]{1,0:T(8,128)(2,1)} %all-gather.3.cloned.1.call-done, f32[4096]{0:T(1024)S(1)} %copy-done.10, f32[4096]{0:T(1024)S(1)} %copy-done.11, f32[512]{0:T(512)S(1)} %add_rsqrt_fusion, ...), kind=kOutput, calls=%fused_computation.54 | convolution fusion | flops 8637120512 | bytes 29401088 | tf_op jit(solution)/shard_map/dot_general | solution.py:120
  92.9 0.0 copy-done.1
  92.9 1.8 copy.68
  94.7 20.8 %all-to-all-done.1 = bf16[8,512,768]{2,1,0:T(8,128)(2,1)} async-done(((bf16[8,512,768]{2,1,0:T(8,128)(2,1)}), bf16[8,512,768]{2,1,0:T(8,128)(2,1)}, u32[]{:S(2)}, u32[]{:S(2)}) %all-to-all-start.1) | async-done | bytes 6291488 | tf_op jit(solution)/shard_map/all_to_all | solution.py:84
  115.5 4.4 %all-to-all-start = ((bf16[9,2,16,16,256]{4,2,1,0,3:T(8,128)(2,1)}), bf16[9,2,16,16,256]{4,2,1,0,3:T(8,128)(2,1)S(1)}, u32[]{:S(2)}, u32[]{:S(2)}) async-start(bf16[9,2,16,16,256]{4,2,1,0,3:T(8,128)(2,1)} %bitcast.49), calls=%async_computation | async-start | bytes 4718592 | tf_op jit(solution)/shard_map/all_to_all | solution.py:75
  119.9 0.0 reduce-scatter.2.cloned.1.call-start
  120.0 0.0 copy-done.12
  120.0 0.0 copy-done.13
  120.0 0.0 copy-done.15
  120.0 9.2 %fusion.42 = f32[512,768]{1,0:T(8,128)} fusion(bf16[4096,768]{1,0:T(8,128)(2,1)} %bitcast.8, bf16[512,4096]{1,0:T(8,128)(2,1)} %all-gather.3.cloned.1.call-done, f32[4096]{0:T(1024)S(1)} %copy-done.12, f32[4096]{0:T(1024)S(1)} %copy-done.13, f32[512]{0:T(512)S(1)} %add_rsqrt_fusion, f32[512]{0:T(512)S(1)} %broadcast_multiply_fusion, f32[768]{0:T(1024)S(1)} %copy-done.15), kind=kOutput, calls=%fused_computation.55 | convolution fusion | flops 3234201600 | bytes 12098560 | tf_op jit(solution)/shard_map/dot_general | solution.py:125
  129.3 3.0 %copy.50 = f32[512,768]{0,1:T(8,128)} copy(f32[512,768]{1,0:T(8,128)} %fusion.42) | data formatting | bytes 3145728 | tf_op jit(solution)/shard_map/add | solution.py:126
  132.3 2.1 fusion.145
  134.4 0.2 copy.58
  134.6 1.2 copy.59
  135.8 0.8 slice.80
  136.7 0.8 slice.81
  137.5 1.8 fusion.94
  139.3 2.5 subtract_convert_fusion.1
  141.8 12.5 %all-to-all-done = bf16[9,2,16,16,256]{4,2,1,0,3:T(8,128)(2,1)S(1)} async-done(((bf16[9,2,16,16,256]{4,2,1,0,3:T(8,128)(2,1)}), bf16[9,2,16,16,256]{4,2,1,0,3:T(8,128)(2,1)S(1)}, u32[]{:S(2)}, u32[]{:S(2)}) %all-to-all-start) | async-done | bytes 2359328 | tf_op jit(solution)/shard_map/all_to_all | solution.py:75
  154.3 2.0 gather_fusion
  156.2 1.7 fusion.144
  157.9 0.5 reshape_squeeze.7
  158.5 1.1 copy.57
  159.6 0.3 reshape_squeeze.6
  159.9 2.1 copy.52
  161.9 0.0 copy-done.2
  161.9 9.9 %fusion.146 = (f32[2,512]{1,0:T(2,128)S(1)}, f32[2,512,2560]{2,1,0:T(8,128)}) fusion(pred[512,2560]{1,0:T(8,128)(4,1)S(1)} %copy-done.2, bf16[512,2,96]{2,0,1:T(8,128)(2,1)} %slice.80, bf16[512,2,16]{2,0,1:T(8,128)(2,1)} %get-tuple-element.21, bf16[512,2,16]{2,0,1:T(8,128)(2,1)} %get-tuple-element.22, bf16[2048,2,128]{2,0,1:T(8,128)(2,1)S(1)} %copy-done.3, ...), kind=kOutput, calls=%fused_computation.182 | convolution fusion | flops 687606272 | bytes 13373440 | tf_op jit(solution)/shard_map/sub | solution.py:64
  171.8 6.0 %fusion.56 = bf16[2,128,512]{2,1,0:T(8,128)(2,1)S(1)} fusion(f32[2,512,2560]{2,1,0:T(8,128)} %get-tuple-element.28, f32[2,512]{1,0:T(2,128)S(1)} %get-tuple-element.27, bf16[512,2,128]{0,2,1:T(8,128)(2,1)} %fusion.94, bf16[2048,2,128]{0,2,1:T(8,128)(2,1)S(1)} %copy-done.4), kind=kOutput, calls=%fused_computation.67 | convolution fusion | flops 679084032 | bytes 12062720 | tf_op jit(solution)/shard_map/htk,khd->thd/dot_general | solution.py:66
  177.8 0.0 all-gather.5.cloned.1.call-done
  177.9 7.3 %add_convert_fusion = bf16[512,4096]{1,0:T(8,128)(2,1)} fusion(f32[512,4096]{1,0:T(8,128)} %fusion.40, bf16[512,256]{0,1:T(8,128)(2,1)S(1)} %bitcast.58, bf16[256,4096]{1,0:T(8,128)(2,1)} %all-gather.5.cloned.1.call-done), kind=kOutput, calls=%fused_computation.16 | convolution fusion | flops 1077936128 | bytes 14942208 | tf_op jit(solution)/shard_map/dot_general | solution.py:144
  185.1 0.0 reduce-scatter.2.cloned.1.call-update
  185.2 65.1 %reduce-scatter.2.cloned.1.call-done = bf16[512,256]{1,0:T(8,128)(2,1)} async-done(((bf16[512,4096]{1,0:T(8,128)(2,1)}), bf16[512,256]{1,0:T(8,128)(2,1)}) %reduce-scatter.2.cloned.1.call-update) | async-done | bytes 262160 | tf_op jit(solution)/shard_map/reduce_scatter | solution.py:145
  250.3 1.7 add_convert_fusion.1
  (32 shorter events, 0.1 us)
Async XLA Ops:
  6.5 57.7 %all-gather.3.cloned.1.call-start = ((), (), s32[]{:S(2)}) async-start(), calls=%async_computation.3 | async-start | bytes 4456448 | tf_op jit(solution)/shard_map/all_gather | solution.py:107
  11.4 9.0 %copy-start.6 = (s32[512]{0:T(512)S(1)}, s32[512]{0:T(512)}, u32[]{:S(2)}) copy-start(s32[512]{0:T(512)} %param.32) | copy-start | bytes 6148
  11.4 9.3 %copy-start.5 = (s32[2]{0:T(128)S(1)}, s32[2]{0:T(128)}, u32[]{:S(2)}) copy-start(s32[2]{0:T(128)} %param.33) | copy-start | bytes 28
  11.4 9.5 %copy-start.9 = (s32[8,2]{0,1:T(2,128)S(1)}, s32[8,2]{0,1:T(2,128)}, u32[]{:S(2)}) copy-start(s32[8,2]{0,1:T(2,128)} %param.35) | copy-start | bytes 196
  11.4 9.5 %copy-start.16 = (s32[2,64]{1,0:T(2,128)S(1)}, s32[2,64]{1,0:T(2,128)}, u32[]{:S(2)}) copy-start(s32[2,64]{1,0:T(2,128)} %param.34) | copy-start | bytes 1540
  11.4 104.1 %all-to-all-start.1 = ((bf16[8,512,768]{2,1,0:T(8,128)(2,1)}), bf16[8,512,768]{2,1,0:T(8,128)(2,1)}, u32[]{:S(2)}, u32[]{:S(2)}) async-start(bf16[8,512,768]{2,1,0:T(8,128)(2,1)} %broadcast_in_dim.47), calls=%async_computation.1 | async-start | bytes 12582912 | tf_op jit(solution)/shard_map/all_to_all | solution.py:84
  19.6 158.3 %all-gather.5.cloned.1.call-start = ((), (), s32[]{:S(2)}) async-start(), calls=%async_computation.4 | async-start | bytes 2359296 | tf_op jit(solution)/shard_map/all_gather | solution.py:109
  64.3 3.4 %copy-start = (bf16[512,4096]{1,0:T(8,128)(2,1)S(1)}, bf16[512,4096]{1,0:T(8,128)(2,1)}, u32[]{:S(2)}) copy-start(bf16[512,4096]{1,0:T(8,128)(2,1)} %all-gather.3.cloned.1.call-done) | copy-start | bytes 12582916
  67.7 1.2 copy-start.10
  67.7 1.2 copy-start.11
  67.7 1.3 copy-start.14
  69.0 24.0 %copy-start.1 = (bf16[9,2,16,4096]{3,2,1,0:T(8,128)(2,1)S(1)}, bf16[9,2,16,4096]{3,2,1,0:T(8,128)(2,1)}, u32[]{:S(2)}) copy-start(bf16[9,2,16,4096]{3,2,1,0:T(8,128)(2,1)} %param.31) | copy-start | bytes 7077892
  115.5 4.5 %copy-start.12 = (f32[4096]{0:T(1024)S(1)}, f32[4096]{0:T(1024)}, u32[]{:S(2)}) copy-start(f32[4096]{0:T(1024)} %param.20) | copy-start | bytes 49156
  115.5 4.5 %copy-start.13 = (f32[4096]{0:T(1024)S(1)}, f32[4096]{0:T(1024)}, u32[]{:S(2)}) copy-start(f32[4096]{0:T(1024)} %param.19) | copy-start | bytes 49156
  115.5 4.5 %copy-start.15 = (f32[768]{0:T(1024)S(1)}, f32[768]{0:T(1024)}, u32[]{:S(2)}) copy-start(f32[768]{0:T(1024)} %param.24) | copy-start | bytes 9220
  115.5 38.7 %all-to-all-start = ((bf16[9,2,16,16,256]{4,2,1,0,3:T(8,128)(2,1)}), bf16[9,2,16,16,256]{4,2,1,0,3:T(8,128)(2,1)S(1)}, u32[]{:S(2)}, u32[]{:S(2)}) async-start(bf16[9,2,16,16,256]{4,2,1,0,3:T(8,128)(2,1)} %bitcast.49), calls=%async_computation | async-start | bytes 4718592 | tf_op jit(solution)/shard_map/all_to_all | solution.py:75
  119.9 130.4 %reduce-scatter.2.cloned.1.call-start = ((), (), s32[]{:S(2)}) async-start(), calls=%async_computation.5 | async-start | bytes 4456448 | tf_op jit(solution)/shard_map/reduce_scatter | solution.py:145
  159.6 2.4 copy-start.2
  159.8 2.1 copy-start.3
  161.9 9.9 %copy-start.4 = (bf16[2048,2,128]{0,2,1:T(8,128)(2,1)S(1)}, bf16[2048,2,128]{0,2,1:T(8,128)(2,1)}, u32[]{:S(2)}) copy-start(bf16[2048,2,128]{0,2,1:T(8,128)(2,1)} %copy.52) | copy-start | bytes 3145732
  185.1 65.2 %copy-start.7 = (f32[256]{0:T(256)S(1)}, f32[256]{0:T(256)}, u32[]{:S(2)}) copy-start(f32[256]{0:T(256)} %param.30) | copy-start | bytes 3076
  185.1 65.2 %copy-start.8 = (f32[256]{0:T(256)S(1)}, f32[256]{0:T(256)}, u32[]{:S(2)}) copy-start(f32[256]{0:T(256)} %param.26) | copy-start | bytes 3076
Sparse Core Ops, SparseCore 0:
  9.0 55.2 all-gather.2
  66.4 97.6 all-gather.4
  185.3 64.9 reduce-scatter.1

commit v5 on v4

--- a/solution.py
+++ b/solution.py
@@ -106,7 +106,6 @@
 ):
     gathered = lax.all_gather(states, "head", axis=1, tiled=True)
     qkv_full = gather_by_all_to_all(qkv_weight, "tok")
-    out_full = lax.all_gather(out_weight, "tok", axis=1, tiled=True)
     wide = gathered.astype(jnp.float32)
     pre_normed = layer_norm(wide, pre_gain, pre_shift)
     mlp_normed = layer_norm(wide, mlp_gain, mlp_shift)
@@ -120,7 +119,10 @@
         return jnp.dot(hidden, down_weight, preferred_element_type=jnp.float32)
 
     feed_part = feed(mlp_normed)
-    kv_cache, feed_part = lax.optimization_barrier((kv_cache, feed_part))
+    kv_cache, feed_part, out_weight, qkv_full = lax.optimization_barrier(
+        (kv_cache, feed_part, out_weight, qkv_full)
+    )
+    out_full = lax.all_gather(out_weight, "tok", axis=1, tiled=True)
     page_pool = share_pages(kv_cache, lax.axis_size("head"))
     joined = jnp.dot(pre_normed, qkv_full, preferred_element_type=jnp.float32)
     joined = (joined + qkv_bias).reshape(tok_rows, -1, 3, HD)

time: 259 us -> 269 us (1.039)
  waiting for transfers between devices: 139 us -> 149 us
    all_gather x1, waiting for transfers between devices: 0.02 us -> 14.8 us  [shards(): out_full = lax.all_gather(out_weight, 'tok', axis=1, tiled=True)]
    all_to_all x1, waiting for transfers between devices: 12.5 us -> 8.08 us  [share_pages(): lax.all_to_all(grouped, 'head', split_axis=3, concat_axis=0, tiled=True)]
  transfers between devices with their start and end apart: 5 -> 5, of which waited for: 4 -> 5; matrix products, arithmetic and copies ran while one was open for 33% -> 31% of each run, Pallas kernels for 0% -> 0%
where the time goes in v5:
time: 269 us
  waiting for transfers between devices  149 us (55%)
  matrix products  56.2 us (21%)
  local copies, waits for them, and re-layouts  26 us (10%)
  between operations  13.3 us (5%)
  starting transfers between devices  12.6 us (5%)
  other arithmetic  11.5 us (4%)
    reduce_scatter x1, waiting for transfers between devices, shards(): lax.psum_scatter((attention_part + feed_part).astype(jnp.bfloat16), 'head...  65.4 us
    all_gather x1, waiting for transfers between devices, shards(): gathered = lax.all_gather(states, 'head', axis=1, tiled=True)  39.6 us
    dot_general x1, matrix products, feed(): return jnp.dot(hidden, down_weight, preferred_element_type=jnp.float32)  23.9 us
    all_to_all x1, waiting for transfers between devices, gather_by_all_to_all(): return lax.all_to_all(copies, axis, split_axis=0, concat_axis=0, tiled=True)  19.9 us
    all_gather x1, waiting for transfers between devices, shards(): out_full = lax.all_gather(out_weight, 'tok', axis=1, tiled=True)  14.8 us
    sub x1, matrix products, attend(): exp_scores = jnp.exp(scores - peak)  9.85 us
    dot_general x1, matrix products, shards(): joined = jnp.dot(pre_normed, qkv_full, preferred_element_type=jnp.float32)  9.1 us
    all_to_all x1, starting transfers between devices, gather_by_all_to_all(): return lax.all_to_all(copies, axis, split_axis=0, concat_axis=0, tiled=True)  8.17 us
  transfers between devices with their start and end apart: 5, of which 5 were waited for; matrix products, arithmetic and copies ran while one was open for 31% of the time, Pallas kernels for 0%

profile of v5, /device:TPU:0, one launch (start us, length us, event | category | flops | bytes accessed | tf_op | source)
XLA Modules:
  0.0 268.8 jit_solution(10845542326433271639)
XLA Ops:
  6.5 0.0 all-gather.3.cloned.1.call-start
  6.5 0.7 all-gather.3.cloned.1.call-update
  7.3 4.1 %broadcast_in_dim.44 = bf16[8,512,768]{2,1,0:T(8,128)(2,1)} broadcast(bf16[512,768]{1,0:T(8,128)(2,1)} %param.23), dimensions={1,2} | broadcast | bytes 7077888 | tf_op jit(solution)/shard_map/broadcast_in_dim | solution.py:81
  11.4 8.2 %all-to-all-start = ((bf16[8,512,768]{2,1,0:T(8,128)(2,1)}), bf16[8,512,768]{2,1,0:T(8,128)(2,1)}, u32[]{:S(2)}, u32[]{:S(2)}) async-start(bf16[8,512,768]{2,1,0:T(8,128)(2,1)} %broadcast_in_dim.44), calls=%async_computation | async-start | bytes 12582912 | tf_op jit(solution)/shard_map/all_to_all | solution.py:84
  19.6 0.0 copy-done.16
  19.6 0.1 eq.58
  19.7 0.0 copy-done.6
  19.7 0.1 convert_reduce_fusion.1
  19.8 0.2 reduce-window.8
  20.0 0.0 copy-done.9
  20.0 0.1 compare_reduce_fusion
  20.1 0.1 fusion.103
  20.2 0.0 copy-done.5
  20.2 0.1 select_reduce_fusion.1
  20.3 0.1 broadcast_bitcast_fusion
  20.4 0.2 multiply_cosine_fusion
  20.6 0.1 reshape.215
  20.7 0.8 copy.54
  21.5 0.8 copy.55
  22.3 0.3 compare_and_fusion.1
  22.6 0.7 compare_and_fusion
  23.4 1.2 pad_add_fusion
  24.6 39.6 %all-gather.3.cloned.1.call-done = bf16[512,4096]{1,0:T(8,128)(2,1)} async-done(((bf16[512,256]{1,0:T(8,128)(2,1)}), bf16[512,4096]{1,0:T(8,128)(2,1)}) %all-gather.3.cloned.1.call-update) | async-done | bytes 4194320 | tf_op jit(solution)/shard_map/all_gather | solution.py:107
  64.1 3.0 %convert_reduce_fusion = f32[512]{0:T(512)S(1)} fusion(bf16[512,4096]{1,0:T(8,128)(2,1)} %all-gather.3.cloned.1.call-done), kind=kLoop, calls=%fused_computation.3 | loop fusion | flops 4193792 | bytes 4196352 | tf_op jit(solution)/shard_map/reduce_sum | solution.py:14
  67.1 0.5 copy-done
  67.6 1.2 fusion.9
  68.8 0.0 copy-done.10
  68.8 0.0 copy-done.11
  68.9 0.0 copy-done.14
  68.9 0.0 copy-start.1
  68.9 23.9 %fusion.40 = f32[512,4096]{1,0:T(8,128)} fusion(bf16[1024,4096]{1,0:T(8,128)(2,1)} %param.29, bf16[4096,1024]{1,0:T(8,128)(2,1)} %param.27, bf16[512,4096]{1,0:T(8,128)(2,1)} %all-gather.3.cloned.1.call-done, f32[4096]{0:T(1024)S(1)} %copy-done.10, f32[4096]{0:T(1024)S(1)} %copy-done.11, f32[512]{0:T(512)S(1)} %add_rsqrt_fusion, ...), kind=kOutput, calls=%fused_computation.54 | convolution fusion | flops 8637120512 | bytes 29401088 | tf_op jit(solution)/shard_map/dot_general | solution.py:119
  92.8 19.9 %all-to-all-done = bf16[8,512,768]{2,1,0:T(8,128)(2,1)} async-done(((bf16[8,512,768]{2,1,0:T(8,128)(2,1)}), bf16[8,512,768]{2,1,0:T(8,128)(2,1)}, u32[]{:S(2)}, u32[]{:S(2)}) %all-to-all-start) | async-done | bytes 6291488 | tf_op jit(solution)/shard_map/all_to_all | solution.py:84
  112.7 1.7 copy.68
  114.5 4.4 %all-to-all-start.1 = ((bf16[9,2,16,16,256]{4,2,1,0,3:T(8,128)(2,1)}), bf16[9,2,16,16,256]{4,2,1,0,3:T(8,128)(2,1)S(1)}, u32[]{:S(2)}, u32[]{:S(2)}) async-start(bf16[9,2,16,16,256]{4,2,1,0,3:T(8,128)(2,1)} %bitcast.49), calls=%async_computation.1 | async-start | bytes 4718592 | tf_op jit(solution)/shard_map/all_to_all | solution.py:75
  118.8 0.0 all-gather.5.cloned.1.call-start
  118.9 0.7 all-gather.5.cloned.1.call-update
  119.6 0.0 reduce-scatter.2.cloned.1.call-start
  119.7 0.0 copy-done.12
  119.7 0.0 copy-done.13
  119.7 0.0 copy-done.15
  119.7 9.1 %fusion.42 = f32[512,768]{1,0:T(8,128)} fusion(bf16[4096,768]{1,0:T(8,128)(2,1)} %bitcast, bf16[512,4096]{1,0:T(8,128)(2,1)} %all-gather.3.cloned.1.call-done, f32[4096]{0:T(1024)S(1)} %copy-done.12, f32[4096]{0:T(1024)S(1)} %copy-done.13, f32[512]{0:T(512)S(1)} %add_rsqrt_fusion, f32[512]{0:T(512)S(1)} %broadcast_multiply_fusion, f32[768]{0:T(1024)S(1)} %copy-done.15), kind=kOutput, calls=%fused_computation.55 | convolution fusion | flops 3234201600 | bytes 12098560 | tf_op jit(solution)/shard_map/dot_general | solution.py:127
  128.8 3.1 %copy.50 = f32[512,768]{0,1:T(8,128)} copy(f32[512,768]{1,0:T(8,128)} %fusion.42) | data formatting | bytes 3145728 | tf_op jit(solution)/shard_map/add | solution.py:128
  131.9 2.1 fusion.145
  134.0 0.2 copy.58
  134.2 1.2 copy.59
  135.4 0.8 slice.80
  136.3 0.8 slice.81
  137.1 1.8 fusion.94
  138.9 2.5 subtract_convert_fusion.1
  141.4 8.1 %all-to-all-done.1 = bf16[9,2,16,16,256]{4,2,1,0,3:T(8,128)(2,1)S(1)} async-done(((bf16[9,2,16,16,256]{4,2,1,0,3:T(8,128)(2,1)}), bf16[9,2,16,16,256]{4,2,1,0,3:T(8,128)(2,1)S(1)}, u32[]{:S(2)}, u32[]{:S(2)}) %all-to-all-start.1) | async-done | bytes 2359328 | tf_op jit(solution)/shard_map/all_to_all | solution.py:75
  149.4 2.0 gather_fusion
  151.4 1.7 fusion.144
  153.1 0.5 reshape_squeeze.7
  153.6 1.1 copy.57
  154.8 0.3 reshape_squeeze.6
  155.1 2.0 copy.52
  157.1 0.0 copy-done.2
  157.1 9.9 %fusion.146 = (f32[2,512]{1,0:T(2,128)S(1)}, f32[2,512,2560]{2,1,0:T(8,128)}) fusion(pred[512,2560]{1,0:T(8,128)(4,1)S(1)} %copy-done.2, bf16[512,2,96]{2,0,1:T(8,128)(2,1)} %slice.80, bf16[512,2,16]{2,0,1:T(8,128)(2,1)} %get-tuple-element.25, bf16[512,2,16]{2,0,1:T(8,128)(2,1)} %get-tuple-element.26, bf16[2048,2,128]{2,0,1:T(8,128)(2,1)S(1)} %copy-done.3, ...), kind=kOutput, calls=%fused_computation.182 | convolution fusion | flops 687606272 | bytes 13373440 | tf_op jit(solution)/shard_map/sub | solution.py:64
  167.0 6.1 %fusion.56 = bf16[2,128,512]{2,1,0:T(8,128)(2,1)S(1)} fusion(f32[2,512,2560]{2,1,0:T(8,128)} %get-tuple-element.32, f32[2,512]{1,0:T(2,128)S(1)} %get-tuple-element.31, bf16[512,2,128]{0,2,1:T(8,128)(2,1)} %fusion.94, bf16[2048,2,128]{0,2,1:T(8,128)(2,1)S(1)} %copy-done.4), kind=kOutput, calls=%fused_computation.67 | convolution fusion | flops 679084032 | bytes 12062720 | tf_op jit(solution)/shard_map/htk,khd->thd/dot_general | solution.py:66
  173.0 14.8 %all-gather.5.cloned.1.call-done = bf16[256,4096]{1,0:T(8,128)(2,1)} async-done(((bf16[256,512]{1,0:T(8,128)(2,1)}), bf16[256,4096]{1,0:T(8,128)(2,1)}) %all-gather.5.cloned.1.call-update) | async-done | bytes 2097168 | tf_op jit(solution)/shard_map/all_gather | solution.py:125
  187.9 7.2 %add_convert_fusion = bf16[512,4096]{1,0:T(8,128)(2,1)} fusion(f32[512,4096]{1,0:T(8,128)} %fusion.40, bf16[512,256]{0,1:T(8,128)(2,1)S(1)} %bitcast.58, bf16[256,4096]{1,0:T(8,128)(2,1)} %all-gather.5.cloned.1.call-done), kind=kOutput, calls=%fused_computation.16 | convolution fusion | flops 1077936128 | bytes 14942208 | tf_op jit(solution)/shard_map/dot_general | solution.py:146
  195.1 0.0 reduce-scatter.2.cloned.1.call-update
  195.1 65.4 %reduce-scatter.2.cloned.1.call-done = bf16[512,256]{1,0:T(8,128)(2,1)} async-done(((bf16[512,4096]{1,0:T(8,128)(2,1)}), bf16[512,256]{1,0:T(8,128)(2,1)}) %reduce-scatter.2.cloned.1.call-update) | async-done | bytes 262160 | tf_op jit(solution)/shard_map/reduce_scatter | solution.py:147
  260.6 1.7 add_convert_fusion.1
  (32 shorter events, 0.1 us)
Async XLA Ops:
  6.5 57.6 %all-gather.3.cloned.1.call-start = ((), (), s32[]{:S(2)}) async-start(), calls=%async_computation.3 | async-start | bytes 4456448 | tf_op jit(solution)/shard_map/all_gather | solution.py:107
  11.4 8.2 %copy-start.16 = (s32[2,64]{1,0:T(2,128)S(1)}, s32[2,64]{1,0:T(2,128)}, u32[]{:S(2)}) copy-start(s32[2,64]{1,0:T(2,128)} %param.34) | copy-start | bytes 1540
  11.4 8.3 %copy-start.6 = (s32[512]{0:T(512)S(1)}, s32[512]{0:T(512)}, u32[]{:S(2)}) copy-start(s32[512]{0:T(512)} %param.32) | copy-start | bytes 6148
  11.4 8.6 %copy-start.9 = (s32[8,2]{0,1:T(2,128)S(1)}, s32[8,2]{0,1:T(2,128)}, u32[]{:S(2)}) copy-start(s32[8,2]{0,1:T(2,128)} %param.35) | copy-start | bytes 196
  11.4 8.8 %copy-start.5 = (s32[2]{0:T(128)S(1)}, s32[2]{0:T(128)}, u32[]{:S(2)}) copy-start(s32[2]{0:T(128)} %param.33) | copy-start | bytes 28
  11.4 101.3 %all-to-all-start = ((bf16[8,512,768]{2,1,0:T(8,128)(2,1)}), bf16[8,512,768]{2,1,0:T(8,128)(2,1)}, u32[]{:S(2)}, u32[]{:S(2)}) async-start(bf16[8,512,768]{2,1,0:T(8,128)(2,1)} %broadcast_in_dim.44), calls=%async_computation | async-start | bytes 12582912 | tf_op jit(solution)/shard_map/all_to_all | solution.py:84
  64.1 3.4 %copy-start = (bf16[512,4096]{1,0:T(8,128)(2,1)S(1)}, bf16[512,4096]{1,0:T(8,128)(2,1)}, u32[]{:S(2)}) copy-start(bf16[512,4096]{1,0:T(8,128)(2,1)} %all-gather.3.cloned.1.call-done) | copy-start | bytes 12582916
  67.6 1.2 copy-start.10
  67.6 1.2 copy-start.11
  67.6 1.3 copy-start.14
  68.9 43.9 %copy-start.1 = (bf16[9,2,16,4096]{3,2,1,0:T(8,128)(2,1)S(1)}, bf16[9,2,16,4096]{3,2,1,0:T(8,128)(2,1)}, u32[]{:S(2)}) copy-start(bf16[9,2,16,4096]{3,2,1,0:T(8,128)(2,1)} %param.31) | copy-start | bytes 7077892
  114.5 5.2 %copy-start.12 = (f32[4096]{0:T(1024)S(1)}, f32[4096]{0:T(1024)}, u32[]{:S(2)}) copy-start(f32[4096]{0:T(1024)} %param.20) | copy-start | bytes 49156
  114.5 5.2 %copy-start.13 = (f32[4096]{0:T(1024)S(1)}, f32[4096]{0:T(1024)}, u32[]{:S(2)}) copy-start(f32[4096]{0:T(1024)} %param.19) | copy-start | bytes 49156
  114.5 5.2 %copy-start.15 = (f32[768]{0:T(1024)S(1)}, f32[768]{0:T(1024)}, u32[]{:S(2)}) copy-start(f32[768]{0:T(1024)} %param.24) | copy-start | bytes 9220
  114.5 35.0 %all-to-all-start.1 = ((bf16[9,2,16,16,256]{4,2,1,0,3:T(8,128)(2,1)}), bf16[9,2,16,16,256]{4,2,1,0,3:T(8,128)(2,1)S(1)}, u32[]{:S(2)}, u32[]{:S(2)}) async-start(bf16[9,2,16,16,256]{4,2,1,0,3:T(8,128)(2,1)} %bitcast.49), calls=%async_computation.1 | async-start | bytes 4718592 | tf_op jit(solution)/shard_map/all_to_all | solution.py:75
  118.8 69.0 %all-gather.5.cloned.1.call-start = ((), (), s32[]{:S(2)}) async-start(), calls=%async_computation.4 | async-start | bytes 2359296 | tf_op jit(solution)/shard_map/all_gather | solution.py:125
  119.6 141.0 %reduce-scatter.2.cloned.1.call-start = ((), (), s32[]{:S(2)}) async-start(), calls=%async_computation.5 | async-start | bytes 4456448 | tf_op jit(solution)/shard_map/reduce_scatter | solution.py:147
  154.8 2.3 copy-start.2
  155.0 2.1 copy-start.3
  157.1 9.9 %copy-start.4 = (bf16[2048,2,128]{0,2,1:T(8,128)(2,1)S(1)}, bf16[2048,2,128]{0,2,1:T(8,128)(2,1)}, u32[]{:S(2)}) copy-start(bf16[2048,2,128]{0,2,1:T(8,128)(2,1)} %copy.52) | copy-start | bytes 3145732
  195.1 65.5 %copy-start.7 = (f32[256]{0:T(256)S(1)}, f32[256]{0:T(256)}, u32[]{:S(2)}) copy-start(f32[256]{0:T(256)} %param.30) | copy-start | bytes 3076
  195.1 65.5 %copy-start.8 = (f32[256]{0:T(256)S(1)}, f32[256]{0:T(256)}, u32[]{:S(2)}) copy-start(f32[256]{0:T(256)} %param.26) | copy-start | bytes 3076
Sparse Core Ops, SparseCore 0:
  9.0 55.1 all-gather.2
  121.9 65.9 all-gather.4
  195.3 65.2 reduce-scatter.1

commit v6 on v4

--- a/solution.py
+++ b/solution.py
@@ -84,6 +84,19 @@
     return lax.all_to_all(copies, axis, split_axis=0, concat_axis=0, tiled=True)
 
 
+def share_pages_by_permutes(local_pool):
+    count = lax.axis_size("head")
+    me = lax.axis_index("head")
+    width = local_pool.shape[3] // count
+    received = [lax.dynamic_slice_in_dim(local_pool, me * width, width, axis=3)]
+    for shift in range(1, count):
+        part = lax.dynamic_slice_in_dim(local_pool, ((me + shift) % count) * width, width, axis=3)
+        perm = [(i, (i + shift) % count) for i in range(count)]
+        received.append(lax.ppermute(part, "head", perm))
+    owners = jnp.arange(count, dtype=jnp.int32)
+    return jnp.concatenate(received, axis=0), (me - owners) % count
+
+
 def shards(
     states,
     pre_gain,
@@ -105,6 +118,7 @@
     migrations,
 ):
     gathered = lax.all_gather(states, "head", axis=1, tiled=True)
+    page_pool, pool_order = share_pages_by_permutes(kv_cache)
     qkv_full = gather_by_all_to_all(qkv_weight, "tok")
     out_full = lax.all_gather(out_weight, "tok", axis=1, tiled=True)
     wide = gathered.astype(jnp.float32)
@@ -120,8 +134,6 @@
         return jnp.dot(hidden, down_weight, preferred_element_type=jnp.float32)
 
     feed_part = feed(mlp_normed)
-    kv_cache, feed_part = lax.optimization_barrier((kv_cache, feed_part))
-    page_pool = share_pages(kv_cache, lax.axis_size("head"))
     joined = jnp.dot(pre_normed, qkv_full, preferred_element_type=jnp.float32)
     joined = (joined + qkv_bias).reshape(tok_rows, -1, 3, HD)
     local_req = token_request - lax.axis_index("tok") * cached_len.shape[0]
@@ -135,7 +147,8 @@
     match = table[:, None] == targets[None, :]
     moved_from = jnp.sum(jnp.where(match, sources[None, :], 0), axis=1)
     table = jnp.where(jnp.any(match, axis=1), moved_from, table)
-    pages = page_pool[table]
+    slots = kv_cache.shape[0]
+    pages = page_pool[pool_order[table // slots] * slots + table % slots]
     cache_keys = pages[:, 0].reshape(-1, queries.shape[1], HD)
     cache_values = pages[:, 1].reshape(-1, queries.shape[1], HD)
     heads_out = attend(

time: 259 us -> 285 us (1.10)
  starting transfers between devices: 12.6 us -> 34.5 us
  other arithmetic: 11.4 us -> 20.3 us
  waiting for transfers between devices: 139 us -> 132 us
  local copies, waits for them, and re-layouts: 26 us -> 29.9 us
    ppermute x0 -> x15, waiting for transfers between devices: none -> 59.4 us  [share_pages_by_permutes(): received.append(lax.ppermute(part, 'head', perm))]
    all_gather x1, waiting for transfers between devices: 39 us -> 0.01 us  [shards(): gathered = lax.all_gather(states, 'head', axis=1, tiled=True)]
    ppermute x0 -> x15, starting transfers between devices: none -> 26.6 us  [share_pages_by_permutes(): received.append(lax.ppermute(part, 'head', perm))]
    all_to_all x1, waiting for transfers between devices: 20.8 us -> 0.01 us  [gather_by_all_to_all(): return lax.all_to_all(copies, axis, split_axis=0, concat_axis=0, tiled=True)]
    all_to_all x1 -> x0, waiting for transfers between devices: 12.5 us -> none  [share_pages(): lax.all_to_all(grouped, 'head', split_axis=3, concat_axis=0, tiled=True)]
    select_n x1 -> x2, other arithmetic: 0.01 us -> 10.2 us  [the longest x1 10.2 us: shards(): pages = page_pool[pool_order[table // slots] * slots + table % slots]]
    unnamed x37 -> x53, local copies, waits for them, and re-layouts: 2.04 us -> 10.3 us
    reduce_scatter x1, waiting for transfers between devices: 65.1 us -> 70.8 us  [shards(): lax.psum_scatter((attention_part + feed_part).astype(jnp.bfloat16), 'head...]
  transfers between devices with their start and end apart: 5 -> 19, of which waited for: 4 -> 3; matrix products, arithmetic and copies ran while one was open for 33% -> 34% of each run, Pallas kernels for 0% -> 0%
where the time goes in v6:
time: 285 us
  waiting for transfers between devices  132 us (46%)
  matrix products  54.7 us (19%)
  starting transfers between devices  34.5 us (12%)
  local copies, waits for them, and re-layouts  29.9 us (10%)
  other arithmetic  20.3 us (7%)
  between operations  13.7 us (5%)
    reduce_scatter x1, waiting for transfers between devices, shards(): lax.psum_scatter((attention_part + feed_part).astype(jnp.bfloat16), 'head...  70.8 us
    ppermute x15, waiting for transfers between devices, share_pages_by_permutes(): received.append(lax.ppermute(part, 'head', perm))  59.4 us
    ppermute x15, starting transfers between devices, share_pages_by_permutes(): received.append(lax.ppermute(part, 'head', perm))  26.6 us
    dot_general x1, matrix products, feed(): return jnp.dot(hidden, down_weight, preferred_element_type=jnp.float32)  23.7 us
    unnamed x53, local copies, waits for them, and re-layouts  10.3 us
    select_n x1, other arithmetic, shards(): pages = page_pool[pool_order[table // slots] * slots + table % slots]  10.2 us
    sub x1, matrix products, attend(): exp_scores = jnp.exp(scores - peak)  10.1 us
    all_to_all x1, starting transfers between devices, gather_by_all_to_all(): return lax.all_to_all(copies, axis, split_axis=0, concat_axis=0, tiled=True)  7.79 us
  transfers between devices with their start and end apart: 19, of which 3 were waited for; matrix products, arithmetic and copies ran while one was open for 34% of the time, Pallas kernels for 0%

profile of v6, /device:TPU:0, one launch (start us, length us, event | category | flops | bytes accessed | tf_op | source)
XLA Modules:
  0.0 284.7 jit_solution(245779073949247896)
XLA Ops:
  6.5 0.7 all-gather.3.cloned.1.call-update
  7.5 2.7 constant_dynamic-slice_fusion
  10.2 1.7 collective-permute-start.1
  12.0 2.3 collective-permute-start.2
  14.3 1.5 collective-permute-start.3
  15.8 3.0 %broadcast_in_dim.47 = bf16[8,512,768]{2,1,0:T(8,128)(2,1)} broadcast(bf16[512,768]{1,0:T(8,128)(2,1)S(1)} %copy-done.4), dimensions={1,2} | broadcast | bytes 7077888 | tf_op jit(solution)/shard_map/broadcast_in_dim | solution.py:81
  18.8 7.8 %all-to-all-start = ((bf16[8,512,768]{2,1,0:T(8,128)(2,1)}), bf16[8,512,768]{2,1,0:T(8,128)(2,1)}, u32[]{:S(2)}, u32[]{:S(2)}) async-start(bf16[8,512,768]{2,1,0:T(8,128)(2,1)} %broadcast_in_dim.47), calls=%async_computation | async-start | bytes 12582912 | tf_op jit(solution)/shard_map/all_to_all | solution.py:84
  26.6 0.7 all-gather.5.cloned.1.call-update
  27.6 0.7 fusion.151
  28.6 0.2 reduce-window.8
  29.0 0.2 multiply_cosine_fusion
  29.2 0.3 compare_and_fusion.1
  29.5 0.7 compare_and_fusion
  30.2 1.2 pad_add_fusion
  31.4 10.2 %fusion.109 = s32[128]{0:T(128)S(1)} fusion(s32[128,1]{0,1:T(1,128)S(1)} %reshape.275, s32[128]{0:T(128)S(1)} %fusion.103, pred[128]{0:T(512)(128)(4,1)S(1)} %compare_reduce_fusion, s32[]{:T(128)} %bitcast.22, s32[]{:T(128)} %bitcast.23, s32[]{:T(128)} %bitcast.24, s32[]{:T(128)} %bitcast.25, s32[]{:T(128)} %bitcast.26, s32[]{:T(128)} %bitcast.28, ...), kind=kLoop, calls=%fused_computation.195 | loop fusion | flops 6528 | bytes 1728 | tf_op jit(solution)/shard_map/select_n | solution.py:151
  41.8 0.8 copy.40
  42.6 0.8 collective-permute-start.5
  43.4 0.7 constant_dynamic-update-slice_fusion.14
  44.0 4.2 %collective-permute-start.6 = (bf16[9,2,16,256]{3,2,1,0:T(8,128)(2,1)S(1)}, bf16[9,2,16,256]{3,2,1,0:T(8,128)(2,1)S(1)}, u32[]{:S(2)}, u32[]{:S(2)}) collective-permute-start(bf16[9,2,16,256]{3,2,1,0:T(8,128)(2,1)S(1)} %get-tuple-element.16), channel_id=1, source_target_pairs={{0,7},{1,8},{2,9},{3,10},{4,11},{5,12},{6,13},{7,14},{8,15},{9,0},... | collective-permute-start | bytes 442376 | tf_op jit(solution)/shard_map/ppermute | solution.py:95
  48.2 0.7 constant_dynamic-update-slice_fusion.13
  48.9 2.0 collective-permute-start.7
  50.9 0.7 constant_dynamic-update-slice_fusion.12
  51.6 0.7 constant_dynamic-update-slice_fusion.11
  52.3 2.2 collective-permute-start.9
  54.5 0.7 constant_dynamic-update-slice_fusion.10
  55.2 2.9 %collective-permute-start.10 = (bf16[9,2,16,256]{3,2,1,0:T(8,128)(2,1)S(1)}, bf16[9,2,16,256]{3,2,1,0:T(8,128)(2,1)S(1)}, u32[]{:S(2)}, u32[]{:S(2)}) collective-permute-start(bf16[9,2,16,256]{3,2,1,0:T(8,128)(2,1)S(1)} %get-tuple-element.12), channel_id=1, source_target_pairs={{0,11},{1,12},{2,13},{3,14},{4,15},{5,0},{6,1},{7,2},{8,3},{9,4},{... | collective-permute-start | bytes 442376 | tf_op jit(solution)/shard_map/ppermute | solution.py:95
  58.1 0.7 constant_dynamic-update-slice_fusion.9
  58.7 2.2 collective-permute-start.11
  60.9 0.7 constant_dynamic-update-slice_fusion.8
  61.6 0.7 constant_dynamic-update-slice_fusion.7
  62.2 1.6 collective-permute-done.8
  63.8 2.6 collective-permute-start.13
  66.5 0.7 constant_dynamic-update-slice_fusion.6
  67.1 4.2 %collective-permute-start.14 = (bf16[9,2,16,256]{3,2,1,0:T(8,128)(2,1)S(1)}, bf16[9,2,16,256]{3,2,1,0:T(8,128)(2,1)S(1)}, u32[]{:S(2)}, u32[]{:S(2)}) collective-permute-start(bf16[9,2,16,256]{3,2,1,0:T(8,128)(2,1)S(1)} %get-tuple-element.9), channel_id=1, source_target_pairs={{0,15},{1,0},{2,1},{3,2},{4,3},{5,4},{6,5},{7,6},{8,7},{9,8},{10,9... | collective-permute-start | bytes 442376 | tf_op jit(solution)/shard_map/ppermute | solution.py:95
  71.3 0.7 constant_dynamic-update-slice_fusion.5
  72.0 0.7 constant_dynamic-update-slice_fusion.4
  72.7 0.7 constant_dynamic-update-slice_fusion.3
  73.3 57.8 %collective-permute-done.12 = bf16[9,2,16,256]{3,2,1,0:T(8,128)(2,1)S(1)} collective-permute-done((bf16[9,2,16,256]{3,2,1,0:T(8,128)(2,1)S(1)}, bf16[9,2,16,256]{3,2,1,0:T(8,128)(2,1)S(1)}, u32[]{:S(2)}, u32[]{:S(2)}) %collective-permute-start.12) | collective-permute-done | bytes 147488 | tf_op jit(solution)/shard_map/ppermute | solution.py:95
  131.2 0.7 constant_dynamic-update-slice_fusion.2
  131.8 0.7 constant_dynamic-update-slice_fusion.1
  132.5 0.7 constant_dynamic-update-slice_fusion
  133.1 2.4 gather_fusion
  135.6 1.2 fusion.149
  136.7 1.3 reshape_squeeze.7
  138.1 1.1 copy.42
  139.2 0.3 reshape_squeeze.6
  139.5 2.1 copy.37
  141.6 3.0 %convert_reduce_fusion = f32[512]{0:T(512)S(1)} fusion(bf16[512,4096]{1,0:T(8,128)(2,1)} %all-gather.3.cloned.1.call-done), kind=kLoop, calls=%fused_computation.3 | loop fusion | flops 4193792 | bytes 4196352 | tf_op jit(solution)/shard_map/reduce_sum | solution.py:14
  144.6 0.4 copy-done
  145.0 1.2 fusion.9
  146.3 7.6 %fusion.42 = f32[512,768]{1,0:T(8,128)S(1)} fusion(bf16[4096,768]{1,0:T(8,128)(2,1)} %bitcast.32, bf16[512,4096]{1,0:T(8,128)(2,1)} %all-gather.3.cloned.1.call-done, f32[4096]{0:T(1024)S(1)} %copy-done.11, f32[4096]{0:T(1024)S(1)} %copy-done.12, f32[512]{0:T(512)S(1)} %add_rsqrt_fusion, f32[512]{0:T(512)S(1)} %broadcast_multiply_fusion, f32[768]{0:T(1024)S(1)} %copy-done.15), kind=kOutput, calls=%fused_computation.54 | convolution fusion | flops 3234201600 | bytes 12098560 | tf_op jit(solution)/shard_map/dot_general | solution.py:137
  153.9 0.5 copy.35
  154.5 0.7 fusion.94
  155.2 0.2 copy.43
  155.4 0.2 copy.44
  155.6 0.8 slice.97
  156.5 0.8 slice.98
  157.3 1.2 subtract_convert_fusion.1
  158.5 10.1 %fusion.152 = (f32[2,512]{1,0:T(2,128)S(1)}, f32[2,512,2560]{2,1,0:T(8,128)}) fusion(pred[512,2560]{1,0:T(8,128)(4,1)S(1)} %copy-done.1, bf16[512,2,96]{2,0,1:T(8,128)(2,1)} %slice.97, bf16[512,2,16]{2,0,1:T(8,128)(2,1)} %get-tuple-element.33, bf16[512,2,16]{2,0,1:T(8,128)(2,1)} %get-tuple-element.34, bf16[2048,2,128]{2,0,1:T(8,128)(2,1)} %copy.42, ...), kind=kOutput, calls=%fused_computation.239 | convolution fusion | flops 687606272 | bytes 13373440 | tf_op jit(solution)/shard_map/sub | solution.py:64
  168.7 5.9 %fusion.56 = bf16[2,128,512]{2,1,0:T(8,128)(2,1)S(1)} fusion(f32[2,512,2560]{2,1,0:T(8,128)} %get-tuple-element.56, f32[2,512]{1,0:T(2,128)S(1)} %get-tuple-element.55, bf16[512,2,128]{0,2,1:T(8,128)(2,1)S(1)} %copy-done.5, bf16[2048,2,128]{0,2,1:T(8,128)(2,1)S(1)} %copy-done.3), kind=kOutput, calls=%fused_computation.66 | convolution fusion | flops 679084032 | bytes 12062720 | tf_op jit(solution)/shard_map/htk,khd->thd/dot_general | solution.py:66
  174.6 23.7 %fusion.40 = f32[512,4096]{1,0:T(8,128)} fusion(bf16[1024,4096]{1,0:T(8,128)(2,1)} %param.29, bf16[4096,1024]{1,0:T(8,128)(2,1)} %param.27, bf16[512,4096]{1,0:T(8,128)(2,1)} %all-gather.3.cloned.1.call-done, f32[4096]{0:T(1024)S(1)} %copy-done.13, f32[4096]{0:T(1024)S(1)} %copy-done.14, f32[512]{0:T(512)S(1)} %add_rsqrt_fusion, ...), kind=kOutput, calls=%fused_computation.53 | convolution fusion | flops 8637120512 | bytes 29401088 | tf_op jit(solution)/shard_map/dot_general | solution.py:134
  198.4 7.3 %add_convert_fusion = bf16[512,4096]{1,0:T(8,128)(2,1)} fusion(f32[512,4096]{1,0:T(8,128)} %fusion.40, bf16[512,256]{0,1:T(8,128)(2,1)S(1)} %bitcast.185, bf16[256,4096]{1,0:T(8,128)(2,1)} %all-gather.5.cloned.1.call-done), kind=kOutput, calls=%fused_computation.16 | convolution fusion | flops 1077936128 | bytes 14942208 | tf_op jit(solution)/shard_map/dot_general | solution.py:157
  205.7 70.8 %reduce-scatter.2.cloned.1.call-done = bf16[512,256]{1,0:T(8,128)(2,1)} async-done(((bf16[512,4096]{1,0:T(8,128)(2,1)}), bf16[512,256]{1,0:T(8,128)(2,1)}) %reduce-scatter.2.cloned.1.call-update) | async-done | bytes 262160 | tf_op jit(solution)/shard_map/reduce_scatter | solution.py:158
  276.5 1.7 add_convert_fusion.1
  (79 shorter events, 1.1 us)
Async XLA Ops:
  6.5 135.0 %all-gather.3.cloned.1.call-start = ((), (), s32[]{:S(2)}) async-start(), calls=%async_computation.2 | async-start | bytes 4456448 | tf_op jit(solution)/shard_map/all_gather | solution.py:120
  7.5 8.3 %copy-start.4 = (bf16[512,768]{1,0:T(8,128)(2,1)S(1)}, bf16[512,768]{1,0:T(8,128)(2,1)}, u32[]{:S(2)}) copy-start(bf16[512,768]{1,0:T(8,128)(2,1)} %param.23) | copy-start | bytes 2359300
  10.2 32.4 %collective-permute-start = (bf16[9,2,16,256]{3,2,1,0:T(8,128)(2,1)S(1)}, bf16[9,2,16,256]{3,2,1,0:T(8,128)(2,1)S(1)}, u32[]{:S(2)}, u32[]{:S(2)}) collective-permute-start(bf16[9,2,16,256]{3,2,1,0:T(8,128)(2,1)S(1)} %get-tuple-element.22), channel_id=1, source_target_pairs={{0,1},{1,2},{2,3},{3,4},{4,5},{5,6},{6,7},{7,8},{8,9},{9,10},{10,1... | collective-permute-start | bytes 442376 | tf_op jit(solution)/shard_map/ppermute | solution.py:95
  10.2 33.8 %collective-permute-start.1 = (bf16[9,2,16,256]{3,2,1,0:T(8,128)(2,1)S(1)}, bf16[9,2,16,256]{3,2,1,0:T(8,128)(2,1)S(1)}, u32[]{:S(2)}, u32[]{:S(2)}) collective-permute-start(bf16[9,2,16,256]{3,2,1,0:T(8,128)(2,1)S(1)} %get-tuple-element.21), channel_id=1, source_target_pairs={{0,2},{1,3},{2,4},{3,5},{4,6},{5,7},{6,8},{7,9},{8,10},{9,11},{10,... | collective-permute-start | bytes 442376 | tf_op jit(solution)/shard_map/ppermute | solution.py:95
  12.0 36.9 %collective-permute-start.2 = (bf16[9,2,16,256]{3,2,1,0:T(8,128)(2,1)S(1)}, bf16[9,2,16,256]{3,2,1,0:T(8,128)(2,1)S(1)}, u32[]{:S(2)}, u32[]{:S(2)}) collective-permute-start(bf16[9,2,16,256]{3,2,1,0:T(8,128)(2,1)S(1)} %get-tuple-element.20), channel_id=1, source_target_pairs={{0,3},{1,4},{2,5},{3,6},{4,7},{5,8},{6,9},{7,10},{8,11},{9,12},{10... | collective-permute-start | bytes 442376 | tf_op jit(solution)/shard_map/ppermute | solution.py:95
  14.3 37.3 %collective-permute-start.3 = (bf16[9,2,16,256]{3,2,1,0:T(8,128)(2,1)S(1)}, bf16[9,2,16,256]{3,2,1,0:T(8,128)(2,1)S(1)}, u32[]{:S(2)}, u32[]{:S(2)}) collective-permute-start(bf16[9,2,16,256]{3,2,1,0:T(8,128)(2,1)S(1)} %get-tuple-element.19), channel_id=1, source_target_pairs={{0,4},{1,5},{2,6},{3,7},{4,8},{5,9},{6,10},{7,11},{8,12},{9,13},{1... | collective-permute-start | bytes 442376 | tf_op jit(solution)/shard_map/ppermute | solution.py:95
  15.8 36.5 %collective-permute-start.4 = (bf16[9,2,16,256]{3,2,1,0:T(8,128)(2,1)S(1)}, bf16[9,2,16,256]{3,2,1,0:T(8,128)(2,1)S(1)}, u32[]{:S(2)}, u32[]{:S(2)}) collective-permute-start(bf16[9,2,16,256]{3,2,1,0:T(8,128)(2,1)S(1)} %get-tuple-element.18), channel_id=1, source_target_pairs={{0,5},{1,6},{2,7},{3,8},{4,9},{5,10},{6,11},{7,12},{8,13},{9,14},{... | collective-permute-start | bytes 442376 | tf_op jit(solution)/shard_map/ppermute | solution.py:95
  18.8 8.6 %copy-start.17 = (s32[2,64]{1,0:T(2,128)S(1)}, s32[2,64]{1,0:T(2,128)}, u32[]{:S(2)}) copy-start(s32[2,64]{1,0:T(2,128)} %param.34) | copy-start | bytes 1540
  18.8 9.5 %copy-start.10 = (s32[8,2]{0,1:T(2,128)S(1)}, s32[8,2]{0,1:T(2,128)}, u32[]{:S(2)}) copy-start(s32[8,2]{0,1:T(2,128)} %param.35) | copy-start | bytes 196
  18.8 9.7 %copy-start.7 = (s32[512]{0:T(512)S(1)}, s32[512]{0:T(512)}, u32[]{:S(2)}) copy-start(s32[512]{0:T(512)} %param.32) | copy-start | bytes 6148
  18.8 10.0 %copy-start.6 = (s32[2]{0:T(128)S(1)}, s32[2]{0:T(128)}, u32[]{:S(2)}) copy-start(s32[2]{0:T(128)} %param.33) | copy-start | bytes 28
  18.8 127.4 %all-to-all-start = ((bf16[8,512,768]{2,1,0:T(8,128)(2,1)}), bf16[8,512,768]{2,1,0:T(8,128)(2,1)}, u32[]{:S(2)}, u32[]{:S(2)}) async-start(bf16[8,512,768]{2,1,0:T(8,128)(2,1)} %broadcast_in_dim.47), calls=%async_computation | async-start | bytes 12582912 | tf_op jit(solution)/shard_map/all_to_all | solution.py:84
  26.6 171.8 %all-gather.5.cloned.1.call-start = ((), (), s32[]{:S(2)}) async-start(), calls=%async_computation.3 | async-start | bytes 2359296 | tf_op jit(solution)/shard_map/all_gather | solution.py:123
  27.3 249.1 %reduce-scatter.2.cloned.1.call-start = ((), (), s32[]{:S(2)}) async-start(), calls=%async_computation.4 | async-start | bytes 4456448 | tf_op jit(solution)/shard_map/reduce_scatter | solution.py:158
  42.6 12.6 %collective-permute-start.5 = (bf16[9,2,16,256]{3,2,1,0:T(8,128)(2,1)S(1)}, bf16[9,2,16,256]{3,2,1,0:T(8,128)(2,1)S(1)}, u32[]{:S(2)}, u32[]{:S(2)}) collective-permute-start(bf16[9,2,16,256]{3,2,1,0:T(8,128)(2,1)S(1)} %get-tuple-element.17), channel_id=1, source_target_pairs={{0,6},{1,7},{2,8},{3,9},{4,10},{5,11},{6,12},{7,13},{8,14},{9,15},... | collective-permute-start | bytes 442376 | tf_op jit(solution)/shard_map/ppermute | solution.py:95
  44.0 14.7 %collective-permute-start.6 = (bf16[9,2,16,256]{3,2,1,0:T(8,128)(2,1)S(1)}, bf16[9,2,16,256]{3,2,1,0:T(8,128)(2,1)S(1)}, u32[]{:S(2)}, u32[]{:S(2)}) collective-permute-start(bf16[9,2,16,256]{3,2,1,0:T(8,128)(2,1)S(1)} %get-tuple-element.16), channel_id=1, source_target_pairs={{0,7},{1,8},{2,9},{3,10},{4,11},{5,12},{6,13},{7,14},{8,15},{9,0},... | collective-permute-start | bytes 442376 | tf_op jit(solution)/shard_map/ppermute | solution.py:95
  48.9 12.7 %collective-permute-start.7 = (bf16[9,2,16,256]{3,2,1,0:T(8,128)(2,1)S(1)}, bf16[9,2,16,256]{3,2,1,0:T(8,128)(2,1)S(1)}, u32[]{:S(2)}, u32[]{:S(2)}) collective-permute-start(bf16[9,2,16,256]{3,2,1,0:T(8,128)(2,1)S(1)} %get-tuple-element.15), channel_id=1, source_target_pairs={{0,8},{1,9},{2,10},{3,11},{4,12},{5,13},{6,14},{7,15},{8,0},{9,1},... | collective-permute-start | bytes 442376 | tf_op jit(solution)/shard_map/ppermute | solution.py:95
  51.6 12.2 %collective-permute-start.8 = (bf16[9,2,16,256]{3,2,1,0:T(8,128)(2,1)S(1)}, bf16[9,2,16,256]{3,2,1,0:T(8,128)(2,1)S(1)}, u32[]{:S(2)}, u32[]{:S(2)}) collective-permute-start(bf16[9,2,16,256]{3,2,1,0:T(8,128)(2,1)S(1)} %get-tuple-element.14), channel_id=1, source_target_pairs={{0,9},{1,10},{2,11},{3,12},{4,13},{5,14},{6,15},{7,0},{8,1},{9,2},... | collective-permute-start | bytes 442376 | tf_op jit(solution)/shard_map/ppermute | solution.py:95
  52.3 14.9 %collective-permute-start.9 = (bf16[9,2,16,256]{3,2,1,0:T(8,128)(2,1)S(1)}, bf16[9,2,16,256]{3,2,1,0:T(8,128)(2,1)S(1)}, u32[]{:S(2)}, u32[]{:S(2)}) collective-permute-start(bf16[9,2,16,256]{3,2,1,0:T(8,128)(2,1)S(1)} %get-tuple-element.13), channel_id=1, source_target_pairs={{0,10},{1,11},{2,12},{3,13},{4,14},{5,15},{6,0},{7,1},{8,2},{9,3},... | collective-permute-start | bytes 442376 | tf_op jit(solution)/shard_map/ppermute | solution.py:95
  55.2 16.8 %collective-permute-start.10 = (bf16[9,2,16,256]{3,2,1,0:T(8,128)(2,1)S(1)}, bf16[9,2,16,256]{3,2,1,0:T(8,128)(2,1)S(1)}, u32[]{:S(2)}, u32[]{:S(2)}) collective-permute-start(bf16[9,2,16,256]{3,2,1,0:T(8,128)(2,1)S(1)} %get-tuple-element.12), channel_id=1, source_target_pairs={{0,11},{1,12},{2,13},{3,14},{4,15},{5,0},{6,1},{7,2},{8,3},{9,4},{... | collective-permute-start | bytes 442376 | tf_op jit(solution)/shard_map/ppermute | solution.py:95
  58.7 13.9 %collective-permute-start.11 = (bf16[9,2,16,256]{3,2,1,0:T(8,128)(2,1)S(1)}, bf16[9,2,16,256]{3,2,1,0:T(8,128)(2,1)S(1)}, u32[]{:S(2)}, u32[]{:S(2)}) collective-permute-start(bf16[9,2,16,256]{3,2,1,0:T(8,128)(2,1)S(1)} %get-tuple-element.11), channel_id=1, source_target_pairs={{0,12},{1,13},{2,14},{3,15},{4,0},{5,1},{6,2},{7,3},{8,4},{9,5},{1... | collective-permute-start | bytes 442376 | tf_op jit(solution)/shard_map/ppermute | solution.py:95
  61.6 69.6 %collective-permute-start.12 = (bf16[9,2,16,256]{3,2,1,0:T(8,128)(2,1)S(1)}, bf16[9,2,16,256]{3,2,1,0:T(8,128)(2,1)S(1)}, u32[]{:S(2)}, u32[]{:S(2)}) collective-permute-start(bf16[9,2,16,256]{3,2,1,0:T(8,128)(2,1)S(1)} %get-tuple-element.10), channel_id=1, source_target_pairs={{0,13},{1,14},{2,15},{3,0},{4,1},{5,2},{6,3},{7,4},{8,5},{9,6},{10... | collective-permute-start | bytes 442376 | tf_op jit(solution)/shard_map/ppermute | solution.py:95
  63.8 68.0 %collective-permute-start.13 = (bf16[9,2,16,256]{3,2,1,0:T(8,128)(2,1)S(1)}, bf16[9,2,16,256]{3,2,1,0:T(8,128)(2,1)S(1)}, u32[]{:S(2)}, u32[]{:S(2)}) collective-permute-start(bf16[9,2,16,256]{3,2,1,0:T(8,128)(2,1)S(1)} %get-tuple-element.24), channel_id=1, source_target_pairs={{0,14},{1,15},{2,0},{3,1},{4,2},{5,3},{6,4},{7,5},{8,6},{9,7},{10,... | collective-permute-start | bytes 442376 | tf_op jit(solution)/shard_map/ppermute | solution.py:95
  67.1 65.3 %collective-permute-start.14 = (bf16[9,2,16,256]{3,2,1,0:T(8,128)(2,1)S(1)}, bf16[9,2,16,256]{3,2,1,0:T(8,128)(2,1)S(1)}, u32[]{:S(2)}, u32[]{:S(2)}) collective-permute-start(bf16[9,2,16,256]{3,2,1,0:T(8,128)(2,1)S(1)} %get-tuple-element.9), channel_id=1, source_target_pairs={{0,15},{1,0},{2,1},{3,2},{4,3},{5,4},{6,5},{7,6},{8,7},{9,8},{10,9... | collective-permute-start | bytes 442376 | tf_op jit(solution)/shard_map/ppermute | solution.py:95
  141.6 3.5 %copy-start = (bf16[512,4096]{1,0:T(8,128)(2,1)S(1)}, bf16[512,4096]{1,0:T(8,128)(2,1)}, u32[]{:S(2)}) copy-start(bf16[512,4096]{1,0:T(8,128)(2,1)} %all-gather.3.cloned.1.call-done) | copy-start | bytes 12582916
  144.5 1.7 copy-start.11
  144.5 1.7 copy-start.12
  144.5 1.7 copy-start.15
  154.5 2.8 copy-start.2
  155.6 2.9 %copy-start.1 = (pred[512,2560]{1,0:T(8,128)(4,1)S(1)}, pred[512,2560]{1,0:T(8,128)(4,1)}, u32[]{:S(2)}) copy-start(pred[512,2560]{1,0:T(8,128)(4,1)} %pad_add_fusion) | copy-start | bytes 3932164
  158.5 10.1 %copy-start.3 = (bf16[2048,2,128]{0,2,1:T(8,128)(2,1)S(1)}, bf16[2048,2,128]{0,2,1:T(8,128)(2,1)}, u32[]{:S(2)}) copy-start(bf16[2048,2,128]{0,2,1:T(8,128)(2,1)} %copy.37) | copy-start | bytes 3145732
  158.5 10.1 %copy-start.5 = (bf16[512,2,128]{0,2,1:T(8,128)(2,1)S(1)}, bf16[512,2,128]{0,2,1:T(8,128)(2,1)}, u32[]{:S(2)}) copy-start(bf16[512,2,128]{0,2,1:T(8,128)(2,1)} %fusion.94) | copy-start | bytes 786436
  168.6 6.0 %copy-start.13 = (f32[4096]{0:T(1024)S(1)}, f32[4096]{0:T(1024)}, u32[]{:S(2)}) copy-start(f32[4096]{0:T(1024)} %param.22) | copy-start | bytes 49156
  168.6 6.0 %copy-start.14 = (f32[4096]{0:T(1024)S(1)}, f32[4096]{0:T(1024)}, u32[]{:S(2)}) copy-start(f32[4096]{0:T(1024)} %param.21) | copy-start | bytes 49156
  168.6 6.0 %copy-start.16 = (f32[1024]{0:T(1024)S(1)}, f32[1024]{0:T(1024)}, u32[]{:S(2)}) copy-start(f32[1024]{0:T(1024)} %param.28) | copy-start | bytes 12292
  205.6 70.8 %copy-start.8 = (f32[256]{0:T(256)S(1)}, f32[256]{0:T(256)}, u32[]{:S(2)}) copy-start(f32[256]{0:T(256)} %param.30) | copy-start | bytes 3076
  205.6 70.8 %copy-start.9 = (f32[256]{0:T(256)S(1)}, f32[256]{0:T(256)}, u32[]{:S(2)}) copy-start(f32[256]{0:T(256)} %param.26) | copy-start | bytes 3076
Sparse Core Ops, SparseCore 0:
  9.0 71.2 all-gather.2
  82.5 72.5 all-gather.4
  205.8 70.6 reduce-scatter.1

commit v7 on v6

--- a/solution.py
+++ b/solution.py
@@ -118,7 +118,6 @@
     migrations,
 ):
     gathered = lax.all_gather(states, "head", axis=1, tiled=True)
-    page_pool, pool_order = share_pages_by_permutes(kv_cache)
     qkv_full = gather_by_all_to_all(qkv_weight, "tok")
     out_full = lax.all_gather(out_weight, "tok", axis=1, tiled=True)
     wide = gathered.astype(jnp.float32)
@@ -134,6 +133,9 @@
         return jnp.dot(hidden, down_weight, preferred_element_type=jnp.float32)
 
     feed_part = feed(mlp_normed)
+    kv_cache, feed_part = lax.optimization_barrier((kv_cache, feed_part))
+    page_pool, pool_order = share_pages_by_permutes(kv_cache)
+    qkv_full, page_pool = lax.optimization_barrier((qkv_full, page_pool))
     joined = jnp.dot(pre_normed, qkv_full, preferred_element_type=jnp.float32)
     joined = (joined + qkv_bias).reshape(tok_rows, -1, 3, HD)
     local_req = token_request - lax.axis_index("tok") * cached_len.shape[0]

time: 285 us -> 279 us (0.979)
  waiting for transfers between devices: 132 us -> 113 us
  starting transfers between devices: 34.5 us -> 40 us
  local copies, waits for them, and re-layouts: 29.9 us -> 33.4 us
    ppermute x15, waiting for transfers between devices: 59.4 us -> 3.86 us  [share_pages_by_permutes(): received.append(lax.ppermute(part, 'head', perm))]
    all_gather x1, waiting for transfers between devices: 0.01 us -> 38.9 us  [shards(): gathered = lax.all_gather(states, 'head', axis=1, tiled=True)]
    ppermute x15, starting transfers between devices: 26.6 us -> 31.7 us  [share_pages_by_permutes(): received.append(lax.ppermute(part, 'head', perm))]
    unnamed x53 -> x55, local copies, waits for them, and re-layouts: 10.3 us -> 10.4 us
  transfers between devices with their start and end apart: 19 -> 19, of which waited for: 3 -> 5; matrix products, arithmetic and copies ran while one was open for 34% -> 37% of each run, Pallas kernels for 0% -> 0%
where the time goes in v7:
time: 279 us
  waiting for transfers between devices  113 us (41%)
  matrix products  56.3 us (20%)
  starting transfers between devices  40 us (14%)
  local copies, waits for them, and re-layouts  33.4 us (12%)
  other arithmetic  22.2 us (8%)
  between operations  13.6 us (5%)
    reduce_scatter x1, waiting for transfers between devices, shards(): lax.psum_scatter((attention_part + feed_part).astype(jnp.bfloat16), 'head...  69.1 us
    all_gather x1, waiting for transfers between devices, shards(): gathered = lax.all_gather(states, 'head', axis=1, tiled=True)  38.9 us
    ppermute x15, starting transfers between devices, share_pages_by_permutes(): received.append(lax.ppermute(part, 'head', perm))  31.7 us
    dot_general x1, matrix products, feed(): return jnp.dot(hidden, down_weight, preferred_element_type=jnp.float32)  23.9 us
    unnamed x55, local copies, waits for them, and re-layouts  10.4 us
    select_n x1, other arithmetic, shards(): pages = page_pool[pool_order[table // slots] * slots + table % slots]  10 us
    sub x1, matrix products, attend(): exp_scores = jnp.exp(scores - peak)  10 us
    dot_general x1, matrix products, shards(): joined = jnp.dot(pre_normed, qkv_full, preferred_element_type=jnp.float32)  9.09 us
  transfers between devices with their start and end apart: 19, of which 5 were waited for; matrix products, arithmetic and copies ran while one was open for 37% of the time, Pallas kernels for 0%

profile of v7, /device:TPU:0, one launch (start us, length us, event | category | flops | bytes accessed | tf_op | source)
XLA Modules:
  0.0 278.8 jit_solution(5380898506298351086)
XLA Ops:
  6.5 0.7 all-gather.3.cloned.1.call-update
  7.3 4.2 %broadcast_in_dim.44 = bf16[8,512,768]{2,1,0:T(8,128)(2,1)} broadcast(bf16[512,768]{1,0:T(8,128)(2,1)} %param.23), dimensions={1,2} | broadcast | bytes 7077888 | tf_op jit(solution)/shard_map/broadcast_in_dim | solution.py:81
  11.4 8.2 %all-to-all-start = ((bf16[8,512,768]{2,1,0:T(8,128)(2,1)}), bf16[8,512,768]{2,1,0:T(8,128)(2,1)}, u32[]{:S(2)}, u32[]{:S(2)}) async-start(bf16[8,512,768]{2,1,0:T(8,128)(2,1)} %broadcast_in_dim.44), calls=%async_computation | async-start | bytes 12582912 | tf_op jit(solution)/shard_map/all_to_all | solution.py:84
  19.7 0.7 all-gather.5.cloned.1.call-update
  21.3 0.3 compare_and_fusion.1
  21.8 0.7 fusion.151
  22.5 0.7 compare_and_fusion
  23.3 1.1 pad_add_fusion
  24.4 0.8 multiply_cosine_fusion
  25.2 38.9 %all-gather.3.cloned.1.call-done = bf16[512,4096]{1,0:T(8,128)(2,1)} async-done(((bf16[512,256]{1,0:T(8,128)(2,1)}), bf16[512,4096]{1,0:T(8,128)(2,1)}) %all-gather.3.cloned.1.call-update) | async-done | bytes 4194320 | tf_op jit(solution)/shard_map/all_gather | solution.py:120
  64.2 3.0 %convert_reduce_fusion = f32[512]{0:T(512)S(1)} fusion(bf16[512,4096]{1,0:T(8,128)(2,1)} %all-gather.3.cloned.1.call-done), kind=kLoop, calls=%fused_computation.3 | loop fusion | flops 4193792 | bytes 4196352 | tf_op jit(solution)/shard_map/reduce_sum | solution.py:14
  67.2 0.4 copy-done
  67.6 1.2 fusion.9
  68.9 23.9 %fusion.40 = f32[512,4096]{1,0:T(8,128)} fusion(bf16[1024,4096]{1,0:T(8,128)(2,1)} %param.29, bf16[4096,1024]{1,0:T(8,128)(2,1)} %param.27, bf16[512,4096]{1,0:T(8,128)(2,1)} %all-gather.3.cloned.1.call-done, f32[4096]{0:T(1024)S(1)} %copy-done.12, f32[4096]{0:T(1024)S(1)} %copy-done.13, f32[512]{0:T(512)S(1)} %add_rsqrt_fusion, ...), kind=kOutput, calls=%fused_computation.53 | convolution fusion | flops 8637120512 | bytes 29401088 | tf_op jit(solution)/shard_map/dot_general | solution.py:133
  92.8 1.2 constant_dynamic-slice_fusion
  94.3 10.0 %fusion.109 = s32[128]{0:T(128)S(1)} fusion(s32[128,1]{0,1:T(1,128)S(1)} %reshape.275, s32[128]{0:T(128)S(1)} %fusion.103, pred[128]{0:T(512)(128)(4,1)S(1)} %compare_reduce_fusion, s32[]{:T(128)} %bitcast.23, s32[]{:T(128)} %bitcast.24, s32[]{:T(128)} %bitcast.25, s32[]{:T(128)} %bitcast.26, s32[]{:T(128)} %bitcast.27, s32[]{:T(128)} %bitcast.29, ...), kind=kLoop, calls=%fused_computation.195 | loop fusion | flops 6528 | bytes 1728 | tf_op jit(solution)/shard_map/select_n | solution.py:153
  104.3 3.6 %collective-permute-start.1 = (bf16[9,2,16,256]{3,2,1,0:T(8,128)(2,1)}, bf16[9,2,16,256]{3,2,1,0:T(8,128)(2,1)S(1)}, u32[]{:S(2)}, u32[]{:S(2)}) collective-permute-start(bf16[9,2,16,256]{3,2,1,0:T(8,128)(2,1)} %get-tuple-element.30), channel_id=1, source_target_pairs={{0,2},{1,3},{2,4},{3,5},{4,6},{5,7},{6,8},{7,9},{8,10},{9,11},{10,... | collective-permute-start | bytes 442376 | tf_op jit(solution)/shard_map/ppermute | solution.py:95
  107.9 0.6 pad_clamp_fusion
  108.5 0.9 copy.40
  109.4 0.8 copy.39
  110.2 0.6 collective-permute-start.2
  110.8 0.7 collective-permute-start.3
  111.5 1.5 collective-permute-start.4
  113.0 1.7 collective-permute-start.5
  114.7 0.7 constant_dynamic-update-slice_fusion.14
  115.4 3.9 %collective-permute-start.6 = (bf16[9,2,16,256]{3,2,1,0:T(8,128)(2,1)}, bf16[9,2,16,256]{3,2,1,0:T(8,128)(2,1)S(1)}, u32[]{:S(2)}, u32[]{:S(2)}) collective-permute-start(bf16[9,2,16,256]{3,2,1,0:T(8,128)(2,1)} %get-tuple-element.25), channel_id=1, source_target_pairs={{0,7},{1,8},{2,9},{3,10},{4,11},{5,12},{6,13},{7,14},{8,15},{9,0},... | collective-permute-start | bytes 442376 | tf_op jit(solution)/shard_map/ppermute | solution.py:95
  119.2 0.7 constant_dynamic-update-slice_fusion.13
  119.9 2.2 collective-permute-start.7
  122.1 0.7 constant_dynamic-update-slice_fusion.12
  122.8 0.5 collective-permute-start.8
  123.3 0.7 constant_dynamic-update-slice_fusion.11
  124.0 1.7 collective-permute-start.9
  125.7 0.7 constant_dynamic-update-slice_fusion.10
  126.4 2.4 collective-permute-done.5
  128.9 8.9 %collective-permute-start.10 = (bf16[9,2,16,256]{3,2,1,0:T(8,128)(2,1)S(1)}, bf16[9,2,16,256]{3,2,1,0:T(8,128)(2,1)S(1)}, u32[]{:S(2)}, u32[]{:S(2)}) collective-permute-start(bf16[9,2,16,256]{3,2,1,0:T(8,128)(2,1)S(1)} %get-tuple-element.21), channel_id=1, source_target_pairs={{0,11},{1,12},{2,13},{3,14},{4,15},{5,0},{6,1},{7,2},{8,3},{9,4},{... | collective-permute-start | bytes 442376 | tf_op jit(solution)/shard_map/ppermute | solution.py:95
  137.8 0.7 constant_dynamic-update-slice_fusion.9
  138.5 0.5 collective-permute-start.11
  138.9 0.7 constant_dynamic-update-slice_fusion.8
  139.6 0.7 constant_dynamic-update-slice_fusion.7
  140.4 0.7 constant_dynamic-update-slice_fusion.6
  141.1 5.6 %collective-permute-start.14 = (bf16[9,2,16,256]{3,2,1,0:T(8,128)(2,1)S(1)}, bf16[9,2,16,256]{3,2,1,0:T(8,128)(2,1)S(1)}, u32[]{:S(2)}, u32[]{:S(2)}) collective-permute-start(bf16[9,2,16,256]{3,2,1,0:T(8,128)(2,1)S(1)} %get-tuple-element.17), channel_id=1, source_target_pairs={{0,15},{1,0},{2,1},{3,2},{4,3},{5,4},{6,5},{7,6},{8,7},{9,8},{10,9... | collective-permute-start | bytes 442376 | tf_op jit(solution)/shard_map/ppermute | solution.py:95
  146.7 0.7 constant_dynamic-update-slice_fusion.5
  147.3 0.7 constant_dynamic-update-slice_fusion.4
  148.0 0.7 constant_dynamic-update-slice_fusion.3
  148.7 0.7 constant_dynamic-update-slice_fusion.2
  149.5 0.7 constant_dynamic-update-slice_fusion.1
  150.2 1.2 collective-permute-done.14
  151.4 0.7 constant_dynamic-update-slice_fusion
  152.1 9.1 %fusion.42 = f32[512,768]{1,0:T(8,128)} fusion(bf16[4096,768]{1,0:T(8,128)(2,1)} %bitcast, bf16[512,4096]{1,0:T(8,128)(2,1)} %all-gather.3.cloned.1.call-done, f32[4096]{0:T(1024)S(1)} %copy-done.14, f32[4096]{0:T(1024)S(1)} %copy-done.15, f32[512]{0:T(512)S(1)} %add_rsqrt_fusion, f32[512]{0:T(512)S(1)} %broadcast_multiply_fusion, f32[768]{0:T(1024)S(1)} %copy-done.17), kind=kOutput, calls=%fused_computation.54 | convolution fusion | flops 3234201600 | bytes 12098560 | tf_op jit(solution)/shard_map/dot_general | solution.py:139
  161.2 1.9 copy.35
  163.3 0.9 slice.97
  164.5 2.5 gather_fusion
  167.0 1.5 fusion.149
  168.5 1.4 reshape_squeeze.7
  169.9 1.1 copy.42
  171.0 0.8 slice.98
  172.1 2.1 copy.37
  174.2 1.9 fusion.94
  176.1 2.1 subtract_convert_fusion.1
  178.2 10.0 %fusion.152 = (f32[2,512]{1,0:T(2,128)S(1)}, f32[2,512,2560]{2,1,0:T(8,128)}) fusion(pred[512,2560]{1,0:T(8,128)(4,1)S(1)} %copy-done.4, bf16[512,2,96]{2,0,1:T(8,128)(2,1)} %slice.97, bf16[512,2,16]{2,0,1:T(8,128)(2,1)S(1)} %get-tuple-element.41, bf16[512,2,16]{2,0,1:T(8,128)(2,1)} %get-tuple-element.42, bf16[2048,2,128]{2,0,1:T(8,128)(2,1)} %copy.42, ...), kind=kOutput, calls=%fused_computation.239 | convolution fusion | flops 687606272 | bytes 13373440 | tf_op jit(solution)/shard_map/sub | solution.py:64
  188.2 5.9 %fusion.56 = bf16[2,128,512]{2,1,0:T(8,128)(2,1)S(1)} fusion(f32[2,512,2560]{2,1,0:T(8,128)} %get-tuple-element.64, f32[2,512]{1,0:T(2,128)S(1)} %get-tuple-element.63, bf16[512,2,128]{0,2,1:T(8,128)(2,1)S(1)} %copy-done.6, bf16[2048,2,128]{0,2,1:T(8,128)(2,1)S(1)} %copy-done.5), kind=kOutput, calls=%fused_computation.66 | convolution fusion | flops 679084032 | bytes 12062720 | tf_op jit(solution)/shard_map/htk,khd->thd/dot_general | solution.py:66
  194.1 7.3 %add_convert_fusion = bf16[512,4096]{1,0:T(8,128)(2,1)} fusion(f32[512,4096]{1,0:T(8,128)} %fusion.40, bf16[512,256]{0,1:T(8,128)(2,1)S(1)} %bitcast.185, bf16[256,4096]{1,0:T(8,128)(2,1)} %all-gather.5.cloned.1.call-done), kind=kOutput, calls=%fused_computation.16 | convolution fusion | flops 1077936128 | bytes 14942208 | tf_op jit(solution)/shard_map/dot_general | solution.py:159
  201.5 69.1 %reduce-scatter.2.cloned.1.call-done = bf16[512,256]{1,0:T(8,128)(2,1)} async-done(((bf16[512,4096]{1,0:T(8,128)(2,1)}), bf16[512,256]{1,0:T(8,128)(2,1)}) %reduce-scatter.2.cloned.1.call-update) | async-done | bytes 262160 | tf_op jit(solution)/shard_map/reduce_scatter | solution.py:160
  270.6 1.7 add_convert_fusion.1
  (81 shorter events, 2.4 us)
Async XLA Ops:
  6.5 57.6 %all-gather.3.cloned.1.call-start = ((), (), s32[]{:S(2)}) async-start(), calls=%async_computation.2 | async-start | bytes 4456448 | tf_op jit(solution)/shard_map/all_gather | solution.py:120
  11.4 9.2 %copy-start.18 = (s32[2,64]{1,0:T(2,128)S(1)}, s32[2,64]{1,0:T(2,128)}, u32[]{:S(2)}) copy-start(s32[2,64]{1,0:T(2,128)} %param.34) | copy-start | bytes 1540
  11.4 9.4 %copy-start.8 = (s32[512]{0:T(512)S(1)}, s32[512]{0:T(512)}, u32[]{:S(2)}) copy-start(s32[512]{0:T(512)} %param.32) | copy-start | bytes 6148
  11.4 9.7 %copy-start.7 = (s32[2]{0:T(128)S(1)}, s32[2]{0:T(128)}, u32[]{:S(2)}) copy-start(s32[2]{0:T(128)} %param.33) | copy-start | bytes 28
  11.4 10.2 %copy-start.11 = (s32[8,2]{0,1:T(2,128)S(1)}, s32[8,2]{0,1:T(2,128)}, u32[]{:S(2)}) copy-start(s32[8,2]{0,1:T(2,128)} %param.35) | copy-start | bytes 196
  11.4 140.6 %all-to-all-start = ((bf16[8,512,768]{2,1,0:T(8,128)(2,1)}), bf16[8,512,768]{2,1,0:T(8,128)(2,1)}, u32[]{:S(2)}, u32[]{:S(2)}) async-start(bf16[8,512,768]{2,1,0:T(8,128)(2,1)} %broadcast_in_dim.44), calls=%async_computation | async-start | bytes 12582912 | tf_op jit(solution)/shard_map/all_to_all | solution.py:84
  19.6 174.5 %all-gather.5.cloned.1.call-start = ((), (), s32[]{:S(2)}) async-start(), calls=%async_computation.3 | async-start | bytes 2359296 | tf_op jit(solution)/shard_map/all_gather | solution.py:122
  20.4 250.2 %reduce-scatter.2.cloned.1.call-start = ((), (), s32[]{:S(2)}) async-start(), calls=%async_computation.4 | async-start | bytes 4456448 | tf_op jit(solution)/shard_map/reduce_scatter | solution.py:160
  64.2 3.4 %copy-start = (bf16[512,4096]{1,0:T(8,128)(2,1)S(1)}, bf16[512,4096]{1,0:T(8,128)(2,1)}, u32[]{:S(2)}) copy-start(bf16[512,4096]{1,0:T(8,128)(2,1)} %all-gather.3.cloned.1.call-done) | copy-start | bytes 12582916
  67.1 1.7 copy-start.12
  67.1 1.7 copy-start.13
  67.1 1.7 copy-start.16
  68.9 23.9 %copy-start.3 = (bf16[9,2,16,4096]{3,2,1,0:T(8,128)(2,1)S(1)}, bf16[9,2,16,4096]{3,2,1,0:T(8,128)(2,1)}, u32[]{:S(2)}) copy-start(bf16[9,2,16,4096]{3,2,1,0:T(8,128)(2,1)} %param.31) | copy-start | bytes 7077892
  94.0 18.9 %collective-permute-start = (bf16[9,2,16,256]{3,2,1,0:T(8,128)(2,1)}, bf16[9,2,16,256]{3,2,1,0:T(8,128)(2,1)S(1)}, u32[]{:S(2)}, u32[]{:S(2)}) collective-permute-start(bf16[9,2,16,256]{3,2,1,0:T(8,128)(2,1)} %get-tuple-element.31), channel_id=1, source_target_pairs={{0,1},{1,2},{2,3},{3,4},{4,5},{5,6},{6,7},{7,8},{8,9},{9,10},{10,1... | collective-permute-start | bytes 442376 | tf_op jit(solution)/shard_map/ppermute | solution.py:95
  104.3 11.0 %collective-permute-start.1 = (bf16[9,2,16,256]{3,2,1,0:T(8,128)(2,1)}, bf16[9,2,16,256]{3,2,1,0:T(8,128)(2,1)S(1)}, u32[]{:S(2)}, u32[]{:S(2)}) collective-permute-start(bf16[9,2,16,256]{3,2,1,0:T(8,128)(2,1)} %get-tuple-element.30), channel_id=1, source_target_pairs={{0,2},{1,3},{2,4},{3,5},{4,6},{5,7},{6,8},{7,9},{8,10},{9,11},{10,... | collective-permute-start | bytes 442376 | tf_op jit(solution)/shard_map/ppermute | solution.py:95
  109.4 42.7 %copy-start.14 = (f32[4096]{0:T(1024)S(1)}, f32[4096]{0:T(1024)}, u32[]{:S(2)}) copy-start(f32[4096]{0:T(1024)} %param.20) | copy-start | bytes 49156
  109.4 42.7 %copy-start.15 = (f32[4096]{0:T(1024)S(1)}, f32[4096]{0:T(1024)}, u32[]{:S(2)}) copy-start(f32[4096]{0:T(1024)} %param.19) | copy-start | bytes 49156
  109.4 42.7 %copy-start.17 = (f32[768]{0:T(1024)S(1)}, f32[768]{0:T(1024)}, u32[]{:S(2)}) copy-start(f32[768]{0:T(1024)} %param.24) | copy-start | bytes 9220
  110.2 9.7 %collective-permute-start.2 = (bf16[9,2,16,256]{3,2,1,0:T(8,128)(2,1)}, bf16[9,2,16,256]{3,2,1,0:T(8,128)(2,1)S(1)}, u32[]{:S(2)}, u32[]{:S(2)}) collective-permute-start(bf16[9,2,16,256]{3,2,1,0:T(8,128)(2,1)} %get-tuple-element.29), channel_id=1, source_target_pairs={{0,3},{1,4},{2,5},{3,6},{4,7},{5,8},{6,9},{7,10},{8,11},{9,12},{10... | collective-permute-start | bytes 442376 | tf_op jit(solution)/shard_map/ppermute | solution.py:95
  110.8 12.0 %collective-permute-start.3 = (bf16[9,2,16,256]{3,2,1,0:T(8,128)(2,1)}, bf16[9,2,16,256]{3,2,1,0:T(8,128)(2,1)S(1)}, u32[]{:S(2)}, u32[]{:S(2)}) collective-permute-start(bf16[9,2,16,256]{3,2,1,0:T(8,128)(2,1)} %get-tuple-element.28), channel_id=1, source_target_pairs={{0,4},{1,5},{2,6},{3,7},{4,8},{5,9},{6,10},{7,11},{8,12},{9,13},{1... | collective-permute-start | bytes 442376 | tf_op jit(solution)/shard_map/ppermute | solution.py:95
  111.5 12.5 %collective-permute-start.4 = (bf16[9,2,16,256]{3,2,1,0:T(8,128)(2,1)}, bf16[9,2,16,256]{3,2,1,0:T(8,128)(2,1)S(1)}, u32[]{:S(2)}, u32[]{:S(2)}) collective-permute-start(bf16[9,2,16,256]{3,2,1,0:T(8,128)(2,1)} %get-tuple-element.27), channel_id=1, source_target_pairs={{0,5},{1,6},{2,7},{3,8},{4,9},{5,10},{6,11},{7,12},{8,13},{9,14},{... | collective-permute-start | bytes 442376 | tf_op jit(solution)/shard_map/ppermute | solution.py:95
  113.0 15.9 %collective-permute-start.5 = (bf16[9,2,16,256]{3,2,1,0:T(8,128)(2,1)}, bf16[9,2,16,256]{3,2,1,0:T(8,128)(2,1)S(1)}, u32[]{:S(2)}, u32[]{:S(2)}) collective-permute-start(bf16[9,2,16,256]{3,2,1,0:T(8,128)(2,1)} %get-tuple-element.26), channel_id=1, source_target_pairs={{0,6},{1,7},{2,8},{3,9},{4,10},{5,11},{6,12},{7,13},{8,14},{9,15},... | collective-permute-start | bytes 442376 | tf_op jit(solution)/shard_map/ppermute | solution.py:95
  115.4 23.1 %collective-permute-start.6 = (bf16[9,2,16,256]{3,2,1,0:T(8,128)(2,1)}, bf16[9,2,16,256]{3,2,1,0:T(8,128)(2,1)S(1)}, u32[]{:S(2)}, u32[]{:S(2)}) collective-permute-start(bf16[9,2,16,256]{3,2,1,0:T(8,128)(2,1)} %get-tuple-element.25), channel_id=1, source_target_pairs={{0,7},{1,8},{2,9},{3,10},{4,11},{5,12},{6,13},{7,14},{8,15},{9,0},... | collective-permute-start | bytes 442376 | tf_op jit(solution)/shard_map/ppermute | solution.py:95
  119.9 19.7 %collective-permute-start.7 = (bf16[9,2,16,256]{3,2,1,0:T(8,128)(2,1)}, bf16[9,2,16,256]{3,2,1,0:T(8,128)(2,1)S(1)}, u32[]{:S(2)}, u32[]{:S(2)}) collective-permute-start(bf16[9,2,16,256]{3,2,1,0:T(8,128)(2,1)} %get-tuple-element.24), channel_id=1, source_target_pairs={{0,8},{1,9},{2,10},{3,11},{4,12},{5,13},{6,14},{7,15},{8,0},{9,1},... | collective-permute-start | bytes 442376 | tf_op jit(solution)/shard_map/ppermute | solution.py:95
  122.8 17.5 %collective-permute-start.8 = (bf16[9,2,16,256]{3,2,1,0:T(8,128)(2,1)}, bf16[9,2,16,256]{3,2,1,0:T(8,128)(2,1)S(1)}, u32[]{:S(2)}, u32[]{:S(2)}) collective-permute-start(bf16[9,2,16,256]{3,2,1,0:T(8,128)(2,1)} %get-tuple-element.23), channel_id=1, source_target_pairs={{0,9},{1,10},{2,11},{3,12},{4,13},{5,14},{6,15},{7,0},{8,1},{9,2},... | collective-permute-start | bytes 442376 | tf_op jit(solution)/shard_map/ppermute | solution.py:95
  124.0 17.1 %collective-permute-start.9 = (bf16[9,2,16,256]{3,2,1,0:T(8,128)(2,1)S(1)}, bf16[9,2,16,256]{3,2,1,0:T(8,128)(2,1)S(1)}, u32[]{:S(2)}, u32[]{:S(2)}) collective-permute-start(bf16[9,2,16,256]{3,2,1,0:T(8,128)(2,1)S(1)} %get-tuple-element.22), channel_id=1, source_target_pairs={{0,10},{1,11},{2,12},{3,13},{4,14},{5,15},{6,0},{7,1},{8,2},{9,3},... | collective-permute-start | bytes 442376 | tf_op jit(solution)/shard_map/ppermute | solution.py:95
  128.9 18.5 %collective-permute-start.10 = (bf16[9,2,16,256]{3,2,1,0:T(8,128)(2,1)S(1)}, bf16[9,2,16,256]{3,2,1,0:T(8,128)(2,1)S(1)}, u32[]{:S(2)}, u32[]{:S(2)}) collective-permute-start(bf16[9,2,16,256]{3,2,1,0:T(8,128)(2,1)S(1)} %get-tuple-element.21), channel_id=1, source_target_pairs={{0,11},{1,12},{2,13},{3,14},{4,15},{5,0},{6,1},{7,2},{8,3},{9,4},{... | collective-permute-start | bytes 442376 | tf_op jit(solution)/shard_map/ppermute | solution.py:95
  138.5 9.5 %collective-permute-start.11 = (bf16[9,2,16,256]{3,2,1,0:T(8,128)(2,1)S(1)}, bf16[9,2,16,256]{3,2,1,0:T(8,128)(2,1)S(1)}, u32[]{:S(2)}, u32[]{:S(2)}) collective-permute-start(bf16[9,2,16,256]{3,2,1,0:T(8,128)(2,1)S(1)} %get-tuple-element.20), channel_id=1, source_target_pairs={{0,12},{1,13},{2,14},{3,15},{4,0},{5,1},{6,2},{7,3},{8,4},{9,5},{1... | collective-permute-start | bytes 442376 | tf_op jit(solution)/shard_map/ppermute | solution.py:95
  139.6 9.1 %collective-permute-start.12 = (bf16[9,2,16,256]{3,2,1,0:T(8,128)(2,1)S(1)}, bf16[9,2,16,256]{3,2,1,0:T(8,128)(2,1)S(1)}, u32[]{:S(2)}, u32[]{:S(2)}) collective-permute-start(bf16[9,2,16,256]{3,2,1,0:T(8,128)(2,1)S(1)} %get-tuple-element.19), channel_id=1, source_target_pairs={{0,13},{1,14},{2,15},{3,0},{4,1},{5,2},{6,3},{7,4},{8,5},{9,6},{10... | collective-permute-start | bytes 442376 | tf_op jit(solution)/shard_map/ppermute | solution.py:95
  140.3 9.2 %collective-permute-start.13 = (bf16[9,2,16,256]{3,2,1,0:T(8,128)(2,1)S(1)}, bf16[9,2,16,256]{3,2,1,0:T(8,128)(2,1)S(1)}, u32[]{:S(2)}, u32[]{:S(2)}) collective-permute-start(bf16[9,2,16,256]{3,2,1,0:T(8,128)(2,1)S(1)} %get-tuple-element.18), channel_id=1, source_target_pairs={{0,14},{1,15},{2,0},{3,1},{4,2},{5,3},{6,4},{7,5},{8,6},{9,7},{10,... | collective-permute-start | bytes 442376 | tf_op jit(solution)/shard_map/ppermute | solution.py:95
  141.1 10.4 %collective-permute-start.14 = (bf16[9,2,16,256]{3,2,1,0:T(8,128)(2,1)S(1)}, bf16[9,2,16,256]{3,2,1,0:T(8,128)(2,1)S(1)}, u32[]{:S(2)}, u32[]{:S(2)}) collective-permute-start(bf16[9,2,16,256]{3,2,1,0:T(8,128)(2,1)S(1)} %get-tuple-element.17), channel_id=1, source_target_pairs={{0,15},{1,0},{2,1},{3,2},{4,3},{5,4},{6,5},{7,6},{8,7},{9,8},{10,9... | collective-permute-start | bytes 442376 | tf_op jit(solution)/shard_map/ppermute | solution.py:95
  163.1 1.2 copy-start.1
  168.5 3.4 %copy-start.2 = (bf16[128,1,16,256]{3,2,1,0:T(8,128)(2,1)S(1)}, bf16[128,1,16,256]{3,2,1,0:T(8,128)(2,1)}, u32[]{:S(2)}) copy-start(bf16[128,1,16,256]{3,2,1,0:T(8,128)(2,1)} %get-tuple-element.33) | copy-start | bytes 3145732
  174.2 3.9 %copy-start.4 = (pred[512,2560]{1,0:T(8,128)(4,1)S(1)}, pred[512,2560]{1,0:T(8,128)(4,1)}, u32[]{:S(2)}) copy-start(pred[512,2560]{1,0:T(8,128)(4,1)} %pad_add_fusion) | copy-start | bytes 3932164
  178.2 10.0 %copy-start.5 = (bf16[2048,2,128]{0,2,1:T(8,128)(2,1)S(1)}, bf16[2048,2,128]{0,2,1:T(8,128)(2,1)}, u32[]{:S(2)}) copy-start(bf16[2048,2,128]{0,2,1:T(8,128)(2,1)} %copy.37) | copy-start | bytes 3145732
  178.2 10.0 %copy-start.6 = (bf16[512,2,128]{0,2,1:T(8,128)(2,1)S(1)}, bf16[512,2,128]{0,2,1:T(8,128)(2,1)}, u32[]{:S(2)}) copy-start(bf16[512,2,128]{0,2,1:T(8,128)(2,1)} %fusion.94) | copy-start | bytes 786436
  201.5 69.1 %copy-start.9 = (f32[256]{0:T(256)S(1)}, f32[256]{0:T(256)}, u32[]{:S(2)}) copy-start(f32[256]{0:T(256)} %param.30) | copy-start | bytes 3076
  201.5 69.1 %copy-start.10 = (f32[256]{0:T(256)S(1)}, f32[256]{0:T(256)}, u32[]{:S(2)}) copy-start(f32[256]{0:T(256)} %param.26) | copy-start | bytes 3076
Sparse Core Ops, SparseCore 0:
  9.0 55.1 all-gather.2
  66.3 87.1 all-gather.4
  201.6 68.8 reduce-scatter.1

commit v8 on v4

--- a/solution.py
+++ b/solution.py
@@ -105,8 +105,10 @@
     migrations,
 ):
     gathered = lax.all_gather(states, "head", axis=1, tiled=True)
-    qkv_full = gather_by_all_to_all(qkv_weight, "tok")
-    out_full = lax.all_gather(out_weight, "tok", axis=1, tiled=True)
+    split = qkv_weight.shape[1] // 2
+    qkv_first = gather_by_all_to_all(qkv_weight[:, :split], "tok")
+    qkv_second, gathered = lax.optimization_barrier((qkv_weight[:, split:], gathered))
+    qkv_second = lax.all_gather(qkv_second, "tok", axis=0, tiled=True)
     wide = gathered.astype(jnp.float32)
     pre_normed = layer_norm(wide, pre_gain, pre_shift)
     mlp_normed = layer_norm(wide, mlp_gain, mlp_shift)
@@ -122,7 +124,17 @@
     feed_part = feed(mlp_normed)
     kv_cache, feed_part = lax.optimization_barrier((kv_cache, feed_part))
     page_pool = share_pages(kv_cache, lax.axis_size("head"))
-    joined = jnp.dot(pre_normed, qkv_full, preferred_element_type=jnp.float32)
+    out_weight, page_pool = lax.optimization_barrier((out_weight, page_pool))
+    out_blocks = gather_by_all_to_all(out_weight, "tok").reshape(
+        (lax.axis_size("tok"),) + out_weight.shape
+    )
+    joined = jnp.concatenate(
+        [
+            jnp.dot(pre_normed, qkv_first, preferred_element_type=jnp.float32),
+            jnp.dot(pre_normed, qkv_second, preferred_element_type=jnp.float32),
+        ],
+        axis=1,
+    )
     joined = (joined + qkv_bias).reshape(tok_rows, -1, 3, HD)
     local_req = token_request - lax.axis_index("tok") * cached_len.shape[0]
     positions = token_positions(local_req, cached_len)
@@ -141,7 +153,9 @@
     heads_out = attend(
         queries, new_keys, new_values, cache_keys, cache_values, local_req, cached_len, positions
     ).reshape(tok_rows, -1)
-    attention_part = jnp.dot(heads_out, out_full, preferred_element_type=jnp.float32)
+    attention_part = jnp.einsum(
+        "td,bdc->tbc", heads_out, out_blocks, preferred_element_type=jnp.float32
+    ).reshape(tok_rows, -1)
     summed = lax.psum_scatter(
         (attention_part + feed_part).astype(jnp.bfloat16), "head", scatter_dimension=1, tiled=True
     ).astype(jnp.float32)

time: 259 us -> 264 us (1.019)
  starting transfers between devices: 12.6 us -> 20.8 us
  waiting for transfers between devices: 139 us -> 135 us
  local copies, waits for them, and re-layouts: 26 us -> 29.8 us
    all_to_all x1 -> x2, waiting for transfers between devices: 20.8 us -> 0.01 us  [gather_by_all_to_all(): return lax.all_to_all(copies, axis, split_axis=0, concat_axis=0, tiled=True)]
    all_to_all x1, waiting for transfers between devices: 12.5 us -> 21.2 us  [share_pages(): lax.all_to_all(grouped, 'head', split_axis=3, concat_axis=0, tiled=True)]
    all_to_all x1 -> x2, starting transfers between devices: 8.17 us -> 14.9 us  [gather_by_all_to_all(): return lax.all_to_all(copies, axis, split_axis=0, concat_axis=0, tiled=True)]
    all_gather x1, waiting for transfers between devices: 39 us -> 43.8 us  [shards(): gathered = lax.all_gather(states, 'head', axis=1, tiled=True)]
    all_gather x1, waiting for transfers between devices: 0.02 us -> 4.12 us  [shards(): qkv_second = lax.all_gather(qkv_second, 'tok', axis=0, tiled=True)]
    sub x1, matrix products: 9.86 us -> 5.76 us  [attend(): exp_scores = jnp.exp(scores - peak)]
    dot_general x0 -> x1, local copies, waits for them, and re-layouts: none -> 3.19 us  [shards(): jnp.dot(pre_normed, qkv_first, preferred_element_type=jnp.float32)]
    add x1, local copies, waits for them, and re-layouts: 3.05 us -> 0.01 us  [shards(): joined = (joined + qkv_bias).reshape(tok_rows, -1, 3, HD)]
  transfers between devices with their start and end apart: 5 -> 6, of which waited for: 4 -> 4; matrix products, arithmetic and copies ran while one was open for 33% -> 32% of each run, Pallas kernels for 0% -> 0%
where the time goes in v8:
time: 264 us; the launch traced here: 263 us
  waiting for transfers between devices  135 us (51%)
  matrix products  54.2 us (21%)
  local copies, waits for them, and re-layouts  29.8 us (11%)
  starting transfers between devices  20.8 us (8%)
  between operations  13.4 us (5%)
  other arithmetic  9.85 us (4%)
    reduce_scatter x1, waiting for transfers between devices, shards(): lax.psum_scatter((attention_part + feed_part).astype(jnp.bfloat16), 'head...  65.3 us
    all_gather x1, waiting for transfers between devices, shards(): gathered = lax.all_gather(states, 'head', axis=1, tiled=True)  43.8 us
    dot_general x1, matrix products, feed(): return jnp.dot(hidden, down_weight, preferred_element_type=jnp.float32)  23.7 us
    all_to_all x1, waiting for transfers between devices, share_pages(): lax.all_to_all(grouped, 'head', split_axis=3, concat_axis=0, tiled=True)  21.2 us
    all_to_all x2, starting transfers between devices, gather_by_all_to_all(): return lax.all_to_all(copies, axis, split_axis=0, concat_axis=0, tiled=True)  14.9 us
    dot_general x1, matrix products, attend(): jnp.einsum('htk,khd->thd', attn_probs, all_values, preferred_element_type...  7.28 us
    dot_general x1, matrix products, shards(): jnp.einsum('td,bdc->tbc', heads_out, out_blocks, preferred_element_type=j...  6.73 us
    all_to_all x1, starting transfers between devices, share_pages(): lax.all_to_all(grouped, 'head', split_axis=3, concat_axis=0, tiled=True)  5.77 us
  transfers between devices with their start and end apart: 6, of which 4 were waited for; matrix products, arithmetic and copies ran while one was open for 32% of the time, Pallas kernels for 0%

profile of v8, /device:TPU:0, one launch (start us, length us, event | category | flops | bytes accessed | tf_op | source)
XLA Modules:
  0.0 263.1 jit_solution(17651064415985388549)
XLA Ops:
  6.5 0.7 all-gather.3.cloned.1.call-update
  7.3 2.0 fusion.151
  9.2 0.2 copy.57
  9.4 1.9 broadcast_in_dim.49
  11.3 0.0 copy-start.6
  11.4 8.2 %all-to-all-start.1 = ((bf16[8,512,384]{1,2,0:T(8,128)(2,1)}), bf16[8,512,384]{1,2,0:T(8,128)(2,1)S(1)}, u32[]{:S(2)}, u32[]{:S(2)}) async-start(bf16[8,512,384]{1,2,0:T(8,128)(2,1)} %broadcast_in_dim.49), calls=%async_computation.1 | async-start | bytes 6291456 | tf_op jit(solution)/shard_map/all_to_all | solution.py:84
  19.5 0.0 all-gather.5.cloned.1.call-start
  19.6 0.1 eq.58
  19.7 0.1 reshape.235
  19.8 0.0 copy-done.5
  19.8 0.1 convert_reduce_fusion.1
  19.9 0.2 reduce-window.8
  20.1 0.1 compare_reduce_fusion
  20.2 0.1 fusion.99
  20.3 0.1 select_reduce_fusion.1
  20.4 0.1 broadcast_bitcast_fusion
  20.5 43.8 %all-gather.3.cloned.1.call-done = bf16[512,4096]{1,0:T(8,128)(2,1)} async-done(((bf16[512,256]{1,0:T(8,128)(2,1)}), bf16[512,4096]{1,0:T(8,128)(2,1)}) %all-gather.3.cloned.1.call-update) | async-done | bytes 4194320 | tf_op jit(solution)/shard_map/all_gather | solution.py:107
  64.3 0.0 all-gather.5.cloned.1.call-update
  64.3 3.0 %convert_reduce_fusion = f32[512]{0:T(512)S(1)} fusion(bf16[512,4096]{1,0:T(8,128)(2,1)} %all-gather.3.cloned.1.call-done), kind=kLoop, calls=%fused_computation.3 | loop fusion | flops 4193792 | bytes 4196352 | tf_op jit(solution)/shard_map/reduce_sum | solution.py:14
  67.3 0.5 copy-done
  67.7 1.2 fusion.9
  69.0 0.0 copy-done.11
  69.0 23.7 %fusion.36 = f32[512,4096]{1,0:T(8,128)} fusion(bf16[1024,4096]{1,0:T(8,128)(2,1)} %param.29, bf16[4096,1024]{1,0:T(8,128)(2,1)} %param.27, bf16[512,4096]{1,0:T(8,128)(2,1)} %all-gather.3.cloned.1.call-done, f32[4096]{0:T(1024)S(1)} %copy-done.11, f32[4096]{0:T(1024)S(1)} %copy-done.12, f32[512]{0:T(512)S(1)} %add_rsqrt_fusion, ...), kind=kOutput, calls=%fused_computation.52 | convolution fusion | flops 8637120512 | bytes 29401088 | tf_op jit(solution)/shard_map/dot_general | solution.py:122
  92.7 3.4 %copy.72 = bf16[9,2,2,16,8,256]{5,4,2,1,0,3:T(8,128)(2,1)} copy(bf16[9,2,2,16,8,256]{5,4,3,2,1,0:T(8,128)(2,1)} %bitcast.72) | data formatting | bytes 4718592 | tf_op jit(solution)/shard_map/reshape | solution.py:72
  96.1 0.0 all-to-all-done.1
  96.1 5.8 %all-to-all-start = ((bf16[9,2,16,16,256]{4,2,1,0,3:T(8,128)(2,1)}), bf16[9,2,16,16,256]{4,2,1,0,3:T(8,128)(2,1)}, u32[]{:S(2)}, u32[]{:S(2)}) async-start(bf16[9,2,16,16,256]{4,2,1,0,3:T(8,128)(2,1)} %bitcast.69), calls=%async_computation | async-start | bytes 4718592 | tf_op jit(solution)/shard_map/all_to_all | solution.py:75
  101.9 0.2 multiply_cosine_fusion
  102.1 0.3 compare_and_fusion.1
  102.4 0.7 compare_and_fusion
  103.1 1.2 pad_add_fusion
  104.3 2.8 %copy.58 = bf16[8,512,384]{2,1,0:T(8,128)(2,1)} copy(bf16[8,512,384]{1,2,0:T(8,128)(2,1)S(1)} %all-to-all-done.1) | data formatting | bytes 6291456 | tf_op jit(solution)/shard_map/all_to_all | solution.py:84
  107.1 3.2 %copy.59 = bf16[384,4096]{1,0:T(8,128)(2,1)S(1)} copy(bf16[384,4096]{0,1:T(8,128)(2,1)} %bitcast.68) | data formatting | bytes 6291456 | tf_op jit(solution)/shard_map/dot_general | solution.py:133
  110.3 0.0 copy-done.13
  110.3 0.0 copy-done.14
  110.3 5.2 %fusion.45 = f32[512,1,3,128]{0,3,2,1:T(8,128)} fusion(bf16[3,128,4096]{2,1,0:T(8,128)(2,1)S(1)} %bitcast.71, bf16[512,4096]{1,0:T(8,128)(2,1)} %all-gather.3.cloned.1.call-done, f32[4096]{0:T(1024)S(1)} %copy-done.13, f32[4096]{0:T(1024)S(1)} %copy-done.14, f32[512]{0:T(512)S(1)} %add_rsqrt_fusion, f32[512]{0:T(512)S(1)} %broadcast_multiply_fusion), kind=kOutput, calls=%fused_computation.60 | convolution fusion | flops 1623195648 | bytes 8163328 | tf_op jit(solution)/shard_map/dot_general | solution.py:133
  115.5 21.2 %all-to-all-done = bf16[9,2,16,16,256]{4,2,1,0,3:T(8,128)(2,1)} async-done(((bf16[9,2,16,16,256]{4,2,1,0,3:T(8,128)(2,1)}), bf16[9,2,16,16,256]{4,2,1,0,3:T(8,128)(2,1)}, u32[]{:S(2)}, u32[]{:S(2)}) %all-to-all-start) | async-done | bytes 2359328 | tf_op jit(solution)/shard_map/all_to_all | solution.py:75
  136.7 2.3 gather_fusion
  139.0 1.1 fusion.150
  140.2 1.4 reshape_squeeze.6
  141.5 2.1 copy.60
  143.6 0.1 copy.65
  143.8 0.3 reshape_squeeze.7
  144.1 1.2 copy.62
  145.2 1.4 broadcast_in_dim.56
  146.6 6.7 %all-to-all-start.2 = ((bf16[8,256,512]{1,2,0:T(8,128)(2,1)}), bf16[8,256,512]{1,2,0:T(8,128)(2,1)S(1)}, u32[]{:S(2)}, u32[]{:S(2)}) async-start(bf16[8,256,512]{1,2,0:T(8,128)(2,1)} %broadcast_in_dim.56), calls=%async_computation.2 | async-start | bytes 4194304 | tf_op jit(solution)/shard_map/all_to_all | solution.py:84
  153.4 0.0 reduce-scatter.2.cloned.1.call-start
  153.4 4.1 %all-gather.5.cloned.1.call-done = bf16[4096,384]{1,0:T(8,128)(2,1)} async-done(((bf16[512,384]{1,0:T(8,128)(2,1)}), bf16[4096,384]{1,0:T(8,128)(2,1)}) %all-gather.5.cloned.1.call-update) | async-done | bytes 3145744 | tf_op jit(solution)/shard_map/all_gather | solution.py:111
  157.6 5.6 %fusion.146 = f32[512,384]{0,1:T(8,128)S(1)} fusion(bf16[4096,384]{1,0:T(8,128)(2,1)} %all-gather.5.cloned.1.call-done, bf16[512,4096]{1,0:T(8,128)(2,1)} %all-gather.3.cloned.1.call-done, f32[4096]{0:T(1024)S(1)} %copy-done.13, f32[4096]{0:T(1024)S(1)} %copy-done.14, f32[512]{0:T(512)S(1)} %add_rsqrt_fusion, f32[512]{0:T(512)S(1)} %broadcast_multiply_fusion), kind=kOutput, calls=%fused_computation.179 | convolution fusion | flops 1623195648 | bytes 8163328 | tf_op jit(solution)/shard_map/dot_general | solution.py:134
  163.2 0.2 maximum_add_fusion
  163.4 1.2 copy-done.1
  164.6 0.1 slice_bitcast_fusion.1
  164.7 0.7 slice.94
  165.5 0.7 pad_maximum_fusion.1
  166.2 1.8 copy.63
  168.0 1.8 fusion.86
  169.8 0.0 copy-done.2
  169.8 5.8 %fusion.152 = f32[2,512]{1,0:T(2,128)S(1)} fusion(pred[512,2560]{1,0:T(8,128)(4,1)S(1)} %copy-done.2, bf16[512,2,128]{2,0,1:T(8,128)(2,1)} %copy.63, bf16[2048,2,128]{2,0,1:T(8,128)(2,1)} %copy.62, bf16[512,2,96]{0,2,1:T(8,128)(2,1)} %slice.94, bf16[512,2,16]{0,2,1:T(8,128)(2,1)S(1)} %get-tuple-element.28, bf16[512,2,16]{0,2,1:T(8,128)(2,1)S(1)} %get-tuple-element.27), kind=kOutput, calls=%fused_computation.183 | convolution fusion | flops 684984832 | bytes 2887680 | tf_op jit(solution)/shard_map/sub | solution.py:64
  175.5 7.3 %fusion.48 = bf16[2,128,512]{2,1,0:T(8,128)(2,1)} fusion(f32[2,512]{1,0:T(2,128)S(1)} %fusion.152, bf16[512,2,128]{0,2,1:T(8,128)(2,1)} %fusion.86, bf16[2048,2,128]{0,2,1:T(8,128)(2,1)} %copy.60, pred[512,2560]{1,0:T(8,128)(4,1)S(1)} %copy-done.2, bf16[512,2,128]{2,0,1:T(8,128)(2,1)} %copy.63, bf16[2048,2,128]{2,0,1:T(8,128)(2,1)} %copy.62, ...), kind=kOutput, calls=%fused_computation.61 | convolution fusion | flops 1361448448 | bytes 4460544 | tf_op jit(solution)/shard_map/htk,khd->thd/dot_general | solution.py:66
  182.8 0.0 all-to-all-done.2
  182.8 6.7 %add_convert_fusion = bf16[512,4096]{1,0:T(8,128)(2,1)} fusion(f32[512,4096]{1,0:T(8,128)} %fusion.36, bf16[512,256]{0,1:T(8,128)(2,1)} %bitcast.74, bf16[4096,256]{1,0:T(8,128)(2,1)S(1)} %bitcast.70), kind=kOutput, calls=%fused_computation.16 | convolution fusion | flops 1077936128 | bytes 14942208 | tf_op jit(solution)/shard_map/td,bdc->tbc/dot_general | solution.py:156
  189.5 0.0 reduce-scatter.2.cloned.1.call-update
  189.6 65.3 %reduce-scatter.2.cloned.1.call-done = bf16[512,256]{1,0:T(8,128)(2,1)} async-done(((bf16[512,4096]{1,0:T(8,128)(2,1)}), bf16[512,256]{1,0:T(8,128)(2,1)}) %reduce-scatter.2.cloned.1.call-update) | async-done | bytes 262160 | tf_op jit(solution)/shard_map/reduce_scatter | solution.py:159
  254.9 0.0 copy-done.9
  254.9 1.7 add_convert_fusion.1
  (40 shorter events, 0.2 us)
Async XLA Ops:
  6.5 57.7 %all-gather.3.cloned.1.call-start = ((), (), s32[]{:S(2)}) async-start(), calls=%async_computation.4 | async-start | bytes 4456448 | tf_op jit(solution)/shard_map/all_gather | solution.py:107
  11.3 8.2 %copy-start.16 = (s32[2,64]{1,0:T(2,128)S(1)}, s32[2,64]{1,0:T(2,128)}, u32[]{:S(2)}) copy-start(s32[2,64]{1,0:T(2,128)} %param.34) | copy-start | bytes 1540
  11.3 8.4 %copy-start.5 = (f32[768]{0:T(1024)S(1)}, f32[768]{0:T(1024)}, u32[]{:S(2)}) copy-start(f32[768]{0:T(1024)} %param.24) | copy-start | bytes 9220
  11.3 8.4 %copy-start.7 = (s32[512]{0:T(512)S(1)}, s32[512]{0:T(512)}, u32[]{:S(2)}) copy-start(s32[512]{0:T(512)} %param.32) | copy-start | bytes 6148
  11.3 8.7 %copy-start.10 = (s32[8,2]{0,1:T(2,128)S(1)}, s32[8,2]{0,1:T(2,128)}, u32[]{:S(2)}) copy-start(s32[8,2]{0,1:T(2,128)} %param.35) | copy-start | bytes 196
  11.3 8.9 %copy-start.6 = (s32[2]{0:T(128)S(1)}, s32[2]{0:T(128)}, u32[]{:S(2)}) copy-start(s32[2]{0:T(128)} %param.33) | copy-start | bytes 28
  11.4 84.7 %all-to-all-start.1 = ((bf16[8,512,384]{1,2,0:T(8,128)(2,1)}), bf16[8,512,384]{1,2,0:T(8,128)(2,1)S(1)}, u32[]{:S(2)}, u32[]{:S(2)}) async-start(bf16[8,512,384]{1,2,0:T(8,128)(2,1)} %broadcast_in_dim.49), calls=%async_computation.1 | async-start | bytes 6291456 | tf_op jit(solution)/shard_map/all_to_all | solution.py:84
  19.5 138.0 %all-gather.5.cloned.1.call-start = ((), (), s32[]{:S(2)}) async-start(), calls=%async_computation.5 | async-start | bytes 3538944 | tf_op jit(solution)/shard_map/all_gather | solution.py:111
  64.3 3.5 %copy-start = (bf16[512,4096]{1,0:T(8,128)(2,1)S(1)}, bf16[512,4096]{1,0:T(8,128)(2,1)}, u32[]{:S(2)}) copy-start(bf16[512,4096]{1,0:T(8,128)(2,1)} %all-gather.3.cloned.1.call-done) | copy-start | bytes 12582916
  67.7 1.3 copy-start.11
  67.7 1.3 copy-start.12
  67.7 1.3 copy-start.15
  96.1 40.5 %all-to-all-start = ((bf16[9,2,16,16,256]{4,2,1,0,3:T(8,128)(2,1)}), bf16[9,2,16,16,256]{4,2,1,0,3:T(8,128)(2,1)}, u32[]{:S(2)}, u32[]{:S(2)}) async-start(bf16[9,2,16,16,256]{4,2,1,0,3:T(8,128)(2,1)} %bitcast.69), calls=%async_computation | async-start | bytes 4718592 | tf_op jit(solution)/shard_map/all_to_all | solution.py:75
  107.1 3.2 %copy-start.13 = (f32[4096]{0:T(1024)S(1)}, f32[4096]{0:T(1024)}, u32[]{:S(2)}) copy-start(f32[4096]{0:T(1024)} %param.20) | copy-start | bytes 49156
  107.1 3.2 %copy-start.14 = (f32[4096]{0:T(1024)S(1)}, f32[4096]{0:T(1024)}, u32[]{:S(2)}) copy-start(f32[4096]{0:T(1024)} %param.19) | copy-start | bytes 49156
  140.1 3.5 %copy-start.4 = (bf16[256,512]{1,0:T(8,128)(2,1)S(1)}, bf16[256,512]{1,0:T(8,128)(2,1)}, u32[]{:S(2)}) copy-start(bf16[256,512]{1,0:T(8,128)(2,1)} %param.25) | copy-start | bytes 786436
  146.6 36.2 %all-to-all-start.2 = ((bf16[8,256,512]{1,2,0:T(8,128)(2,1)}), bf16[8,256,512]{1,2,0:T(8,128)(2,1)S(1)}, u32[]{:S(2)}, u32[]{:S(2)}) async-start(bf16[8,256,512]{1,2,0:T(8,128)(2,1)} %broadcast_in_dim.56), calls=%async_computation.2 | async-start | bytes 4194304 | tf_op jit(solution)/shard_map/all_to_all | solution.py:84
  153.4 9.8 %copy-start.3 = (f32[512,1,3,128]{0,3,2,1:T(8,128)S(1)}, f32[512,1,3,128]{0,3,2,1:T(8,128)}, u32[]{:S(2)}) copy-start(f32[512,1,3,128]{0,3,2,1:T(8,128)} %fusion.45) | copy-start | bytes 2359300
  153.4 101.5 %reduce-scatter.2.cloned.1.call-start = ((), (), s32[]{:S(2)}) async-start(), calls=%async_computation.6 | async-start | bytes 4456448 | tf_op jit(solution)/shard_map/reduce_scatter | solution.py:159
  163.4 1.2 copy-start.1
  164.6 5.1 %copy-start.2 = (pred[512,2560]{1,0:T(8,128)(4,1)S(1)}, pred[512,2560]{1,0:T(8,128)(4,1)}, u32[]{:S(2)}) copy-start(pred[512,2560]{1,0:T(8,128)(4,1)} %pad_add_fusion) | copy-start | bytes 3932164
  189.5 65.3 %copy-start.8 = (f32[256]{0:T(256)S(1)}, f32[256]{0:T(256)}, u32[]{:S(2)}) copy-start(f32[256]{0:T(256)} %param.30) | copy-start | bytes 3076
  189.5 65.3 %copy-start.9 = (f32[256]{0:T(256)S(1)}, f32[256]{0:T(256)}, u32[]{:S(2)}) copy-start(f32[256]{0:T(256)} %param.26) | copy-start | bytes 3076
Sparse Core Ops, SparseCore 0:
  9.0 55.2 all-gather.2
  66.5 90.9 all-gather.4
  189.7 65.1 reduce-scatter.1

commit v9 on v4

--- a/solution.py
+++ b/solution.py
@@ -2,6 +2,8 @@
 import jax.numpy as jnp
 from jax import lax
 from jax.sharding import PartitionSpec as P
+from jax.experimental import pallas as pl
+from jax.experimental.pallas import tpu as pltpu
 
 HD = 128
 ROT = 32
@@ -66,6 +68,73 @@
     return jnp.einsum(
         "htk,khd->thd", attn_probs, all_values, preferred_element_type=jnp.float32
     ).astype(jnp.bfloat16)
+
+
+def attention_kernel(
+    q_ref, kc_ref, vc_ref, kn_ref, vn_ref, req_col, pos_col, owner_row, limit_row, req_row, pos_row, o_ref
+):
+    queries = q_ref[...]
+    cache_keys = kc_ref[...].reshape(-1, queries.shape[1])
+    cache_values = vc_ref[...].reshape(-1, queries.shape[1])
+    dims = (((1,), (1,)), ((), ()))
+    scale = HD ** (-0.5)
+    cache_scores = lax.dot_general(queries, cache_keys, dims, preferred_element_type=jnp.float32) * scale
+    new_scores = lax.dot_general(queries, kn_ref[...], dims, preferred_element_type=jnp.float32) * scale
+    cache_place = lax.broadcasted_iota(jnp.int32, cache_scores.shape, 1) % (
+        cache_scores.shape[1] // 2
+    )
+    cache_ok = (req_col[...] == owner_row[...]) & (cache_place < limit_row[...])
+    new_ok = (req_col[...] == req_row[...]) & (pos_row[...] <= pos_col[...])
+    cache_scores = jnp.where(cache_ok, cache_scores, -1e30)
+    new_scores = jnp.where(new_ok, new_scores, -1e30)
+    peak = jnp.maximum(
+        jnp.max(cache_scores, axis=1, keepdims=True), jnp.max(new_scores, axis=1, keepdims=True)
+    )
+    cache_exp = jnp.exp(cache_scores - peak)
+    new_exp = jnp.exp(new_scores - peak)
+    total = jnp.sum(cache_exp, axis=1, keepdims=True) + jnp.sum(new_exp, axis=1, keepdims=True)
+    cache_probs = (cache_exp / total).astype(jnp.bfloat16)
+    new_probs = (new_exp / total).astype(jnp.bfloat16)
+    mixed = jnp.dot(cache_probs, cache_values, preferred_element_type=jnp.float32) + jnp.dot(
+        new_probs, vn_ref[...], preferred_element_type=jnp.float32
+    )
+    o_ref[...] = mixed.astype(o_ref.dtype)
+
+
+def attend_kernel(queries, new_keys, new_values, pages, local_req, cached, positions):
+    tokens, heads = queries.shape[0], queries.shape[1]
+    page_count, page_len = pages.shape[0], pages.shape[2]
+    span = page_count * page_len // cached.shape[0]
+    key_slot = jnp.arange(page_count * page_len, dtype=jnp.int32)
+    owner_row = (key_slot // span)[None, :]
+    limit_row = jnp.repeat(cached, span)[None, :]
+    flat = lambda x: x.reshape(tokens, heads * HD)
+    row_block = pl.BlockSpec((tokens, HD), lambda h: (0, h))
+    page_block = lambda part: pl.BlockSpec((page_count, 1, page_len, HD), lambda h: (0, part, 0, h))
+    whole = lambda x: pl.BlockSpec(x.shape, lambda h: (0,) * x.ndim)
+    extras = (
+        local_req[:, None],
+        positions[:, None],
+        owner_row,
+        limit_row,
+        local_req[None, :],
+        positions[None, :],
+    )
+    keys_seen = page_count * page_len + tokens
+    out = pl.pallas_call(
+        attention_kernel,
+        grid=(heads,),
+        in_specs=[row_block, page_block(0), page_block(1), row_block, row_block]
+        + [whole(x) for x in extras],
+        out_specs=row_block,
+        out_shape=jax.ShapeDtypeStruct((tokens, heads * HD), jnp.bfloat16),
+        cost_estimate=pl.CostEstimate(
+            flops=4 * heads * tokens * keys_seen * HD,
+            transcendentals=heads * tokens * keys_seen,
+            bytes_accessed=2 * HD * heads * (2 * tokens + 2 * keys_seen),
+        ),
+    )(flat(queries), pages, pages, flat(new_keys), flat(new_values), *extras)
+    return out
 
 
 def share_pages(local_pool, groups):
@@ -136,11 +205,9 @@
     moved_from = jnp.sum(jnp.where(match, sources[None, :], 0), axis=1)
     table = jnp.where(jnp.any(match, axis=1), moved_from, table)
     pages = page_pool[table]
-    cache_keys = pages[:, 0].reshape(-1, queries.shape[1], HD)
-    cache_values = pages[:, 1].reshape(-1, queries.shape[1], HD)
-    heads_out = attend(
-        queries, new_keys, new_values, cache_keys, cache_values, local_req, cached_len, positions
-    ).reshape(tok_rows, -1)
+    heads_out = attend_kernel(
+        queries, new_keys, new_values, pages, local_req, cached_len, positions
+    )
     attention_part = jnp.dot(heads_out, out_full, preferred_element_type=jnp.float32)
     summed = lax.psum_scatter(
         (attention_part + feed_part).astype(jnp.bfloat16), "head", scatter_dimension=1, tiled=True

time: 259 us -> 248 us (0.958)
  matrix products: 56.3 us -> 40.3 us
  Pallas kernels: 0 us -> 10.2 us
  local copies, waits for them, and re-layouts: 26 us -> 18.5 us
  waiting for transfers between devices: 139 us -> 144 us
  other arithmetic: 11.4 us -> 8.75 us
    pallas_call x0 -> x1, Pallas kernels: none -> 10.2 us  [attend_kernel(): pl.pallas_call(attention_kernel, grid=(heads,), in_specs=[row_block, page...]
    sub x1 -> x0, matrix products: 9.86 us -> none  [attend(): exp_scores = jnp.exp(scores - peak)]
    dot_general x1 -> x0, matrix products: 6.01 us -> none  [attend(): jnp.einsum('htk,khd->thd', attn_probs, all_values, preferred_element_type...]
    another operation x4 -> x0, local copies, waits for them, and re-layouts: 3.98 us -> none  [the longest x2 2.35 us: shards(): cache_values = pages[:, 1].reshape(-1, queries.shape[1], HD)]
    all_to_all x1, waiting for transfers between devices: 12.5 us -> 16.2 us  [share_pages(): lax.all_to_all(grouped, 'head', split_axis=3, concat_axis=0, tiled=True)]
    slice x2 -> x1, local copies, waits for them, and re-layouts: 3.8 us -> 1.07 us  [shards(): new_values = joined[:, :, 2].astype(jnp.bfloat16)]
  transfers between devices with their start and end apart: 5 -> 5, of which waited for: 4 -> 4; matrix products, arithmetic and copies ran while one was open for 33% -> 23% of each run, Pallas kernels for 0% -> 4%
where the time goes in v9:
time: 248 us
  waiting for transfers between devices  144 us (58%)
  matrix products  40.3 us (16%)
  local copies, waits for them, and re-layouts  18.5 us (7%)
  between operations  13.3 us (5%)
  starting transfers between devices  12.6 us (5%)
  Pallas kernels  10.2 us (4%)
  other arithmetic  8.75 us (4%)
    reduce_scatter x1, waiting for transfers between devices, shards(): lax.psum_scatter((attention_part + feed_part).astype(jnp.bfloat16), 'head...  65.9 us
    all_gather x1, waiting for transfers between devices, shards(): gathered = lax.all_gather(states, 'head', axis=1, tiled=True)  39.9 us
    dot_general x1, matrix products, feed(): return jnp.dot(hidden, down_weight, preferred_element_type=jnp.float32)  23.8 us
    all_to_all x1, waiting for transfers between devices, gather_by_all_to_all(): return lax.all_to_all(copies, axis, split_axis=0, concat_axis=0, tiled=True)  20.9 us
    all_to_all x1, waiting for transfers between devices, share_pages(): lax.all_to_all(grouped, 'head', split_axis=3, concat_axis=0, tiled=True)  16.2 us
    pallas_call x1, Pallas kernels, attend_kernel(): pl.pallas_call(attention_kernel, grid=(heads,), in_specs=[row_block, page...  10.2 us
    dot_general x1, matrix products, shards(): joined = jnp.dot(pre_normed, qkv_full, preferred_element_type=jnp.float32)  9.15 us
    all_to_all x1, starting transfers between devices, gather_by_all_to_all(): return lax.all_to_all(copies, axis, split_axis=0, concat_axis=0, tiled=True)  8.17 us
  transfers between devices with their start and end apart: 5, of which 4 were waited for; matrix products, arithmetic and copies ran while one was open for 23% of the time, Pallas kernels for 4%

profile of v9, /device:TPU:0, one launch (start us, length us, event | category | flops | bytes accessed | tf_op | source)
XLA Modules:
  0.0 248.0 jit_solution(7122696950671739024)
XLA Ops:
  6.5 0.0 all-gather.3.cloned.1.call-start
  6.5 0.7 all-gather.3.cloned.1.call-update
  7.3 4.1 %broadcast_in_dim.36 = bf16[8,512,768]{2,1,0:T(8,128)(2,1)} broadcast(bf16[512,768]{1,0:T(8,128)(2,1)} %param.23), dimensions={1,2} | broadcast | bytes 7077888 | tf_op jit(solution)/shard_map/broadcast_in_dim | solution.py:150
  11.4 0.0 copy-start.14
  11.4 0.0 copy-start.4
  11.4 0.0 copy-start.3
  11.4 0.0 copy-start.7
  11.4 8.2 %all-to-all-start = ((bf16[8,512,768]{2,1,0:T(8,128)(2,1)}), bf16[8,512,768]{2,1,0:T(8,128)(2,1)}, u32[]{:S(2)}, u32[]{:S(2)}) async-start(bf16[8,512,768]{2,1,0:T(8,128)(2,1)} %broadcast_in_dim.36), calls=%async_computation | async-start | bytes 12582912 | tf_op jit(solution)/shard_map/all_to_all | solution.py:153
  19.6 0.0 all-gather.5.cloned.1.call-start
  19.6 0.7 all-gather.5.cloned.1.call-update
  20.3 0.0 copy-done.14
  20.3 0.1 eq.33
  20.4 0.1 reshape.242
  20.5 0.0 copy-done.4
  20.5 0.1 convert_reduce_fusion.1
  20.6 0.2 reduce-window.8
  20.8 0.0 copy-done.3
  20.8 0.1 broadcast_bitcast_fusion
  20.9 0.1 select_reduce_fusion.1
  21.0 0.1 copy.63
  21.1 0.1 copy.64
  21.3 0.0 copy-done.7
  21.3 0.9 copy.65.req_col
  22.2 0.6 copy.71
  22.8 0.7 sub.69.pos_col
  23.5 0.1 compare_reduce_fusion
  23.6 0.1 fusion.70
  23.8 0.6 and_select_fusion.owner_row
  24.4 39.9 %all-gather.3.cloned.1.call-done = bf16[512,4096]{1,0:T(8,128)(2,1)} async-done(((bf16[512,256]{1,0:T(8,128)(2,1)}), bf16[512,4096]{1,0:T(8,128)(2,1)}) %all-gather.3.cloned.1.call-update) | async-done | bytes 4194320 | tf_op jit(solution)/shard_map/all_gather | solution.py:176
  64.3 3.0 %convert_reduce_fusion = f32[512]{0:T(512)S(1)} fusion(bf16[512,4096]{1,0:T(8,128)(2,1)} %all-gather.3.cloned.1.call-done), kind=kLoop, calls=%fused_computation.2 | loop fusion | flops 4193792 | bytes 4196352 | tf_op jit(solution)/shard_map/reduce_sum | solution.py:16
  67.2 0.0 copy-done.2
  67.2 0.5 copy-done
  67.7 1.2 fusion.8
  69.0 0.0 copy-done.8
  69.0 0.0 copy-done.9
  69.0 0.0 copy-done.12
  69.0 0.0 copy-start.1
  69.0 23.8 %fusion.34 = f32[512,4096]{1,0:T(8,128)} fusion(bf16[1024,4096]{1,0:T(8,128)(2,1)} %param.29, bf16[4096,1024]{1,0:T(8,128)(2,1)} %param.27, bf16[512,4096]{1,0:T(8,128)(2,1)} %all-gather.3.cloned.1.call-done, f32[4096]{0:T(1024)S(1)} %copy-done.8, f32[4096]{0:T(1024)S(1)} %copy-done.9, f32[512]{0:T(512)S(1)} %add_rsqrt_fusion, ...), kind=kOutput, calls=%fused_computation.43 | convolution fusion | flops 8637120512 | bytes 29401088 | tf_op jit(solution)/shard_map/dot_general | solution.py:189
  92.8 0.0 copy-done.1
  92.8 1.8 copy.73
  94.6 20.9 %all-to-all-done = bf16[8,512,768]{2,1,0:T(8,128)(2,1)} async-done(((bf16[8,512,768]{2,1,0:T(8,128)(2,1)}), bf16[8,512,768]{2,1,0:T(8,128)(2,1)}, u32[]{:S(2)}, u32[]{:S(2)}) %all-to-all-start) | async-done | bytes 6291488 | tf_op jit(solution)/shard_map/all_to_all | solution.py:153
  115.5 4.4 %all-to-all-start.1 = ((bf16[9,2,16,16,256]{4,2,1,0,3:T(8,128)(2,1)}), bf16[9,2,16,16,256]{4,2,1,0,3:T(8,128)(2,1)S(1)}, u32[]{:S(2)}, u32[]{:S(2)}) async-start(bf16[9,2,16,16,256]{4,2,1,0,3:T(8,128)(2,1)} %bitcast.53), calls=%async_computation.1 | async-start | bytes 4718592 | tf_op jit(solution)/shard_map/all_to_all | solution.py:144
  119.9 0.0 reduce-scatter.2.cloned.1.call-start
  120.0 0.6 add_subtract_fusion.pos_row
  120.6 0.2 multiply_cosine_fusion
  120.8 0.0 copy-done.10
  120.8 0.0 copy-done.11
  120.8 0.0 copy-done.13
  120.8 9.2 %fusion.36 = f32[512,768]{1,0:T(8,128)} fusion(bf16[4096,768]{1,0:T(8,128)(2,1)} %bitcast, bf16[512,4096]{1,0:T(8,128)(2,1)} %all-gather.3.cloned.1.call-done, f32[4096]{0:T(1024)S(1)} %copy-done.10, f32[4096]{0:T(1024)S(1)} %copy-done.11, f32[512]{0:T(512)S(1)} %add_rsqrt_fusion, f32[512]{0:T(512)S(1)} %broadcast_multiply_fusion, f32[768]{0:T(1024)S(1)} %copy-done.13), kind=kOutput, calls=%fused_computation.44 | convolution fusion | flops 3234201600 | bytes 12098560 | tf_op jit(solution)/shard_map/dot_general | solution.py:194
  129.9 3.1 %copy.57 = f32[512,768]{0,1:T(8,128)} copy(f32[512,768]{1,0:T(8,128)} %fusion.36) | data formatting | bytes 3145728 | tf_op jit(solution)/shard_map/add | solution.py:195
  133.0 1.1 slice.73
  134.1 1.3 slice_bitcast_fusion
  135.5 0.8 copy.66.q_ref
  136.4 0.8 copy.67.kn_ref
  137.2 0.8 copy.68.vn_ref
  138.1 16.2 %all-to-all-done.1 = bf16[9,2,16,16,256]{4,2,1,0,3:T(8,128)(2,1)S(1)} async-done(((bf16[9,2,16,16,256]{4,2,1,0,3:T(8,128)(2,1)}), bf16[9,2,16,16,256]{4,2,1,0,3:T(8,128)(2,1)S(1)}, u32[]{:S(2)}, u32[]{:S(2)}) %all-to-all-start.1) | async-done | bytes 2359328 | tf_op jit(solution)/shard_map/all_to_all | solution.py:144
  154.2 2.0 gather_fusion
  156.3 10.2 %shard_map.172 = bf16[512,256]{1,0:T(8,128)(2,1)} custom-call(bf16[512,256]{1,0:T(8,128)(2,1)} %copy.66.q_ref, bf16[128,2,16,256]{3,2,1,0:T(8,128)(2,1)} %gather_fusion, bf16[128,2,16,256]{3,2,1,0:T(8,128)(2,1)} %gather_fusion, bf16[512,256]{1,0:T(8,128)(2,1)} %copy.67.kn_ref, bf16[512,256]{1,0:T(8,128)(2,1)} %copy.68.vn_ref, s32[512,1]{1,0:T(8,128)} %copy.65.req_col, ...), custom_call_target="tpu_custom_call" | custom-call | flops 1342177280 | bytes 3145728 | tf_op jit(solution)/shard_map/pallas_call | solution.py:124
  166.5 7.3 %add_convert_fusion = bf16[512,4096]{1,0:T(8,128)(2,1)} fusion(f32[512,4096]{1,0:T(8,128)} %fusion.34, bf16[512,256]{1,0:T(8,128)(2,1)} %shard_map.172, bf16[256,4096]{1,0:T(8,128)(2,1)} %all-gather.5.cloned.1.call-done), kind=kOutput, calls=%fused_computation.12 | convolution fusion | flops 1077936128 | bytes 14942208 | tf_op jit(solution)/shard_map/dot_general | solution.py:211
  173.8 0.0 reduce-scatter.2.cloned.1.call-update
  173.8 65.9 %reduce-scatter.2.cloned.1.call-done = bf16[512,256]{1,0:T(8,128)(2,1)} async-done(((bf16[512,4096]{1,0:T(8,128)(2,1)}), bf16[512,256]{1,0:T(8,128)(2,1)}) %reduce-scatter.2.cloned.1.call-update) | async-done | bytes 262160 | tf_op jit(solution)/shard_map/reduce_scatter | solution.py:212
  239.7 0.0 copy-done.5
  239.7 0.0 copy-done.6
  239.7 1.7 add_convert_fusion.1
  (25 shorter events, 0.2 us)
Async XLA Ops:
  6.5 57.7 %all-gather.3.cloned.1.call-start = ((), (), s32[]{:S(2)}) async-start(), calls=%async_computation.3 | async-start | bytes 4456448 | tf_op jit(solution)/shard_map/all_gather | solution.py:176
  11.4 8.9 %copy-start.14 = (s32[2,64]{1,0:T(2,128)S(1)}, s32[2,64]{1,0:T(2,128)}, u32[]{:S(2)}) copy-start(s32[2,64]{1,0:T(2,128)} %param.34) | copy-start | bytes 1540
  11.4 9.1 %copy-start.4 = (s32[512]{0:T(512)S(1)}, s32[512]{0:T(512)}, u32[]{:S(2)}) copy-start(s32[512]{0:T(512)} %param.32) | copy-start | bytes 6148
  11.4 9.4 %copy-start.3 = (s32[2]{0:T(128)S(1)}, s32[2]{0:T(128)}, u32[]{:S(2)}) copy-start(s32[2]{0:T(128)} %param.33) | copy-start | bytes 28
  11.4 9.9 %copy-start.7 = (s32[8,2]{0,1:T(2,128)S(1)}, s32[8,2]{0,1:T(2,128)}, u32[]{:S(2)}) copy-start(s32[8,2]{0,1:T(2,128)} %param.35) | copy-start | bytes 196
  11.4 104.1 %all-to-all-start = ((bf16[8,512,768]{2,1,0:T(8,128)(2,1)}), bf16[8,512,768]{2,1,0:T(8,128)(2,1)}, u32[]{:S(2)}, u32[]{:S(2)}) async-start(bf16[8,512,768]{2,1,0:T(8,128)(2,1)} %broadcast_in_dim.36), calls=%async_computation | async-start | bytes 12582912 | tf_op jit(solution)/shard_map/all_to_all | solution.py:153
  19.6 146.9 %all-gather.5.cloned.1.call-start = ((), (), s32[]{:S(2)}) async-start(), calls=%async_computation.4 | async-start | bytes 2359296 | tf_op jit(solution)/shard_map/all_gather | solution.py:178
  20.5 46.7 %copy-start.2 = (s32[512]{0:T(512)}, s32[512]{0:T(512)S(1)}, u32[]{:S(2)}) copy-start(s32[512]{0:T(512)S(1)} %broadcast_subtract_fusion) | copy-start | bytes 6148
  64.3 3.4 %copy-start = (bf16[512,4096]{1,0:T(8,128)(2,1)S(1)}, bf16[512,4096]{1,0:T(8,128)(2,1)}, u32[]{:S(2)}) copy-start(bf16[512,4096]{1,0:T(8,128)(2,1)} %all-gather.3.cloned.1.call-done) | copy-start | bytes 12582916
  67.7 1.3 copy-start.8
  67.7 1.3 copy-start.9
  67.7 1.3 copy-start.12
  69.0 23.8 %copy-start.1 = (bf16[9,2,16,4096]{3,2,1,0:T(8,128)(2,1)S(1)}, bf16[9,2,16,4096]{3,2,1,0:T(8,128)(2,1)}, u32[]{:S(2)}) copy-start(bf16[9,2,16,4096]{3,2,1,0:T(8,128)(2,1)} %param.31) | copy-start | bytes 7077892
  115.5 5.2 %copy-start.10 = (f32[4096]{0:T(1024)S(1)}, f32[4096]{0:T(1024)}, u32[]{:S(2)}) copy-start(f32[4096]{0:T(1024)} %param.20) | copy-start | bytes 49156
  115.5 5.3 %copy-start.11 = (f32[4096]{0:T(1024)S(1)}, f32[4096]{0:T(1024)}, u32[]{:S(2)}) copy-start(f32[4096]{0:T(1024)} %param.19) | copy-start | bytes 49156
  115.5 5.3 %copy-start.13 = (f32[768]{0:T(1024)S(1)}, f32[768]{0:T(1024)}, u32[]{:S(2)}) copy-start(f32[768]{0:T(1024)} %param.24) | copy-start | bytes 9220
  115.5 38.7 %all-to-all-start.1 = ((bf16[9,2,16,16,256]{4,2,1,0,3:T(8,128)(2,1)}), bf16[9,2,16,16,256]{4,2,1,0,3:T(8,128)(2,1)S(1)}, u32[]{:S(2)}, u32[]{:S(2)}) async-start(bf16[9,2,16,16,256]{4,2,1,0,3:T(8,128)(2,1)} %bitcast.53), calls=%async_computation.1 | async-start | bytes 4718592 | tf_op jit(solution)/shard_map/all_to_all | solution.py:144
  119.9 119.8 %reduce-scatter.2.cloned.1.call-start = ((), (), s32[]{:S(2)}) async-start(), calls=%async_computation.5 | async-start | bytes 4456448 | tf_op jit(solution)/shard_map/reduce_scatter | solution.py:212
  173.8 66.0 %copy-start.5 = (f32[256]{0:T(256)S(1)}, f32[256]{0:T(256)}, u32[]{:S(2)}) copy-start(f32[256]{0:T(256)} %param.30) | copy-start | bytes 3076
  173.8 66.0 %copy-start.6 = (f32[256]{0:T(256)S(1)}, f32[256]{0:T(256)}, u32[]{:S(2)}) copy-start(f32[256]{0:T(256)} %param.26) | copy-start | bytes 3076
Sparse Core Ops, SparseCore 0:
  9.0 55.2 all-gather.2
  66.4 97.6 all-gather.4
  173.9 65.7 reduce-scatter.1

commit v10 on v9

--- a/solution.py
+++ b/solution.py
@@ -174,6 +174,8 @@
     migrations,
 ):
     gathered = lax.all_gather(states, "head", axis=1, tiled=True)
+    page_pool = share_pages(kv_cache, lax.axis_size("head"))
+    qkv_weight, page_pool = lax.optimization_barrier((qkv_weight, page_pool))
     qkv_full = gather_by_all_to_all(qkv_weight, "tok")
     out_full = lax.all_gather(out_weight, "tok", axis=1, tiled=True)
     wide = gathered.astype(jnp.float32)
@@ -189,8 +191,6 @@
         return jnp.dot(hidden, down_weight, preferred_element_type=jnp.float32)
 
     feed_part = feed(mlp_normed)
-    kv_cache, feed_part = lax.optimization_barrier((kv_cache, feed_part))
-    page_pool = share_pages(kv_cache, lax.axis_size("head"))
     joined = jnp.dot(pre_normed, qkv_full, preferred_element_type=jnp.float32)
     joined = (joined + qkv_bias).reshape(tok_rows, -1, 3, HD)
     local_req = token_request - lax.axis_index("tok") * cached_len.shape[0]

time: 248 us -> 269 us (1.085)
  blocking collectives: 0 us -> 42.9 us
  waiting for transfers between devices: 144 us -> 134 us
  local copies, waits for them, and re-layouts: 18.5 us -> 12.7 us
  starting transfers between devices: 12.6 us -> 7.87 us
    all_to_all x1, waiting for transfers between devices: 20.9 us -> 63.9 us  [gather_by_all_to_all(): return lax.all_to_all(copies, axis, split_axis=0, concat_axis=0, tiled=True)]
    all_to_all x0 -> x1, blocking collectives: none -> 42.9 us  [share_pages(): lax.all_to_all(grouped, 'head', split_axis=3, concat_axis=0, tiled=True)]
    all_gather x1, waiting for transfers between devices: 39.9 us -> 5.98 us  [shards(): gathered = lax.all_gather(states, 'head', axis=1, tiled=True)]
    all_to_all x1 -> x0, waiting for transfers between devices: 16.2 us -> none  [share_pages(): lax.all_to_all(grouped, 'head', split_axis=3, concat_axis=0, tiled=True)]
    all_to_all x1 -> x0, starting transfers between devices: 4.38 us -> none  [share_pages(): lax.all_to_all(grouped, 'head', split_axis=3, concat_axis=0, tiled=True)]
    reduce_scatter x1, waiting for transfers between devices: 65.9 us -> 62.9 us  [shards(): lax.psum_scatter((attention_part + feed_part).astype(jnp.bfloat16), 'head...]
  transfers between devices with their start and end apart: 5 -> 4, of which waited for: 4 -> 3; matrix products, arithmetic and copies ran while one was open for 23% -> 19% of each run, Pallas kernels for 4% -> 4%
where the time goes in v10:
time: 269 us
  waiting for transfers between devices  134 us (50%)
  blocking collectives  42.9 us (16%)
  matrix products  38.4 us (14%)
  between operations  13.3 us (5%)
  local copies, waits for them, and re-layouts  12.7 us (5%)
  Pallas kernels  10.3 us (4%)
  other arithmetic  8.74 us (3%)
  starting transfers between devices  7.87 us (3%)
    all_to_all x1, waiting for transfers between devices, gather_by_all_to_all(): return lax.all_to_all(copies, axis, split_axis=0, concat_axis=0, tiled=True)  63.9 us
    reduce_scatter x1, waiting for transfers between devices, shards(): lax.psum_scatter((attention_part + feed_part).astype(jnp.bfloat16), 'head...  62.9 us
    all_to_all x1, blocking collectives, share_pages(): lax.all_to_all(grouped, 'head', split_axis=3, concat_axis=0, tiled=True)  42.9 us
    dot_general x1, matrix products, feed(): return jnp.dot(hidden, down_weight, preferred_element_type=jnp.float32)  23.5 us
    pallas_call x1, Pallas kernels, attend_kernel(): pl.pallas_call(attention_kernel, grid=(heads,), in_specs=[row_block, page...  10.3 us
    all_to_all x1, starting transfers between devices, gather_by_all_to_all(): return lax.all_to_all(copies, axis, split_axis=0, concat_axis=0, tiled=True)  7.79 us
    dot_general x1, matrix products, shards(): joined = jnp.dot(pre_normed, qkv_full, preferred_element_type=jnp.float32)  7.61 us
    dot_general x1, matrix products, shards(): jnp.dot(heads_out, out_full, preferred_element_type=jnp.float32)  7.25 us
  transfers between devices with their start and end apart: 4, of which 3 were waited for; matrix products, arithmetic and copies ran while one was open for 19% of the time, Pallas kernels for 4%

profile of v10, /device:TPU:0, one launch (start us, length us, event | category | flops | bytes accessed | tf_op | source)
XLA Modules:
  0.0 268.5 jit_solution(4847516974456794680)
XLA Ops:
  6.5 0.0 all-gather.3.cloned.1.call-start
  6.5 0.7 all-gather.3.cloned.1.call-update
  7.3 2.0 copy.73
  9.2 0.0 copy-start.2
  9.3 42.9 %all_to_all.24 = bf16[9,2,16,16,256]{4,2,1,0,3:T(8,128)(2,1)S(1)} all-to-all(bf16[9,2,16,16,256]{4,2,1,0,3:T(8,128)(2,1)S(1)} %bitcast.54), channel_id=1, replica_groups=mesh['tok'=8,'head'=16] {'head'}, dimensions={3} | all-to-all | bytes 4718592 | tf_op jit(solution)/shard_map/all_to_all | solution.py:144
  52.2 0.0 copy-done.2
  52.2 3.0 %broadcast_in_dim.36 = bf16[8,512,768]{2,1,0:T(8,128)(2,1)} broadcast(bf16[512,768]{1,0:T(8,128)(2,1)S(1)} %copy-done.2), dimensions={1,2} | broadcast | bytes 7077888 | tf_op jit(solution)/shard_map/broadcast_in_dim | solution.py:150
  55.3 0.0 copy-start.15
  55.3 0.0 copy-start.5
  55.3 0.0 copy-start.4
  55.3 0.0 copy-start.8
  55.3 7.8 %all-to-all-start.1 = ((bf16[8,512,768]{2,1,0:T(8,128)(2,1)}), bf16[8,512,768]{2,1,0:T(8,128)(2,1)}, u32[]{:S(2)}, u32[]{:S(2)}) async-start(bf16[8,512,768]{2,1,0:T(8,128)(2,1)} %broadcast_in_dim.36), calls=%async_computation.1 | async-start | bytes 12582912 | tf_op jit(solution)/shard_map/all_to_all | solution.py:153
  63.1 0.0 all-gather.5.cloned.1.call-start
  63.1 0.7 all-gather.5.cloned.1.call-update
  63.8 0.0 reduce-scatter.2.cloned.1.call-start
  63.9 0.0 copy-done.15
  63.9 0.1 eq.33
  63.9 0.1 reshape.242
  64.0 0.0 copy-done.5
  64.0 0.1 convert_reduce_fusion.1
  64.2 0.2 reduce-window.8
  64.3 0.0 copy-done.4
  64.3 0.1 select_reduce_fusion.1
  64.4 0.1 copy.63
  64.6 0.1 copy.64
  64.8 0.9 copy.65.req_col
  65.6 0.1 broadcast_bitcast_fusion
  65.7 0.6 copy.71
  66.3 0.7 sub.69.pos_col
  67.1 0.0 copy-done.8
  67.1 0.1 compare_reduce_fusion
  67.2 0.1 fusion.70
  67.3 0.6 add_subtract_fusion.pos_row
  67.9 0.6 and_select_fusion.owner_row
  68.5 0.2 multiply_cosine_fusion
  68.7 2.0 gather_fusion
  70.7 0.0 copy-done.3
  70.7 6.0 %all-gather.3.cloned.1.call-done = bf16[512,4096]{1,0:T(8,128)(2,1)} async-done(((bf16[512,256]{1,0:T(8,128)(2,1)}), bf16[512,4096]{1,0:T(8,128)(2,1)}) %all-gather.3.cloned.1.call-update) | async-done | bytes 4194320 | tf_op jit(solution)/shard_map/all_gather | solution.py:176
  76.6 3.0 %convert_reduce_fusion = f32[512]{0:T(512)S(1)} fusion(bf16[512,4096]{1,0:T(8,128)(2,1)} %all-gather.3.cloned.1.call-done), kind=kLoop, calls=%fused_computation.2 | loop fusion | flops 4193792 | bytes 4196352 | tf_op jit(solution)/shard_map/reduce_sum | solution.py:16
  79.6 0.5 copy-done
  80.1 1.2 fusion.8
  81.3 63.9 %all-to-all-done.1 = bf16[8,512,768]{2,1,0:T(8,128)(2,1)} async-done(((bf16[8,512,768]{2,1,0:T(8,128)(2,1)}), bf16[8,512,768]{2,1,0:T(8,128)(2,1)}, u32[]{:S(2)}, u32[]{:S(2)}) %all-to-all-start.1) | async-done | bytes 6291488 | tf_op jit(solution)/shard_map/all_to_all | solution.py:153
  145.3 0.0 copy-done.9
  145.3 0.0 copy-done.10
  145.3 0.0 copy-done.13
  145.3 7.6 %fusion.36 = f32[512,768]{1,0:T(8,128)S(1)} fusion(bf16[4096,768]{1,0:T(8,128)(2,1)} %bitcast.3, bf16[512,4096]{1,0:T(8,128)(2,1)} %all-gather.3.cloned.1.call-done, f32[4096]{0:T(1024)S(1)} %copy-done.9, f32[4096]{0:T(1024)S(1)} %copy-done.10, f32[512]{0:T(512)S(1)} %add_rsqrt_fusion, f32[512]{0:T(512)S(1)} %broadcast_multiply_fusion, f32[768]{0:T(1024)S(1)} %copy-done.13), kind=kOutput, calls=%fused_computation.44 | convolution fusion | flops 3234201600 | bytes 12098560 | tf_op jit(solution)/shard_map/dot_general | solution.py:194
  152.9 0.5 copy.58
  153.4 0.1 slice_bitcast_fusion
  153.7 0.8 copy.66.q_ref
  154.5 0.8 copy.67.kn_ref
  155.3 0.9 copy.68.vn_ref
  156.2 10.3 %shard_map.172 = bf16[512,256]{1,0:T(8,128)(2,1)} custom-call(bf16[512,256]{1,0:T(8,128)(2,1)} %copy.66.q_ref, bf16[128,2,16,256]{3,2,1,0:T(8,128)(2,1)} %gather_fusion, bf16[128,2,16,256]{3,2,1,0:T(8,128)(2,1)} %gather_fusion, bf16[512,256]{1,0:T(8,128)(2,1)} %copy.67.kn_ref, bf16[512,256]{1,0:T(8,128)(2,1)} %copy.68.vn_ref, s32[512,1]{1,0:T(8,128)} %copy.65.req_col, ...), custom_call_target="tpu_custom_call" | custom-call | flops 1342177280 | bytes 3145728 | tf_op jit(solution)/shard_map/pallas_call | solution.py:124
  166.5 0.0 copy-done.11
  166.5 0.0 copy-done.12
  166.5 0.0 copy-done.14
  166.5 0.0 copy-start.1
  166.5 23.5 %fusion.34 = f32[512,4096]{1,0:T(8,128)} fusion(bf16[1024,4096]{1,0:T(8,128)(2,1)} %param.29, bf16[4096,1024]{1,0:T(8,128)(2,1)} %param.27, bf16[512,4096]{1,0:T(8,128)(2,1)} %all-gather.3.cloned.1.call-done, f32[4096]{0:T(1024)S(1)} %copy-done.11, f32[4096]{0:T(1024)S(1)} %copy-done.12, f32[512]{0:T(512)S(1)} %add_rsqrt_fusion, ...), kind=kOutput, calls=%fused_computation.43 | convolution fusion | flops 8637120512 | bytes 29401088 | tf_op jit(solution)/shard_map/dot_general | solution.py:191
  190.1 0.0 copy-done.1
  190.1 7.3 %add_convert_fusion = bf16[512,4096]{1,0:T(8,128)(2,1)} fusion(f32[512,4096]{1,0:T(8,128)} %fusion.34, bf16[512,256]{1,0:T(8,128)(2,1)S(1)} %copy-done.1, bf16[256,4096]{1,0:T(8,128)(2,1)} %all-gather.5.cloned.1.call-done), kind=kOutput, calls=%fused_computation.12 | convolution fusion | flops 1077936128 | bytes 14942208 | tf_op jit(solution)/shard_map/dot_general | solution.py:211
  197.3 0.0 reduce-scatter.2.cloned.1.call-update
  197.4 62.9 %reduce-scatter.2.cloned.1.call-done = bf16[512,256]{1,0:T(8,128)(2,1)} async-done(((bf16[512,4096]{1,0:T(8,128)(2,1)}), bf16[512,256]{1,0:T(8,128)(2,1)}) %reduce-scatter.2.cloned.1.call-update) | async-done | bytes 262160 | tf_op jit(solution)/shard_map/reduce_scatter | solution.py:212
  260.3 0.0 copy-done.6
  260.3 0.0 copy-done.7
  260.3 1.7 add_convert_fusion.1
  (26 shorter events, 0.2 us)
Async XLA Ops:
  6.5 70.1 %all-gather.3.cloned.1.call-start = ((), (), s32[]{:S(2)}) async-start(), calls=%async_computation.3 | async-start | bytes 4456448 | tf_op jit(solution)/shard_map/all_gather | solution.py:176
  9.2 43.0 %copy-start.2 = (bf16[512,768]{1,0:T(8,128)(2,1)S(1)}, bf16[512,768]{1,0:T(8,128)(2,1)}, u32[]{:S(2)}) copy-start(bf16[512,768]{1,0:T(8,128)(2,1)} %param.23) | copy-start | bytes 2359300
  55.3 8.6 %copy-start.15 = (s32[2,64]{1,0:T(2,128)S(1)}, s32[2,64]{1,0:T(2,128)}, u32[]{:S(2)}) copy-start(s32[2,64]{1,0:T(2,128)} %param.34) | copy-start | bytes 1540
  55.3 8.8 %copy-start.5 = (s32[512]{0:T(512)S(1)}, s32[512]{0:T(512)}, u32[]{:S(2)}) copy-start(s32[512]{0:T(512)} %param.32) | copy-start | bytes 6148
  55.3 9.1 %copy-start.4 = (s32[2]{0:T(128)S(1)}, s32[2]{0:T(128)}, u32[]{:S(2)}) copy-start(s32[2]{0:T(128)} %param.33) | copy-start | bytes 28
  55.3 11.8 %copy-start.8 = (s32[8,2]{0,1:T(2,128)S(1)}, s32[8,2]{0,1:T(2,128)}, u32[]{:S(2)}) copy-start(s32[8,2]{0,1:T(2,128)} %param.35) | copy-start | bytes 196
  55.3 90.0 %all-to-all-start.1 = ((bf16[8,512,768]{2,1,0:T(8,128)(2,1)}), bf16[8,512,768]{2,1,0:T(8,128)(2,1)}, u32[]{:S(2)}, u32[]{:S(2)}) async-start(bf16[8,512,768]{2,1,0:T(8,128)(2,1)} %broadcast_in_dim.36), calls=%async_computation.1 | async-start | bytes 12582912 | tf_op jit(solution)/shard_map/all_to_all | solution.py:153
  63.1 127.0 %all-gather.5.cloned.1.call-start = ((), (), s32[]{:S(2)}) async-start(), calls=%async_computation.4 | async-start | bytes 2359296 | tf_op jit(solution)/shard_map/all_gather | solution.py:180
  63.8 196.5 %reduce-scatter.2.cloned.1.call-start = ((), (), s32[]{:S(2)}) async-start(), calls=%async_computation.5 | async-start | bytes 4456448 | tf_op jit(solution)/shard_map/reduce_scatter | solution.py:212
  64.0 6.6 %copy-start.3 = (s32[512]{0:T(512)}, s32[512]{0:T(512)S(1)}, u32[]{:S(2)}) copy-start(s32[512]{0:T(512)S(1)} %broadcast_subtract_fusion) | copy-start | bytes 6148
  76.6 3.4 %copy-start = (bf16[512,4096]{1,0:T(8,128)(2,1)S(1)}, bf16[512,4096]{1,0:T(8,128)(2,1)}, u32[]{:S(2)}) copy-start(bf16[512,4096]{1,0:T(8,128)(2,1)} %all-gather.3.cloned.1.call-done) | copy-start | bytes 12582916
  80.1 65.2 %copy-start.9 = (f32[4096]{0:T(1024)S(1)}, f32[4096]{0:T(1024)}, u32[]{:S(2)}) copy-start(f32[4096]{0:T(1024)} %param.20) | copy-start | bytes 49156
  80.1 65.2 %copy-start.10 = (f32[4096]{0:T(1024)S(1)}, f32[4096]{0:T(1024)}, u32[]{:S(2)}) copy-start(f32[4096]{0:T(1024)} %param.19) | copy-start | bytes 49156
  80.1 65.2 %copy-start.13 = (f32[768]{0:T(1024)S(1)}, f32[768]{0:T(1024)}, u32[]{:S(2)}) copy-start(f32[768]{0:T(1024)} %param.24) | copy-start | bytes 9220
  156.2 10.3 %copy-start.11 = (f32[4096]{0:T(1024)S(1)}, f32[4096]{0:T(1024)}, u32[]{:S(2)}) copy-start(f32[4096]{0:T(1024)} %param.22) | copy-start | bytes 49156
  156.2 10.3 %copy-start.12 = (f32[4096]{0:T(1024)S(1)}, f32[4096]{0:T(1024)}, u32[]{:S(2)}) copy-start(f32[4096]{0:T(1024)} %param.21) | copy-start | bytes 49156
  156.2 10.3 %copy-start.14 = (f32[1024]{0:T(1024)S(1)}, f32[1024]{0:T(1024)}, u32[]{:S(2)}) copy-start(f32[1024]{0:T(1024)} %param.28) | copy-start | bytes 12292
  166.5 23.5 %copy-start.1 = (bf16[512,256]{1,0:T(8,128)(2,1)S(1)}, bf16[512,256]{1,0:T(8,128)(2,1)}, u32[]{:S(2)}) copy-start(bf16[512,256]{1,0:T(8,128)(2,1)} %shard_map.172) | copy-start | bytes 786436
  197.3 63.0 %copy-start.6 = (f32[256]{0:T(256)S(1)}, f32[256]{0:T(256)}, u32[]{:S(2)}) copy-start(f32[256]{0:T(256)} %param.30) | copy-start | bytes 3076
  197.3 63.0 %copy-start.7 = (f32[256]{0:T(256)S(1)}, f32[256]{0:T(256)}, u32[]{:S(2)}) copy-start(f32[256]{0:T(256)} %param.26) | copy-start | bytes 3076
Sparse Core Ops, SparseCore 0:
  9.0 67.6 all-gather.2
  78.8 92.8 all-gather.4
  197.5 62.7 reduce-scatter.1

commit v11 on v9

--- a/solution.py
+++ b/solution.py
@@ -70,9 +70,7 @@
     ).astype(jnp.bfloat16)
 
 
-def attention_kernel(
-    q_ref, kc_ref, vc_ref, kn_ref, vn_ref, req_col, pos_col, owner_row, limit_row, req_row, pos_row, o_ref
-):
+def attention_kernel(q_ref, kc_ref, vc_ref, kn_ref, vn_ref, lo_col, hi_col, start_col, o_ref):
     queries = q_ref[...]
     cache_keys = kc_ref[...].reshape(-1, queries.shape[1])
     cache_values = vc_ref[...].reshape(-1, queries.shape[1])
@@ -80,11 +78,11 @@
     scale = HD ** (-0.5)
     cache_scores = lax.dot_general(queries, cache_keys, dims, preferred_element_type=jnp.float32) * scale
     new_scores = lax.dot_general(queries, kn_ref[...], dims, preferred_element_type=jnp.float32) * scale
-    cache_place = lax.broadcasted_iota(jnp.int32, cache_scores.shape, 1) % (
-        cache_scores.shape[1] // 2
-    )
-    cache_ok = (req_col[...] == owner_row[...]) & (cache_place < limit_row[...])
-    new_ok = (req_col[...] == req_row[...]) & (pos_row[...] <= pos_col[...])
+    cache_slot = lax.broadcasted_iota(jnp.int32, cache_scores.shape, 1)
+    cache_ok = (cache_slot >= lo_col[...]) & (cache_slot < hi_col[...])
+    new_slot = lax.broadcasted_iota(jnp.int32, new_scores.shape, 1)
+    own_slot = lax.broadcasted_iota(jnp.int32, new_scores.shape, 0)
+    new_ok = (new_slot >= start_col[...]) & (new_slot <= own_slot)
     cache_scores = jnp.where(cache_ok, cache_scores, -1e30)
     new_scores = jnp.where(new_ok, new_scores, -1e30)
     peak = jnp.maximum(
@@ -105,21 +103,15 @@
     tokens, heads = queries.shape[0], queries.shape[1]
     page_count, page_len = pages.shape[0], pages.shape[2]
     span = page_count * page_len // cached.shape[0]
-    key_slot = jnp.arange(page_count * page_len, dtype=jnp.int32)
-    owner_row = (key_slot // span)[None, :]
-    limit_row = jnp.repeat(cached, span)[None, :]
+    own_cached = jnp.take(cached, local_req)
+    lo_col = (local_req * span)[:, None]
+    hi_col = lo_col + own_cached[:, None]
+    start_col = (jnp.arange(tokens, dtype=jnp.int32) - positions + own_cached)[:, None]
     flat = lambda x: x.reshape(tokens, heads * HD)
     row_block = pl.BlockSpec((tokens, HD), lambda h: (0, h))
     page_block = lambda part: pl.BlockSpec((page_count, 1, page_len, HD), lambda h: (0, part, 0, h))
     whole = lambda x: pl.BlockSpec(x.shape, lambda h: (0,) * x.ndim)
-    extras = (
-        local_req[:, None],
-        positions[:, None],
-        owner_row,
-        limit_row,
-        local_req[None, :],
-        positions[None, :],
-    )
+    extras = (lo_col, hi_col, start_col)
     keys_seen = page_count * page_len + tokens
     out = pl.pallas_call(
         attention_kernel,
@@ -209,10 +201,18 @@
         queries, new_keys, new_values, pages, local_req, cached_len, positions
     )
     attention_part = jnp.dot(heads_out, out_full, preferred_element_type=jnp.float32)
-    summed = lax.psum_scatter(
-        (attention_part + feed_part).astype(jnp.bfloat16), "head", scatter_dimension=1, tiled=True
-    ).astype(jnp.float32)
-    return (summed + out_bias + down_bias).astype(jnp.bfloat16)
+    bias_row = lax.dynamic_update_slice_in_dim(
+        jnp.zeros((attention_part.shape[1],), jnp.float32),
+        out_bias + down_bias,
+        lax.axis_index("head") * out_bias.shape[0],
+        axis=0,
+    )
+    return lax.psum_scatter(
+        (attention_part + feed_part + bias_row).astype(jnp.bfloat16),
+        "head",
+        scatter_dimension=1,
+        tiled=True,
+    )
 
 
 def solution(mesh):

time: 248 us -> 247 us (level)
    add x1 -> x2, other arithmetic: 0.01 us -> 2.54 us  [the longest x1 1.27 us: attend_kernel(): jnp.arange(tokens, dtype=jnp.int32) - positions + own_cached]
    all_gather x1, waiting for transfers between devices: 39.9 us -> 37.4 us  [shards(): gathered = lax.all_gather(states, 'head', axis=1, tiled=True)]
  transfers between devices with their start and end apart: 5 -> 5, of which waited for: 4 -> 4; matrix products, arithmetic and copies ran while one was open for 23% -> 24% of each run, Pallas kernels for 4% -> 4%
where the time goes in v11:
time: 247 us; the launch traced here: 246 us
  waiting for transfers between devices  142 us (57%)
  matrix products  40.4 us (16%)
  local copies, waits for them, and re-layouts  19.9 us (8%)
  between operations  13.3 us (5%)
  starting transfers between devices  12.6 us (5%)
  Pallas kernels  10.4 us (4%)
  other arithmetic  7.74 us (3%)
    reduce_scatter x1, waiting for transfers between devices, shards(): lax.psum_scatter((attention_part + feed_part + bias_row).astype(jnp.bfloa...  65.7 us
    all_gather x1, waiting for transfers between devices, shards(): gathered = lax.all_gather(states, 'head', axis=1, tiled=True)  37.4 us
    dot_general x1, matrix products, feed(): return jnp.dot(hidden, down_weight, preferred_element_type=jnp.float32)  23.8 us
    all_to_all x1, waiting for transfers between devices, gather_by_all_to_all(): return lax.all_to_all(copies, axis, split_axis=0, concat_axis=0, tiled=True)  20.8 us
    all_to_all x1, waiting for transfers between devices, share_pages(): lax.all_to_all(grouped, 'head', split_axis=3, concat_axis=0, tiled=True)  16.6 us
    pallas_call x1, Pallas kernels, attend_kernel(): pl.pallas_call(attention_kernel, grid=(heads,), in_specs=[row_block, page...  10.4 us
    dot_general x1, matrix products, shards(): joined = jnp.dot(pre_normed, qkv_full, preferred_element_type=jnp.float32)  9.19 us
    all_to_all x1, starting transfers between devices, gather_by_all_to_all(): return lax.all_to_all(copies, axis, split_axis=0, concat_axis=0, tiled=True)  8.17 us
  transfers between devices with their start and end apart: 5, of which 4 were waited for; matrix products, arithmetic and copies ran while one was open for 24% of the time, Pallas kernels for 4%

profile of v11, /device:TPU:0, one launch (start us, length us, event | category | flops | bytes accessed | tf_op | source)
XLA Modules:
  0.0 246.3 jit_solution(11209086175559573247)
XLA Ops:
  6.5 0.0 all-gather.3.cloned.1.call-start
  6.5 0.7 all-gather.3.cloned.1.call-update
  7.3 4.1 %broadcast_in_dim.38 = bf16[8,512,768]{2,1,0:T(8,128)(2,1)} broadcast(bf16[512,768]{1,0:T(8,128)(2,1)} %param.23), dimensions={1,2} | broadcast | bytes 7077888 | tf_op jit(solution)/shard_map/broadcast_in_dim | solution.py:142
  11.4 0.0 copy-start.13
  11.4 0.0 copy-start.3
  11.4 0.0 copy-start.2
  11.4 0.0 copy-start.6
  11.4 8.2 %all-to-all-start = ((bf16[8,512,768]{2,1,0:T(8,128)(2,1)}), bf16[8,512,768]{2,1,0:T(8,128)(2,1)}, u32[]{:S(2)}, u32[]{:S(2)}) async-start(bf16[8,512,768]{2,1,0:T(8,128)(2,1)} %broadcast_in_dim.38), calls=%async_computation | async-start | bytes 12582912 | tf_op jit(solution)/shard_map/all_to_all | solution.py:145
  19.5 0.0 all-gather.5.cloned.1.call-start
  19.6 0.7 all-gather.5.cloned.1.call-update
  20.3 0.0 copy-done.13
  20.3 0.1 eq.33
  20.4 0.1 reshape.193
  20.5 0.0 copy-done.3
  20.5 0.1 convert_reduce_fusion.1
  20.6 0.2 reduce-window.8
  20.8 0.0 copy-done.2
  20.8 0.6 fusion.107
  21.4 0.1 select_reduce_fusion.1
  21.5 1.3 fusion.71
  22.8 1.3 fusion.72
  24.1 0.9 copy.55.hi_col
  25.0 0.9 copy.56.start_col
  25.8 0.9 copy.54.lo_col
  26.7 0.0 copy-done.6
  26.7 0.1 compare_reduce_fusion
  26.8 0.1 fusion.70
  26.9 37.4 %all-gather.3.cloned.1.call-done = bf16[512,4096]{1,0:T(8,128)(2,1)} async-done(((bf16[512,256]{1,0:T(8,128)(2,1)}), bf16[512,4096]{1,0:T(8,128)(2,1)}) %all-gather.3.cloned.1.call-update) | async-done | bytes 4194320 | tf_op jit(solution)/shard_map/all_gather | solution.py:168
  64.3 0.0 copy-start
  64.3 3.0 %convert_reduce_fusion = f32[512]{0:T(512)S(1)} fusion(bf16[512,4096]{1,0:T(8,128)(2,1)} %all-gather.3.cloned.1.call-done), kind=kLoop, calls=%fused_computation.2 | loop fusion | flops 4193792 | bytes 4196352 | tf_op jit(solution)/shard_map/reduce_sum | solution.py:16
  67.2 0.5 copy-done
  67.7 0.0 copy-start.7
  67.7 1.2 fusion.8
  69.0 0.0 copy-done.7
  69.0 0.0 copy-done.8
  69.0 0.0 copy-done.11
  69.0 0.0 copy-start.1
  69.0 23.8 %fusion.34 = f32[512,4096]{1,0:T(8,128)} fusion(bf16[1024,4096]{1,0:T(8,128)(2,1)} %param.29, bf16[4096,1024]{1,0:T(8,128)(2,1)} %param.27, bf16[512,4096]{1,0:T(8,128)(2,1)} %all-gather.3.cloned.1.call-done, f32[4096]{0:T(1024)S(1)} %copy-done.7, f32[4096]{0:T(1024)S(1)} %copy-done.8, f32[512]{0:T(512)S(1)} %add_rsqrt_fusion, ...), kind=kOutput, calls=%fused_computation.43 | convolution fusion | flops 8637120512 | bytes 29401088 | tf_op jit(solution)/shard_map/dot_general | solution.py:181
  92.8 0.0 copy-done.1
  92.9 1.8 copy.63
  94.7 20.8 %all-to-all-done = bf16[8,512,768]{2,1,0:T(8,128)(2,1)} async-done(((bf16[8,512,768]{2,1,0:T(8,128)(2,1)}), bf16[8,512,768]{2,1,0:T(8,128)(2,1)}, u32[]{:S(2)}, u32[]{:S(2)}) %all-to-all-start) | async-done | bytes 6291488 | tf_op jit(solution)/shard_map/all_to_all | solution.py:145
  115.5 0.0 copy-start.12
  115.5 4.4 %all-to-all-start.1 = ((bf16[9,2,16,16,256]{4,2,1,0,3:T(8,128)(2,1)}), bf16[9,2,16,16,256]{4,2,1,0,3:T(8,128)(2,1)S(1)}, u32[]{:S(2)}, u32[]{:S(2)}) async-start(bf16[9,2,16,16,256]{4,2,1,0,3:T(8,128)(2,1)} %bitcast.48), calls=%async_computation.1 | async-start | bytes 4718592 | tf_op jit(solution)/shard_map/all_to_all | solution.py:136
  119.9 0.0 reduce-scatter.2.cloned.1.call-start
  120.0 0.0 copy-done.4
  120.0 0.0 copy-done.5
  120.0 0.1 add_dynamic-update-slice_fusion
  120.1 0.2 multiply_cosine_fusion
  120.3 0.0 copy-done.9
  120.3 0.0 copy-done.10
  120.4 0.0 copy-done.12
  120.4 9.2 %fusion.36 = f32[512,768]{1,0:T(8,128)} fusion(bf16[4096,768]{1,0:T(8,128)(2,1)} %bitcast, bf16[512,4096]{1,0:T(8,128)(2,1)} %all-gather.3.cloned.1.call-done, f32[4096]{0:T(1024)S(1)} %copy-done.9, f32[4096]{0:T(1024)S(1)} %copy-done.10, f32[512]{0:T(512)S(1)} %add_rsqrt_fusion, f32[512]{0:T(512)S(1)} %broadcast_multiply_fusion.1, f32[768]{0:T(1024)S(1)} %copy-done.12), kind=kOutput, calls=%fused_computation.44 | convolution fusion | flops 3234201600 | bytes 12098560 | tf_op jit(solution)/shard_map/dot_general | solution.py:186
  129.6 3.1 %copy.48 = f32[512,768]{0,1:T(8,128)} copy(f32[512,768]{1,0:T(8,128)} %fusion.36) | data formatting | bytes 3145728 | tf_op jit(solution)/shard_map/add | solution.py:187
  132.6 1.1 slice.76
  133.7 1.3 slice_bitcast_fusion
  135.1 0.8 copy.57.q_ref
  136.0 0.8 copy.58.kn_ref
  136.8 0.8 copy.59.vn_ref
  137.7 16.6 %all-to-all-done.1 = bf16[9,2,16,16,256]{4,2,1,0,3:T(8,128)(2,1)S(1)} async-done(((bf16[9,2,16,16,256]{4,2,1,0,3:T(8,128)(2,1)}), bf16[9,2,16,16,256]{4,2,1,0,3:T(8,128)(2,1)S(1)}, u32[]{:S(2)}, u32[]{:S(2)}) %all-to-all-start.1) | async-done | bytes 2359328 | tf_op jit(solution)/shard_map/all_to_all | solution.py:136
  154.3 2.0 gather_fusion
  156.3 10.4 %shard_map.172 = bf16[512,256]{1,0:T(8,128)(2,1)} custom-call(bf16[512,256]{1,0:T(8,128)(2,1)} %copy.57.q_ref, bf16[128,2,16,256]{3,2,1,0:T(8,128)(2,1)} %gather_fusion, bf16[128,2,16,256]{3,2,1,0:T(8,128)(2,1)} %gather_fusion, bf16[512,256]{1,0:T(8,128)(2,1)} %copy.58.kn_ref, bf16[512,256]{1,0:T(8,128)(2,1)} %copy.59.vn_ref, s32[512,1]{1,0:T(8,128)} %copy.54.lo_col, ...), custom_call_target="tpu_custom_call" | custom-call | flops 1342177280 | bytes 3145728 | tf_op jit(solution)/shard_map/pallas_call | solution.py:116
  166.7 7.3 %add_convert_fusion = bf16[512,4096]{1,0:T(8,128)(2,1)} fusion(f32[512,4096]{1,0:T(8,128)} %fusion.34, bf16[512,256]{1,0:T(8,128)(2,1)} %shard_map.172, bf16[256,4096]{1,0:T(8,128)(2,1)} %all-gather.5.cloned.1.call-done, f32[4096]{0:T(1024)S(1)} %add_dynamic-update-slice_fusion), kind=kOutput, calls=%fused_computation.12 | convolution fusion | flops 1080033280 | bytes 14958592 | tf_op jit(solution)/shard_map/dot_general | solution.py:203
  174.1 0.0 reduce-scatter.2.cloned.1.call-update
  174.1 65.7 %reduce-scatter.2.cloned.1.call-done = bf16[512,256]{1,0:T(8,128)(2,1)} async-done(((bf16[512,4096]{1,0:T(8,128)(2,1)}), bf16[512,256]{1,0:T(8,128)(2,1)}) %reduce-scatter.2.cloned.1.call-update) | async-done | bytes 262160 | tf_op jit(solution)/shard_map/reduce_scatter | solution.py:210
  (20 shorter events, 0.2 us)
Async XLA Ops:
  6.5 57.7 %all-gather.3.cloned.1.call-start = ((), (), s32[]{:S(2)}) async-start(), calls=%async_computation.3 | async-start | bytes 4456448 | tf_op jit(solution)/shard_map/all_gather | solution.py:168
  11.4 8.9 %copy-start.13 = (s32[2,64]{1,0:T(2,128)S(1)}, s32[2,64]{1,0:T(2,128)}, u32[]{:S(2)}) copy-start(s32[2,64]{1,0:T(2,128)} %param.34) | copy-start | bytes 1540
  11.4 9.1 %copy-start.3 = (s32[512]{0:T(512)S(1)}, s32[512]{0:T(512)}, u32[]{:S(2)}) copy-start(s32[512]{0:T(512)} %param.32) | copy-start | bytes 6148
  11.4 9.4 %copy-start.2 = (s32[2]{0:T(128)S(1)}, s32[2]{0:T(128)}, u32[]{:S(2)}) copy-start(s32[2]{0:T(128)} %param.33) | copy-start | bytes 28
  11.4 15.3 %copy-start.6 = (s32[8,2]{0,1:T(2,128)S(1)}, s32[8,2]{0,1:T(2,128)}, u32[]{:S(2)}) copy-start(s32[8,2]{0,1:T(2,128)} %param.35) | copy-start | bytes 196
  11.4 104.1 %all-to-all-start = ((bf16[8,512,768]{2,1,0:T(8,128)(2,1)}), bf16[8,512,768]{2,1,0:T(8,128)(2,1)}, u32[]{:S(2)}, u32[]{:S(2)}) async-start(bf16[8,512,768]{2,1,0:T(8,128)(2,1)} %broadcast_in_dim.38), calls=%async_computation | async-start | bytes 12582912 | tf_op jit(solution)/shard_map/all_to_all | solution.py:145
  19.5 147.2 %all-gather.5.cloned.1.call-start = ((), (), s32[]{:S(2)}) async-start(), calls=%async_computation.4 | async-start | bytes 2359296 | tf_op jit(solution)/shard_map/all_gather | solution.py:170
  64.3 3.4 %copy-start = (bf16[512,4096]{1,0:T(8,128)(2,1)S(1)}, bf16[512,4096]{1,0:T(8,128)(2,1)}, u32[]{:S(2)}) copy-start(bf16[512,4096]{1,0:T(8,128)(2,1)} %all-gather.3.cloned.1.call-done) | copy-start | bytes 12582916
  67.7 1.2 copy-start.7
  67.7 1.2 copy-start.8
  67.7 1.3 copy-start.11
  69.0 23.9 %copy-start.1 = (bf16[9,2,16,4096]{3,2,1,0:T(8,128)(2,1)S(1)}, bf16[9,2,16,4096]{3,2,1,0:T(8,128)(2,1)}, u32[]{:S(2)}) copy-start(bf16[9,2,16,4096]{3,2,1,0:T(8,128)(2,1)} %param.31) | copy-start | bytes 7077892
  115.5 4.5 %copy-start.4 = (f32[256]{0:T(256)S(1)}, f32[256]{0:T(256)}, u32[]{:S(2)}) copy-start(f32[256]{0:T(256)} %param.26) | copy-start | bytes 3076
  115.5 4.5 %copy-start.5 = (f32[256]{0:T(256)S(1)}, f32[256]{0:T(256)}, u32[]{:S(2)}) copy-start(f32[256]{0:T(256)} %param.30) | copy-start | bytes 3076
  115.5 4.8 %copy-start.9 = (f32[4096]{0:T(1024)S(1)}, f32[4096]{0:T(1024)}, u32[]{:S(2)}) copy-start(f32[4096]{0:T(1024)} %param.20) | copy-start | bytes 49156
  115.5 4.8 %copy-start.10 = (f32[4096]{0:T(1024)S(1)}, f32[4096]{0:T(1024)}, u32[]{:S(2)}) copy-start(f32[4096]{0:T(1024)} %param.19) | copy-start | bytes 49156
  115.5 4.8 %copy-start.12 = (f32[768]{0:T(1024)S(1)}, f32[768]{0:T(1024)}, u32[]{:S(2)}) copy-start(f32[768]{0:T(1024)} %param.24) | copy-start | bytes 9220
  115.5 38.7 %all-to-all-start.1 = ((bf16[9,2,16,16,256]{4,2,1,0,3:T(8,128)(2,1)}), bf16[9,2,16,16,256]{4,2,1,0,3:T(8,128)(2,1)S(1)}, u32[]{:S(2)}, u32[]{:S(2)}) async-start(bf16[9,2,16,16,256]{4,2,1,0,3:T(8,128)(2,1)} %bitcast.48), calls=%async_computation.1 | async-start | bytes 4718592 | tf_op jit(solution)/shard_map/all_to_all | solution.py:136
  119.9 119.8 %reduce-scatter.2.cloned.1.call-start = ((), (), s32[]{:S(2)}) async-start(), calls=%async_computation.5 | async-start | bytes 4456448 | tf_op jit(solution)/shard_map/reduce_scatter | solution.py:210
Sparse Core Ops, SparseCore 0:
  9.0 55.2 all-gather.2
  66.5 97.6 all-gather.4
  174.2 65.5 reduce-scatter.1

commit v12 on v11

--- a/solution.py
+++ b/solution.py
@@ -91,8 +91,9 @@
     cache_exp = jnp.exp(cache_scores - peak)
     new_exp = jnp.exp(new_scores - peak)
     total = jnp.sum(cache_exp, axis=1, keepdims=True) + jnp.sum(new_exp, axis=1, keepdims=True)
-    cache_probs = (cache_exp / total).astype(jnp.bfloat16)
-    new_probs = (new_exp / total).astype(jnp.bfloat16)
+    inverse = 1.0 / total
+    cache_probs = (cache_exp * inverse).astype(jnp.bfloat16)
+    new_probs = (new_exp * inverse).astype(jnp.bfloat16)
     mixed = jnp.dot(cache_probs, cache_values, preferred_element_type=jnp.float32) + jnp.dot(
         new_probs, vn_ref[...], preferred_element_type=jnp.float32
     )
@@ -129,6 +130,33 @@
     return out
 
 
+def project_kernel(heads_ref, weight_ref, feed_ref, bias_ref, o_ref):
+    product = jnp.dot(heads_ref[...], weight_ref[...], preferred_element_type=jnp.float32)
+    o_ref[...] = (product + feed_ref[...] + bias_ref[...]).astype(o_ref.dtype)
+
+
+def project_and_add(heads_out, weight, feed_part, bias_row):
+    tokens, width = feed_part.shape
+    tile = 512
+    return pl.pallas_call(
+        project_kernel,
+        grid=(width // tile,),
+        in_specs=[
+            pl.BlockSpec(heads_out.shape, lambda j: (0, 0)),
+            pl.BlockSpec((weight.shape[0], tile), lambda j: (0, j)),
+            pl.BlockSpec((tokens, tile), lambda j: (0, j)),
+            pl.BlockSpec((1, tile), lambda j: (0, j)),
+        ],
+        out_specs=pl.BlockSpec((tokens, tile), lambda j: (0, j)),
+        out_shape=jax.ShapeDtypeStruct((tokens, width), jnp.bfloat16),
+        cost_estimate=pl.CostEstimate(
+            flops=2 * tokens * heads_out.shape[1] * width,
+            transcendentals=0,
+            bytes_accessed=2 * heads_out.size + 2 * weight.size + 4 * feed_part.size + 2 * tokens * width,
+        ),
+    )(heads_out, weight, feed_part, bias_row[None, :])
+
+
 def share_pages(local_pool, groups):
     grouped = local_pool.reshape(
         local_pool.shape[0], 2, local_pool.shape[2], groups, local_pool.shape[3] // groups
@@ -200,15 +228,14 @@
     heads_out = attend_kernel(
         queries, new_keys, new_values, pages, local_req, cached_len, positions
     )
-    attention_part = jnp.dot(heads_out, out_full, preferred_element_type=jnp.float32)
     bias_row = lax.dynamic_update_slice_in_dim(
-        jnp.zeros((attention_part.shape[1],), jnp.float32),
+        jnp.zeros((out_full.shape[1],), jnp.float32),
         out_bias + down_bias,
         lax.axis_index("head") * out_bias.shape[0],
         axis=0,
     )
     return lax.psum_scatter(
-        (attention_part + feed_part + bias_row).astype(jnp.bfloat16),
+        project_and_add(heads_out, out_full, feed_part, bias_row),
         "head",
         scatter_dimension=1,
         tiled=True,

time: 247 us -> 249 us (level)
  Pallas kernels: 10.4 us -> 19.6 us
  matrix products: 40.4 us -> 33 us
    pallas_call x0 -> x1, Pallas kernels: none -> 9.16 us  [project_and_add(): pl.pallas_call(project_kernel, grid=(width // tile,), in_specs=[pl.BlockS...]
    dot_general x1 -> x0, matrix products: 7.34 us -> none  [shards(): jnp.dot(heads_out, out_full, preferred_element_type=jnp.float32)]
where the time goes in v12:
time: 249 us; the launch traced here: 248 us
  waiting for transfers between devices  142 us (57%)
  matrix products  33 us (13%)
  local copies, waits for them, and re-layouts  19.9 us (8%)
  Pallas kernels  19.6 us (8%)
  between operations  13.3 us (5%)
  starting transfers between devices  12.6 us (5%)
  other arithmetic  7.76 us (3%)
    reduce_scatter x1, waiting for transfers between devices, shards(): lax.psum_scatter(project_and_add(heads_out, out_full, feed_part, bias_row...  65.8 us
    all_gather x1, waiting for transfers between devices, shards(): gathered = lax.all_gather(states, 'head', axis=1, tiled=True)  37.1 us
    dot_general x1, matrix products, feed(): return jnp.dot(hidden, down_weight, preferred_element_type=jnp.float32)  23.8 us
    all_to_all x1, waiting for transfers between devices, gather_by_all_to_all(): return lax.all_to_all(copies, axis, split_axis=0, concat_axis=0, tiled=True)  21 us
    all_to_all x1, waiting for transfers between devices, share_pages(): lax.all_to_all(grouped, 'head', split_axis=3, concat_axis=0, tiled=True)  16.7 us
    pallas_call x1, Pallas kernels, attend_kernel(): pl.pallas_call(attention_kernel, grid=(heads,), in_specs=[row_block, page...  10.4 us
    dot_general x1, matrix products, shards(): joined = jnp.dot(pre_normed, qkv_full, preferred_element_type=jnp.float32)  9.2 us
    pallas_call x1, Pallas kernels, project_and_add(): pl.pallas_call(project_kernel, grid=(width // tile,), in_specs=[pl.BlockS...  9.16 us
  transfers between devices with their start and end apart: 5, of which 4 were waited for; matrix products, arithmetic and copies ran while one was open for 24% of the time, Pallas kernels for 4%

profile of v12, /device:TPU:0, one launch (start us, length us, event | category | flops | bytes accessed | tf_op | source)
XLA Modules:
  0.0 248.2 jit_solution(8032821322948170097)
XLA Ops:
  6.5 0.0 all-gather.3.cloned.1.call-start
  6.5 0.7 all-gather.3.cloned.1.call-update
  7.3 4.1 %broadcast_in_dim.48 = bf16[8,512,768]{2,1,0:T(8,128)(2,1)} broadcast(bf16[512,768]{1,0:T(8,128)(2,1)} %param.23), dimensions={1,2} | broadcast | bytes 7077888 | tf_op jit(solution)/shard_map/broadcast_in_dim | solution.py:170
  11.4 0.0 copy-start.4
  11.4 0.0 copy-start.14
  11.4 0.0 copy-start.5
  11.4 0.0 copy-start.6
  11.4 0.0 copy-start.7
  11.4 8.2 %all-to-all-start = ((bf16[8,512,768]{2,1,0:T(8,128)(2,1)}), bf16[8,512,768]{2,1,0:T(8,128)(2,1)}, u32[]{:S(2)}, u32[]{:S(2)}) async-start(bf16[8,512,768]{2,1,0:T(8,128)(2,1)} %broadcast_in_dim.48), calls=%async_computation | async-start | bytes 12582912 | tf_op jit(solution)/shard_map/all_to_all | solution.py:173
  19.6 0.0 all-gather.5.cloned.1.call-start
  19.6 0.7 all-gather.5.cloned.1.call-update
  20.3 0.0 copy-done.3
  20.3 0.7 fusion.107
  21.0 0.0 copy-done.4
  21.0 0.1 convert_reduce_fusion.1
  21.1 0.2 reduce-window.8
  21.3 0.1 select_reduce_fusion.1
  21.4 1.3 fusion.71
  22.8 0.0 copy-done.14
  22.8 0.1 reshape.190
  22.8 0.1 eq.33
  22.9 0.9 copy.54.lo_col
  23.8 1.3 fusion.72
  25.1 0.9 copy.55.hi_col
  26.0 0.9 copy.56.start_col
  26.9 0.0 copy-done.5
  26.9 0.0 copy-done.6
  26.9 0.0 copy-done.7
  26.9 0.0 copy-start.2
  27.0 0.1 compare_reduce_fusion
  27.0 0.1 fusion.70
  27.1 37.1 %all-gather.3.cloned.1.call-done = bf16[512,4096]{1,0:T(8,128)(2,1)} async-done(((bf16[512,256]{1,0:T(8,128)(2,1)}), bf16[512,4096]{1,0:T(8,128)(2,1)}) %all-gather.3.cloned.1.call-update) | async-done | bytes 4194320 | tf_op jit(solution)/shard_map/all_gather | solution.py:196
  64.2 0.0 copy-start
  64.2 3.0 %convert_reduce_fusion = f32[512]{0:T(512)S(1)} fusion(bf16[512,4096]{1,0:T(8,128)(2,1)} %all-gather.3.cloned.1.call-done), kind=kLoop, calls=%fused_computation.2 | loop fusion | flops 4193792 | bytes 4196352 | tf_op jit(solution)/shard_map/reduce_sum | solution.py:16
  67.2 0.0 copy-done.2
  67.2 0.5 copy-done
  67.7 1.2 fusion.8
  68.9 0.0 copy-done.8
  68.9 0.0 copy-done.9
  68.9 0.0 copy-done.12
  68.9 0.0 copy-start.1
  68.9 23.8 %fusion.34.feed_ref = f32[512,4096]{1,0:T(8,128)} fusion(bf16[1024,4096]{1,0:T(8,128)(2,1)} %param.29, bf16[4096,1024]{1,0:T(8,128)(2,1)} %param.27, bf16[512,4096]{1,0:T(8,128)(2,1)} %all-gather.3.cloned.1.call-done, f32[4096]{0:T(1024)S(1)} %copy-done.8, f32[4096]{0:T(1024)S(1)} %copy-done.9, f32[512]{0:T(512)S(1)} %add_rsqrt_fusion, ...), kind=kOutput, calls=%fused_computation.42 | convolution fusion | flops 8637120512 | bytes 29401088 | tf_op jit(solution)/shard_map/dot_general | solution.py:209
  92.8 0.0 copy-done.1
  92.8 1.8 copy.63
  94.6 21.0 %all-to-all-done = bf16[8,512,768]{2,1,0:T(8,128)(2,1)} async-done(((bf16[8,512,768]{2,1,0:T(8,128)(2,1)}), bf16[8,512,768]{2,1,0:T(8,128)(2,1)}, u32[]{:S(2)}, u32[]{:S(2)}) %all-to-all-start) | async-done | bytes 6291488 | tf_op jit(solution)/shard_map/all_to_all | solution.py:173
  115.5 4.4 %all-to-all-start.1 = ((bf16[9,2,16,16,256]{4,2,1,0,3:T(8,128)(2,1)}), bf16[9,2,16,16,256]{4,2,1,0,3:T(8,128)(2,1)S(1)}, u32[]{:S(2)}, u32[]{:S(2)}) async-start(bf16[9,2,16,16,256]{4,2,1,0,3:T(8,128)(2,1)} %bitcast.47), calls=%async_computation.1 | async-start | bytes 4718592 | tf_op jit(solution)/shard_map/all_to_all | solution.py:164
  119.9 0.0 reduce-scatter.2.cloned.1.call-start
  120.0 0.2 multiply_cosine_fusion
  120.2 0.0 copy-done.10
  120.2 0.0 copy-done.11
  120.2 0.0 copy-done.13
  120.2 9.2 %fusion.36 = f32[512,768]{1,0:T(8,128)} fusion(bf16[4096,768]{1,0:T(8,128)(2,1)} %bitcast, bf16[512,4096]{1,0:T(8,128)(2,1)} %all-gather.3.cloned.1.call-done, f32[4096]{0:T(1024)S(1)} %copy-done.10, f32[4096]{0:T(1024)S(1)} %copy-done.11, f32[512]{0:T(512)S(1)} %add_rsqrt_fusion, f32[512]{0:T(512)S(1)} %broadcast_multiply_fusion.1, f32[768]{0:T(1024)S(1)} %copy-done.13), kind=kOutput, calls=%fused_computation.43 | convolution fusion | flops 3234201600 | bytes 12098560 | tf_op jit(solution)/shard_map/dot_general | solution.py:214
  129.4 3.1 %copy.48 = f32[512,768]{0,1:T(8,128)} copy(f32[512,768]{1,0:T(8,128)} %fusion.36) | data formatting | bytes 3145728 | tf_op jit(solution)/shard_map/add | solution.py:215
  132.5 1.1 slice.76
  133.6 1.3 slice_bitcast_fusion
  135.0 0.8 copy.57.q_ref
  135.9 0.8 copy.58.kn_ref
  136.7 0.8 copy.59.vn_ref
  137.6 16.7 %all-to-all-done.1 = bf16[9,2,16,16,256]{4,2,1,0,3:T(8,128)(2,1)S(1)} async-done(((bf16[9,2,16,16,256]{4,2,1,0,3:T(8,128)(2,1)}), bf16[9,2,16,16,256]{4,2,1,0,3:T(8,128)(2,1)S(1)}, u32[]{:S(2)}, u32[]{:S(2)}) %all-to-all-start.1) | async-done | bytes 2359328 | tf_op jit(solution)/shard_map/all_to_all | solution.py:164
  154.3 2.0 gather_fusion
  156.3 10.4 %shard_map.172.heads_ref = bf16[512,256]{1,0:T(8,128)(2,1)} custom-call(bf16[512,256]{1,0:T(8,128)(2,1)} %copy.57.q_ref, bf16[128,2,16,256]{3,2,1,0:T(8,128)(2,1)} %gather_fusion, bf16[128,2,16,256]{3,2,1,0:T(8,128)(2,1)} %gather_fusion, bf16[512,256]{1,0:T(8,128)(2,1)} %copy.58.kn_ref, bf16[512,256]{1,0:T(8,128)(2,1)} %copy.59.vn_ref, ...), custom_call_target="tpu_custom_call" | custom-call | flops 1342177280 | bytes 3145728 | tf_op jit(solution)/shard_map/pallas_call | solution.py:117
  166.7 9.2 %shard_map.173 = bf16[512,4096]{1,0:T(8,128)(2,1)} custom-call(bf16[512,256]{1,0:T(8,128)(2,1)} %shard_map.172.heads_ref, bf16[256,4096]{1,0:T(8,128)(2,1)} %all-gather.5.cloned.1.call-done.weight_ref, f32[512,4096]{1,0:T(8,128)} %fusion.34.feed_ref, f32[1,4096]{1,0:T(1,128)} %copy-done.2), custom_call_target="tpu_custom_call" | custom-call | flops 1073741824 | bytes 14942208 | tf_op jit(solution)/shard_map/pallas_call | solution.py:141
  175.9 0.0 reduce-scatter.2.cloned.1.call-update
  175.9 65.8 %reduce-scatter.2.cloned.1.call-done = bf16[512,256]{1,0:T(8,128)(2,1)} async-done(((bf16[512,4096]{1,0:T(8,128)(2,1)}), bf16[512,256]{1,0:T(8,128)(2,1)}) %reduce-scatter.2.cloned.1.call-update) | async-done | bytes 262160 | tf_op jit(solution)/shard_map/reduce_scatter | solution.py:237
  (23 shorter events, 0.2 us)
Async XLA Ops:
  6.5 57.7 %all-gather.3.cloned.1.call-start = ((), (), s32[]{:S(2)}) async-start(), calls=%async_computation.3 | async-start | bytes 4456448 | tf_op jit(solution)/shard_map/all_gather | solution.py:196
  11.4 9.0 %copy-start.3 = (s32[2]{0:T(128)S(1)}, s32[2]{0:T(128)}, u32[]{:S(2)}) copy-start(s32[2]{0:T(128)} %param.33) | copy-start | bytes 28
  11.4 9.6 %copy-start.4 = (s32[512]{0:T(512)S(1)}, s32[512]{0:T(512)}, u32[]{:S(2)}) copy-start(s32[512]{0:T(512)} %param.32) | copy-start | bytes 6148
  11.4 11.4 %copy-start.14 = (s32[2,64]{1,0:T(2,128)S(1)}, s32[2,64]{1,0:T(2,128)}, u32[]{:S(2)}) copy-start(s32[2,64]{1,0:T(2,128)} %param.34) | copy-start | bytes 1540
  11.4 15.5 %copy-start.5 = (f32[256]{0:T(256)S(1)}, f32[256]{0:T(256)}, u32[]{:S(2)}) copy-start(f32[256]{0:T(256)} %param.26) | copy-start | bytes 3076
  11.4 15.5 %copy-start.6 = (f32[256]{0:T(256)S(1)}, f32[256]{0:T(256)}, u32[]{:S(2)}) copy-start(f32[256]{0:T(256)} %param.30) | copy-start | bytes 3076
  11.4 15.5 %copy-start.7 = (s32[8,2]{0,1:T(2,128)S(1)}, s32[8,2]{0,1:T(2,128)}, u32[]{:S(2)}) copy-start(s32[8,2]{0,1:T(2,128)} %param.35) | copy-start | bytes 196
  11.4 104.1 %all-to-all-start = ((bf16[8,512,768]{2,1,0:T(8,128)(2,1)}), bf16[8,512,768]{2,1,0:T(8,128)(2,1)}, u32[]{:S(2)}, u32[]{:S(2)}) async-start(bf16[8,512,768]{2,1,0:T(8,128)(2,1)} %broadcast_in_dim.48), calls=%async_computation | async-start | bytes 12582912 | tf_op jit(solution)/shard_map/all_to_all | solution.py:173
  19.6 147.1 %all-gather.5.cloned.1.call-start = ((), (), s32[]{:S(2)}) async-start(), calls=%async_computation.4 | async-start | bytes 2359296 | tf_op jit(solution)/shard_map/all_gather | solution.py:198
  26.9 40.2 %copy-start.2 = (f32[1,4096]{1,0:T(1,128)}, f32[1,4096]{1,0:T(1,128)S(1)}, u32[]{:S(2)}) copy-start(f32[1,4096]{1,0:T(1,128)S(1)} %constant_dynamic-update-slice_fusion.bias_ref) | copy-start | bytes 49156
  64.2 3.4 %copy-start = (bf16[512,4096]{1,0:T(8,128)(2,1)S(1)}, bf16[512,4096]{1,0:T(8,128)(2,1)}, u32[]{:S(2)}) copy-start(bf16[512,4096]{1,0:T(8,128)(2,1)} %all-gather.3.cloned.1.call-done) | copy-start | bytes 12582916
  67.7 1.2 copy-start.8
  67.7 1.2 copy-start.9
  67.7 1.3 copy-start.12
  68.9 23.8 %copy-start.1 = (bf16[9,2,16,4096]{3,2,1,0:T(8,128)(2,1)S(1)}, bf16[9,2,16,4096]{3,2,1,0:T(8,128)(2,1)}, u32[]{:S(2)}) copy-start(bf16[9,2,16,4096]{3,2,1,0:T(8,128)(2,1)} %param.31) | copy-start | bytes 7077892
  115.5 4.7 %copy-start.10 = (f32[4096]{0:T(1024)S(1)}, f32[4096]{0:T(1024)}, u32[]{:S(2)}) copy-start(f32[4096]{0:T(1024)} %param.20) | copy-start | bytes 49156
  115.5 4.7 %copy-start.11 = (f32[4096]{0:T(1024)S(1)}, f32[4096]{0:T(1024)}, u32[]{:S(2)}) copy-start(f32[4096]{0:T(1024)} %param.19) | copy-start | bytes 49156
  115.5 4.7 %copy-start.13 = (f32[768]{0:T(1024)S(1)}, f32[768]{0:T(1024)}, u32[]{:S(2)}) copy-start(f32[768]{0:T(1024)} %param.24) | copy-start | bytes 9220
  115.5 38.7 %all-to-all-start.1 = ((bf16[9,2,16,16,256]{4,2,1,0,3:T(8,128)(2,1)}), bf16[9,2,16,16,256]{4,2,1,0,3:T(8,128)(2,1)S(1)}, u32[]{:S(2)}, u32[]{:S(2)}) async-start(bf16[9,2,16,16,256]{4,2,1,0,3:T(8,128)(2,1)} %bitcast.47), calls=%async_computation.1 | async-start | bytes 4718592 | tf_op jit(solution)/shard_map/all_to_all | solution.py:164
  119.9 121.7 %reduce-scatter.2.cloned.1.call-start = ((), (), s32[]{:S(2)}) async-start(), calls=%async_computation.5 | async-start | bytes 4456448 | tf_op jit(solution)/shard_map/reduce_scatter | solution.py:237
Sparse Core Ops, SparseCore 0:
  9.0 55.1 all-gather.2
  66.4 97.6 all-gather.4
  176.0 65.5 reduce-scatter.1

commit v13 on v11

--- a/solution.py
+++ b/solution.py
@@ -178,7 +178,7 @@
             jnp.dot(normed, up_weight, preferred_element_type=jnp.float32) + up_bias,
             approximate=False,
         ).astype(jnp.bfloat16)
-        return jnp.dot(hidden, down_weight, preferred_element_type=jnp.float32)
+        return jnp.dot(hidden, down_weight, preferred_element_type=jnp.float32).astype(jnp.bfloat16)
 
     feed_part = feed(mlp_normed)
     kv_cache, feed_part = lax.optimization_barrier((kv_cache, feed_part))

time: 247 us -> 246 us (level)
  matrix products: 40.4 us -> 36.9 us
where the time goes in v13:
time: 246 us; the launch traced here: 245 us
  waiting for transfers between devices  144 us (59%)
  matrix products  36.9 us (15%)
  local copies, waits for them, and re-layouts  19.9 us (8%)
  between operations  13.3 us (5%)
  starting transfers between devices  12.6 us (5%)
  Pallas kernels  10.4 us (4%)
  other arithmetic  7.99 us (3%)
    reduce_scatter x1, waiting for transfers between devices, shards(): lax.psum_scatter((attention_part + feed_part + bias_row).astype(jnp.bfloa...  65.8 us
    all_gather x1, waiting for transfers between devices, shards(): gathered = lax.all_gather(states, 'head', axis=1, tiled=True)  37.1 us
    all_to_all x1, waiting for transfers between devices, gather_by_all_to_all(): return lax.all_to_all(copies, axis, split_axis=0, concat_axis=0, tiled=True)  23.3 us
    dot_general x1, matrix products, feed(): jnp.dot(hidden, down_weight, preferred_element_type=jnp.float32)  21.6 us
    all_to_all x1, waiting for transfers between devices, share_pages(): lax.all_to_all(grouped, 'head', split_axis=3, concat_axis=0, tiled=True)  16.5 us
    pallas_call x1, Pallas kernels, attend_kernel(): pl.pallas_call(attention_kernel, grid=(heads,), in_specs=[row_block, page...  10.4 us
    dot_general x1, matrix products, shards(): joined = jnp.dot(pre_normed, qkv_full, preferred_element_type=jnp.float32)  9.16 us
    all_to_all x1, starting transfers between devices, gather_by_all_to_all(): return lax.all_to_all(copies, axis, split_axis=0, concat_axis=0, tiled=True)  8.17 us
  transfers between devices with their start and end apart: 5, of which 4 were waited for; matrix products, arithmetic and copies ran while one was open for 24% of the time, Pallas kernels for 4%

profile of v13, /device:TPU:0, one launch (start us, length us, event | category | flops | bytes accessed | tf_op | source)
XLA Modules:
  0.0 245.3 jit_solution(5785743721854486809)
XLA Ops:
  6.5 0.0 all-gather.3.cloned.1.call-start
  6.5 0.7 all-gather.3.cloned.1.call-update
  7.3 4.2 %broadcast_in_dim.38 = bf16[8,512,768]{2,1,0:T(8,128)(2,1)} broadcast(bf16[512,768]{1,0:T(8,128)(2,1)} %param.23), dimensions={1,2} | broadcast | bytes 7077888 | tf_op jit(solution)/shard_map/broadcast_in_dim | solution.py:142
  11.4 0.0 copy-start.13
  11.4 0.0 copy-start.3
  11.4 0.0 copy-start.2
  11.4 0.0 copy-start.6
  11.5 8.2 %all-to-all-start = ((bf16[8,512,768]{2,1,0:T(8,128)(2,1)}), bf16[8,512,768]{2,1,0:T(8,128)(2,1)}, u32[]{:S(2)}, u32[]{:S(2)}) async-start(bf16[8,512,768]{2,1,0:T(8,128)(2,1)} %broadcast_in_dim.38), calls=%async_computation | async-start | bytes 12582912 | tf_op jit(solution)/shard_map/all_to_all | solution.py:145
  19.6 0.0 all-gather.5.cloned.1.call-start
  19.7 0.7 all-gather.5.cloned.1.call-update
  20.4 0.0 copy-done.13
  20.4 0.1 eq.33
  20.5 0.1 reshape.193
  20.5 0.0 copy-done.3
  20.6 0.1 convert_reduce_fusion.1
  20.7 0.2 reduce-window.8
  20.9 0.0 copy-done.2
  20.9 0.7 fusion.106
  21.5 0.1 select_reduce_fusion.1
  21.6 1.3 fusion.70
  22.9 1.3 fusion.71
  24.3 0.9 copy.55.hi_col
  25.2 0.9 copy.56.start_col
  26.0 0.9 copy.54.lo_col
  26.9 0.0 copy-done.6
  26.9 0.1 compare_reduce_fusion
  27.0 0.1 fusion.69
  27.1 37.1 %all-gather.3.cloned.1.call-done = bf16[512,4096]{1,0:T(8,128)(2,1)} async-done(((bf16[512,256]{1,0:T(8,128)(2,1)}), bf16[512,4096]{1,0:T(8,128)(2,1)}) %all-gather.3.cloned.1.call-update) | async-done | bytes 4194320 | tf_op jit(solution)/shard_map/all_gather | solution.py:168
  64.2 0.0 copy-start
  64.2 3.0 %convert_reduce_fusion = f32[512]{0:T(512)S(1)} fusion(bf16[512,4096]{1,0:T(8,128)(2,1)} %all-gather.3.cloned.1.call-done), kind=kLoop, calls=%fused_computation.2 | loop fusion | flops 4193792 | bytes 4196352 | tf_op jit(solution)/shard_map/reduce_sum | solution.py:16
  67.1 0.5 copy-done
  67.6 0.0 copy-start.8
  67.6 1.2 fusion.8
  68.8 0.0 copy-done.7
  68.9 0.0 copy-done.8
  68.9 0.0 copy-done.11
  68.9 0.0 copy-start.1
  68.9 21.6 %convolution_convert_fusion = bf16[512,4096]{1,0:T(8,128)(2,1)} fusion(bf16[1024,4096]{1,0:T(8,128)(2,1)} %param.29, bf16[4096,1024]{1,0:T(8,128)(2,1)} %param.27, bf16[512,4096]{1,0:T(8,128)(2,1)} %all-gather.3.cloned.1.call-done, f32[4096]{0:T(1024)S(1)} %copy-done.7, f32[4096]{0:T(1024)S(1)} %copy-done.8, f32[512]{0:T(512)S(1)} %add_rsqrt_fusion, ...), kind=kOutput, calls=%fused_computation.13 | convolution fusion | flops 8639217664 | bytes 25206784 | tf_op jit(solution)/shard_map/dot_general | solution.py:181
  90.5 0.0 copy-done.1
  90.5 1.8 copy.63
  92.3 23.3 %all-to-all-done = bf16[8,512,768]{2,1,0:T(8,128)(2,1)} async-done(((bf16[8,512,768]{2,1,0:T(8,128)(2,1)}), bf16[8,512,768]{2,1,0:T(8,128)(2,1)}, u32[]{:S(2)}, u32[]{:S(2)}) %all-to-all-start) | async-done | bytes 6291488 | tf_op jit(solution)/shard_map/all_to_all | solution.py:145
  115.6 0.0 copy-start.12
  115.6 4.4 %all-to-all-start.1 = ((bf16[9,2,16,16,256]{4,2,1,0,3:T(8,128)(2,1)}), bf16[9,2,16,16,256]{4,2,1,0,3:T(8,128)(2,1)S(1)}, u32[]{:S(2)}, u32[]{:S(2)}) async-start(bf16[9,2,16,16,256]{4,2,1,0,3:T(8,128)(2,1)} %bitcast.48), calls=%async_computation.1 | async-start | bytes 4718592 | tf_op jit(solution)/shard_map/all_to_all | solution.py:136
  120.0 0.0 reduce-scatter.2.cloned.1.call-start
  120.1 0.0 copy-done.4
  120.1 0.0 copy-done.5
  120.1 0.3 add_dynamic-update-slice_fusion
  120.4 0.2 multiply_cosine_fusion
  120.6 0.0 copy-done.9
  120.6 0.0 copy-done.10
  120.6 0.0 copy-done.12
  120.6 9.2 %fusion.35 = f32[512,768]{1,0:T(8,128)} fusion(bf16[4096,768]{1,0:T(8,128)(2,1)} %bitcast, bf16[512,4096]{1,0:T(8,128)(2,1)} %all-gather.3.cloned.1.call-done, f32[4096]{0:T(1024)S(1)} %copy-done.9, f32[4096]{0:T(1024)S(1)} %copy-done.10, f32[512]{0:T(512)S(1)} %add_rsqrt_fusion, f32[512]{0:T(512)S(1)} %broadcast_multiply_fusion.1, f32[768]{0:T(1024)S(1)} %copy-done.12), kind=kOutput, calls=%fused_computation.44 | convolution fusion | flops 3234201600 | bytes 12098560 | tf_op jit(solution)/shard_map/dot_general | solution.py:186
  129.7 3.0 %copy.48 = f32[512,768]{0,1:T(8,128)} copy(f32[512,768]{1,0:T(8,128)} %fusion.35) | data formatting | bytes 3145728 | tf_op jit(solution)/shard_map/add | solution.py:187
  132.8 1.1 slice.76
  133.9 1.3 slice_bitcast_fusion
  135.3 0.8 copy.57.q_ref
  136.1 0.8 copy.58.kn_ref
  137.0 0.8 copy.59.vn_ref
  137.8 16.5 %all-to-all-done.1 = bf16[9,2,16,16,256]{4,2,1,0,3:T(8,128)(2,1)S(1)} async-done(((bf16[9,2,16,16,256]{4,2,1,0,3:T(8,128)(2,1)}), bf16[9,2,16,16,256]{4,2,1,0,3:T(8,128)(2,1)S(1)}, u32[]{:S(2)}, u32[]{:S(2)}) %all-to-all-start.1) | async-done | bytes 2359328 | tf_op jit(solution)/shard_map/all_to_all | solution.py:136
  154.3 2.0 gather_fusion
  156.4 10.4 %shard_map.172 = bf16[512,256]{1,0:T(8,128)(2,1)} custom-call(bf16[512,256]{1,0:T(8,128)(2,1)} %copy.57.q_ref, bf16[128,2,16,256]{3,2,1,0:T(8,128)(2,1)} %gather_fusion, bf16[128,2,16,256]{3,2,1,0:T(8,128)(2,1)} %gather_fusion, bf16[512,256]{1,0:T(8,128)(2,1)} %copy.58.kn_ref, bf16[512,256]{1,0:T(8,128)(2,1)} %copy.59.vn_ref, s32[512,1]{1,0:T(8,128)} %copy.54.lo_col, ...), custom_call_target="tpu_custom_call" | custom-call | flops 1342177280 | bytes 3145728 | tf_op jit(solution)/shard_map/pallas_call | solution.py:116
  166.8 6.1 %add_convert_fusion = bf16[512,4096]{1,0:T(8,128)(2,1)} fusion(bf16[512,4096]{1,0:T(8,128)(2,1)} %convolution_convert_fusion, bf16[512,256]{1,0:T(8,128)(2,1)} %shard_map.172, bf16[256,4096]{1,0:T(8,128)(2,1)} %all-gather.5.cloned.1.call-done, f32[4096]{0:T(1024)S(1)} %add_dynamic-update-slice_fusion), kind=kOutput, calls=%fused_computation.12 | convolution fusion | flops 1082130432 | bytes 10764288 | tf_op jit(solution)/shard_map/dot_general | solution.py:203
  172.9 0.0 reduce-scatter.2.cloned.1.call-update
  172.9 65.8 %reduce-scatter.2.cloned.1.call-done = bf16[512,256]{1,0:T(8,128)(2,1)} async-done(((bf16[512,4096]{1,0:T(8,128)(2,1)}), bf16[512,256]{1,0:T(8,128)(2,1)}) %reduce-scatter.2.cloned.1.call-update) | async-done | bytes 262160 | tf_op jit(solution)/shard_map/reduce_scatter | solution.py:210
  (20 shorter events, 0.2 us)
Async XLA Ops:
  6.5 57.6 %all-gather.3.cloned.1.call-start = ((), (), s32[]{:S(2)}) async-start(), calls=%async_computation.3 | async-start | bytes 4456448 | tf_op jit(solution)/shard_map/all_gather | solution.py:168
  11.4 8.9 %copy-start.13 = (s32[2,64]{1,0:T(2,128)S(1)}, s32[2,64]{1,0:T(2,128)}, u32[]{:S(2)}) copy-start(s32[2,64]{1,0:T(2,128)} %param.34) | copy-start | bytes 1540
  11.4 9.1 %copy-start.3 = (s32[512]{0:T(512)S(1)}, s32[512]{0:T(512)}, u32[]{:S(2)}) copy-start(s32[512]{0:T(512)} %param.32) | copy-start | bytes 6148
  11.4 9.4 %copy-start.2 = (s32[2]{0:T(128)S(1)}, s32[2]{0:T(128)}, u32[]{:S(2)}) copy-start(s32[2]{0:T(128)} %param.33) | copy-start | bytes 28
  11.4 15.4 %copy-start.6 = (s32[8,2]{0,1:T(2,128)S(1)}, s32[8,2]{0,1:T(2,128)}, u32[]{:S(2)}) copy-start(s32[8,2]{0,1:T(2,128)} %param.35) | copy-start | bytes 196
  11.5 104.1 %all-to-all-start = ((bf16[8,512,768]{2,1,0:T(8,128)(2,1)}), bf16[8,512,768]{2,1,0:T(8,128)(2,1)}, u32[]{:S(2)}, u32[]{:S(2)}) async-start(bf16[8,512,768]{2,1,0:T(8,128)(2,1)} %broadcast_in_dim.38), calls=%async_computation | async-start | bytes 12582912 | tf_op jit(solution)/shard_map/all_to_all | solution.py:145
  19.6 147.2 %all-gather.5.cloned.1.call-start = ((), (), s32[]{:S(2)}) async-start(), calls=%async_computation.4 | async-start | bytes 2359296 | tf_op jit(solution)/shard_map/all_gather | solution.py:170
  64.2 3.4 %copy-start = (bf16[512,4096]{1,0:T(8,128)(2,1)S(1)}, bf16[512,4096]{1,0:T(8,128)(2,1)}, u32[]{:S(2)}) copy-start(bf16[512,4096]{1,0:T(8,128)(2,1)} %all-gather.3.cloned.1.call-done) | copy-start | bytes 12582916
  67.6 1.2 copy-start.7
  67.6 1.2 copy-start.8
  67.6 1.3 copy-start.11
  68.9 21.6 %copy-start.1 = (bf16[9,2,16,4096]{3,2,1,0:T(8,128)(2,1)S(1)}, bf16[9,2,16,4096]{3,2,1,0:T(8,128)(2,1)}, u32[]{:S(2)}) copy-start(bf16[9,2,16,4096]{3,2,1,0:T(8,128)(2,1)} %param.31) | copy-start | bytes 7077892
  115.6 4.5 %copy-start.4 = (f32[256]{0:T(256)S(1)}, f32[256]{0:T(256)}, u32[]{:S(2)}) copy-start(f32[256]{0:T(256)} %param.26) | copy-start | bytes 3076
  115.6 4.5 %copy-start.5 = (f32[256]{0:T(256)S(1)}, f32[256]{0:T(256)}, u32[]{:S(2)}) copy-start(f32[256]{0:T(256)} %param.30) | copy-start | bytes 3076
  115.6 5.0 %copy-start.9 = (f32[4096]{0:T(1024)S(1)}, f32[4096]{0:T(1024)}, u32[]{:S(2)}) copy-start(f32[4096]{0:T(1024)} %param.20) | copy-start | bytes 49156
  115.6 5.0 %copy-start.10 = (f32[4096]{0:T(1024)S(1)}, f32[4096]{0:T(1024)}, u32[]{:S(2)}) copy-start(f32[4096]{0:T(1024)} %param.19) | copy-start | bytes 49156
  115.6 5.0 %copy-start.12 = (f32[768]{0:T(1024)S(1)}, f32[768]{0:T(1024)}, u32[]{:S(2)}) copy-start(f32[768]{0:T(1024)} %param.24) | copy-start | bytes 9220
  115.6 38.7 %all-to-all-start.1 = ((bf16[9,2,16,16,256]{4,2,1,0,3:T(8,128)(2,1)}), bf16[9,2,16,16,256]{4,2,1,0,3:T(8,128)(2,1)S(1)}, u32[]{:S(2)}, u32[]{:S(2)}) async-start(bf16[9,2,16,16,256]{4,2,1,0,3:T(8,128)(2,1)} %bitcast.48), calls=%async_computation.1 | async-start | bytes 4718592 | tf_op jit(solution)/shard_map/all_to_all | solution.py:136
  120.0 118.7 %reduce-scatter.2.cloned.1.call-start = ((), (), s32[]{:S(2)}) async-start(), calls=%async_computation.5 | async-start | bytes 4456448 | tf_op jit(solution)/shard_map/reduce_scatter | solution.py:210
Sparse Core Ops, SparseCore 0:
  9.0 55.1 all-gather.2
  66.3 97.8 all-gather.4
  173.0 65.6 reduce-scatter.1

commit v14 on v13

--- a/solution.py
+++ b/solution.py
@@ -70,10 +70,9 @@
     ).astype(jnp.bfloat16)
 
 
-def attention_kernel(q_ref, kc_ref, vc_ref, kn_ref, vn_ref, lo_col, hi_col, start_col, o_ref):
+def scores_kernel(q_ref, kc_ref, kn_ref, vn_ref, lo_col, hi_col, start_col, p_ref, n_ref):
     queries = q_ref[...]
     cache_keys = kc_ref[...].reshape(-1, queries.shape[1])
-    cache_values = vc_ref[...].reshape(-1, queries.shape[1])
     dims = (((1,), (1,)), ((), ()))
     scale = HD ** (-0.5)
     cache_scores = lax.dot_general(queries, cache_keys, dims, preferred_element_type=jnp.float32) * scale
@@ -91,50 +90,68 @@
     cache_exp = jnp.exp(cache_scores - peak)
     new_exp = jnp.exp(new_scores - peak)
     total = jnp.sum(cache_exp, axis=1, keepdims=True) + jnp.sum(new_exp, axis=1, keepdims=True)
-    cache_probs = (cache_exp / total).astype(jnp.bfloat16)
+    p_ref[0] = (cache_exp / total).astype(jnp.bfloat16)
     new_probs = (new_exp / total).astype(jnp.bfloat16)
-    mixed = jnp.dot(cache_probs, cache_values, preferred_element_type=jnp.float32) + jnp.dot(
-        new_probs, vn_ref[...], preferred_element_type=jnp.float32
-    )
+    n_ref[...] = jnp.dot(new_probs, vn_ref[...], preferred_element_type=jnp.float32)
+
+
+def values_kernel(p_ref, vc_ref, n_ref, o_ref):
+    cache_values = vc_ref[...].reshape(-1, o_ref.shape[1])
+    mixed = jnp.dot(p_ref[0], cache_values, preferred_element_type=jnp.float32) + n_ref[...]
     o_ref[...] = mixed.astype(o_ref.dtype)
 
 
-def attend_kernel(queries, new_keys, new_values, pages, local_req, cached, positions):
+def attend_kernel(queries, new_keys, new_values, key_pages, value_pool, table, local_req, cached, positions):
     tokens, heads = queries.shape[0], queries.shape[1]
-    page_count, page_len = pages.shape[0], pages.shape[2]
-    span = page_count * page_len // cached.shape[0]
+    page_count, page_len = key_pages.shape[0], key_pages.shape[2]
+    keys_cached = page_count * page_len
+    span = keys_cached // cached.shape[0]
     own_cached = jnp.take(cached, local_req)
     lo_col = (local_req * span)[:, None]
     hi_col = lo_col + own_cached[:, None]
     start_col = (jnp.arange(tokens, dtype=jnp.int32) - positions + own_cached)[:, None]
     flat = lambda x: x.reshape(tokens, heads * HD)
     row_block = pl.BlockSpec((tokens, HD), lambda h: (0, h))
-    page_block = lambda part: pl.BlockSpec((page_count, 1, page_len, HD), lambda h: (0, part, 0, h))
+    page_block = pl.BlockSpec((page_count, 1, page_len, HD), lambda h: (0, 0, 0, h))
+    prob_block = pl.BlockSpec((1, tokens, keys_cached), lambda h: (h, 0, 0))
     whole = lambda x: pl.BlockSpec(x.shape, lambda h: (0,) * x.ndim)
     extras = (lo_col, hi_col, start_col)
-    keys_seen = page_count * page_len + tokens
-    out = pl.pallas_call(
-        attention_kernel,
+    keys_seen = keys_cached + tokens
+    probs, partial = pl.pallas_call(
+        scores_kernel,
         grid=(heads,),
-        in_specs=[row_block, page_block(0), page_block(1), row_block, row_block]
-        + [whole(x) for x in extras],
+        in_specs=[row_block, page_block, row_block, row_block] + [whole(x) for x in extras],
+        out_specs=[prob_block, row_block],
+        out_shape=[
+            jax.ShapeDtypeStruct((heads, tokens, keys_cached), jnp.bfloat16),
+            jax.ShapeDtypeStruct((tokens, heads * HD), jnp.float32),
+        ],
+        cost_estimate=pl.CostEstimate(
+            flops=2 * heads * tokens * (keys_seen + tokens) * HD,
+            transcendentals=heads * tokens * keys_seen,
+            bytes_accessed=2 * HD * heads * (3 * tokens + keys_cached) + 2 * heads * tokens * keys_cached,
+        ),
+    )(flat(queries), key_pages, flat(new_keys), flat(new_values), *extras)
+    value_pool, probs = lax.optimization_barrier((value_pool, probs))
+    value_pages = value_pool[table]
+    return pl.pallas_call(
+        values_kernel,
+        grid=(heads,),
+        in_specs=[prob_block, page_block, row_block],
         out_specs=row_block,
         out_shape=jax.ShapeDtypeStruct((tokens, heads * HD), jnp.bfloat16),
         cost_estimate=pl.CostEstimate(
-            flops=4 * heads * tokens * keys_seen * HD,
-            transcendentals=heads * tokens * keys_seen,
-            bytes_accessed=2 * HD * heads * (2 * tokens + 2 * keys_seen),
+            flops=2 * heads * tokens * keys_cached * HD,
+            transcendentals=0,
+            bytes_accessed=2 * heads * tokens * keys_cached + 2 * HD * heads * keys_cached + 6 * tokens * heads * HD,
         ),
-    )(flat(queries), pages, pages, flat(new_keys), flat(new_values), *extras)
-    return out
+    )(probs, value_pages, partial)
 
 
 def share_pages(local_pool, groups):
-    grouped = local_pool.reshape(
-        local_pool.shape[0], 2, local_pool.shape[2], groups, local_pool.shape[3] // groups
-    )
+    grouped = local_pool.reshape(local_pool.shape[:3] + (groups, local_pool.shape[3] // groups))
     shared = lax.all_to_all(grouped, "head", split_axis=3, concat_axis=0, tiled=True)
-    return shared.reshape(shared.shape[0], 2, shared.shape[2], shared.shape[4])
+    return shared.reshape(shared.shape[:3] + (shared.shape[4],))
 
 
 def gather_by_all_to_all(block, axis):
@@ -182,7 +199,8 @@
 
     feed_part = feed(mlp_normed)
     kv_cache, feed_part = lax.optimization_barrier((kv_cache, feed_part))
-    page_pool = share_pages(kv_cache, lax.axis_size("head"))
+    key_pool = share_pages(kv_cache[:, :1], lax.axis_size("head"))
+    value_pool = share_pages(kv_cache[:, 1:], lax.axis_size("head"))
     joined = jnp.dot(pre_normed, qkv_full, preferred_element_type=jnp.float32)
     joined = (joined + qkv_bias).reshape(tok_rows, -1, 3, HD)
     local_req = token_request - lax.axis_index("tok") * cached_len.shape[0]
@@ -196,9 +214,8 @@
     match = table[:, None] == targets[None, :]
     moved_from = jnp.sum(jnp.where(match, sources[None, :], 0), axis=1)
     table = jnp.where(jnp.any(match, axis=1), moved_from, table)
-    pages = page_pool[table]
     heads_out = attend_kernel(
-        queries, new_keys, new_values, pages, local_req, cached_len, positions
+        queries, new_keys, new_values, key_pool[table], value_pool, table, local_req, cached_len, positions
     )
     attention_part = jnp.dot(heads_out, out_full, preferred_element_type=jnp.float32)
     bias_row = lax.dynamic_update_slice_in_dim(

time: 246 us -> 253 us (1.028)
  starting transfers between devices: 12.6 us -> 17.8 us
  local copies, waits for them, and re-layouts: 19.9 us -> 22.5 us
    all_to_all x1 -> x2, starting transfers between devices: 4.4 us -> 9.32 us  [share_pages(): lax.all_to_all(grouped, 'head', split_axis=3, concat_axis=0, tiled=True)]
    pallas_call x1 -> x2, Pallas kernels: 10.4 us -> 12.3 us  [the longest x1 8.27 us: attend_kernel(): pl.pallas_call(scores_kernel, grid=(heads,), in_specs=[row_block, page_bl...]
    all_to_all x1 -> x2, waiting for transfers between devices: 16.5 us -> 16.2 us  [share_pages(): lax.all_to_all(grouped, 'head', split_axis=3, concat_axis=0, tiled=True)]
  transfers between devices with their start and end apart: 5 -> 6, of which waited for: 4 -> 4; matrix products, arithmetic and copies ran while one was open for 24% -> 24% of each run, Pallas kernels for 4% -> 5%
where the time goes in v14:
time: 253 us
  waiting for transfers between devices  142 us (56%)
  matrix products  36.9 us (15%)
  local copies, waits for them, and re-layouts  22.5 us (9%)
  starting transfers between devices  17.8 us (7%)
  between operations  13.4 us (5%)
  Pallas kernels  12.3 us (5%)
  other arithmetic  7.76 us (3%)
    reduce_scatter x1, waiting for transfers between devices, shards(): lax.psum_scatter((attention_part + feed_part + bias_row).astype(jnp.bfloa...  65.8 us
    all_gather x1, waiting for transfers between devices, shards(): gathered = lax.all_gather(states, 'head', axis=1, tiled=True)  35.8 us
    all_to_all x1, waiting for transfers between devices, gather_by_all_to_all(): return lax.all_to_all(copies, axis, split_axis=0, concat_axis=0, tiled=True)  23 us
    dot_general x1, matrix products, feed(): jnp.dot(hidden, down_weight, preferred_element_type=jnp.float32)  21.6 us
    all_to_all x2, waiting for transfers between devices, share_pages(): lax.all_to_all(grouped, 'head', split_axis=3, concat_axis=0, tiled=True)  16.2 us
    all_to_all x2, starting transfers between devices, share_pages(): lax.all_to_all(grouped, 'head', split_axis=3, concat_axis=0, tiled=True)  9.32 us
    dot_general x1, matrix products, shards(): joined = jnp.dot(pre_normed, qkv_full, preferred_element_type=jnp.float32)  9.15 us
    pallas_call x1, Pallas kernels, attend_kernel(): pl.pallas_call(scores_kernel, grid=(heads,), in_specs=[row_block, page_bl...  8.27 us
  transfers between devices with their start and end apart: 6, of which 4 were waited for; matrix products, arithmetic and copies ran while one was open for 24% of the time, Pallas kernels for 5%

profile of v14, /device:TPU:0, one launch (start us, length us, event | category | flops | bytes accessed | tf_op | source)
XLA Modules:
  0.0 252.7 jit_solution(8612376727700833775)
XLA Ops:
  6.5 0.0 all-gather.3.cloned.1.call-start
  6.5 0.7 all-gather.3.cloned.1.call-update
  7.3 4.2 %broadcast_in_dim.38 = bf16[8,512,768]{2,1,0:T(8,128)(2,1)} broadcast(bf16[512,768]{1,0:T(8,128)(2,1)} %param.23), dimensions={1,2} | broadcast | bytes 7077888 | tf_op jit(solution)/shard_map/broadcast_in_dim | solution.py:159
  11.4 8.2 %all-to-all-start.1 = ((bf16[8,512,768]{2,1,0:T(8,128)(2,1)}), bf16[8,512,768]{2,1,0:T(8,128)(2,1)}, u32[]{:S(2)}, u32[]{:S(2)}) async-start(bf16[8,512,768]{2,1,0:T(8,128)(2,1)} %broadcast_in_dim.38), calls=%async_computation.1 | async-start | bytes 12582912 | tf_op jit(solution)/shard_map/all_to_all | solution.py:162
  19.6 0.0 all-gather.5.cloned.1.call-start
  19.7 0.7 all-gather.5.cloned.1.call-update
  20.4 0.0 copy-done.3
  20.4 0.1 convert_reduce_fusion.1
  20.5 0.2 reduce-window.8
  20.7 0.0 copy-done.2
  20.7 0.6 fusion.107
  21.3 0.1 select_reduce_fusion.1
  21.4 1.3 fusion.70
  22.7 1.3 fusion.71
  24.0 0.0 copy-done.7
  24.0 0.6 slice_bitcast_fusion.3
  24.6 0.0 copy-done.16
  24.6 0.6 eq.33
  25.3 0.6 reshape.202
  25.8 0.9 copy.58.hi_col
  26.7 0.9 copy.59.start_col
  27.6 0.8 copy.57.lo_col
  28.5 35.8 %all-gather.3.cloned.1.call-done = bf16[512,4096]{1,0:T(8,128)(2,1)} async-done(((bf16[512,256]{1,0:T(8,128)(2,1)}), bf16[512,4096]{1,0:T(8,128)(2,1)}) %all-gather.3.cloned.1.call-update) | async-done | bytes 4194320 | tf_op jit(solution)/shard_map/all_gather | solution.py:185
  64.2 3.0 %convert_reduce_fusion = f32[512]{0:T(512)S(1)} fusion(bf16[512,4096]{1,0:T(8,128)(2,1)} %all-gather.3.cloned.1.call-done), kind=kLoop, calls=%fused_computation.3 | loop fusion | flops 4193792 | bytes 4196352 | tf_op jit(solution)/shard_map/reduce_sum | solution.py:16
  67.2 0.5 copy-done
  67.7 1.2 fusion.8
  68.9 0.0 copy-done.10
  68.9 0.0 copy-done.11
  69.0 0.0 copy-start.1
  69.0 21.6 %convolution_convert_fusion = bf16[512,4096]{1,0:T(8,128)(2,1)} fusion(bf16[1024,4096]{1,0:T(8,128)(2,1)} %param.29, bf16[4096,1024]{1,0:T(8,128)(2,1)} %param.27, bf16[512,4096]{1,0:T(8,128)(2,1)} %all-gather.3.cloned.1.call-done, f32[4096]{0:T(1024)S(1)} %copy-done.10, f32[4096]{0:T(1024)S(1)} %copy-done.11, f32[512]{0:T(512)S(1)} %add_rsqrt_fusion, ...), kind=kOutput, calls=%fused_computation.14 | convolution fusion | flops 8639217664 | bytes 25206784 | tf_op jit(solution)/shard_map/dot_general | solution.py:198
  90.6 0.2 fusion.106
  90.8 0.3 copy.65
  91.1 0.0 copy-start.8
  91.1 0.0 copy-start.5
  91.1 0.0 copy-start.6
  91.1 1.4 copy.54
  92.5 23.0 %all-to-all-done.1 = bf16[8,512,768]{2,1,0:T(8,128)(2,1)} async-done(((bf16[8,512,768]{2,1,0:T(8,128)(2,1)}), bf16[8,512,768]{2,1,0:T(8,128)(2,1)}, u32[]{:S(2)}, u32[]{:S(2)}) %all-to-all-start.1) | async-done | bytes 6291488 | tf_op jit(solution)/shard_map/all_to_all | solution.py:162
  115.6 4.3 %all-to-all-start.2 = ((bf16[9,1,16,16,256]{4,2,0,1,3:T(8,128)(2,1)}), bf16[9,1,16,16,256]{4,2,0,1,3:T(8,128)(2,1)S(1)}, u32[]{:S(2)}, u32[]{:S(2)}) async-start(bf16[9,1,16,16,256]{4,2,0,1,3:T(8,128)(2,1)} %copy.54), calls=%async_computation.2 | async-start | bytes 2359296 | tf_op jit(solution)/shard_map/all_to_all | solution.py:153
  119.9 0.1 compare_reduce_fusion
  119.9 0.1 fusion.69
  120.1 0.1 add_dynamic-update-slice_fusion
  120.2 0.2 multiply_cosine_fusion
  120.4 0.3 copy.64
  120.7 0.0 copy-start.12
  120.7 0.0 copy-start.13
  120.7 0.0 copy-start.15
  120.8 1.4 copy.50
  122.2 16.2 %all-to-all-done.2 = bf16[9,1,16,16,256]{4,2,0,1,3:T(8,128)(2,1)S(1)} async-done(((bf16[9,1,16,16,256]{4,2,0,1,3:T(8,128)(2,1)}), bf16[9,1,16,16,256]{4,2,0,1,3:T(8,128)(2,1)S(1)}, u32[]{:S(2)}, u32[]{:S(2)}) %all-to-all-start.2) | async-done | bytes 1179680 | tf_op jit(solution)/shard_map/all_to_all | solution.py:153
  138.3 5.1 %all-to-all-start = ((bf16[9,1,16,16,256]{4,2,0,1,3:T(8,128)(2,1)}), bf16[9,1,16,16,256]{4,2,0,1,3:T(8,128)(2,1)}, u32[]{:S(2)}, u32[]{:S(2)}) async-start(bf16[9,1,16,16,256]{4,2,0,1,3:T(8,128)(2,1)} %copy.50), calls=%async_computation | async-start | bytes 2359296 | tf_op jit(solution)/shard_map/all_to_all | solution.py:153
  143.4 0.2 reduce-scatter.2.cloned.1.call-start
  143.7 9.2 %fusion.35 = f32[512,768]{1,0:T(8,128)} fusion(bf16[4096,768]{1,0:T(8,128)(2,1)} %bitcast.3, bf16[512,4096]{1,0:T(8,128)(2,1)} %all-gather.3.cloned.1.call-done, f32[4096]{0:T(1024)S(1)} %copy-done.12, f32[4096]{0:T(1024)S(1)} %copy-done.13, f32[512]{0:T(512)S(1)} %add_rsqrt_fusion, f32[512]{0:T(512)S(1)} %broadcast_multiply_fusion.1, f32[768]{0:T(1024)S(1)} %copy-done.15), kind=kOutput, calls=%fused_computation.44 | convolution fusion | flops 3234201600 | bytes 12098560 | tf_op jit(solution)/shard_map/dot_general | solution.py:204
  152.8 1.9 copy.51
  154.7 0.1 slice_bitcast_fusion
  155.0 0.8 copy.60.q_ref
  155.8 0.8 copy.61.kn_ref
  156.7 0.9 copy.62.vn_ref
  157.5 1.6 gather_fusion
  159.1 8.3 %shard_map.172 = (bf16[2,512,2048]{2,1,0:T(8,128)(2,1)}, f32[512,256]{1,0:T(8,128)}) custom-call(bf16[512,256]{1,0:T(8,128)(2,1)} %copy.60.q_ref, bf16[128,1,16,256]{3,2,1,0:T(8,128)(2,1)} %bitcast.73, bf16[512,256]{1,0:T(8,128)(2,1)} %copy.61.kn_ref, bf16[512,256]{1,0:T(8,128)(2,1)} %copy.62.vn_ref, s32[512,1]{1,0:T(8,128)} %copy.57.lo_col, ...), custom_call_target="tpu_custom_call" | custom-call | flops 805306368 | bytes 6029312 | tf_op jit(solution)/shard_map/pallas_call | solution.py:120
  167.4 0.0 all-to-all-done
  167.4 2.9 %gather_fusion.1 = bf16[128,16,256]{2,1,0:T(8,128)(2,1)} fusion(bf16[144,16,256]{2,1,0:T(8,128)(2,1)} %bitcast.26, s32[1024]{0:T(1024)S(1)} %pad_clamp_fusion), kind=kCustom, calls=%fused_computation.1 | custom fusion | bytes 2097664 | tf_op jit(solution)/shard_map/gather | solution.py:136
  170.3 4.0 %shard_map.173 = bf16[512,256]{1,0:T(8,128)(2,1)} custom-call(bf16[2,512,2048]{2,1,0:T(8,128)(2,1)} %get-tuple-element.13.p_ref, bf16[128,1,16,256]{3,2,1,0:T(8,128)(2,1)} %bitcast.72, f32[512,256]{1,0:T(8,128)} %get-tuple-element.15.n_ref), custom_call_target="tpu_custom_call" | custom-call | flops 536870912 | bytes 6029312 | tf_op jit(solution)/shard_map/pallas_call | solution.py:137
  174.3 6.1 %add_convert_fusion = bf16[512,4096]{1,0:T(8,128)(2,1)} fusion(bf16[512,4096]{1,0:T(8,128)(2,1)} %convolution_convert_fusion, bf16[512,256]{1,0:T(8,128)(2,1)} %shard_map.173, bf16[256,4096]{1,0:T(8,128)(2,1)} %all-gather.5.cloned.1.call-done, f32[4096]{0:T(1024)S(1)} %add_dynamic-update-slice_fusion), kind=kOutput, calls=%fused_computation.13 | convolution fusion | flops 1082130432 | bytes 10764288 | tf_op jit(solution)/shard_map/dot_general | solution.py:220
  180.4 0.0 reduce-scatter.2.cloned.1.call-update
  180.4 65.8 %reduce-scatter.2.cloned.1.call-done = bf16[512,256]{1,0:T(8,128)(2,1)} async-done(((bf16[512,4096]{1,0:T(8,128)(2,1)}), bf16[512,256]{1,0:T(8,128)(2,1)}) %reduce-scatter.2.cloned.1.call-update) | async-done | bytes 262160 | tf_op jit(solution)/shard_map/reduce_scatter | solution.py:227
  (34 shorter events, 0.3 us)
Async XLA Ops:
  6.5 57.7 %all-gather.3.cloned.1.call-start = ((), (), s32[]{:S(2)}) async-start(), calls=%async_computation.4 | async-start | bytes 4456448 | tf_op jit(solution)/shard_map/all_gather | solution.py:185
  11.4 8.9 %copy-start.3 = (s32[512]{0:T(512)S(1)}, s32[512]{0:T(512)}, u32[]{:S(2)}) copy-start(s32[512]{0:T(512)} %param.32) | copy-start | bytes 6148
  11.4 9.3 %copy-start.2 = (s32[2]{0:T(128)S(1)}, s32[2]{0:T(128)}, u32[]{:S(2)}) copy-start(s32[2]{0:T(128)} %param.33) | copy-start | bytes 28
  11.4 12.6 %copy-start.7 = (s32[8,2]{0,1:T(2,128)S(1)}, s32[8,2]{0,1:T(2,128)}, u32[]{:S(2)}) copy-start(s32[8,2]{0,1:T(2,128)} %param.35) | copy-start | bytes 196
  11.4 13.2 %copy-start.16 = (s32[2,64]{1,0:T(2,128)S(1)}, s32[2,64]{1,0:T(2,128)}, u32[]{:S(2)}) copy-start(s32[2,64]{1,0:T(2,128)} %param.34) | copy-start | bytes 1540
  11.4 104.1 %all-to-all-start.1 = ((bf16[8,512,768]{2,1,0:T(8,128)(2,1)}), bf16[8,512,768]{2,1,0:T(8,128)(2,1)}, u32[]{:S(2)}, u32[]{:S(2)}) async-start(bf16[8,512,768]{2,1,0:T(8,128)(2,1)} %broadcast_in_dim.38), calls=%async_computation.1 | async-start | bytes 12582912 | tf_op jit(solution)/shard_map/all_to_all | solution.py:162
  19.6 154.7 %all-gather.5.cloned.1.call-start = ((), (), s32[]{:S(2)}) async-start(), calls=%async_computation.5 | async-start | bytes 2359296 | tf_op jit(solution)/shard_map/all_gather | solution.py:187
  64.2 3.4 %copy-start = (bf16[512,4096]{1,0:T(8,128)(2,1)S(1)}, bf16[512,4096]{1,0:T(8,128)(2,1)}, u32[]{:S(2)}) copy-start(bf16[512,4096]{1,0:T(8,128)(2,1)} %all-gather.3.cloned.1.call-done) | copy-start | bytes 12582916
  67.7 1.2 copy-start.10
  67.7 1.2 copy-start.11
  67.7 1.3 copy-start.14
  69.0 21.6 %copy-start.1 = (bf16[9,2,16,4096]{3,2,1,0:T(8,128)(2,1)S(1)}, bf16[9,2,16,4096]{3,2,1,0:T(8,128)(2,1)}, u32[]{:S(2)}) copy-start(bf16[9,2,16,4096]{3,2,1,0:T(8,128)(2,1)} %param.31) | copy-start | bytes 7077892
  91.1 28.8 %copy-start.9 = (s32[128]{0:T(128)S(1)}, s32[128]{0:T(128)}, u32[]{:S(2)}) copy-start(s32[128]{0:T(128)} %eq.33) | copy-start | bytes 1540
  91.1 28.9 %copy-start.4 = (s32[8]{0:T(128)S(1)}, s32[8]{0:T(128)}, u32[]{:S(2)}) copy-start(s32[8]{0:T(128)} %get-tuple-element.37) | copy-start | bytes 100
  91.1 29.0 %copy-start.8 = (s32[128,1]{0,1:T(1,128)S(1)}, s32[128,1]{0,1:T(1,128)}, u32[]{:S(2)}) copy-start(s32[128,1]{0,1:T(1,128)} %reshape.202) | copy-start | bytes 1540
  91.1 29.0 %copy-start.5 = (f32[256]{0:T(256)S(1)}, f32[256]{0:T(256)}, u32[]{:S(2)}) copy-start(f32[256]{0:T(256)} %param.26) | copy-start | bytes 3076
  91.1 29.0 %copy-start.6 = (f32[256]{0:T(256)S(1)}, f32[256]{0:T(256)}, u32[]{:S(2)}) copy-start(f32[256]{0:T(256)} %param.30) | copy-start | bytes 3076
  115.6 22.8 %all-to-all-start.2 = ((bf16[9,1,16,16,256]{4,2,0,1,3:T(8,128)(2,1)}), bf16[9,1,16,16,256]{4,2,0,1,3:T(8,128)(2,1)S(1)}, u32[]{:S(2)}, u32[]{:S(2)}) async-start(bf16[9,1,16,16,256]{4,2,0,1,3:T(8,128)(2,1)} %copy.54), calls=%async_computation.2 | async-start | bytes 2359296 | tf_op jit(solution)/shard_map/all_to_all | solution.py:153
  120.7 22.9 %copy-start.12 = (f32[4096]{0:T(1024)S(1)}, f32[4096]{0:T(1024)}, u32[]{:S(2)}) copy-start(f32[4096]{0:T(1024)} %param.20) | copy-start | bytes 49156
  120.7 22.9 %copy-start.13 = (f32[4096]{0:T(1024)S(1)}, f32[4096]{0:T(1024)}, u32[]{:S(2)}) copy-start(f32[4096]{0:T(1024)} %param.19) | copy-start | bytes 49156
  120.7 22.9 %copy-start.15 = (f32[768]{0:T(1024)S(1)}, f32[768]{0:T(1024)}, u32[]{:S(2)}) copy-start(f32[768]{0:T(1024)} %param.24) | copy-start | bytes 9220
  138.3 29.1 %all-to-all-start = ((bf16[9,1,16,16,256]{4,2,0,1,3:T(8,128)(2,1)}), bf16[9,1,16,16,256]{4,2,0,1,3:T(8,128)(2,1)}, u32[]{:S(2)}, u32[]{:S(2)}) async-start(bf16[9,1,16,16,256]{4,2,0,1,3:T(8,128)(2,1)} %copy.50), calls=%async_computation | async-start | bytes 2359296 | tf_op jit(solution)/shard_map/all_to_all | solution.py:153
  143.4 102.8 %reduce-scatter.2.cloned.1.call-start = ((), (), s32[]{:S(2)}) async-start(), calls=%async_computation.6 | async-start | bytes 4456448 | tf_op jit(solution)/shard_map/reduce_scatter | solution.py:227
Sparse Core Ops, SparseCore 0:
  9.0 55.2 all-gather.2
  66.4 85.9 all-gather.4
  180.5 65.6 reduce-scatter.1

commit v15 on v13

--- a/solution.py
+++ b/solution.py
@@ -207,12 +207,14 @@
         lax.axis_index("head") * out_bias.shape[0],
         axis=0,
     )
-    return lax.psum_scatter(
-        (attention_part + feed_part + bias_row).astype(jnp.bfloat16),
-        "head",
-        scatter_dimension=1,
-        tiled=True,
-    )
+    both = (attention_part + feed_part + bias_row).astype(jnp.bfloat16)
+    half = both.shape[0] // 2
+    groups = lax.axis_size("head")
+    later = lax.psum_scatter(both[half:], "head", scatter_dimension=1, tiled=True)
+    spread = both[:half].reshape(half, groups, both.shape[1] // groups)
+    swapped = lax.all_to_all(spread, "head", split_axis=1, concat_axis=1, tiled=True)
+    first = jnp.sum(swapped.astype(jnp.float32), axis=1).astype(jnp.bfloat16)
+    return jnp.concatenate([first, later], axis=0)
 
 
 def solution(mesh):

time: 246 us -> 257 us (1.045)
  blocking collectives: 0 us -> 35.1 us
  waiting for transfers between devices: 144 us -> 118 us
    all_to_all x0 -> x1, blocking collectives: none -> 35.1 us  [shards(): lax.all_to_all(spread, 'head', split_axis=1, concat_axis=1, tiled=True)]
    reduce_scatter x1, waiting for transfers between devices: 65.8 us -> 39.9 us  [shards(): lax.psum_scatter(both[half:], 'head', scatter_dimension=1, tiled=True)]
  transfers between devices with their start and end apart: 5 -> 5, of which waited for: 4 -> 4; matrix products, arithmetic and copies ran while one was open for 24% -> 23% of each run, Pallas kernels for 4% -> 4%
where the time goes in v15:
time: 257 us; the launch traced here: 256 us
  waiting for transfers between devices  118 us (46%)
  blocking collectives  35.1 us (14%)
  matrix products  35 us (14%)
  local copies, waits for them, and re-layouts  21.8 us (8%)
  between operations  13.3 us (5%)
  starting transfers between devices  12.6 us (5%)
  Pallas kernels  10.4 us (4%)
  other arithmetic  9.78 us (4%)
    reduce_scatter x1, waiting for transfers between devices, shards(): lax.psum_scatter(both[half:], 'head', scatter_dimension=1, tiled=True)  39.9 us
    all_gather x1, waiting for transfers between devices, shards(): gathered = lax.all_gather(states, 'head', axis=1, tiled=True)  37.4 us
    all_to_all x1, blocking collectives, shards(): lax.all_to_all(spread, 'head', split_axis=1, concat_axis=1, tiled=True)  35.1 us
    all_to_all x1, waiting for transfers between devices, gather_by_all_to_all(): return lax.all_to_all(copies, axis, split_axis=0, concat_axis=0, tiled=True)  23.1 us
    dot_general x1, matrix products, feed(): jnp.dot(hidden, down_weight, preferred_element_type=jnp.float32)  21.6 us
    all_to_all x1, waiting for transfers between devices, share_pages(): lax.all_to_all(grouped, 'head', split_axis=3, concat_axis=0, tiled=True)  16.5 us
    pallas_call x1, Pallas kernels, attend_kernel(): pl.pallas_call(attention_kernel, grid=(heads,), in_specs=[row_block, page...  10.4 us
    dot_general x1, matrix products, shards(): joined = jnp.dot(pre_normed, qkv_full, preferred_element_type=jnp.float32)  9.15 us
  transfers between devices with their start and end apart: 5, of which 4 were waited for; matrix products, arithmetic and copies ran while one was open for 23% of the time, Pallas kernels for 4%

profile of v15, /device:TPU:0, one launch (start us, length us, event | category | flops | bytes accessed | tf_op | source)
XLA Modules:
  0.0 256.4 jit_solution(16587619254638261762)
XLA Ops:
  6.5 0.0 all-gather.3.cloned.1.call-start
  6.5 0.7 all-gather.3.cloned.1.call-update
  7.3 4.2 %broadcast_in_dim.38 = bf16[8,512,768]{2,1,0:T(8,128)(2,1)} broadcast(bf16[512,768]{1,0:T(8,128)(2,1)} %param.23), dimensions={1,2} | broadcast | bytes 7077888 | tf_op jit(solution)/shard_map/broadcast_in_dim | solution.py:142
  11.4 0.0 copy-start.13
  11.4 8.2 %all-to-all-start = ((bf16[8,512,768]{2,1,0:T(8,128)(2,1)}), bf16[8,512,768]{2,1,0:T(8,128)(2,1)}, u32[]{:S(2)}, u32[]{:S(2)}) async-start(bf16[8,512,768]{2,1,0:T(8,128)(2,1)} %broadcast_in_dim.38), calls=%async_computation | async-start | bytes 12582912 | tf_op jit(solution)/shard_map/all_to_all | solution.py:145
  19.6 0.0 all-gather.5.cloned.1.call-start
  19.7 0.7 all-gather.5.cloned.1.call-update
  20.4 0.0 copy-done.13
  20.4 0.1 eq.33
  20.5 0.1 reshape.196
  20.5 0.0 copy-done.3
  20.5 0.1 convert_reduce_fusion.1
  20.7 0.2 reduce-window.8
  20.9 0.0 copy-done.2
  20.9 0.6 fusion.107
  21.4 0.1 select_reduce_fusion.1
  21.5 1.3 fusion.70
  22.8 1.3 fusion.71
  24.1 0.9 copy.56.hi_col
  25.0 0.9 copy.57.start_col
  25.8 0.9 copy.55.lo_col
  26.7 0.0 copy-done.6
  26.7 0.1 compare_reduce_fusion
  26.8 0.1 fusion.69
  26.9 37.4 %all-gather.3.cloned.1.call-done = bf16[512,4096]{1,0:T(8,128)(2,1)} async-done(((bf16[512,256]{1,0:T(8,128)(2,1)}), bf16[512,4096]{1,0:T(8,128)(2,1)}) %all-gather.3.cloned.1.call-update) | async-done | bytes 4194320 | tf_op jit(solution)/shard_map/all_gather | solution.py:168
  64.3 3.0 %convert_reduce_fusion = f32[512]{0:T(512)S(1)} fusion(bf16[512,4096]{1,0:T(8,128)(2,1)} %all-gather.3.cloned.1.call-done), kind=kLoop, calls=%fused_computation.2 | loop fusion | flops 4193792 | bytes 4196352 | tf_op jit(solution)/shard_map/reduce_sum | solution.py:16
  67.3 0.5 copy-done
  67.8 1.2 fusion.8
  69.0 0.0 copy-done.7
  69.0 0.0 copy-done.8
  69.0 0.0 copy-done.11
  69.0 0.0 copy-start.1
  69.0 21.6 %convolution_convert_fusion = bf16[512,4096]{1,0:T(8,128)(2,1)} fusion(bf16[1024,4096]{1,0:T(8,128)(2,1)} %param.29, bf16[4096,1024]{1,0:T(8,128)(2,1)} %param.27, bf16[512,4096]{1,0:T(8,128)(2,1)} %all-gather.3.cloned.1.call-done, f32[4096]{0:T(1024)S(1)} %copy-done.7, f32[4096]{0:T(1024)S(1)} %copy-done.8, f32[512]{0:T(512)S(1)} %add_rsqrt_fusion, ...), kind=kOutput, calls=%fused_computation.13 | convolution fusion | flops 8639217664 | bytes 25206784 | tf_op jit(solution)/shard_map/dot_general | solution.py:181
  90.7 0.0 copy-done.1
  90.7 1.7 copy.67
  92.4 23.1 %all-to-all-done = bf16[8,512,768]{2,1,0:T(8,128)(2,1)} async-done(((bf16[8,512,768]{2,1,0:T(8,128)(2,1)}), bf16[8,512,768]{2,1,0:T(8,128)(2,1)}, u32[]{:S(2)}, u32[]{:S(2)}) %all-to-all-start) | async-done | bytes 6291488 | tf_op jit(solution)/shard_map/all_to_all | solution.py:145
  115.6 0.0 copy-start.12
  115.6 4.4 %all-to-all-start.1 = ((bf16[9,2,16,16,256]{4,2,1,0,3:T(8,128)(2,1)}), bf16[9,2,16,16,256]{4,2,1,0,3:T(8,128)(2,1)S(1)}, u32[]{:S(2)}, u32[]{:S(2)}) async-start(bf16[9,2,16,16,256]{4,2,1,0,3:T(8,128)(2,1)} %bitcast.51), calls=%async_computation.1 | async-start | bytes 4718592 | tf_op jit(solution)/shard_map/all_to_all | solution.py:136
  120.0 0.0 reduce-scatter.2.cloned.1.call-start
  120.1 0.0 copy-done.4
  120.1 0.0 copy-done.5
  120.1 0.3 add_dynamic-update-slice_fusion
  120.3 0.2 multiply_cosine_fusion
  120.5 0.0 copy-done.9
  120.6 0.0 copy-done.10
  120.6 0.0 copy-done.12
  120.6 9.2 %fusion.35 = f32[512,768]{1,0:T(8,128)} fusion(bf16[4096,768]{1,0:T(8,128)(2,1)} %bitcast, bf16[512,4096]{1,0:T(8,128)(2,1)} %all-gather.3.cloned.1.call-done, f32[4096]{0:T(1024)S(1)} %copy-done.9, f32[4096]{0:T(1024)S(1)} %copy-done.10, f32[512]{0:T(512)S(1)} %add_rsqrt_fusion, f32[512]{0:T(512)S(1)} %broadcast_multiply_fusion.1, f32[768]{0:T(1024)S(1)} %copy-done.12), kind=kOutput, calls=%fused_computation.45 | convolution fusion | flops 3234201600 | bytes 12098560 | tf_op jit(solution)/shard_map/dot_general | solution.py:186
  129.7 3.0 %copy.49 = f32[512,768]{0,1:T(8,128)} copy(f32[512,768]{1,0:T(8,128)} %fusion.35) | data formatting | bytes 3145728 | tf_op jit(solution)/shard_map/add | solution.py:187
  132.8 1.1 slice.86
  133.8 1.3 slice_bitcast_fusion
  135.3 0.8 copy.59.q_ref
  136.1 0.8 copy.60.kn_ref
  137.0 0.8 copy.61.vn_ref
  137.8 16.5 %all-to-all-done.1 = bf16[9,2,16,16,256]{4,2,1,0,3:T(8,128)(2,1)S(1)} async-done(((bf16[9,2,16,16,256]{4,2,1,0,3:T(8,128)(2,1)}), bf16[9,2,16,16,256]{4,2,1,0,3:T(8,128)(2,1)S(1)}, u32[]{:S(2)}, u32[]{:S(2)}) %all-to-all-start.1) | async-done | bytes 2359328 | tf_op jit(solution)/shard_map/all_to_all | solution.py:136
  154.3 2.0 gather_fusion
  156.4 10.4 %shard_map.172 = bf16[512,256]{1,0:T(8,128)(2,1)} custom-call(bf16[512,256]{1,0:T(8,128)(2,1)} %copy.59.q_ref, bf16[128,2,16,256]{3,2,1,0:T(8,128)(2,1)} %gather_fusion, bf16[128,2,16,256]{3,2,1,0:T(8,128)(2,1)} %gather_fusion, bf16[512,256]{1,0:T(8,128)(2,1)} %copy.60.kn_ref, bf16[512,256]{1,0:T(8,128)(2,1)} %copy.61.vn_ref, s32[512,1]{1,0:T(8,128)} %copy.55.lo_col, ...), custom_call_target="tpu_custom_call" | custom-call | flops 1342177280 | bytes 3145728 | tf_op jit(solution)/shard_map/pallas_call | solution.py:116
  166.8 4.2 %add_convert_fusion = bf16[512,4096]{1,0:T(8,128)(2,1)S(1)} fusion(bf16[512,4096]{1,0:T(8,128)(2,1)} %convolution_convert_fusion, bf16[512,256]{1,0:T(8,128)(2,1)} %shard_map.172, bf16[256,4096]{1,0:T(8,128)(2,1)} %all-gather.5.cloned.1.call-done, f32[4096]{0:T(1024)S(1)} %add_dynamic-update-slice_fusion), kind=kOutput, calls=%fused_computation.12 | convolution fusion | flops 1082130432 | bytes 10764288 | tf_op jit(solution)/shard_map/dot_general | solution.py:203
  171.0 1.7 fusion.106
  172.7 0.0 reduce-scatter.2.cloned.1.call-update
  172.7 0.2 copy.68
  172.9 35.1 %all_to_all.29 = bf16[256,16,256]{2,0,1:T(8,128)(2,1)S(1)} all-to-all(bf16[256,16,256]{2,0,1:T(8,128)(2,1)S(1)} %bitcast.54), channel_id=1, replica_groups=mesh['tok'=8,'head'=16] {'head'}, dimensions={1} | all-to-all | bytes 4194304 | tf_op jit(solution)/shard_map/all_to_all | solution.py:215
  208.0 0.3 reduce_sum.83
  208.3 39.9 %reduce-scatter.2.cloned.1.call-done = bf16[256,256]{1,0:T(8,128)(2,1)} async-done(((bf16[256,4096]{1,0:T(8,128)(2,1)}), bf16[256,256]{1,0:T(8,128)(2,1)}) %reduce-scatter.2.cloned.1.call-update) | async-done | bytes 131088 | tf_op jit(solution)/shard_map/reduce_scatter | solution.py:213
  248.3 1.6 pad_maximum_fusion.2
  (25 shorter events, 0.2 us)
Async XLA Ops:
  6.5 57.8 %all-gather.3.cloned.1.call-start = ((), (), s32[]{:S(2)}) async-start(), calls=%async_computation.4 | async-start | bytes 4456448 | tf_op jit(solution)/shard_map/all_gather | solution.py:168
  11.4 8.9 %copy-start.13 = (s32[2,64]{1,0:T(2,128)S(1)}, s32[2,64]{1,0:T(2,128)}, u32[]{:S(2)}) copy-start(s32[2,64]{1,0:T(2,128)} %param.34) | copy-start | bytes 1540
  11.4 9.1 %copy-start.3 = (s32[512]{0:T(512)S(1)}, s32[512]{0:T(512)}, u32[]{:S(2)}) copy-start(s32[512]{0:T(512)} %param.32) | copy-start | bytes 6148
  11.4 9.4 %copy-start.2 = (s32[2]{0:T(128)S(1)}, s32[2]{0:T(128)}, u32[]{:S(2)}) copy-start(s32[2]{0:T(128)} %param.33) | copy-start | bytes 28
  11.4 15.3 %copy-start.6 = (s32[8,2]{0,1:T(2,128)S(1)}, s32[8,2]{0,1:T(2,128)}, u32[]{:S(2)}) copy-start(s32[8,2]{0,1:T(2,128)} %param.35) | copy-start | bytes 196
  11.4 104.1 %all-to-all-start = ((bf16[8,512,768]{2,1,0:T(8,128)(2,1)}), bf16[8,512,768]{2,1,0:T(8,128)(2,1)}, u32[]{:S(2)}, u32[]{:S(2)}) async-start(bf16[8,512,768]{2,1,0:T(8,128)(2,1)} %broadcast_in_dim.38), calls=%async_computation | async-start | bytes 12582912 | tf_op jit(solution)/shard_map/all_to_all | solution.py:145
  19.6 147.2 %all-gather.5.cloned.1.call-start = ((), (), s32[]{:S(2)}) async-start(), calls=%async_computation.5 | async-start | bytes 2359296 | tf_op jit(solution)/shard_map/all_gather | solution.py:170
  64.3 3.4 %copy-start = (bf16[512,4096]{1,0:T(8,128)(2,1)S(1)}, bf16[512,4096]{1,0:T(8,128)(2,1)}, u32[]{:S(2)}) copy-start(bf16[512,4096]{1,0:T(8,128)(2,1)} %all-gather.3.cloned.1.call-done) | copy-start | bytes 12582916
  67.7 1.2 copy-start.7
  67.7 1.2 copy-start.8
  67.8 1.3 copy-start.11
  69.0 21.7 %copy-start.1 = (bf16[9,2,16,4096]{3,2,1,0:T(8,128)(2,1)S(1)}, bf16[9,2,16,4096]{3,2,1,0:T(8,128)(2,1)}, u32[]{:S(2)}) copy-start(bf16[9,2,16,4096]{3,2,1,0:T(8,128)(2,1)} %param.31) | copy-start | bytes 7077892
  115.6 4.5 %copy-start.4 = (f32[256]{0:T(256)S(1)}, f32[256]{0:T(256)}, u32[]{:S(2)}) copy-start(f32[256]{0:T(256)} %param.26) | copy-start | bytes 3076
  115.6 4.5 %copy-start.5 = (f32[256]{0:T(256)S(1)}, f32[256]{0:T(256)}, u32[]{:S(2)}) copy-start(f32[256]{0:T(256)} %param.30) | copy-start | bytes 3076
  115.6 5.0 %copy-start.9 = (f32[4096]{0:T(1024)S(1)}, f32[4096]{0:T(1024)}, u32[]{:S(2)}) copy-start(f32[4096]{0:T(1024)} %param.20) | copy-start | bytes 49156
  115.6 5.0 %copy-start.10 = (f32[4096]{0:T(1024)S(1)}, f32[4096]{0:T(1024)}, u32[]{:S(2)}) copy-start(f32[4096]{0:T(1024)} %param.19) | copy-start | bytes 49156
  115.6 5.0 %copy-start.12 = (f32[768]{0:T(1024)S(1)}, f32[768]{0:T(1024)}, u32[]{:S(2)}) copy-start(f32[768]{0:T(1024)} %param.24) | copy-start | bytes 9220
  115.6 38.7 %all-to-all-start.1 = ((bf16[9,2,16,16,256]{4,2,1,0,3:T(8,128)(2,1)}), bf16[9,2,16,16,256]{4,2,1,0,3:T(8,128)(2,1)S(1)}, u32[]{:S(2)}, u32[]{:S(2)}) async-start(bf16[9,2,16,16,256]{4,2,1,0,3:T(8,128)(2,1)} %bitcast.51), calls=%async_computation.1 | async-start | bytes 4718592 | tf_op jit(solution)/shard_map/all_to_all | solution.py:136
  120.0 128.3 %reduce-scatter.2.cloned.1.call-start = ((), (), s32[]{:S(2)}) async-start(), calls=%async_computation.6 | async-start | bytes 2228224 | tf_op jit(solution)/shard_map/reduce_scatter | solution.py:213
Sparse Core Ops, SparseCore 0:
  9.0 55.2 all-gather.2
  66.5 97.6 all-gather.4
  172.9 75.3 reduce-scatter.1

commit v16 on v13

--- a/solution.py
+++ b/solution.py
@@ -81,7 +81,7 @@
     cache_slot = lax.broadcasted_iota(jnp.int32, cache_scores.shape, 1)
     cache_ok = (cache_slot >= lo_col[...]) & (cache_slot < hi_col[...])
     new_slot = lax.broadcasted_iota(jnp.int32, new_scores.shape, 1)
-    own_slot = lax.broadcasted_iota(jnp.int32, new_scores.shape, 0)
+    own_slot = lax.broadcasted_iota(jnp.int32, new_scores.shape, 0) + pl.program_id(1) * queries.shape[0]
     new_ok = (new_slot >= start_col[...]) & (new_slot <= own_slot)
     cache_scores = jnp.where(cache_ok, cache_scores, -1e30)
     new_scores = jnp.where(new_ok, new_scores, -1e30)
@@ -108,17 +108,19 @@
     hi_col = lo_col + own_cached[:, None]
     start_col = (jnp.arange(tokens, dtype=jnp.int32) - positions + own_cached)[:, None]
     flat = lambda x: x.reshape(tokens, heads * HD)
-    row_block = pl.BlockSpec((tokens, HD), lambda h: (0, h))
-    page_block = lambda part: pl.BlockSpec((page_count, 1, page_len, HD), lambda h: (0, part, 0, h))
-    whole = lambda x: pl.BlockSpec(x.shape, lambda h: (0,) * x.ndim)
+    rows = tokens // 2
+    tile_block = pl.BlockSpec((rows, HD), lambda h, i: (i, h))
+    row_block = pl.BlockSpec((tokens, HD), lambda h, i: (0, h))
+    page_block = lambda part: pl.BlockSpec((page_count, 1, page_len, HD), lambda h, i: (0, part, 0, h))
+    column = lambda x: pl.BlockSpec((rows, 1), lambda h, i: (i, 0))
     extras = (lo_col, hi_col, start_col)
     keys_seen = page_count * page_len + tokens
     out = pl.pallas_call(
         attention_kernel,
-        grid=(heads,),
-        in_specs=[row_block, page_block(0), page_block(1), row_block, row_block]
-        + [whole(x) for x in extras],
-        out_specs=row_block,
+        grid=(heads, 2),
+        in_specs=[tile_block, page_block(0), page_block(1), row_block, row_block]
+        + [column(x) for x in extras],
+        out_specs=tile_block,
         out_shape=jax.ShapeDtypeStruct((tokens, heads * HD), jnp.bfloat16),
         cost_estimate=pl.CostEstimate(
             flops=4 * heads * tokens * keys_seen * HD,

time: 246 us -> 246 us (level)
  no operation moved by 1% of the time
where the time goes in v16:
time: 246 us; the launch traced here: 245 us
  waiting for transfers between devices  145 us (59%)
  matrix products  36.9 us (15%)
  local copies, waits for them, and re-layouts  19.9 us (8%)
  between operations  13.3 us (5%)
  starting transfers between devices  12.6 us (5%)
  Pallas kernels  9.38 us (4%)
  other arithmetic  7.99 us (3%)
    reduce_scatter x1, waiting for transfers between devices, shards(): lax.psum_scatter((attention_part + feed_part + bias_row).astype(jnp.bfloa...  66.7 us
    all_gather x1, waiting for transfers between devices, shards(): gathered = lax.all_gather(states, 'head', axis=1, tiled=True)  37.1 us
    all_to_all x1, waiting for transfers between devices, gather_by_all_to_all(): return lax.all_to_all(copies, axis, split_axis=0, concat_axis=0, tiled=True)  23.3 us
    dot_general x1, matrix products, feed(): jnp.dot(hidden, down_weight, preferred_element_type=jnp.float32)  21.6 us
    all_to_all x1, waiting for transfers between devices, share_pages(): lax.all_to_all(grouped, 'head', split_axis=3, concat_axis=0, tiled=True)  16.5 us
    pallas_call x1, Pallas kernels, attend_kernel(): pl.pallas_call(attention_kernel, grid=(heads, 2), in_specs=[tile_block, p...  9.38 us
    dot_general x1, matrix products, shards(): joined = jnp.dot(pre_normed, qkv_full, preferred_element_type=jnp.float32)  9.16 us
    all_to_all x1, starting transfers between devices, gather_by_all_to_all(): return lax.all_to_all(copies, axis, split_axis=0, concat_axis=0, tiled=True)  8.17 us
  transfers between devices with their start and end apart: 5, of which 4 were waited for; matrix products, arithmetic and copies ran while one was open for 24% of the time, Pallas kernels for 4%

profile of v16, /device:TPU:0, one launch (start us, length us, event | category | flops | bytes accessed | tf_op | source)
XLA Modules:
  0.0 245.1 jit_solution(15627110449093715719)
XLA Ops:
  6.5 0.0 all-gather.3.cloned.1.call-start
  6.5 0.7 all-gather.3.cloned.1.call-update
  7.3 4.2 %broadcast_in_dim.38 = bf16[8,512,768]{2,1,0:T(8,128)(2,1)} broadcast(bf16[512,768]{1,0:T(8,128)(2,1)} %param.23), dimensions={1,2} | broadcast | bytes 7077888 | tf_op jit(solution)/shard_map/broadcast_in_dim | solution.py:144
  11.4 0.0 copy-start.13
  11.4 0.0 copy-start.3
  11.4 0.0 copy-start.2
  11.4 0.0 copy-start.6
  11.5 8.2 %all-to-all-start = ((bf16[8,512,768]{2,1,0:T(8,128)(2,1)}), bf16[8,512,768]{2,1,0:T(8,128)(2,1)}, u32[]{:S(2)}, u32[]{:S(2)}) async-start(bf16[8,512,768]{2,1,0:T(8,128)(2,1)} %broadcast_in_dim.38), calls=%async_computation | async-start | bytes 12582912 | tf_op jit(solution)/shard_map/all_to_all | solution.py:147
  19.6 0.0 all-gather.5.cloned.1.call-start
  19.7 0.7 all-gather.5.cloned.1.call-update
  20.4 0.0 copy-done.13
  20.4 0.1 eq.33
  20.5 0.1 reshape.193
  20.5 0.0 copy-done.3
  20.6 0.1 convert_reduce_fusion.1
  20.7 0.2 reduce-window.8
  20.9 0.0 copy-done.2
  20.9 0.7 fusion.106
  21.5 0.1 select_reduce_fusion.1
  21.6 1.3 fusion.70
  22.9 1.3 fusion.71
  24.3 0.9 copy.55.hi_col
  25.2 0.9 copy.56.start_col
  26.0 0.9 copy.54.lo_col
  26.9 0.0 copy-done.6
  26.9 0.1 compare_reduce_fusion
  27.0 0.1 fusion.69
  27.1 37.1 %all-gather.3.cloned.1.call-done = bf16[512,4096]{1,0:T(8,128)(2,1)} async-done(((bf16[512,256]{1,0:T(8,128)(2,1)}), bf16[512,4096]{1,0:T(8,128)(2,1)}) %all-gather.3.cloned.1.call-update) | async-done | bytes 4194320 | tf_op jit(solution)/shard_map/all_gather | solution.py:170
  64.2 0.0 copy-start
  64.2 3.0 %convert_reduce_fusion = f32[512]{0:T(512)S(1)} fusion(bf16[512,4096]{1,0:T(8,128)(2,1)} %all-gather.3.cloned.1.call-done), kind=kLoop, calls=%fused_computation.2 | loop fusion | flops 4193792 | bytes 4196352 | tf_op jit(solution)/shard_map/reduce_sum | solution.py:16
  67.1 0.5 copy-done
  67.6 0.0 copy-start.7
  67.6 1.2 fusion.8
  68.8 0.0 copy-done.7
  68.9 0.0 copy-done.8
  68.9 0.0 copy-done.11
  68.9 0.0 copy-start.1
  68.9 21.6 %convolution_convert_fusion = bf16[512,4096]{1,0:T(8,128)(2,1)} fusion(bf16[1024,4096]{1,0:T(8,128)(2,1)} %param.29, bf16[4096,1024]{1,0:T(8,128)(2,1)} %param.27, bf16[512,4096]{1,0:T(8,128)(2,1)} %all-gather.3.cloned.1.call-done, f32[4096]{0:T(1024)S(1)} %copy-done.7, f32[4096]{0:T(1024)S(1)} %copy-done.8, f32[512]{0:T(512)S(1)} %add_rsqrt_fusion, ...), kind=kOutput, calls=%fused_computation.13 | convolution fusion | flops 8639217664 | bytes 25206784 | tf_op jit(solution)/shard_map/dot_general | solution.py:183
  90.5 0.0 copy-done.1
  90.5 1.8 copy.63
  92.3 23.3 %all-to-all-done = bf16[8,512,768]{2,1,0:T(8,128)(2,1)} async-done(((bf16[8,512,768]{2,1,0:T(8,128)(2,1)}), bf16[8,512,768]{2,1,0:T(8,128)(2,1)}, u32[]{:S(2)}, u32[]{:S(2)}) %all-to-all-start) | async-done | bytes 6291488 | tf_op jit(solution)/shard_map/all_to_all | solution.py:147
  115.6 0.0 copy-start.12
  115.6 4.4 %all-to-all-start.1 = ((bf16[9,2,16,16,256]{4,2,1,0,3:T(8,128)(2,1)}), bf16[9,2,16,16,256]{4,2,1,0,3:T(8,128)(2,1)S(1)}, u32[]{:S(2)}, u32[]{:S(2)}) async-start(bf16[9,2,16,16,256]{4,2,1,0,3:T(8,128)(2,1)} %bitcast.48), calls=%async_computation.1 | async-start | bytes 4718592 | tf_op jit(solution)/shard_map/all_to_all | solution.py:138
  120.0 0.0 reduce-scatter.2.cloned.1.call-start
  120.1 0.0 copy-done.4
  120.1 0.0 copy-done.5
  120.1 0.3 add_dynamic-update-slice_fusion
  120.4 0.2 multiply_cosine_fusion
  120.6 0.0 copy-done.9
  120.6 0.0 copy-done.10
  120.6 0.0 copy-done.12
  120.6 9.2 %fusion.35 = f32[512,768]{1,0:T(8,128)} fusion(bf16[4096,768]{1,0:T(8,128)(2,1)} %bitcast, bf16[512,4096]{1,0:T(8,128)(2,1)} %all-gather.3.cloned.1.call-done, f32[4096]{0:T(1024)S(1)} %copy-done.9, f32[4096]{0:T(1024)S(1)} %copy-done.10, f32[512]{0:T(512)S(1)} %add_rsqrt_fusion, f32[512]{0:T(512)S(1)} %broadcast_multiply_fusion.1, f32[768]{0:T(1024)S(1)} %copy-done.12), kind=kOutput, calls=%fused_computation.44 | convolution fusion | flops 3234201600 | bytes 12098560 | tf_op jit(solution)/shard_map/dot_general | solution.py:188
  129.7 3.0 %copy.48 = f32[512,768]{0,1:T(8,128)} copy(f32[512,768]{1,0:T(8,128)} %fusion.35) | data formatting | bytes 3145728 | tf_op jit(solution)/shard_map/add | solution.py:189
  132.8 1.1 slice.76
  133.9 1.3 slice_bitcast_fusion
  135.3 0.8 copy.57.q_ref
  136.1 0.8 copy.58.kn_ref
  137.0 0.8 copy.59.vn_ref
  137.8 16.5 %all-to-all-done.1 = bf16[9,2,16,16,256]{4,2,1,0,3:T(8,128)(2,1)S(1)} async-done(((bf16[9,2,16,16,256]{4,2,1,0,3:T(8,128)(2,1)}), bf16[9,2,16,16,256]{4,2,1,0,3:T(8,128)(2,1)S(1)}, u32[]{:S(2)}, u32[]{:S(2)}) %all-to-all-start.1) | async-done | bytes 2359328 | tf_op jit(solution)/shard_map/all_to_all | solution.py:138
  154.3 2.0 gather_fusion
  156.4 9.4 %shard_map.172 = bf16[512,256]{1,0:T(8,128)(2,1)} custom-call(bf16[512,256]{1,0:T(8,128)(2,1)} %copy.57.q_ref, bf16[128,2,16,256]{3,2,1,0:T(8,128)(2,1)} %gather_fusion, bf16[128,2,16,256]{3,2,1,0:T(8,128)(2,1)} %gather_fusion, bf16[512,256]{1,0:T(8,128)(2,1)} %copy.58.kn_ref, bf16[512,256]{1,0:T(8,128)(2,1)} %copy.59.vn_ref, s32[512,1]{1,0:T(8,128)} %copy.54.lo_col, ...), custom_call_target="tpu_custom_call" | custom-call | flops 1342177280 | bytes 3145728 | tf_op jit(solution)/shard_map/pallas_call | solution.py:118
  165.7 6.1 %add_convert_fusion = bf16[512,4096]{1,0:T(8,128)(2,1)} fusion(bf16[512,4096]{1,0:T(8,128)(2,1)} %convolution_convert_fusion, bf16[512,256]{1,0:T(8,128)(2,1)} %shard_map.172, bf16[256,4096]{1,0:T(8,128)(2,1)} %all-gather.5.cloned.1.call-done, f32[4096]{0:T(1024)S(1)} %add_dynamic-update-slice_fusion), kind=kOutput, calls=%fused_computation.12 | convolution fusion | flops 1082130432 | bytes 10764288 | tf_op jit(solution)/shard_map/dot_general | solution.py:205
  171.8 0.0 reduce-scatter.2.cloned.1.call-update
  171.9 66.7 %reduce-scatter.2.cloned.1.call-done = bf16[512,256]{1,0:T(8,128)(2,1)} async-done(((bf16[512,4096]{1,0:T(8,128)(2,1)}), bf16[512,256]{1,0:T(8,128)(2,1)}) %reduce-scatter.2.cloned.1.call-update) | async-done | bytes 262160 | tf_op jit(solution)/shard_map/reduce_scatter | solution.py:212
  (20 shorter events, 0.2 us)
Async XLA Ops:
  6.5 57.6 %all-gather.3.cloned.1.call-start = ((), (), s32[]{:S(2)}) async-start(), calls=%async_computation.3 | async-start | bytes 4456448 | tf_op jit(solution)/shard_map/all_gather | solution.py:170
  11.4 8.9 %copy-start.13 = (s32[2,64]{1,0:T(2,128)S(1)}, s32[2,64]{1,0:T(2,128)}, u32[]{:S(2)}) copy-start(s32[2,64]{1,0:T(2,128)} %param.34) | copy-start | bytes 1540
  11.4 9.1 %copy-start.3 = (s32[512]{0:T(512)S(1)}, s32[512]{0:T(512)}, u32[]{:S(2)}) copy-start(s32[512]{0:T(512)} %param.32) | copy-start | bytes 6148
  11.4 9.4 %copy-start.2 = (s32[2]{0:T(128)S(1)}, s32[2]{0:T(128)}, u32[]{:S(2)}) copy-start(s32[2]{0:T(128)} %param.33) | copy-start | bytes 28
  11.4 15.4 %copy-start.6 = (s32[8,2]{0,1:T(2,128)S(1)}, s32[8,2]{0,1:T(2,128)}, u32[]{:S(2)}) copy-start(s32[8,2]{0,1:T(2,128)} %param.35) | copy-start | bytes 196
  11.5 104.1 %all-to-all-start = ((bf16[8,512,768]{2,1,0:T(8,128)(2,1)}), bf16[8,512,768]{2,1,0:T(8,128)(2,1)}, u32[]{:S(2)}, u32[]{:S(2)}) async-start(bf16[8,512,768]{2,1,0:T(8,128)(2,1)} %broadcast_in_dim.38), calls=%async_computation | async-start | bytes 12582912 | tf_op jit(solution)/shard_map/all_to_all | solution.py:147
  19.6 146.1 %all-gather.5.cloned.1.call-start = ((), (), s32[]{:S(2)}) async-start(), calls=%async_computation.4 | async-start | bytes 2359296 | tf_op jit(solution)/shard_map/all_gather | solution.py:172
  64.2 3.4 %copy-start = (bf16[512,4096]{1,0:T(8,128)(2,1)S(1)}, bf16[512,4096]{1,0:T(8,128)(2,1)}, u32[]{:S(2)}) copy-start(bf16[512,4096]{1,0:T(8,128)(2,1)} %all-gather.3.cloned.1.call-done) | copy-start | bytes 12582916
  67.6 1.2 copy-start.7
  67.6 1.2 copy-start.8
  67.6 1.3 copy-start.11
  68.9 21.6 %copy-start.1 = (bf16[9,2,16,4096]{3,2,1,0:T(8,128)(2,1)S(1)}, bf16[9,2,16,4096]{3,2,1,0:T(8,128)(2,1)}, u32[]{:S(2)}) copy-start(bf16[9,2,16,4096]{3,2,1,0:T(8,128)(2,1)} %param.31) | copy-start | bytes 7077892
  115.6 4.5 %copy-start.4 = (f32[256]{0:T(256)S(1)}, f32[256]{0:T(256)}, u32[]{:S(2)}) copy-start(f32[256]{0:T(256)} %param.26) | copy-start | bytes 3076
  115.6 4.5 %copy-start.5 = (f32[256]{0:T(256)S(1)}, f32[256]{0:T(256)}, u32[]{:S(2)}) copy-start(f32[256]{0:T(256)} %param.30) | copy-start | bytes 3076
  115.6 5.0 %copy-start.9 = (f32[4096]{0:T(1024)S(1)}, f32[4096]{0:T(1024)}, u32[]{:S(2)}) copy-start(f32[4096]{0:T(1024)} %param.20) | copy-start | bytes 49156
  115.6 5.0 %copy-start.10 = (f32[4096]{0:T(1024)S(1)}, f32[4096]{0:T(1024)}, u32[]{:S(2)}) copy-start(f32[4096]{0:T(1024)} %param.19) | copy-start | bytes 49156
  115.6 5.0 %copy-start.12 = (f32[768]{0:T(1024)S(1)}, f32[768]{0:T(1024)}, u32[]{:S(2)}) copy-start(f32[768]{0:T(1024)} %param.24) | copy-start | bytes 9220
  115.6 38.7 %all-to-all-start.1 = ((bf16[9,2,16,16,256]{4,2,1,0,3:T(8,128)(2,1)}), bf16[9,2,16,16,256]{4,2,1,0,3:T(8,128)(2,1)S(1)}, u32[]{:S(2)}, u32[]{:S(2)}) async-start(bf16[9,2,16,16,256]{4,2,1,0,3:T(8,128)(2,1)} %bitcast.48), calls=%async_computation.1 | async-start | bytes 4718592 | tf_op jit(solution)/shard_map/all_to_all | solution.py:138
  120.0 118.6 %reduce-scatter.2.cloned.1.call-start = ((), (), s32[]{:S(2)}) async-start(), calls=%async_computation.5 | async-start | bytes 4456448 | tf_op jit(solution)/shard_map/reduce_scatter | solution.py:212
Sparse Core Ops, SparseCore 0:
  9.0 55.1 all-gather.2
  66.3 97.8 all-gather.4
  172.0 66.5 reduce-scatter.1

commit v17 on v16

--- a/solution.py
+++ b/solution.py
@@ -168,6 +168,8 @@
     migrations,
 ):
     gathered = lax.all_gather(states, "head", axis=1, tiled=True)
+    page_pool = share_pages(kv_cache, lax.axis_size("head"))
+    qkv_weight, page_pool = lax.optimization_barrier((qkv_weight, page_pool))
     qkv_full = gather_by_all_to_all(qkv_weight, "tok")
     out_full = lax.all_gather(out_weight, "tok", axis=1, tiled=True)
     wide = gathered.astype(jnp.float32)
@@ -183,8 +185,7 @@
         return jnp.dot(hidden, down_weight, preferred_element_type=jnp.float32).astype(jnp.bfloat16)
 
     feed_part = feed(mlp_normed)
-    kv_cache, feed_part = lax.optimization_barrier((kv_cache, feed_part))
-    page_pool = share_pages(kv_cache, lax.axis_size("head"))
+    qkv_full, feed_part = lax.optimization_barrier((qkv_full, feed_part))
     joined = jnp.dot(pre_normed, qkv_full, preferred_element_type=jnp.float32)
     joined = (joined + qkv_bias).reshape(tok_rows, -1, 3, HD)
     local_req = token_request - lax.axis_index("tok") * cached_len.shape[0]

time: 246 us -> 253 us (1.028)
  waiting for transfers between devices: 145 us -> 157 us
  local copies, waits for them, and re-layouts: 19.9 us -> 15.6 us
    all_gather x1, waiting for transfers between devices: 37.1 us -> 13.2 us  [shards(): gathered = lax.all_gather(states, 'head', axis=1, tiled=True)]
    all_to_all x1, waiting for transfers between devices: 23.3 us -> 41.1 us  [gather_by_all_to_all(): return lax.all_to_all(copies, axis, split_axis=0, concat_axis=0, tiled=True)]
    all_to_all x1, waiting for transfers between devices: 16.5 us -> 27.9 us  [share_pages(): lax.all_to_all(grouped, 'head', split_axis=3, concat_axis=0, tiled=True)]
    all_gather x1, waiting for transfers between devices: 0.01 us -> 8.07 us  [shards(): out_full = lax.all_gather(out_weight, 'tok', axis=1, tiled=True)]
    add x1, local copies, waits for them, and re-layouts: 3.03 us -> 0.47 us  [shards(): joined = (joined + qkv_bias).reshape(tok_rows, -1, 3, HD)]
  transfers between devices with their start and end apart: 5 -> 5, of which waited for: 4 -> 5; matrix products, arithmetic and copies ran while one was open for 24% -> 21% of each run, Pallas kernels for 4% -> 4%
where the time goes in v17:
time: 253 us; the launch traced here: 252 us
  waiting for transfers between devices  157 us (62%)
  matrix products  35.4 us (14%)
  local copies, waits for them, and re-layouts  15.6 us (6%)
  starting transfers between devices  13.6 us (5%)
  between operations  13.3 us (5%)
  Pallas kernels  9.37 us (4%)
  other arithmetic  7.75 us (3%)
    reduce_scatter x1, waiting for transfers between devices, shards(): lax.psum_scatter((attention_part + feed_part + bias_row).astype(jnp.bfloa...  65.4 us
    all_to_all x1, waiting for transfers between devices, gather_by_all_to_all(): return lax.all_to_all(copies, axis, split_axis=0, concat_axis=0, tiled=True)  41.1 us
    all_to_all x1, waiting for transfers between devices, share_pages(): lax.all_to_all(grouped, 'head', split_axis=3, concat_axis=0, tiled=True)  27.9 us
    dot_general x1, matrix products, feed(): jnp.dot(hidden, down_weight, preferred_element_type=jnp.float32)  21.7 us
    all_gather x1, waiting for transfers between devices, shards(): gathered = lax.all_gather(states, 'head', axis=1, tiled=True)  13.2 us
    pallas_call x1, Pallas kernels, attend_kernel(): pl.pallas_call(attention_kernel, grid=(heads, 2), in_specs=[tile_block, p...  9.37 us
    all_gather x1, waiting for transfers between devices, shards(): out_full = lax.all_gather(out_weight, 'tok', axis=1, tiled=True)  8.07 us
    all_to_all x1, starting transfers between devices, gather_by_all_to_all(): return lax.all_to_all(copies, axis, split_axis=0, concat_axis=0, tiled=True)  7.89 us
  transfers between devices with their start and end apart: 5, of which 5 were waited for; matrix products, arithmetic and copies ran while one was open for 21% of the time, Pallas kernels for 4%

profile of v17, /device:TPU:0, one launch (start us, length us, event | category | flops | bytes accessed | tf_op | source)
XLA Modules:
  0.0 252.2 jit_solution(15159504963739835757)
XLA Ops:
  6.5 0.0 all-gather.3.cloned.1.call-start
  6.5 0.7 all-gather.3.cloned.1.call-update
  7.3 3.4 %copy.63 = bf16[9,2,2,16,8,256]{5,4,2,1,0,3:T(8,128)(2,1)} copy(bf16[9,2,2,16,8,256]{5,4,3,2,1,0:T(8,128)(2,1)} %bitcast.52) | data formatting | bytes 4718592 | tf_op jit(solution)/shard_map/reshape | solution.py:135
  10.7 0.0 copy-start.13
  10.7 0.0 copy-start.2
  10.7 0.0 copy-start.6
  10.7 0.0 copy-start.1
  10.7 5.6 %all-to-all-start = ((bf16[9,2,16,16,256]{4,2,1,0,3:T(8,128)(2,1)}), bf16[9,2,16,16,256]{4,2,1,0,3:T(8,128)(2,1)S(1)}, u32[]{:S(2)}, u32[]{:S(2)}) async-start(bf16[9,2,16,16,256]{4,2,1,0,3:T(8,128)(2,1)} %bitcast.48), calls=%async_computation | async-start | bytes 4718592 | tf_op jit(solution)/shard_map/all_to_all | solution.py:138
  16.3 0.0 all-gather.5.cloned.1.call-start
  16.4 0.7 all-gather.5.cloned.1.call-update
  17.1 0.0 copy-done.13
  17.1 0.1 reshape.193
  17.2 0.1 eq.33
  17.3 0.0 copy-done.3
  17.3 0.9 copy.54.lo_col
  18.2 0.1 convert_reduce_fusion.1
  18.3 0.2 reduce-window.8
  18.5 0.0 copy-done.2
  18.5 0.6 fusion.106
  19.1 0.1 select_reduce_fusion.1
  19.2 1.3 fusion.70
  20.5 1.3 fusion.71
  21.8 0.9 copy.55.hi_col
  22.6 0.9 copy.56.start_col
  23.5 0.0 copy-done.6
  23.5 27.9 %all-to-all-done = bf16[9,2,16,16,256]{4,2,1,0,3:T(8,128)(2,1)S(1)} async-done(((bf16[9,2,16,16,256]{4,2,1,0,3:T(8,128)(2,1)}), bf16[9,2,16,16,256]{4,2,1,0,3:T(8,128)(2,1)S(1)}, u32[]{:S(2)}, u32[]{:S(2)}) %all-to-all-start) | async-done | bytes 2359328 | tf_op jit(solution)/shard_map/all_to_all | solution.py:138
  51.4 0.0 copy-done.1
  51.4 3.1 %broadcast_in_dim.38 = bf16[8,512,768]{2,1,0:T(8,128)(2,1)} broadcast(bf16[512,768]{1,0:T(8,128)(2,1)S(1)} %copy-done.1), dimensions={1,2} | broadcast | bytes 7077888 | tf_op jit(solution)/shard_map/broadcast_in_dim | solution.py:144
  54.5 0.0 copy-start.4
  54.5 7.9 %all-to-all-start.1 = ((bf16[8,512,768]{2,1,0:T(8,128)(2,1)}), bf16[8,512,768]{2,1,0:T(8,128)(2,1)}, u32[]{:S(2)}, u32[]{:S(2)}) async-start(bf16[8,512,768]{2,1,0:T(8,128)(2,1)} %broadcast_in_dim.38), calls=%async_computation.1 | async-start | bytes 12582912 | tf_op jit(solution)/shard_map/all_to_all | solution.py:147
  62.4 0.0 reduce-scatter.2.cloned.1.call-start
  62.4 0.1 compare_reduce_fusion
  62.5 0.1 fusion.69
  62.6 0.0 copy-done.4
  62.6 0.0 copy-done.5
  62.6 0.1 add_dynamic-update-slice_fusion
  62.8 0.2 multiply_cosine_fusion
  63.0 2.0 gather_fusion
  65.0 13.2 %all-gather.3.cloned.1.call-done = bf16[512,4096]{1,0:T(8,128)(2,1)} async-done(((bf16[512,256]{1,0:T(8,128)(2,1)}), bf16[512,4096]{1,0:T(8,128)(2,1)}) %all-gather.3.cloned.1.call-update) | async-done | bytes 4194320 | tf_op jit(solution)/shard_map/all_gather | solution.py:170
  78.2 3.0 %convert_reduce_fusion = f32[512]{0:T(512)S(1)} fusion(bf16[512,4096]{1,0:T(8,128)(2,1)} %all-gather.3.cloned.1.call-done), kind=kLoop, calls=%fused_computation.2 | loop fusion | flops 4193792 | bytes 4196352 | tf_op jit(solution)/shard_map/reduce_sum | solution.py:16
  81.2 0.5 copy-done
  81.7 1.2 fusion.8
  82.9 0.0 copy-done.7
  82.9 0.0 copy-done.8
  82.9 0.0 copy-done.11
  82.9 0.0 copy-start.9
  82.9 0.0 copy-start.10
  82.9 0.0 copy-start.12
  83.0 21.7 %convolution_convert_fusion = bf16[512,4096]{1,0:T(8,128)(2,1)} fusion(bf16[1024,4096]{1,0:T(8,128)(2,1)} %param.29, bf16[4096,1024]{1,0:T(8,128)(2,1)} %param.27, bf16[512,4096]{1,0:T(8,128)(2,1)} %all-gather.3.cloned.1.call-done, f32[4096]{0:T(1024)S(1)} %copy-done.7, f32[4096]{0:T(1024)S(1)} %copy-done.8, f32[512]{0:T(512)S(1)} %add_rsqrt_fusion, ...), kind=kOutput, calls=%fused_computation.13 | convolution fusion | flops 8639217664 | bytes 25206784 | tf_op jit(solution)/shard_map/dot_general | solution.py:185
  104.6 41.1 %all-to-all-done.1 = bf16[8,512,768]{2,1,0:T(8,128)(2,1)} async-done(((bf16[8,512,768]{2,1,0:T(8,128)(2,1)}), bf16[8,512,768]{2,1,0:T(8,128)(2,1)}, u32[]{:S(2)}, u32[]{:S(2)}) %all-to-all-start.1) | async-done | bytes 6291488 | tf_op jit(solution)/shard_map/all_to_all | solution.py:147
  145.7 0.0 copy-done.9
  145.7 0.0 copy-done.10
  145.7 0.0 copy-done.12
  145.7 7.6 %fusion.35 = f32[512,768]{1,0:T(8,128)S(1)} fusion(bf16[4096,768]{1,0:T(8,128)(2,1)} %bitcast.3, bf16[512,4096]{1,0:T(8,128)(2,1)} %all-gather.3.cloned.1.call-done, f32[4096]{0:T(1024)S(1)} %copy-done.9, f32[4096]{0:T(1024)S(1)} %copy-done.10, f32[512]{0:T(512)S(1)} %add_rsqrt_fusion, f32[512]{0:T(512)S(1)} %broadcast_multiply_fusion.1, f32[768]{0:T(1024)S(1)} %copy-done.12), kind=kOutput, calls=%fused_computation.44 | convolution fusion | flops 3234201600 | bytes 12098560 | tf_op jit(solution)/shard_map/dot_general | solution.py:189
  153.3 0.5 copy.49
  153.8 0.1 slice_bitcast_fusion
  154.1 0.8 copy.57.q_ref
  154.9 0.8 copy.58.kn_ref
  155.8 0.8 copy.59.vn_ref
  156.6 9.4 %shard_map.172 = bf16[512,256]{1,0:T(8,128)(2,1)} custom-call(bf16[512,256]{1,0:T(8,128)(2,1)} %copy.57.q_ref, bf16[128,2,16,256]{3,2,1,0:T(8,128)(2,1)} %gather_fusion, bf16[128,2,16,256]{3,2,1,0:T(8,128)(2,1)} %gather_fusion, bf16[512,256]{1,0:T(8,128)(2,1)} %copy.58.kn_ref, bf16[512,256]{1,0:T(8,128)(2,1)} %copy.59.vn_ref, s32[512,1]{1,0:T(8,128)} %copy.54.lo_col, ...), custom_call_target="tpu_custom_call" | custom-call | flops 1342177280 | bytes 3145728 | tf_op jit(solution)/shard_map/pallas_call | solution.py:118
  166.0 8.1 %all-gather.5.cloned.1.call-done = bf16[256,4096]{1,0:T(8,128)(2,1)} async-done(((bf16[256,512]{1,0:T(8,128)(2,1)}), bf16[256,4096]{1,0:T(8,128)(2,1)}) %all-gather.5.cloned.1.call-update) | async-done | bytes 2097168 | tf_op jit(solution)/shard_map/all_gather | solution.py:174
  174.0 6.1 %add_convert_fusion = bf16[512,4096]{1,0:T(8,128)(2,1)} fusion(bf16[512,4096]{1,0:T(8,128)(2,1)} %convolution_convert_fusion, bf16[512,256]{1,0:T(8,128)(2,1)} %shard_map.172, bf16[256,4096]{1,0:T(8,128)(2,1)} %all-gather.5.cloned.1.call-done, f32[4096]{0:T(1024)S(1)} %add_dynamic-update-slice_fusion), kind=kOutput, calls=%fused_computation.12 | convolution fusion | flops 1082130432 | bytes 10764288 | tf_op jit(solution)/shard_map/dot_general | solution.py:206
  180.2 0.0 reduce-scatter.2.cloned.1.call-update
  180.2 65.4 %reduce-scatter.2.cloned.1.call-done = bf16[512,256]{1,0:T(8,128)(2,1)} async-done(((bf16[512,4096]{1,0:T(8,128)(2,1)}), bf16[512,256]{1,0:T(8,128)(2,1)}) %reduce-scatter.2.cloned.1.call-update) | async-done | bytes 262160 | tf_op jit(solution)/shard_map/reduce_scatter | solution.py:213
  (20 shorter events, 0.2 us)
Async XLA Ops:
  6.5 71.7 %all-gather.3.cloned.1.call-start = ((), (), s32[]{:S(2)}) async-start(), calls=%async_computation.3 | async-start | bytes 4456448 | tf_op jit(solution)/shard_map/all_gather | solution.py:170
  10.7 6.4 %copy-start.13 = (s32[2,64]{1,0:T(2,128)S(1)}, s32[2,64]{1,0:T(2,128)}, u32[]{:S(2)}) copy-start(s32[2,64]{1,0:T(2,128)} %param.34) | copy-start | bytes 1540
  10.7 6.6 %copy-start.3 = (s32[512]{0:T(512)S(1)}, s32[512]{0:T(512)}, u32[]{:S(2)}) copy-start(s32[512]{0:T(512)} %param.32) | copy-start | bytes 6148
  10.7 7.8 %copy-start.2 = (s32[2]{0:T(128)S(1)}, s32[2]{0:T(128)}, u32[]{:S(2)}) copy-start(s32[2]{0:T(128)} %param.33) | copy-start | bytes 28
  10.7 12.8 %copy-start.6 = (s32[8,2]{0,1:T(2,128)S(1)}, s32[8,2]{0,1:T(2,128)}, u32[]{:S(2)}) copy-start(s32[8,2]{0,1:T(2,128)} %param.35) | copy-start | bytes 196
  10.7 40.7 %copy-start.1 = (bf16[512,768]{1,0:T(8,128)(2,1)S(1)}, bf16[512,768]{1,0:T(8,128)(2,1)}, u32[]{:S(2)}) copy-start(bf16[512,768]{1,0:T(8,128)(2,1)} %param.23) | copy-start | bytes 2359300
  10.7 40.7 %all-to-all-start = ((bf16[9,2,16,16,256]{4,2,1,0,3:T(8,128)(2,1)}), bf16[9,2,16,16,256]{4,2,1,0,3:T(8,128)(2,1)S(1)}, u32[]{:S(2)}, u32[]{:S(2)}) async-start(bf16[9,2,16,16,256]{4,2,1,0,3:T(8,128)(2,1)} %bitcast.48), calls=%async_computation | async-start | bytes 4718592 | tf_op jit(solution)/shard_map/all_to_all | solution.py:138
  16.3 157.7 %all-gather.5.cloned.1.call-start = ((), (), s32[]{:S(2)}) async-start(), calls=%async_computation.4 | async-start | bytes 2359296 | tf_op jit(solution)/shard_map/all_gather | solution.py:174
  54.5 8.2 %copy-start.4 = (f32[256]{0:T(256)S(1)}, f32[256]{0:T(256)}, u32[]{:S(2)}) copy-start(f32[256]{0:T(256)} %param.26) | copy-start | bytes 3076
  54.5 8.2 %copy-start.5 = (f32[256]{0:T(256)S(1)}, f32[256]{0:T(256)}, u32[]{:S(2)}) copy-start(f32[256]{0:T(256)} %param.30) | copy-start | bytes 3076
  54.5 91.2 %all-to-all-start.1 = ((bf16[8,512,768]{2,1,0:T(8,128)(2,1)}), bf16[8,512,768]{2,1,0:T(8,128)(2,1)}, u32[]{:S(2)}, u32[]{:S(2)}) async-start(bf16[8,512,768]{2,1,0:T(8,128)(2,1)} %broadcast_in_dim.38), calls=%async_computation.1 | async-start | bytes 12582912 | tf_op jit(solution)/shard_map/all_to_all | solution.py:147
  62.4 183.3 %reduce-scatter.2.cloned.1.call-start = ((), (), s32[]{:S(2)}) async-start(), calls=%async_computation.5 | async-start | bytes 4456448 | tf_op jit(solution)/shard_map/reduce_scatter | solution.py:213
  78.2 3.4 %copy-start = (bf16[512,4096]{1,0:T(8,128)(2,1)S(1)}, bf16[512,4096]{1,0:T(8,128)(2,1)}, u32[]{:S(2)}) copy-start(bf16[512,4096]{1,0:T(8,128)(2,1)} %all-gather.3.cloned.1.call-done) | copy-start | bytes 12582916
  81.6 1.2 copy-start.7
  81.6 1.2 copy-start.8
  81.7 1.3 copy-start.11
  82.9 62.8 %copy-start.9 = (f32[4096]{0:T(1024)S(1)}, f32[4096]{0:T(1024)}, u32[]{:S(2)}) copy-start(f32[4096]{0:T(1024)} %param.20) | copy-start | bytes 49156
  82.9 62.8 %copy-start.10 = (f32[4096]{0:T(1024)S(1)}, f32[4096]{0:T(1024)}, u32[]{:S(2)}) copy-start(f32[4096]{0:T(1024)} %param.19) | copy-start | bytes 49156
  82.9 62.8 %copy-start.12 = (f32[768]{0:T(1024)S(1)}, f32[768]{0:T(1024)}, u32[]{:S(2)}) copy-start(f32[768]{0:T(1024)} %param.24) | copy-start | bytes 9220
Sparse Core Ops, SparseCore 0:
  9.0 69.1 all-gather.2
  80.4 93.6 all-gather.4
  180.3 65.2 reduce-scatter.1

commit v18 on v16

--- a/solution.py
+++ b/solution.py
@@ -108,7 +108,7 @@
     hi_col = lo_col + own_cached[:, None]
     start_col = (jnp.arange(tokens, dtype=jnp.int32) - positions + own_cached)[:, None]
     flat = lambda x: x.reshape(tokens, heads * HD)
-    rows = tokens // 2
+    rows = tokens // 4
     tile_block = pl.BlockSpec((rows, HD), lambda h, i: (i, h))
     row_block = pl.BlockSpec((tokens, HD), lambda h, i: (0, h))
     page_block = lambda part: pl.BlockSpec((page_count, 1, page_len, HD), lambda h, i: (0, part, 0, h))
@@ -117,7 +117,7 @@
     keys_seen = page_count * page_len + tokens
     out = pl.pallas_call(
         attention_kernel,
-        grid=(heads, 2),
+        grid=(heads, 4),
         in_specs=[tile_block, page_block(0), page_block(1), row_block, row_block]
         + [column(x) for x in extras],
         out_specs=tile_block,

time: 246 us -> 246 us (level)
  transfers between devices with their start and end apart: 5 -> 5, of which waited for: 4 -> 4; matrix products, arithmetic and copies ran while one was open for 24% -> 24% of each run, Pallas kernels for 4% -> 5%
where the time goes in v18:
time: 246 us
  waiting for transfers between devices  144 us (59%)
  matrix products  36.9 us (15%)
  local copies, waits for them, and re-layouts  19.9 us (8%)
  between operations  13.3 us (5%)
  starting transfers between devices  12.6 us (5%)
  Pallas kernels  11.4 us (5%)
  other arithmetic  7.99 us (3%)
    reduce_scatter x1, waiting for transfers between devices, shards(): lax.psum_scatter((attention_part + feed_part + bias_row).astype(jnp.bfloa...  65.3 us
    all_gather x1, waiting for transfers between devices, shards(): gathered = lax.all_gather(states, 'head', axis=1, tiled=True)  37.1 us
    all_to_all x1, waiting for transfers between devices, gather_by_all_to_all(): return lax.all_to_all(copies, axis, split_axis=0, concat_axis=0, tiled=True)  23.3 us
    dot_general x1, matrix products, feed(): jnp.dot(hidden, down_weight, preferred_element_type=jnp.float32)  21.6 us
    all_to_all x1, waiting for transfers between devices, share_pages(): lax.all_to_all(grouped, 'head', split_axis=3, concat_axis=0, tiled=True)  16.5 us
    pallas_call x1, Pallas kernels, attend_kernel(): pl.pallas_call(attention_kernel, grid=(heads, 4), in_specs=[tile_block, p...  11.4 us
    dot_general x1, matrix products, shards(): joined = jnp.dot(pre_normed, qkv_full, preferred_element_type=jnp.float32)  9.16 us
    all_to_all x1, starting transfers between devices, gather_by_all_to_all(): return lax.all_to_all(copies, axis, split_axis=0, concat_axis=0, tiled=True)  8.17 us
  transfers between devices with their start and end apart: 5, of which 4 were waited for; matrix products, arithmetic and copies ran while one was open for 24% of the time, Pallas kernels for 5%

profile of v18, /device:TPU:0, one launch (start us, length us, event | category | flops | bytes accessed | tf_op | source)
XLA Modules:
  0.0 245.7 jit_solution(16228331965128498526)
XLA Ops:
  6.5 0.0 all-gather.3.cloned.1.call-start
  6.5 0.7 all-gather.3.cloned.1.call-update
  7.3 4.2 %broadcast_in_dim.38 = bf16[8,512,768]{2,1,0:T(8,128)(2,1)} broadcast(bf16[512,768]{1,0:T(8,128)(2,1)} %param.23), dimensions={1,2} | broadcast | bytes 7077888 | tf_op jit(solution)/shard_map/broadcast_in_dim | solution.py:144
  11.4 0.0 copy-start.13
  11.4 0.0 copy-start.3
  11.4 0.0 copy-start.2
  11.4 0.0 copy-start.6
  11.5 8.2 %all-to-all-start = ((bf16[8,512,768]{2,1,0:T(8,128)(2,1)}), bf16[8,512,768]{2,1,0:T(8,128)(2,1)}, u32[]{:S(2)}, u32[]{:S(2)}) async-start(bf16[8,512,768]{2,1,0:T(8,128)(2,1)} %broadcast_in_dim.38), calls=%async_computation | async-start | bytes 12582912 | tf_op jit(solution)/shard_map/all_to_all | solution.py:147
  19.6 0.0 all-gather.5.cloned.1.call-start
  19.7 0.7 all-gather.5.cloned.1.call-update
  20.4 0.0 copy-done.13
  20.4 0.1 eq.33
  20.5 0.1 reshape.193
  20.5 0.0 copy-done.3
  20.6 0.1 convert_reduce_fusion.1
  20.7 0.2 reduce-window.8
  20.9 0.0 copy-done.2
  20.9 0.7 fusion.106
  21.5 0.1 select_reduce_fusion.1
  21.6 1.3 fusion.70
  22.9 1.3 fusion.71
  24.3 0.9 copy.55.hi_col
  25.2 0.9 copy.56.start_col
  26.0 0.9 copy.54.lo_col
  26.9 0.0 copy-done.6
  26.9 0.1 compare_reduce_fusion
  27.0 0.1 fusion.69
  27.1 37.1 %all-gather.3.cloned.1.call-done = bf16[512,4096]{1,0:T(8,128)(2,1)} async-done(((bf16[512,256]{1,0:T(8,128)(2,1)}), bf16[512,4096]{1,0:T(8,128)(2,1)}) %all-gather.3.cloned.1.call-update) | async-done | bytes 4194320 | tf_op jit(solution)/shard_map/all_gather | solution.py:170
  64.2 0.0 copy-start
  64.2 3.0 %convert_reduce_fusion = f32[512]{0:T(512)S(1)} fusion(bf16[512,4096]{1,0:T(8,128)(2,1)} %all-gather.3.cloned.1.call-done), kind=kLoop, calls=%fused_computation.2 | loop fusion | flops 4193792 | bytes 4196352 | tf_op jit(solution)/shard_map/reduce_sum | solution.py:16
  67.1 0.5 copy-done
  67.6 0.0 copy-start.7
  67.6 1.2 fusion.8
  68.8 0.0 copy-done.7
  68.9 0.0 copy-done.8
  68.9 0.0 copy-done.11
  68.9 0.0 copy-start.1
  68.9 21.6 %convolution_convert_fusion = bf16[512,4096]{1,0:T(8,128)(2,1)} fusion(bf16[1024,4096]{1,0:T(8,128)(2,1)} %param.29, bf16[4096,1024]{1,0:T(8,128)(2,1)} %param.27, bf16[512,4096]{1,0:T(8,128)(2,1)} %all-gather.3.cloned.1.call-done, f32[4096]{0:T(1024)S(1)} %copy-done.7, f32[4096]{0:T(1024)S(1)} %copy-done.8, f32[512]{0:T(512)S(1)} %add_rsqrt_fusion, ...), kind=kOutput, calls=%fused_computation.13 | convolution fusion | flops 8639217664 | bytes 25206784 | tf_op jit(solution)/shard_map/dot_general | solution.py:183
  90.5 0.0 copy-done.1
  90.5 1.8 copy.63
  92.3 23.3 %all-to-all-done = bf16[8,512,768]{2,1,0:T(8,128)(2,1)} async-done(((bf16[8,512,768]{2,1,0:T(8,128)(2,1)}), bf16[8,512,768]{2,1,0:T(8,128)(2,1)}, u32[]{:S(2)}, u32[]{:S(2)}) %all-to-all-start) | async-done | bytes 6291488 | tf_op jit(solution)/shard_map/all_to_all | solution.py:147
  115.6 0.0 copy-start.12
  115.6 4.4 %all-to-all-start.1 = ((bf16[9,2,16,16,256]{4,2,1,0,3:T(8,128)(2,1)}), bf16[9,2,16,16,256]{4,2,1,0,3:T(8,128)(2,1)S(1)}, u32[]{:S(2)}, u32[]{:S(2)}) async-start(bf16[9,2,16,16,256]{4,2,1,0,3:T(8,128)(2,1)} %bitcast.48), calls=%async_computation.1 | async-start | bytes 4718592 | tf_op jit(solution)/shard_map/all_to_all | solution.py:138
  120.0 0.0 reduce-scatter.2.cloned.1.call-start
  120.1 0.0 copy-done.4
  120.1 0.0 copy-done.5
  120.1 0.3 add_dynamic-update-slice_fusion
  120.4 0.2 multiply_cosine_fusion
  120.6 0.0 copy-done.9
  120.6 0.0 copy-done.10
  120.6 0.0 copy-done.12
  120.6 9.2 %fusion.35 = f32[512,768]{1,0:T(8,128)} fusion(bf16[4096,768]{1,0:T(8,128)(2,1)} %bitcast, bf16[512,4096]{1,0:T(8,128)(2,1)} %all-gather.3.cloned.1.call-done, f32[4096]{0:T(1024)S(1)} %copy-done.9, f32[4096]{0:T(1024)S(1)} %copy-done.10, f32[512]{0:T(512)S(1)} %add_rsqrt_fusion, f32[512]{0:T(512)S(1)} %broadcast_multiply_fusion.1, f32[768]{0:T(1024)S(1)} %copy-done.12), kind=kOutput, calls=%fused_computation.44 | convolution fusion | flops 3234201600 | bytes 12098560 | tf_op jit(solution)/shard_map/dot_general | solution.py:188
  129.7 3.0 %copy.48 = f32[512,768]{0,1:T(8,128)} copy(f32[512,768]{1,0:T(8,128)} %fusion.35) | data formatting | bytes 3145728 | tf_op jit(solution)/shard_map/add | solution.py:189
  132.8 1.1 slice.76
  133.9 1.3 slice_bitcast_fusion
  135.3 0.8 copy.57.q_ref
  136.1 0.8 copy.58.kn_ref
  137.0 0.8 copy.59.vn_ref
  137.8 16.5 %all-to-all-done.1 = bf16[9,2,16,16,256]{4,2,1,0,3:T(8,128)(2,1)S(1)} async-done(((bf16[9,2,16,16,256]{4,2,1,0,3:T(8,128)(2,1)}), bf16[9,2,16,16,256]{4,2,1,0,3:T(8,128)(2,1)S(1)}, u32[]{:S(2)}, u32[]{:S(2)}) %all-to-all-start.1) | async-done | bytes 2359328 | tf_op jit(solution)/shard_map/all_to_all | solution.py:138
  154.3 2.0 gather_fusion
  156.4 11.4 %shard_map.172 = bf16[512,256]{1,0:T(8,128)(2,1)} custom-call(bf16[512,256]{1,0:T(8,128)(2,1)} %copy.57.q_ref, bf16[128,2,16,256]{3,2,1,0:T(8,128)(2,1)} %gather_fusion, bf16[128,2,16,256]{3,2,1,0:T(8,128)(2,1)} %gather_fusion, bf16[512,256]{1,0:T(8,128)(2,1)} %copy.58.kn_ref, bf16[512,256]{1,0:T(8,128)(2,1)} %copy.59.vn_ref, s32[512,1]{1,0:T(8,128)} %copy.54.lo_col, ...), custom_call_target="tpu_custom_call" | custom-call | flops 1342177280 | bytes 3145728 | tf_op jit(solution)/shard_map/pallas_call | solution.py:118
  167.7 6.1 %add_convert_fusion = bf16[512,4096]{1,0:T(8,128)(2,1)} fusion(bf16[512,4096]{1,0:T(8,128)(2,1)} %convolution_convert_fusion, bf16[512,256]{1,0:T(8,128)(2,1)} %shard_map.172, bf16[256,4096]{1,0:T(8,128)(2,1)} %all-gather.5.cloned.1.call-done, f32[4096]{0:T(1024)S(1)} %add_dynamic-update-slice_fusion), kind=kOutput, calls=%fused_computation.12 | convolution fusion | flops 1082130432 | bytes 10764288 | tf_op jit(solution)/shard_map/dot_general | solution.py:205
  173.8 0.0 reduce-scatter.2.cloned.1.call-update
  173.9 65.3 %reduce-scatter.2.cloned.1.call-done = bf16[512,256]{1,0:T(8,128)(2,1)} async-done(((bf16[512,4096]{1,0:T(8,128)(2,1)}), bf16[512,256]{1,0:T(8,128)(2,1)}) %reduce-scatter.2.cloned.1.call-update) | async-done | bytes 262160 | tf_op jit(solution)/shard_map/reduce_scatter | solution.py:212
  (20 shorter events, 0.2 us)
Async XLA Ops:
  6.5 57.6 %all-gather.3.cloned.1.call-start = ((), (), s32[]{:S(2)}) async-start(), calls=%async_computation.3 | async-start | bytes 4456448 | tf_op jit(solution)/shard_map/all_gather | solution.py:170
  11.4 8.9 %copy-start.13 = (s32[2,64]{1,0:T(2,128)S(1)}, s32[2,64]{1,0:T(2,128)}, u32[]{:S(2)}) copy-start(s32[2,64]{1,0:T(2,128)} %param.34) | copy-start | bytes 1540
  11.4 9.1 %copy-start.3 = (s32[512]{0:T(512)S(1)}, s32[512]{0:T(512)}, u32[]{:S(2)}) copy-start(s32[512]{0:T(512)} %param.32) | copy-start | bytes 6148
  11.4 9.4 %copy-start.2 = (s32[2]{0:T(128)S(1)}, s32[2]{0:T(128)}, u32[]{:S(2)}) copy-start(s32[2]{0:T(128)} %param.33) | copy-start | bytes 28
  11.4 15.4 %copy-start.6 = (s32[8,2]{0,1:T(2,128)S(1)}, s32[8,2]{0,1:T(2,128)}, u32[]{:S(2)}) copy-start(s32[8,2]{0,1:T(2,128)} %param.35) | copy-start | bytes 196
  11.5 104.1 %all-to-all-start = ((bf16[8,512,768]{2,1,0:T(8,128)(2,1)}), bf16[8,512,768]{2,1,0:T(8,128)(2,1)}, u32[]{:S(2)}, u32[]{:S(2)}) async-start(bf16[8,512,768]{2,1,0:T(8,128)(2,1)} %broadcast_in_dim.38), calls=%async_computation | async-start | bytes 12582912 | tf_op jit(solution)/shard_map/all_to_all | solution.py:147
  19.6 148.1 %all-gather.5.cloned.1.call-start = ((), (), s32[]{:S(2)}) async-start(), calls=%async_computation.4 | async-start | bytes 2359296 | tf_op jit(solution)/shard_map/all_gather | solution.py:172
  64.2 3.4 %copy-start = (bf16[512,4096]{1,0:T(8,128)(2,1)S(1)}, bf16[512,4096]{1,0:T(8,128)(2,1)}, u32[]{:S(2)}) copy-start(bf16[512,4096]{1,0:T(8,128)(2,1)} %all-gather.3.cloned.1.call-done) | copy-start | bytes 12582916
  67.6 1.2 copy-start.7
  67.6 1.2 copy-start.8
  67.6 1.3 copy-start.11
  68.9 21.6 %copy-start.1 = (bf16[9,2,16,4096]{3,2,1,0:T(8,128)(2,1)S(1)}, bf16[9,2,16,4096]{3,2,1,0:T(8,128)(2,1)}, u32[]{:S(2)}) copy-start(bf16[9,2,16,4096]{3,2,1,0:T(8,128)(2,1)} %param.31) | copy-start | bytes 7077892
  115.6 4.5 %copy-start.4 = (f32[256]{0:T(256)S(1)}, f32[256]{0:T(256)}, u32[]{:S(2)}) copy-start(f32[256]{0:T(256)} %param.26) | copy-start | bytes 3076
  115.6 4.5 %copy-start.5 = (f32[256]{0:T(256)S(1)}, f32[256]{0:T(256)}, u32[]{:S(2)}) copy-start(f32[256]{0:T(256)} %param.30) | copy-start | bytes 3076
  115.6 5.0 %copy-start.9 = (f32[4096]{0:T(1024)S(1)}, f32[4096]{0:T(1024)}, u32[]{:S(2)}) copy-start(f32[4096]{0:T(1024)} %param.20) | copy-start | bytes 49156
  115.6 5.0 %copy-start.10 = (f32[4096]{0:T(1024)S(1)}, f32[4096]{0:T(1024)}, u32[]{:S(2)}) copy-start(f32[4096]{0:T(1024)} %param.19) | copy-start | bytes 49156
  115.6 5.0 %copy-start.12 = (f32[768]{0:T(1024)S(1)}, f32[768]{0:T(1024)}, u32[]{:S(2)}) copy-start(f32[768]{0:T(1024)} %param.24) | copy-start | bytes 9220
  115.6 38.7 %all-to-all-start.1 = ((bf16[9,2,16,16,256]{4,2,1,0,3:T(8,128)(2,1)}), bf16[9,2,16,16,256]{4,2,1,0,3:T(8,128)(2,1)S(1)}, u32[]{:S(2)}, u32[]{:S(2)}) async-start(bf16[9,2,16,16,256]{4,2,1,0,3:T(8,128)(2,1)} %bitcast.48), calls=%async_computation.1 | async-start | bytes 4718592 | tf_op jit(solution)/shard_map/all_to_all | solution.py:138
  120.0 119.1 %reduce-scatter.2.cloned.1.call-start = ((), (), s32[]{:S(2)}) async-start(), calls=%async_computation.5 | async-start | bytes 4456448 | tf_op jit(solution)/shard_map/reduce_scatter | solution.py:212
Sparse Core Ops, SparseCore 0:
  9.0 55.1 all-gather.2
  66.3 97.8 all-gather.4
  174.0 65.1 reduce-scatter.1
